TPU v7x, 256 devices: a whole 4x4x8 slice. The times are simulated.
256 devices in a mesh: seq: 64 (over x, z, core), head: 4 (over y).
Axes of the slice: x: 4, y: 4, z: 8, core: 2. Of those that a mesh axis runs over, the one named last changes fastest.
Arguments:
- acceptance_linear: bfloat16 [32768, 4096], P(('seq', 'head')), may hold values from -6 to 6
- lookup_linear: bfloat16 [32768, 4096], P(('seq', 'head')), may hold values from -6 to 6
- payload_linear: bfloat16 [32768, 4096], P(('seq', 'head')), may hold values from -6 to 6
- valve_linear: bfloat16 [32768, 4096], P(('seq', 'head')), may hold values from -6 to 6
- layer_entries: bfloat16 [32768, 4096], P(('seq', 'head')), may hold values from -6 to 6
- prompt_label: int32 [32768], replicated, may hold values from 0 to 15, never falling along the last dimension, each value on 1 to 8192 neighbouring positions
- fading_baseline: float32 [4096], replicated, may hold values from -12 to -3
- previous_mixing_share: float32 [4096], replicated, may hold values from 0.2 to 0.9
- fading_lower_map: bfloat16 [4096, 128], replicated, may hold values from -0.09375 to 0.09375
- fading_raise_map: bfloat16 [128, 4096], replicated, may hold values from -0.5 to 0.5
- diagonal_reward: float32 [4096], replicated, may hold values from -0.5 to 1
- cluster_gain_vector: float32 [4096], replicated, may hold values from 0.25 to 1.75
- cluster_mean_shift_add: float32 [4096], replicated, may hold values from -1.5 to 1.5
Outputs:
- gated: bfloat16 [32768, 4096], P(('seq', 'head'))
All inputs are finite; a program needn't handle non-finite values.
Results may differ from a plain program's by a relative error of at most 0.001.
The roundings to bfloat16 on the way count: a program that leaves them out, or rounds other values in their place, can miss the bound.
Values may be sent and summed in bfloat16 or wider, within the bound.
No kernel may reach another device: no remote copies, remote signals or barrier semaphores. Data moves between devices by JAX's collectives and lax.ppermute only.
A program may use at most 192 MiB of HBM per device.

v0:
```python
import jax
import jax.numpy as jnp
from jax import lax
from jax.sharding import PartitionSpec as P

ATTENTION_SPAN = 64
CH = 128


norm_eps = 0.00064
decay_floor = -0.5
highest = lax.Precision.HIGHEST


def shifted(value, axis, by):
    size = lax.axis_size(axis)
    pairs = [(i, i + by) for i in range(size) if 0 <= i + by < size]
    return lax.ppermute(value, axis, pairs)


def earlier_segment(prompt_label, position):
    earlier = lax.dynamic_slice_in_dim(prompt_label, jnp.maximum(position - 1, 0), 1, 0)
    return jnp.where(position > 0, earlier, jnp.full_like(earlier, -1))


def local(
    acceptance_linear,
    lookup_linear,
    payload_linear,
    valve_linear,
    layer_entries,
    prompt_label,
    fading_baseline,
    previous_mixing_share,
    fading_lower_map,
    fading_raise_map,
    diagonal_reward,
    cluster_gain_vector,
    cluster_mean_shift_add,
):
    head_count = lax.axis_size("head")
    seq_index = lax.axis_index("seq")
    head_index = lax.axis_index("head")
    row_count = layer_entries.shape[0]
    block_start = (seq_index * head_count + head_index) * row_count
    own_seg = lax.dynamic_slice_in_dim(prompt_label, block_start, row_count, 0)
    prior_seg = jnp.concatenate([earlier_segment(prompt_label, block_start), own_seg[:-1]])
    edge_row = shifted(layer_entries[-1:], ("seq", "head"), 1)
    prev_rows = jnp.concatenate([edge_row, layer_entries[:-1]], axis=0)
    prev_rows = jnp.where((prior_seg == own_seg)[:, None], prev_rows, jnp.zeros_like(prev_rows))
    current = layer_entries.astype(jnp.float32)
    blended_input = (
        current + (prev_rows.astype(jnp.float32) - current) * previous_mixing_share
    ).astype(jnp.bfloat16)
    decay_hidden_rows = jnp.tanh(
        jnp.dot(blended_input, fading_lower_map, preferred_element_type=jnp.float32)
    ).astype(jnp.bfloat16)
    decay_score = fading_baseline + jnp.dot(
        decay_hidden_rows, fading_raise_map, preferred_element_type=jnp.float32
    )
    log_decay = jnp.maximum(-jnp.exp(decay_score), decay_floor).astype(jnp.bfloat16)
    query_head, key_head, value_head, decay_head = (
        lax.all_to_all(acceptance_linear, "head", split_axis=1, concat_axis=0, tiled=True),
        lax.all_to_all(lookup_linear, "head", split_axis=1, concat_axis=0, tiled=True),
        lax.all_to_all(payload_linear, "head", split_axis=1, concat_axis=0, tiled=True),
        lax.all_to_all(log_decay, "head", split_axis=1, concat_axis=0, tiled=True),
    )
    tokens = query_head.shape[0]
    partition_extent = query_head.shape[1]
    local_heads = partition_extent // ATTENTION_SPAN
    stretches = tokens // CH
    seq_start = seq_index * tokens
    seg_block = lax.dynamic_slice_in_dim(prompt_label, seq_start, tokens, 0).reshape(stretches, CH)
    seg_before = earlier_segment(prompt_label, seq_start)
    stretch_prior = jnp.concatenate([seg_before, seg_block[:-1, -1]])
    feature_start = head_index * partition_extent
    partition_reward = lax.dynamic_slice_in_dim(
        diagonal_reward, feature_start, partition_extent, 0
    ).reshape(local_heads, ATTENTION_SPAN)
    gain_local = lax.dynamic_slice_in_dim(
        cluster_gain_vector, feature_start, partition_extent, 0
    ).reshape(local_heads, ATTENTION_SPAN)
    bias_local = lax.dynamic_slice_in_dim(
        cluster_mean_shift_add, feature_start, partition_extent, 0
    ).reshape(local_heads, ATTENTION_SPAN)
    blocked = (stretches, CH, local_heads, ATTENTION_SPAN)
    request_vectors = query_head.reshape(blocked).astype(jnp.float32)
    lookup_vectors = key_head.reshape(blocked).astype(jnp.float32)
    payload_vectors = value_head.reshape(blocked).astype(jnp.float32)
    decays = decay_head.reshape(blocked).astype(jnp.float32)
    cumulative = jnp.cumsum(decays, axis=1)
    before = cumulative - decays
    ending = cumulative[:, -1]
    scaled_query = request_vectors * jnp.exp(before)
    scaled_key = lookup_vectors * jnp.exp(-cumulative)
    scores = jnp.einsum("cthd,cshd->chts", scaled_query, scaled_key, precision=highest)
    causal = lax.broadcasted_iota(jnp.int32, (CH, CH), 0) > lax.broadcasted_iota(
        jnp.int32, (CH, CH), 1
    )
    allowed = causal[None] & (seg_block[:, :, None] == seg_block[:, None, :])
    scores = jnp.where(allowed[:, None], scores, jnp.zeros_like(scores))
    within = jnp.einsum("chts,cshd->cthd", scores, payload_vectors, precision=highest)
    diagonal_contribution = (
        jnp.sum(request_vectors * partition_reward * lookup_vectors, axis=3, keepdims=True)
        * payload_vectors
    )
    keep_last = (seg_block == seg_block[:, -1:]).astype(jnp.float32)
    tail_keys = lookup_vectors * jnp.exp(ending[:, None] - cumulative) * keep_last[:, :, None, None]
    stretch_state = jnp.einsum("cthd,cthe->chde", tail_keys, payload_vectors, precision=highest)
    stretch_decay = (
        jnp.exp(ending) * (seg_block[:, -1] == stretch_prior).astype(jnp.float32)[:, None, None]
    )

    def advance(carry_state, pieces):
        factor, new_part = pieces
        return (factor[:, :, None] * carry_state + new_part, carry_state)

    zero_state = jnp.zeros((local_heads, ATTENTION_SPAN, ATTENTION_SPAN), jnp.float32)
    span_state, local_start = lax.scan(advance, zero_state, (stretch_decay, stretch_state))

    def multiply(product, factor):
        return (product * factor, product)

    span_decay, decay_before = lax.scan(
        multiply, jnp.ones((local_heads, ATTENTION_SPAN), jnp.float32), stretch_decay
    )

    def relay(iteration, incoming):
        return shifted(span_decay[:, :, None] * incoming + span_state, "seq", 1)

    incoming = lax.fori_loop(0, lax.axis_size("seq") - 1, relay, zero_state)
    start_state = local_start + decay_before[:, :, :, None] * incoming[None]
    keep_first = (seg_block == stretch_prior[:, None]).astype(jnp.float32)
    carried = jnp.einsum(
        "cthd,chde->cthe",
        scaled_query * keep_first[:, :, None, None],
        start_state,
        precision=highest,
    )
    mixing = within + diagonal_contribution + carried
    center = mixing - jnp.mean(mixing, axis=3, keepdims=True)
    spread = jnp.mean(center * center, axis=3, keepdims=True)
    normed = center * lax.rsqrt(spread + norm_eps) * gain_local + bias_local
    normed = normed.astype(jnp.bfloat16).reshape(tokens, partition_extent)
    returned = lax.all_to_all(normed, "head", split_axis=0, concat_axis=1, tiled=True)
    return (returned.astype(jnp.float32) * jax.nn.silu(valve_linear.astype(jnp.float32))).astype(
        jnp.bfloat16
    )


def solution(mesh):
    return jax.shard_map(
        local,
        mesh=mesh,
        in_specs=(
            P(("seq", "head"), None),
            P(("seq", "head"), None),
            P(("seq", "head"), None),
            P(("seq", "head"), None),
            P(("seq", "head"), None),
            P(),
            P(),
            P(),
            P(),
            P(),
            P(),
            P(),
            P(),
        ),
        out_specs=P(("seq", "head"), None),
        check_vma=False,
    )
```

profile of v0, /device:TPU:6, one launch (start us, length us, event | category | flops | bytes accessed | tf_op | source)
XLA Modules:
  0.0 969.8 jit_solution(17044973248832983668)
XLA Ops:
  79.1 11.1 %exponential_multiply_fusion = (f32[4,128,16,64]{3,2,1,0:T(8,128)}, f32[4,128,16,64]{3,2,1,0:T(8,128)}, f32[4,128,16,64]{3,2,1,0:T(8,128)}, f32[4,128,16,64]{3,2,1,0:T(8,128)}) fusion(f32[4,128,16,64]{3,2,1,0:T(8,128)} %copy.45, f32[4,128,16,64]{3,2,1,0:T(8,128)} %copy-done.2, f32[4,128]{1,0:T(4,128)S(1)} %get-tuple-element.152, ...), kind=kLoop, calls=%fused_computation.22 | loop fusion | flops 4194304 | bytes 16797696 | tf_op jit(solution)/shard_map/mul | solution.py:95
  106.8 16.4 %fusion.9 = f32[4,16,128,128]{3,2,1,0:T(8,128)} fusion(f32[4,128,16,64]{3,2,1,0:T(8,128)} %get-tuple-element.146, f32[4,128,16,64]{3,2,1,0:T(8,128)} %get-tuple-element.149), kind=kOutput, calls=%fused_computation.16 | convolution fusion | flops 805306368 | bytes 8388608 | tf_op jit(solution)/shard_map/cthd,cshd->chts/dot_general | solution.py:96
  123.2 807.3 %while.36 = (s32[]{:T(128)}, f32[16,64,64]{2,1,0:T(8,128)S(1)}, f32[16,64]{1,0:T(8,128)S(1)}, f32[16,64,64]{2,1,0:T(8,128)S(1)}, s32[]{:T(128)}) while((s32[]{:T(128)}, f32[16,64,64]{2,1,0:T(8,128)S(1)}, f32[16,64]{1,0:T(8,128)S(1)}, f32[16,64,64]{2,1,0:T(8,128)S(1)}, s32[]{:T(128)}) %tuple.66), condition=%wide.region_7.8_spmd, body=%wide.region_6.7_spmd.sunk | while | flops 131074 | bytes 1839205 | solution.py:131
  125.3 10.7 %collective-permute-done = f32[16,64,64]{2,1,0:T(8,128)S(1)} collective-permute-done((f32[16,64,64]{2,1,0:T(8,128)S(1)}, f32[16,64,64]{2,1,0:T(8,128)S(1)}, u32[]{:S(2)}, u32[]{:S(2)}) %collective-permute-start) | collective-permute-done | bytes 262176 | tf_op jit(solution)/shard_map/while/body/eval_jaxpr/ppermute | solution.py:18
  138.1 10.7 %collective-permute-done = f32[16,64,64]{2,1,0:T(8,128)S(1)} collective-permute-done((f32[16,64,64]{2,1,0:T(8,128)S(1)}, f32[16,64,64]{2,1,0:T(8,128)S(1)}, u32[]{:S(2)}, u32[]{:S(2)}) %collective-permute-start) | collective-permute-done | bytes 262176 | tf_op jit(solution)/shard_map/while/body/eval_jaxpr/ppermute | solution.py:18
  151.0 10.7 %collective-permute-done = f32[16,64,64]{2,1,0:T(8,128)S(1)} collective-permute-done((f32[16,64,64]{2,1,0:T(8,128)S(1)}, f32[16,64,64]{2,1,0:T(8,128)S(1)}, u32[]{:S(2)}, u32[]{:S(2)}) %collective-permute-start) | collective-permute-done | bytes 262176 | tf_op jit(solution)/shard_map/while/body/eval_jaxpr/ppermute | solution.py:18
  163.8 10.7 %collective-permute-done = f32[16,64,64]{2,1,0:T(8,128)S(1)} collective-permute-done((f32[16,64,64]{2,1,0:T(8,128)S(1)}, f32[16,64,64]{2,1,0:T(8,128)S(1)}, u32[]{:S(2)}, u32[]{:S(2)}) %collective-permute-start) | collective-permute-done | bytes 262176 | tf_op jit(solution)/shard_map/while/body/eval_jaxpr/ppermute | solution.py:18
  176.6 10.7 %collective-permute-done = f32[16,64,64]{2,1,0:T(8,128)S(1)} collective-permute-done((f32[16,64,64]{2,1,0:T(8,128)S(1)}, f32[16,64,64]{2,1,0:T(8,128)S(1)}, u32[]{:S(2)}, u32[]{:S(2)}) %collective-permute-start) | collective-permute-done | bytes 262176 | tf_op jit(solution)/shard_map/while/body/eval_jaxpr/ppermute | solution.py:18
  189.4 10.7 %collective-permute-done = f32[16,64,64]{2,1,0:T(8,128)S(1)} collective-permute-done((f32[16,64,64]{2,1,0:T(8,128)S(1)}, f32[16,64,64]{2,1,0:T(8,128)S(1)}, u32[]{:S(2)}, u32[]{:S(2)}) %collective-permute-start) | collective-permute-done | bytes 262176 | tf_op jit(solution)/shard_map/while/body/eval_jaxpr/ppermute | solution.py:18
  202.2 10.7 %collective-permute-done = f32[16,64,64]{2,1,0:T(8,128)S(1)} collective-permute-done((f32[16,64,64]{2,1,0:T(8,128)S(1)}, f32[16,64,64]{2,1,0:T(8,128)S(1)}, u32[]{:S(2)}, u32[]{:S(2)}) %collective-permute-start) | collective-permute-done | bytes 262176 | tf_op jit(solution)/shard_map/while/body/eval_jaxpr/ppermute | solution.py:18
  215.0 10.7 %collective-permute-done = f32[16,64,64]{2,1,0:T(8,128)S(1)} collective-permute-done((f32[16,64,64]{2,1,0:T(8,128)S(1)}, f32[16,64,64]{2,1,0:T(8,128)S(1)}, u32[]{:S(2)}, u32[]{:S(2)}) %collective-permute-start) | collective-permute-done | bytes 262176 | tf_op jit(solution)/shard_map/while/body/eval_jaxpr/ppermute | solution.py:18
  227.8 10.7 %collective-permute-done = f32[16,64,64]{2,1,0:T(8,128)S(1)} collective-permute-done((f32[16,64,64]{2,1,0:T(8,128)S(1)}, f32[16,64,64]{2,1,0:T(8,128)S(1)}, u32[]{:S(2)}, u32[]{:S(2)}) %collective-permute-start) | collective-permute-done | bytes 262176 | tf_op jit(solution)/shard_map/while/body/eval_jaxpr/ppermute | solution.py:18
  240.7 10.7 %collective-permute-done = f32[16,64,64]{2,1,0:T(8,128)S(1)} collective-permute-done((f32[16,64,64]{2,1,0:T(8,128)S(1)}, f32[16,64,64]{2,1,0:T(8,128)S(1)}, u32[]{:S(2)}, u32[]{:S(2)}) %collective-permute-start) | collective-permute-done | bytes 262176 | tf_op jit(solution)/shard_map/while/body/eval_jaxpr/ppermute | solution.py:18
  253.5 10.7 %collective-permute-done = f32[16,64,64]{2,1,0:T(8,128)S(1)} collective-permute-done((f32[16,64,64]{2,1,0:T(8,128)S(1)}, f32[16,64,64]{2,1,0:T(8,128)S(1)}, u32[]{:S(2)}, u32[]{:S(2)}) %collective-permute-start) | collective-permute-done | bytes 262176 | tf_op jit(solution)/shard_map/while/body/eval_jaxpr/ppermute | solution.py:18
  266.3 10.7 %collective-permute-done = f32[16,64,64]{2,1,0:T(8,128)S(1)} collective-permute-done((f32[16,64,64]{2,1,0:T(8,128)S(1)}, f32[16,64,64]{2,1,0:T(8,128)S(1)}, u32[]{:S(2)}, u32[]{:S(2)}) %collective-permute-start) | collective-permute-done | bytes 262176 | tf_op jit(solution)/shard_map/while/body/eval_jaxpr/ppermute | solution.py:18
  279.1 10.7 %collective-permute-done = f32[16,64,64]{2,1,0:T(8,128)S(1)} collective-permute-done((f32[16,64,64]{2,1,0:T(8,128)S(1)}, f32[16,64,64]{2,1,0:T(8,128)S(1)}, u32[]{:S(2)}, u32[]{:S(2)}) %collective-permute-start) | collective-permute-done | bytes 262176 | tf_op jit(solution)/shard_map/while/body/eval_jaxpr/ppermute | solution.py:18
  291.9 10.7 %collective-permute-done = f32[16,64,64]{2,1,0:T(8,128)S(1)} collective-permute-done((f32[16,64,64]{2,1,0:T(8,128)S(1)}, f32[16,64,64]{2,1,0:T(8,128)S(1)}, u32[]{:S(2)}, u32[]{:S(2)}) %collective-permute-start) | collective-permute-done | bytes 262176 | tf_op jit(solution)/shard_map/while/body/eval_jaxpr/ppermute | solution.py:18
  304.7 10.7 %collective-permute-done = f32[16,64,64]{2,1,0:T(8,128)S(1)} collective-permute-done((f32[16,64,64]{2,1,0:T(8,128)S(1)}, f32[16,64,64]{2,1,0:T(8,128)S(1)}, u32[]{:S(2)}, u32[]{:S(2)}) %collective-permute-start) | collective-permute-done | bytes 262176 | tf_op jit(solution)/shard_map/while/body/eval_jaxpr/ppermute | solution.py:18
  317.5 10.7 %collective-permute-done = f32[16,64,64]{2,1,0:T(8,128)S(1)} collective-permute-done((f32[16,64,64]{2,1,0:T(8,128)S(1)}, f32[16,64,64]{2,1,0:T(8,128)S(1)}, u32[]{:S(2)}, u32[]{:S(2)}) %collective-permute-start) | collective-permute-done | bytes 262176 | tf_op jit(solution)/shard_map/while/body/eval_jaxpr/ppermute | solution.py:18
  330.4 10.7 %collective-permute-done = f32[16,64,64]{2,1,0:T(8,128)S(1)} collective-permute-done((f32[16,64,64]{2,1,0:T(8,128)S(1)}, f32[16,64,64]{2,1,0:T(8,128)S(1)}, u32[]{:S(2)}, u32[]{:S(2)}) %collective-permute-start) | collective-permute-done | bytes 262176 | tf_op jit(solution)/shard_map/while/body/eval_jaxpr/ppermute | solution.py:18
  343.2 10.7 %collective-permute-done = f32[16,64,64]{2,1,0:T(8,128)S(1)} collective-permute-done((f32[16,64,64]{2,1,0:T(8,128)S(1)}, f32[16,64,64]{2,1,0:T(8,128)S(1)}, u32[]{:S(2)}, u32[]{:S(2)}) %collective-permute-start) | collective-permute-done | bytes 262176 | tf_op jit(solution)/shard_map/while/body/eval_jaxpr/ppermute | solution.py:18
  356.0 10.7 %collective-permute-done = f32[16,64,64]{2,1,0:T(8,128)S(1)} collective-permute-done((f32[16,64,64]{2,1,0:T(8,128)S(1)}, f32[16,64,64]{2,1,0:T(8,128)S(1)}, u32[]{:S(2)}, u32[]{:S(2)}) %collective-permute-start) | collective-permute-done | bytes 262176 | tf_op jit(solution)/shard_map/while/body/eval_jaxpr/ppermute | solution.py:18
  368.8 10.7 %collective-permute-done = f32[16,64,64]{2,1,0:T(8,128)S(1)} collective-permute-done((f32[16,64,64]{2,1,0:T(8,128)S(1)}, f32[16,64,64]{2,1,0:T(8,128)S(1)}, u32[]{:S(2)}, u32[]{:S(2)}) %collective-permute-start) | collective-permute-done | bytes 262176 | tf_op jit(solution)/shard_map/while/body/eval_jaxpr/ppermute | solution.py:18
  381.6 10.7 %collective-permute-done = f32[16,64,64]{2,1,0:T(8,128)S(1)} collective-permute-done((f32[16,64,64]{2,1,0:T(8,128)S(1)}, f32[16,64,64]{2,1,0:T(8,128)S(1)}, u32[]{:S(2)}, u32[]{:S(2)}) %collective-permute-start) | collective-permute-done | bytes 262176 | tf_op jit(solution)/shard_map/while/body/eval_jaxpr/ppermute | solution.py:18
  394.4 10.7 %collective-permute-done = f32[16,64,64]{2,1,0:T(8,128)S(1)} collective-permute-done((f32[16,64,64]{2,1,0:T(8,128)S(1)}, f32[16,64,64]{2,1,0:T(8,128)S(1)}, u32[]{:S(2)}, u32[]{:S(2)}) %collective-permute-start) | collective-permute-done | bytes 262176 | tf_op jit(solution)/shard_map/while/body/eval_jaxpr/ppermute | solution.py:18
  407.2 10.7 %collective-permute-done = f32[16,64,64]{2,1,0:T(8,128)S(1)} collective-permute-done((f32[16,64,64]{2,1,0:T(8,128)S(1)}, f32[16,64,64]{2,1,0:T(8,128)S(1)}, u32[]{:S(2)}, u32[]{:S(2)}) %collective-permute-start) | collective-permute-done | bytes 262176 | tf_op jit(solution)/shard_map/while/body/eval_jaxpr/ppermute | solution.py:18
  420.0 10.7 %collective-permute-done = f32[16,64,64]{2,1,0:T(8,128)S(1)} collective-permute-done((f32[16,64,64]{2,1,0:T(8,128)S(1)}, f32[16,64,64]{2,1,0:T(8,128)S(1)}, u32[]{:S(2)}, u32[]{:S(2)}) %collective-permute-start) | collective-permute-done | bytes 262176 | tf_op jit(solution)/shard_map/while/body/eval_jaxpr/ppermute | solution.py:18
  432.9 10.7 %collective-permute-done = f32[16,64,64]{2,1,0:T(8,128)S(1)} collective-permute-done((f32[16,64,64]{2,1,0:T(8,128)S(1)}, f32[16,64,64]{2,1,0:T(8,128)S(1)}, u32[]{:S(2)}, u32[]{:S(2)}) %collective-permute-start) | collective-permute-done | bytes 262176 | tf_op jit(solution)/shard_map/while/body/eval_jaxpr/ppermute | solution.py:18
  445.7 10.7 %collective-permute-done = f32[16,64,64]{2,1,0:T(8,128)S(1)} collective-permute-done((f32[16,64,64]{2,1,0:T(8,128)S(1)}, f32[16,64,64]{2,1,0:T(8,128)S(1)}, u32[]{:S(2)}, u32[]{:S(2)}) %collective-permute-start) | collective-permute-done | bytes 262176 | tf_op jit(solution)/shard_map/while/body/eval_jaxpr/ppermute | solution.py:18
  458.5 10.7 %collective-permute-done = f32[16,64,64]{2,1,0:T(8,128)S(1)} collective-permute-done((f32[16,64,64]{2,1,0:T(8,128)S(1)}, f32[16,64,64]{2,1,0:T(8,128)S(1)}, u32[]{:S(2)}, u32[]{:S(2)}) %collective-permute-start) | collective-permute-done | bytes 262176 | tf_op jit(solution)/shard_map/while/body/eval_jaxpr/ppermute | solution.py:18
  471.3 10.7 %collective-permute-done = f32[16,64,64]{2,1,0:T(8,128)S(1)} collective-permute-done((f32[16,64,64]{2,1,0:T(8,128)S(1)}, f32[16,64,64]{2,1,0:T(8,128)S(1)}, u32[]{:S(2)}, u32[]{:S(2)}) %collective-permute-start) | collective-permute-done | bytes 262176 | tf_op jit(solution)/shard_map/while/body/eval_jaxpr/ppermute | solution.py:18
  484.1 10.7 %collective-permute-done = f32[16,64,64]{2,1,0:T(8,128)S(1)} collective-permute-done((f32[16,64,64]{2,1,0:T(8,128)S(1)}, f32[16,64,64]{2,1,0:T(8,128)S(1)}, u32[]{:S(2)}, u32[]{:S(2)}) %collective-permute-start) | collective-permute-done | bytes 262176 | tf_op jit(solution)/shard_map/while/body/eval_jaxpr/ppermute | solution.py:18
  496.9 10.7 %collective-permute-done = f32[16,64,64]{2,1,0:T(8,128)S(1)} collective-permute-done((f32[16,64,64]{2,1,0:T(8,128)S(1)}, f32[16,64,64]{2,1,0:T(8,128)S(1)}, u32[]{:S(2)}, u32[]{:S(2)}) %collective-permute-start) | collective-permute-done | bytes 262176 | tf_op jit(solution)/shard_map/while/body/eval_jaxpr/ppermute | solution.py:18
  509.7 10.7 %collective-permute-done = f32[16,64,64]{2,1,0:T(8,128)S(1)} collective-permute-done((f32[16,64,64]{2,1,0:T(8,128)S(1)}, f32[16,64,64]{2,1,0:T(8,128)S(1)}, u32[]{:S(2)}, u32[]{:S(2)}) %collective-permute-start) | collective-permute-done | bytes 262176 | tf_op jit(solution)/shard_map/while/body/eval_jaxpr/ppermute | solution.py:18
  522.6 10.7 %collective-permute-done = f32[16,64,64]{2,1,0:T(8,128)S(1)} collective-permute-done((f32[16,64,64]{2,1,0:T(8,128)S(1)}, f32[16,64,64]{2,1,0:T(8,128)S(1)}, u32[]{:S(2)}, u32[]{:S(2)}) %collective-permute-start) | collective-permute-done | bytes 262176 | tf_op jit(solution)/shard_map/while/body/eval_jaxpr/ppermute | solution.py:18
  561.0 10.7 %collective-permute-done = f32[16,64,64]{2,1,0:T(8,128)S(1)} collective-permute-done((f32[16,64,64]{2,1,0:T(8,128)S(1)}, f32[16,64,64]{2,1,0:T(8,128)S(1)}, u32[]{:S(2)}, u32[]{:S(2)}) %collective-permute-start) | collective-permute-done | bytes 262176 | tf_op jit(solution)/shard_map/while/body/eval_jaxpr/ppermute | solution.py:18
  573.8 10.7 %collective-permute-done = f32[16,64,64]{2,1,0:T(8,128)S(1)} collective-permute-done((f32[16,64,64]{2,1,0:T(8,128)S(1)}, f32[16,64,64]{2,1,0:T(8,128)S(1)}, u32[]{:S(2)}, u32[]{:S(2)}) %collective-permute-start) | collective-permute-done | bytes 262176 | tf_op jit(solution)/shard_map/while/body/eval_jaxpr/ppermute | solution.py:18
  625.1 10.7 %collective-permute-done = f32[16,64,64]{2,1,0:T(8,128)S(1)} collective-permute-done((f32[16,64,64]{2,1,0:T(8,128)S(1)}, f32[16,64,64]{2,1,0:T(8,128)S(1)}, u32[]{:S(2)}, u32[]{:S(2)}) %collective-permute-start) | collective-permute-done | bytes 262176 | tf_op jit(solution)/shard_map/while/body/eval_jaxpr/ppermute | solution.py:18
  637.9 10.7 %collective-permute-done = f32[16,64,64]{2,1,0:T(8,128)S(1)} collective-permute-done((f32[16,64,64]{2,1,0:T(8,128)S(1)}, f32[16,64,64]{2,1,0:T(8,128)S(1)}, u32[]{:S(2)}, u32[]{:S(2)}) %collective-permute-start) | collective-permute-done | bytes 262176 | tf_op jit(solution)/shard_map/while/body/eval_jaxpr/ppermute | solution.py:18
  689.1 10.7 %collective-permute-done = f32[16,64,64]{2,1,0:T(8,128)S(1)} collective-permute-done((f32[16,64,64]{2,1,0:T(8,128)S(1)}, f32[16,64,64]{2,1,0:T(8,128)S(1)}, u32[]{:S(2)}, u32[]{:S(2)}) %collective-permute-start) | collective-permute-done | bytes 262176 | tf_op jit(solution)/shard_map/while/body/eval_jaxpr/ppermute | solution.py:18
  701.9 10.7 %collective-permute-done = f32[16,64,64]{2,1,0:T(8,128)S(1)} collective-permute-done((f32[16,64,64]{2,1,0:T(8,128)S(1)}, f32[16,64,64]{2,1,0:T(8,128)S(1)}, u32[]{:S(2)}, u32[]{:S(2)}) %collective-permute-start) | collective-permute-done | bytes 262176 | tf_op jit(solution)/shard_map/while/body/eval_jaxpr/ppermute | solution.py:18
  753.2 10.7 %collective-permute-done = f32[16,64,64]{2,1,0:T(8,128)S(1)} collective-permute-done((f32[16,64,64]{2,1,0:T(8,128)S(1)}, f32[16,64,64]{2,1,0:T(8,128)S(1)}, u32[]{:S(2)}, u32[]{:S(2)}) %collective-permute-start) | collective-permute-done | bytes 262176 | tf_op jit(solution)/shard_map/while/body/eval_jaxpr/ppermute | solution.py:18
  766.0 10.7 %collective-permute-done = f32[16,64,64]{2,1,0:T(8,128)S(1)} collective-permute-done((f32[16,64,64]{2,1,0:T(8,128)S(1)}, f32[16,64,64]{2,1,0:T(8,128)S(1)}, u32[]{:S(2)}, u32[]{:S(2)}) %collective-permute-start) | collective-permute-done | bytes 262176 | tf_op jit(solution)/shard_map/while/body/eval_jaxpr/ppermute | solution.py:18
  804.5 10.7 %collective-permute-done = f32[16,64,64]{2,1,0:T(8,128)S(1)} collective-permute-done((f32[16,64,64]{2,1,0:T(8,128)S(1)}, f32[16,64,64]{2,1,0:T(8,128)S(1)}, u32[]{:S(2)}, u32[]{:S(2)}) %collective-permute-start) | collective-permute-done | bytes 262176 | tf_op jit(solution)/shard_map/while/body/eval_jaxpr/ppermute | solution.py:18
  817.3 10.7 %collective-permute-done = f32[16,64,64]{2,1,0:T(8,128)S(1)} collective-permute-done((f32[16,64,64]{2,1,0:T(8,128)S(1)}, f32[16,64,64]{2,1,0:T(8,128)S(1)}, u32[]{:S(2)}, u32[]{:S(2)}) %collective-permute-start) | collective-permute-done | bytes 262176 | tf_op jit(solution)/shard_map/while/body/eval_jaxpr/ppermute | solution.py:18
  868.5 10.7 %collective-permute-done = f32[16,64,64]{2,1,0:T(8,128)S(1)} collective-permute-done((f32[16,64,64]{2,1,0:T(8,128)S(1)}, f32[16,64,64]{2,1,0:T(8,128)S(1)}, u32[]{:S(2)}, u32[]{:S(2)}) %collective-permute-start) | collective-permute-done | bytes 262176 | tf_op jit(solution)/shard_map/while/body/eval_jaxpr/ppermute | solution.py:18
  881.3 10.7 %collective-permute-done = f32[16,64,64]{2,1,0:T(8,128)S(1)} collective-permute-done((f32[16,64,64]{2,1,0:T(8,128)S(1)}, f32[16,64,64]{2,1,0:T(8,128)S(1)}, u32[]{:S(2)}, u32[]{:S(2)}) %collective-permute-start) | collective-permute-done | bytes 262176 | tf_op jit(solution)/shard_map/while/body/eval_jaxpr/ppermute | solution.py:18
  946.6 15.5 %all_to_all.68 = bf16[4,128,1024]{1,2,0:T(8,128)(2,1)S(1)} all-to-all(bf16[4,128,1024]{1,2,0:T(8,128)(2,1)S(1)} %bitcast.73), channel_id=1, replica_groups=mesh['seq'=64,'head'=4] {'head'}, dimensions={0} | all-to-all | bytes 2097152 | tf_op jit(solution)/shard_map/all_to_all | solution.py:145
  (240 shorter events, 463.3 us)
Async XLA Ops:
  2.3 19.9 %all-to-all-start = ((bf16[128,4,1024]{0,2,1:T(8,128)(2,1)}), bf16[128,4,1024]{0,2,1:T(8,128)(2,1)S(1)}, u32[]{:S(2)}, u32[]{:S(2)}) async-start(bf16[128,4,1024]{0,2,1:T(8,128)(2,1)} %bitcast.76), calls=%async_computation | async-start | bytes 2097152 | tf_op jit(solution)/shard_map/all_to_all | solution.py:63
  7.7 27.9 %collective-permute-start.1 = (bf16[1,4096]{1,0:T(2,128)(2,1)S(1)}, bf16[1,4096]{1,0:T(2,128)(2,1)S(1)}, u32[]{:S(2)}, u32[]{:S(2)}) collective-permute-start(bf16[1,4096]{1,0:T(2,128)(2,1)S(1)} %slice.20), channel_id=1, source_target_pairs={{0,1},{1,2},{2,3},{3,4},{4,5},{5,6},{6,7},{7,8},{8,9},{9,10},{10,1... | collective-permute-start | bytes 24584 | tf_op jit(solution)/shard_map/ppermute | solution.py:18
  22.2 20.0 %all-to-all-start.2 = ((bf16[128,4,1024]{0,2,1:T(8,128)(2,1)}), bf16[128,4,1024]{0,2,1:T(8,128)(2,1)}, u32[]{:S(2)}, u32[]{:S(2)}) async-start(bf16[128,4,1024]{0,2,1:T(8,128)(2,1)} %bitcast.75), calls=%async_computation.2 | async-start | bytes 2097152 | tf_op jit(solution)/shard_map/all_to_all | solution.py:64
  42.2 21.8 %all-to-all-start.1 = ((bf16[128,4,1024]{0,2,1:T(8,128)(2,1)}), bf16[128,4,1024]{0,2,1:T(8,128)(2,1)S(1)}, u32[]{:S(2)}, u32[]{:S(2)}) async-start(bf16[128,4,1024]{0,2,1:T(8,128)(2,1)} %bitcast.77), calls=%async_computation.1 | async-start | bytes 2097152 | tf_op jit(solution)/shard_map/all_to_all | solution.py:66
  64.0 26.2 %all-to-all-start.3 = ((bf16[128,4,1024]{0,2,1:T(8,128)(2,1)}), bf16[128,4,1024]{0,2,1:T(8,128)(2,1)S(1)}, u32[]{:S(2)}, u32[]{:S(2)}) async-start(bf16[128,4,1024]{0,2,1:T(8,128)(2,1)} %bitcast.74), calls=%async_computation.3 | async-start | bytes 2097152 | tf_op jit(solution)/shard_map/all_to_all | solution.py:65
  123.4 12.6 %collective-permute-start = (f32[16,64,64]{2,1,0:T(8,128)S(1)}, f32[16,64,64]{2,1,0:T(8,128)S(1)}, u32[]{:S(2)}, u32[]{:S(2)}) collective-permute-start(f32[16,64,64]{2,1,0:T(8,128)S(1)} %multiply_add_fusion.2), channel_id=1, source_target_pairs={{0,4},{4,8},{8,12},{12,16},{16,20},{20,24},{24,28},{28,32},{32,36}... | collective-permute-start | bytes 786440 | tf_op jit(solution)/shard_map/while/body/eval_jaxpr/ppermute | solution.py:18
  136.2 12.6 %collective-permute-start = (f32[16,64,64]{2,1,0:T(8,128)S(1)}, f32[16,64,64]{2,1,0:T(8,128)S(1)}, u32[]{:S(2)}, u32[]{:S(2)}) collective-permute-start(f32[16,64,64]{2,1,0:T(8,128)S(1)} %multiply_add_fusion.2), channel_id=1, source_target_pairs={{0,4},{4,8},{8,12},{12,16},{16,20},{20,24},{24,28},{28,32},{32,36}... | collective-permute-start | bytes 786440 | tf_op jit(solution)/shard_map/while/body/eval_jaxpr/ppermute | solution.py:18
  149.0 12.6 %collective-permute-start = (f32[16,64,64]{2,1,0:T(8,128)S(1)}, f32[16,64,64]{2,1,0:T(8,128)S(1)}, u32[]{:S(2)}, u32[]{:S(2)}) collective-permute-start(f32[16,64,64]{2,1,0:T(8,128)S(1)} %multiply_add_fusion.2), channel_id=1, source_target_pairs={{0,4},{4,8},{8,12},{12,16},{16,20},{20,24},{24,28},{28,32},{32,36}... | collective-permute-start | bytes 786440 | tf_op jit(solution)/shard_map/while/body/eval_jaxpr/ppermute | solution.py:18
  161.8 12.6 %collective-permute-start = (f32[16,64,64]{2,1,0:T(8,128)S(1)}, f32[16,64,64]{2,1,0:T(8,128)S(1)}, u32[]{:S(2)}, u32[]{:S(2)}) collective-permute-start(f32[16,64,64]{2,1,0:T(8,128)S(1)} %multiply_add_fusion.2), channel_id=1, source_target_pairs={{0,4},{4,8},{8,12},{12,16},{16,20},{20,24},{24,28},{28,32},{32,36}... | collective-permute-start | bytes 786440 | tf_op jit(solution)/shard_map/while/body/eval_jaxpr/ppermute | solution.py:18
  200.3 12.6 %collective-permute-start = (f32[16,64,64]{2,1,0:T(8,128)S(1)}, f32[16,64,64]{2,1,0:T(8,128)S(1)}, u32[]{:S(2)}, u32[]{:S(2)}) collective-permute-start(f32[16,64,64]{2,1,0:T(8,128)S(1)} %multiply_add_fusion.2), channel_id=1, source_target_pairs={{0,4},{4,8},{8,12},{12,16},{16,20},{20,24},{24,28},{28,32},{32,36}... | collective-permute-start | bytes 786440 | tf_op jit(solution)/shard_map/while/body/eval_jaxpr/ppermute | solution.py:18
  213.1 12.6 %collective-permute-start = (f32[16,64,64]{2,1,0:T(8,128)S(1)}, f32[16,64,64]{2,1,0:T(8,128)S(1)}, u32[]{:S(2)}, u32[]{:S(2)}) collective-permute-start(f32[16,64,64]{2,1,0:T(8,128)S(1)} %multiply_add_fusion.2), channel_id=1, source_target_pairs={{0,4},{4,8},{8,12},{12,16},{16,20},{20,24},{24,28},{28,32},{32,36}... | collective-permute-start | bytes 786440 | tf_op jit(solution)/shard_map/while/body/eval_jaxpr/ppermute | solution.py:18
  225.9 12.6 %collective-permute-start = (f32[16,64,64]{2,1,0:T(8,128)S(1)}, f32[16,64,64]{2,1,0:T(8,128)S(1)}, u32[]{:S(2)}, u32[]{:S(2)}) collective-permute-start(f32[16,64,64]{2,1,0:T(8,128)S(1)} %multiply_add_fusion.2), channel_id=1, source_target_pairs={{0,4},{4,8},{8,12},{12,16},{16,20},{20,24},{24,28},{28,32},{32,36}... | collective-permute-start | bytes 786440 | tf_op jit(solution)/shard_map/while/body/eval_jaxpr/ppermute | solution.py:18
  264.4 12.6 %collective-permute-start = (f32[16,64,64]{2,1,0:T(8,128)S(1)}, f32[16,64,64]{2,1,0:T(8,128)S(1)}, u32[]{:S(2)}, u32[]{:S(2)}) collective-permute-start(f32[16,64,64]{2,1,0:T(8,128)S(1)} %multiply_add_fusion.2), channel_id=1, source_target_pairs={{0,4},{4,8},{8,12},{12,16},{16,20},{20,24},{24,28},{28,32},{32,36}... | collective-permute-start | bytes 786440 | tf_op jit(solution)/shard_map/while/body/eval_jaxpr/ppermute | solution.py:18
  277.2 12.6 %collective-permute-start = (f32[16,64,64]{2,1,0:T(8,128)S(1)}, f32[16,64,64]{2,1,0:T(8,128)S(1)}, u32[]{:S(2)}, u32[]{:S(2)}) collective-permute-start(f32[16,64,64]{2,1,0:T(8,128)S(1)} %multiply_add_fusion.2), channel_id=1, source_target_pairs={{0,4},{4,8},{8,12},{12,16},{16,20},{20,24},{24,28},{28,32},{32,36}... | collective-permute-start | bytes 786440 | tf_op jit(solution)/shard_map/while/body/eval_jaxpr/ppermute | solution.py:18
  290.0 12.6 %collective-permute-start = (f32[16,64,64]{2,1,0:T(8,128)S(1)}, f32[16,64,64]{2,1,0:T(8,128)S(1)}, u32[]{:S(2)}, u32[]{:S(2)}) collective-permute-start(f32[16,64,64]{2,1,0:T(8,128)S(1)} %multiply_add_fusion.2), channel_id=1, source_target_pairs={{0,4},{4,8},{8,12},{12,16},{16,20},{20,24},{24,28},{28,32},{32,36}... | collective-permute-start | bytes 786440 | tf_op jit(solution)/shard_map/while/body/eval_jaxpr/ppermute | solution.py:18
  315.6 12.6 %collective-permute-start = (f32[16,64,64]{2,1,0:T(8,128)S(1)}, f32[16,64,64]{2,1,0:T(8,128)S(1)}, u32[]{:S(2)}, u32[]{:S(2)}) collective-permute-start(f32[16,64,64]{2,1,0:T(8,128)S(1)} %multiply_add_fusion.2), channel_id=1, source_target_pairs={{0,4},{4,8},{8,12},{12,16},{16,20},{20,24},{24,28},{28,32},{32,36}... | collective-permute-start | bytes 786440 | tf_op jit(solution)/shard_map/while/body/eval_jaxpr/ppermute | solution.py:18
  328.4 12.6 %collective-permute-start = (f32[16,64,64]{2,1,0:T(8,128)S(1)}, f32[16,64,64]{2,1,0:T(8,128)S(1)}, u32[]{:S(2)}, u32[]{:S(2)}) collective-permute-start(f32[16,64,64]{2,1,0:T(8,128)S(1)} %multiply_add_fusion.2), channel_id=1, source_target_pairs={{0,4},{4,8},{8,12},{12,16},{16,20},{20,24},{24,28},{28,32},{32,36}... | collective-permute-start | bytes 786440 | tf_op jit(solution)/shard_map/while/body/eval_jaxpr/ppermute | solution.py:18
  341.2 12.6 %collective-permute-start = (f32[16,64,64]{2,1,0:T(8,128)S(1)}, f32[16,64,64]{2,1,0:T(8,128)S(1)}, u32[]{:S(2)}, u32[]{:S(2)}) collective-permute-start(f32[16,64,64]{2,1,0:T(8,128)S(1)} %multiply_add_fusion.2), channel_id=1, source_target_pairs={{0,4},{4,8},{8,12},{12,16},{16,20},{20,24},{24,28},{28,32},{32,36}... | collective-permute-start | bytes 786440 | tf_op jit(solution)/shard_map/while/body/eval_jaxpr/ppermute | solution.py:18
  354.0 12.6 %collective-permute-start = (f32[16,64,64]{2,1,0:T(8,128)S(1)}, f32[16,64,64]{2,1,0:T(8,128)S(1)}, u32[]{:S(2)}, u32[]{:S(2)}) collective-permute-start(f32[16,64,64]{2,1,0:T(8,128)S(1)} %multiply_add_fusion.2), channel_id=1, source_target_pairs={{0,4},{4,8},{8,12},{12,16},{16,20},{20,24},{24,28},{28,32},{32,36}... | collective-permute-start | bytes 786440 | tf_op jit(solution)/shard_map/while/body/eval_jaxpr/ppermute | solution.py:18
  379.7 12.6 %collective-permute-start = (f32[16,64,64]{2,1,0:T(8,128)S(1)}, f32[16,64,64]{2,1,0:T(8,128)S(1)}, u32[]{:S(2)}, u32[]{:S(2)}) collective-permute-start(f32[16,64,64]{2,1,0:T(8,128)S(1)} %multiply_add_fusion.2), channel_id=1, source_target_pairs={{0,4},{4,8},{8,12},{12,16},{16,20},{20,24},{24,28},{28,32},{32,36}... | collective-permute-start | bytes 786440 | tf_op jit(solution)/shard_map/while/body/eval_jaxpr/ppermute | solution.py:18
  392.5 12.6 %collective-permute-start = (f32[16,64,64]{2,1,0:T(8,128)S(1)}, f32[16,64,64]{2,1,0:T(8,128)S(1)}, u32[]{:S(2)}, u32[]{:S(2)}) collective-permute-start(f32[16,64,64]{2,1,0:T(8,128)S(1)} %multiply_add_fusion.2), channel_id=1, source_target_pairs={{0,4},{4,8},{8,12},{12,16},{16,20},{20,24},{24,28},{28,32},{32,36}... | collective-permute-start | bytes 786440 | tf_op jit(solution)/shard_map/while/body/eval_jaxpr/ppermute | solution.py:18
  405.3 12.6 %collective-permute-start = (f32[16,64,64]{2,1,0:T(8,128)S(1)}, f32[16,64,64]{2,1,0:T(8,128)S(1)}, u32[]{:S(2)}, u32[]{:S(2)}) collective-permute-start(f32[16,64,64]{2,1,0:T(8,128)S(1)} %multiply_add_fusion.2), channel_id=1, source_target_pairs={{0,4},{4,8},{8,12},{12,16},{16,20},{20,24},{24,28},{28,32},{32,36}... | collective-permute-start | bytes 786440 | tf_op jit(solution)/shard_map/while/body/eval_jaxpr/ppermute | solution.py:18
  443.7 12.6 %collective-permute-start = (f32[16,64,64]{2,1,0:T(8,128)S(1)}, f32[16,64,64]{2,1,0:T(8,128)S(1)}, u32[]{:S(2)}, u32[]{:S(2)}) collective-permute-start(f32[16,64,64]{2,1,0:T(8,128)S(1)} %multiply_add_fusion.2), channel_id=1, source_target_pairs={{0,4},{4,8},{8,12},{12,16},{16,20},{20,24},{24,28},{28,32},{32,36}... | collective-permute-start | bytes 786440 | tf_op jit(solution)/shard_map/while/body/eval_jaxpr/ppermute | solution.py:18
  456.6 12.6 %collective-permute-start = (f32[16,64,64]{2,1,0:T(8,128)S(1)}, f32[16,64,64]{2,1,0:T(8,128)S(1)}, u32[]{:S(2)}, u32[]{:S(2)}) collective-permute-start(f32[16,64,64]{2,1,0:T(8,128)S(1)} %multiply_add_fusion.2), channel_id=1, source_target_pairs={{0,4},{4,8},{8,12},{12,16},{16,20},{20,24},{24,28},{28,32},{32,36}... | collective-permute-start | bytes 786440 | tf_op jit(solution)/shard_map/while/body/eval_jaxpr/ppermute | solution.py:18
  469.4 12.6 %collective-permute-start = (f32[16,64,64]{2,1,0:T(8,128)S(1)}, f32[16,64,64]{2,1,0:T(8,128)S(1)}, u32[]{:S(2)}, u32[]{:S(2)}) collective-permute-start(f32[16,64,64]{2,1,0:T(8,128)S(1)} %multiply_add_fusion.2), channel_id=1, source_target_pairs={{0,4},{4,8},{8,12},{12,16},{16,20},{20,24},{24,28},{28,32},{32,36}... | collective-permute-start | bytes 786440 | tf_op jit(solution)/shard_map/while/body/eval_jaxpr/ppermute | solution.py:18
  507.8 12.6 %collective-permute-start = (f32[16,64,64]{2,1,0:T(8,128)S(1)}, f32[16,64,64]{2,1,0:T(8,128)S(1)}, u32[]{:S(2)}, u32[]{:S(2)}) collective-permute-start(f32[16,64,64]{2,1,0:T(8,128)S(1)} %multiply_add_fusion.2), channel_id=1, source_target_pairs={{0,4},{4,8},{8,12},{12,16},{16,20},{20,24},{24,28},{28,32},{32,36}... | collective-permute-start | bytes 786440 | tf_op jit(solution)/shard_map/while/body/eval_jaxpr/ppermute | solution.py:18
  520.6 12.6 %collective-permute-start = (f32[16,64,64]{2,1,0:T(8,128)S(1)}, f32[16,64,64]{2,1,0:T(8,128)S(1)}, u32[]{:S(2)}, u32[]{:S(2)}) collective-permute-start(f32[16,64,64]{2,1,0:T(8,128)S(1)} %multiply_add_fusion.2), channel_id=1, source_target_pairs={{0,4},{4,8},{8,12},{12,16},{16,20},{20,24},{24,28},{28,32},{32,36}... | collective-permute-start | bytes 786440 | tf_op jit(solution)/shard_map/while/body/eval_jaxpr/ppermute | solution.py:18
  533.4 12.6 %collective-permute-start = (f32[16,64,64]{2,1,0:T(8,128)S(1)}, f32[16,64,64]{2,1,0:T(8,128)S(1)}, u32[]{:S(2)}, u32[]{:S(2)}) collective-permute-start(f32[16,64,64]{2,1,0:T(8,128)S(1)} %multiply_add_fusion.2), channel_id=1, source_target_pairs={{0,4},{4,8},{8,12},{12,16},{16,20},{20,24},{24,28},{28,32},{32,36}... | collective-permute-start | bytes 786440 | tf_op jit(solution)/shard_map/while/body/eval_jaxpr/ppermute | solution.py:18
  559.1 12.6 %collective-permute-start = (f32[16,64,64]{2,1,0:T(8,128)S(1)}, f32[16,64,64]{2,1,0:T(8,128)S(1)}, u32[]{:S(2)}, u32[]{:S(2)}) collective-permute-start(f32[16,64,64]{2,1,0:T(8,128)S(1)} %multiply_add_fusion.2), channel_id=1, source_target_pairs={{0,4},{4,8},{8,12},{12,16},{16,20},{20,24},{24,28},{28,32},{32,36}... | collective-permute-start | bytes 786440 | tf_op jit(solution)/shard_map/while/body/eval_jaxpr/ppermute | solution.py:18
  571.9 12.6 %collective-permute-start = (f32[16,64,64]{2,1,0:T(8,128)S(1)}, f32[16,64,64]{2,1,0:T(8,128)S(1)}, u32[]{:S(2)}, u32[]{:S(2)}) collective-permute-start(f32[16,64,64]{2,1,0:T(8,128)S(1)} %multiply_add_fusion.2), channel_id=1, source_target_pairs={{0,4},{4,8},{8,12},{12,16},{16,20},{20,24},{24,28},{28,32},{32,36}... | collective-permute-start | bytes 786440 | tf_op jit(solution)/shard_map/while/body/eval_jaxpr/ppermute | solution.py:18
  584.7 12.6 %collective-permute-start = (f32[16,64,64]{2,1,0:T(8,128)S(1)}, f32[16,64,64]{2,1,0:T(8,128)S(1)}, u32[]{:S(2)}, u32[]{:S(2)}) collective-permute-start(f32[16,64,64]{2,1,0:T(8,128)S(1)} %multiply_add_fusion.2), channel_id=1, source_target_pairs={{0,4},{4,8},{8,12},{12,16},{16,20},{20,24},{24,28},{28,32},{32,36}... | collective-permute-start | bytes 786440 | tf_op jit(solution)/shard_map/while/body/eval_jaxpr/ppermute | solution.py:18
  597.5 12.6 %collective-permute-start = (f32[16,64,64]{2,1,0:T(8,128)S(1)}, f32[16,64,64]{2,1,0:T(8,128)S(1)}, u32[]{:S(2)}, u32[]{:S(2)}) collective-permute-start(f32[16,64,64]{2,1,0:T(8,128)S(1)} %multiply_add_fusion.2), channel_id=1, source_target_pairs={{0,4},{4,8},{8,12},{12,16},{16,20},{20,24},{24,28},{28,32},{32,36}... | collective-permute-start | bytes 786440 | tf_op jit(solution)/shard_map/while/body/eval_jaxpr/ppermute | solution.py:18
  623.1 12.6 %collective-permute-start = (f32[16,64,64]{2,1,0:T(8,128)S(1)}, f32[16,64,64]{2,1,0:T(8,128)S(1)}, u32[]{:S(2)}, u32[]{:S(2)}) collective-permute-start(f32[16,64,64]{2,1,0:T(8,128)S(1)} %multiply_add_fusion.2), channel_id=1, source_target_pairs={{0,4},{4,8},{8,12},{12,16},{16,20},{20,24},{24,28},{28,32},{32,36}... | collective-permute-start | bytes 786440 | tf_op jit(solution)/shard_map/while/body/eval_jaxpr/ppermute | solution.py:18
  635.9 12.6 %collective-permute-start = (f32[16,64,64]{2,1,0:T(8,128)S(1)}, f32[16,64,64]{2,1,0:T(8,128)S(1)}, u32[]{:S(2)}, u32[]{:S(2)}) collective-permute-start(f32[16,64,64]{2,1,0:T(8,128)S(1)} %multiply_add_fusion.2), channel_id=1, source_target_pairs={{0,4},{4,8},{8,12},{12,16},{16,20},{20,24},{24,28},{28,32},{32,36}... | collective-permute-start | bytes 786440 | tf_op jit(solution)/shard_map/while/body/eval_jaxpr/ppermute | solution.py:18
  648.8 12.6 %collective-permute-start = (f32[16,64,64]{2,1,0:T(8,128)S(1)}, f32[16,64,64]{2,1,0:T(8,128)S(1)}, u32[]{:S(2)}, u32[]{:S(2)}) collective-permute-start(f32[16,64,64]{2,1,0:T(8,128)S(1)} %multiply_add_fusion.2), channel_id=1, source_target_pairs={{0,4},{4,8},{8,12},{12,16},{16,20},{20,24},{24,28},{28,32},{32,36}... | collective-permute-start | bytes 786440 | tf_op jit(solution)/shard_map/while/body/eval_jaxpr/ppermute | solution.py:18
  687.2 12.6 %collective-permute-start = (f32[16,64,64]{2,1,0:T(8,128)S(1)}, f32[16,64,64]{2,1,0:T(8,128)S(1)}, u32[]{:S(2)}, u32[]{:S(2)}) collective-permute-start(f32[16,64,64]{2,1,0:T(8,128)S(1)} %multiply_add_fusion.2), channel_id=1, source_target_pairs={{0,4},{4,8},{8,12},{12,16},{16,20},{20,24},{24,28},{28,32},{32,36}... | collective-permute-start | bytes 786440 | tf_op jit(solution)/shard_map/while/body/eval_jaxpr/ppermute | solution.py:18
  700.0 12.6 %collective-permute-start = (f32[16,64,64]{2,1,0:T(8,128)S(1)}, f32[16,64,64]{2,1,0:T(8,128)S(1)}, u32[]{:S(2)}, u32[]{:S(2)}) collective-permute-start(f32[16,64,64]{2,1,0:T(8,128)S(1)} %multiply_add_fusion.2), channel_id=1, source_target_pairs={{0,4},{4,8},{8,12},{12,16},{16,20},{20,24},{24,28},{28,32},{32,36}... | collective-permute-start | bytes 786440 | tf_op jit(solution)/shard_map/while/body/eval_jaxpr/ppermute | solution.py:18
  712.8 12.6 %collective-permute-start = (f32[16,64,64]{2,1,0:T(8,128)S(1)}, f32[16,64,64]{2,1,0:T(8,128)S(1)}, u32[]{:S(2)}, u32[]{:S(2)}) collective-permute-start(f32[16,64,64]{2,1,0:T(8,128)S(1)} %multiply_add_fusion.2), channel_id=1, source_target_pairs={{0,4},{4,8},{8,12},{12,16},{16,20},{20,24},{24,28},{28,32},{32,36}... | collective-permute-start | bytes 786440 | tf_op jit(solution)/shard_map/while/body/eval_jaxpr/ppermute | solution.py:18
  751.3 12.6 %collective-permute-start = (f32[16,64,64]{2,1,0:T(8,128)S(1)}, f32[16,64,64]{2,1,0:T(8,128)S(1)}, u32[]{:S(2)}, u32[]{:S(2)}) collective-permute-start(f32[16,64,64]{2,1,0:T(8,128)S(1)} %multiply_add_fusion.2), channel_id=1, source_target_pairs={{0,4},{4,8},{8,12},{12,16},{16,20},{20,24},{24,28},{28,32},{32,36}... | collective-permute-start | bytes 786440 | tf_op jit(solution)/shard_map/while/body/eval_jaxpr/ppermute | solution.py:18
  764.1 12.6 %collective-permute-start = (f32[16,64,64]{2,1,0:T(8,128)S(1)}, f32[16,64,64]{2,1,0:T(8,128)S(1)}, u32[]{:S(2)}, u32[]{:S(2)}) collective-permute-start(f32[16,64,64]{2,1,0:T(8,128)S(1)} %multiply_add_fusion.2), channel_id=1, source_target_pairs={{0,4},{4,8},{8,12},{12,16},{16,20},{20,24},{24,28},{28,32},{32,36}... | collective-permute-start | bytes 786440 | tf_op jit(solution)/shard_map/while/body/eval_jaxpr/ppermute | solution.py:18
  776.9 12.6 %collective-permute-start = (f32[16,64,64]{2,1,0:T(8,128)S(1)}, f32[16,64,64]{2,1,0:T(8,128)S(1)}, u32[]{:S(2)}, u32[]{:S(2)}) collective-permute-start(f32[16,64,64]{2,1,0:T(8,128)S(1)} %multiply_add_fusion.2), channel_id=1, source_target_pairs={{0,4},{4,8},{8,12},{12,16},{16,20},{20,24},{24,28},{28,32},{32,36}... | collective-permute-start | bytes 786440 | tf_op jit(solution)/shard_map/while/body/eval_jaxpr/ppermute | solution.py:18
  802.5 12.6 %collective-permute-start = (f32[16,64,64]{2,1,0:T(8,128)S(1)}, f32[16,64,64]{2,1,0:T(8,128)S(1)}, u32[]{:S(2)}, u32[]{:S(2)}) collective-permute-start(f32[16,64,64]{2,1,0:T(8,128)S(1)} %multiply_add_fusion.2), channel_id=1, source_target_pairs={{0,4},{4,8},{8,12},{12,16},{16,20},{20,24},{24,28},{28,32},{32,36}... | collective-permute-start | bytes 786440 | tf_op jit(solution)/shard_map/while/body/eval_jaxpr/ppermute | solution.py:18
  815.3 12.6 %collective-permute-start = (f32[16,64,64]{2,1,0:T(8,128)S(1)}, f32[16,64,64]{2,1,0:T(8,128)S(1)}, u32[]{:S(2)}, u32[]{:S(2)}) collective-permute-start(f32[16,64,64]{2,1,0:T(8,128)S(1)} %multiply_add_fusion.2), channel_id=1, source_target_pairs={{0,4},{4,8},{8,12},{12,16},{16,20},{20,24},{24,28},{28,32},{32,36}... | collective-permute-start | bytes 786440 | tf_op jit(solution)/shard_map/while/body/eval_jaxpr/ppermute | solution.py:18
  828.2 12.6 %collective-permute-start = (f32[16,64,64]{2,1,0:T(8,128)S(1)}, f32[16,64,64]{2,1,0:T(8,128)S(1)}, u32[]{:S(2)}, u32[]{:S(2)}) collective-permute-start(f32[16,64,64]{2,1,0:T(8,128)S(1)} %multiply_add_fusion.2), channel_id=1, source_target_pairs={{0,4},{4,8},{8,12},{12,16},{16,20},{20,24},{24,28},{28,32},{32,36}... | collective-permute-start | bytes 786440 | tf_op jit(solution)/shard_map/while/body/eval_jaxpr/ppermute | solution.py:18
  841.0 12.6 %collective-permute-start = (f32[16,64,64]{2,1,0:T(8,128)S(1)}, f32[16,64,64]{2,1,0:T(8,128)S(1)}, u32[]{:S(2)}, u32[]{:S(2)}) collective-permute-start(f32[16,64,64]{2,1,0:T(8,128)S(1)} %multiply_add_fusion.2), channel_id=1, source_target_pairs={{0,4},{4,8},{8,12},{12,16},{16,20},{20,24},{24,28},{28,32},{32,36}... | collective-permute-start | bytes 786440 | tf_op jit(solution)/shard_map/while/body/eval_jaxpr/ppermute | solution.py:18
  866.6 12.6 %collective-permute-start = (f32[16,64,64]{2,1,0:T(8,128)S(1)}, f32[16,64,64]{2,1,0:T(8,128)S(1)}, u32[]{:S(2)}, u32[]{:S(2)}) collective-permute-start(f32[16,64,64]{2,1,0:T(8,128)S(1)} %multiply_add_fusion.2), channel_id=1, source_target_pairs={{0,4},{4,8},{8,12},{12,16},{16,20},{20,24},{24,28},{28,32},{32,36}... | collective-permute-start | bytes 786440 | tf_op jit(solution)/shard_map/while/body/eval_jaxpr/ppermute | solution.py:18
  879.4 12.6 %collective-permute-start = (f32[16,64,64]{2,1,0:T(8,128)S(1)}, f32[16,64,64]{2,1,0:T(8,128)S(1)}, u32[]{:S(2)}, u32[]{:S(2)}) collective-permute-start(f32[16,64,64]{2,1,0:T(8,128)S(1)} %multiply_add_fusion.2), channel_id=1, source_target_pairs={{0,4},{4,8},{8,12},{12,16},{16,20},{20,24},{24,28},{28,32},{32,36}... | collective-permute-start | bytes 786440 | tf_op jit(solution)/shard_map/while/body/eval_jaxpr/ppermute | solution.py:18
  892.2 12.6 %collective-permute-start = (f32[16,64,64]{2,1,0:T(8,128)S(1)}, f32[16,64,64]{2,1,0:T(8,128)S(1)}, u32[]{:S(2)}, u32[]{:S(2)}) collective-permute-start(f32[16,64,64]{2,1,0:T(8,128)S(1)} %multiply_add_fusion.2), channel_id=1, source_target_pairs={{0,4},{4,8},{8,12},{12,16},{16,20},{20,24},{24,28},{28,32},{32,36}... | collective-permute-start | bytes 786440 | tf_op jit(solution)/shard_map/while/body/eval_jaxpr/ppermute | solution.py:18
  (28 other events, 346.7 us)
where the time goes:
time: 973 us; the launch traced here: 970 us
  waiting for transfers between devices  680 us (70%)
  starting transfers between devices  143 us (15%)
  other arithmetic  52.1 us (5%)
  matrix products  43.1 us (4%)
  local copies, waits for them, and re-layouts  32.8 us (3%)
  blocking collectives  15.5 us (2%)
    ppermute x64, waiting for transfers between devices, shifted(): return lax.ppermute(value, axis, pairs)  673 us
    ppermute x64, starting transfers between devices, shifted(): return lax.ppermute(value, axis, pairs)  125 us
  transfers between devices with their start and end apart: 68, of which 64 were waited for; matrix products, arithmetic and copies ran while one was open for 6% of the time, Pallas kernels for 0%

commit v1 on v0

--- a/solution.py
+++ b/solution.py
@@ -125,10 +125,27 @@
         multiply, jnp.ones((local_heads, ATTENTION_SPAN), jnp.float32), stretch_decay
     )
 
-    def relay(iteration, incoming):
-        return shifted(span_decay[:, :, None] * incoming + span_state, "seq", 1)
+    seq_count = lax.axis_size("seq")
+    packed = jnp.concatenate([span_state, span_decay[:, None, :]], axis=1)
 
-    incoming = lax.fori_loop(0, lax.axis_size("seq") - 1, relay, zero_state)
+    def unpack(value):
+        return value[:, :ATTENTION_SPAN], value[:, ATTENTION_SPAN]
+
+    prior_state, prior_decay = unpack(shifted(packed, "seq", 1))
+    incoming, cover = prior_state, prior_decay
+    reach = 1
+    if seq_count > 2:
+        far_state, far_decay = unpack(shifted(packed, "seq", 2))
+        incoming = prior_decay[:, :, None] * far_state + prior_state
+        cover = prior_decay * far_decay
+        reach = 2
+    while reach < seq_count - 1:
+        far_state, far_decay = unpack(
+            shifted(jnp.concatenate([incoming, cover[:, None, :]], axis=1), "seq", reach)
+        )
+        incoming = cover[:, :, None] * far_state + incoming
+        cover = cover * far_decay
+        reach *= 2
     start_state = local_start + decay_before[:, :, :, None] * incoming[None]
     keep_first = (seg_block == stretch_prior[:, None]).astype(jnp.float32)
     carried = jnp.einsum(

time: 973 us -> 320 us (0.33)
  the two profiles are of different devices: /device:TPU:6 before, /device:TPU:162 now
where the time goes in v1:
time: 320 us; the launch traced here: 318 us
  waiting for transfers between devices  90.9 us (28%)
  starting transfers between devices  64.3 us (20%)
  other arithmetic  51.7 us (16%)
  local copies, waits for them, and re-layouts  45.7 us (14%)
  matrix products  45.2 us (14%)
  blocking collectives  18.4 us (6%)
    ppermute x8, waiting for transfers between devices, shifted(): return lax.ppermute(value, axis, pairs)  76.6 us
    ppermute x8, starting transfers between devices, shifted(): return lax.ppermute(value, axis, pairs)  46.5 us
    all_to_all x1, blocking collectives, local(): lax.all_to_all(normed, 'head', split_axis=0, concat_axis=1, tiled=True)  18.4 us
    dot_general x1, matrix products, local(): jnp.einsum('cthd,cshd->chts', scaled_query, scaled_key, precision=highest)  16.5 us
    all_to_all x1, waiting for transfers between devices, local(): lax.all_to_all(acceptance_linear, 'head', split_axis=1, concat_axis=0, ti...  13.8 us
    unnamed x42, local copies, waits for them, and re-layouts  11.8 us
    mul x1, other arithmetic, local(): scaled_key = lookup_vectors * jnp.exp(-cumulative)  11.3 us
    dot_general x1, matrix products, local(): jnp.einsum('cthd,chde->cthe', scaled_query * keep_first[:, :, None, None]...  10.6 us
  transfers between devices with their start and end apart: 12, of which 9 were waited for; matrix products, arithmetic and copies ran while one was open for 22% of the time, Pallas kernels for 0%

profile of v1, /device:TPU:162, one launch (start us, length us, event | category | flops | bytes accessed | tf_op | source)
XLA Modules:
  0.0 318.2 jit_solution(3429438494521364704)
XLA Ops:
  0.0 2.4 copy.126
  2.4 4.5 %all-to-all-start = ((bf16[128,4,1024]{0,2,1:T(8,128)(2,1)}), bf16[128,4,1024]{0,2,1:T(8,128)(2,1)S(1)}, u32[]{:S(2)}, u32[]{:S(2)}) async-start(bf16[128,4,1024]{0,2,1:T(8,128)(2,1)} %bitcast.1), calls=%async_computation | async-start | bytes 2097152 | tf_op jit(solution)/shard_map/all_to_all | solution.py:63
  8.2 13.8 %all-to-all-done = bf16[128,4,1024]{0,2,1:T(8,128)(2,1)S(1)} async-done(((bf16[128,4,1024]{0,2,1:T(8,128)(2,1)}), bf16[128,4,1024]{0,2,1:T(8,128)(2,1)S(1)}, u32[]{:S(2)}, u32[]{:S(2)}) %all-to-all-start) | async-done | bytes 1048608 | tf_op jit(solution)/shard_map/all_to_all | solution.py:63
  22.0 3.5 %all-to-all-start.2 = ((bf16[128,4,1024]{0,2,1:T(8,128)(2,1)}), bf16[128,4,1024]{0,2,1:T(8,128)(2,1)S(1)}, u32[]{:S(2)}, u32[]{:S(2)}) async-start(bf16[128,4,1024]{0,2,1:T(8,128)(2,1)} %bitcast.88), calls=%async_computation.2 | async-start | bytes 2097152 | tf_op jit(solution)/shard_map/all_to_all | solution.py:64
  26.4 3.9 %collective-permute-start = (bf16[1,4096]{1,0:T(2,128)(2,1)S(1)}, bf16[1,4096]{1,0:T(2,128)(2,1)S(1)}, u32[]{:S(2)}, u32[]{:S(2)}) collective-permute-start(bf16[1,4096]{1,0:T(2,128)(2,1)S(1)} %slice.59), channel_id=1, source_target_pairs={{0,1},{1,2},{2,3},{3,4},{4,5},{5,6},{6,7},{7,8},{8,9},{9,10},{10,1... | collective-permute-start | bytes 24584 | tf_op jit(solution)/shard_map/ppermute | solution.py:18
  31.1 1.4 fusion.55
  34.0 2.5 collective-permute-done
  36.4 4.3 %fusion.4 = bf16[128,4096]{1,0:T(8,128)(2,1)} fusion(bf16[128,4096]{1,0:T(8,128)(2,1)S(1)} %copy-done, bf16[4096,128]{1,0:T(8,128)(2,1)} %param.25, bf16[128,4096]{1,0:T(8,128)(2,1)} %param.21, bf16[127,4096]{1,0:T(8,128)(2,1)} %bitcast.92, bf16[1,4096]{1,0:T(2,128)(2,1)S(1)} %collective-permute-done, f32[4096]{0:T(1024)S(1)} %copy-done.15, ...), kind=kOutput, calls=%fused_computation.10 | convolution fusion | flops 276316160 | bytes 5275776 | tf_op jit(solution)/shard_map/dot_general | solution.py:58
  40.7 2.4 copy.156
  43.1 5.5 %all-to-all-start.1 = ((bf16[128,4,1024]{0,2,1:T(8,128)(2,1)}), bf16[128,4,1024]{0,2,1:T(8,128)(2,1)}, u32[]{:S(2)}, u32[]{:S(2)}) async-start(bf16[128,4,1024]{0,2,1:T(8,128)(2,1)} %bitcast.5), calls=%async_computation.1 | async-start | bytes 2097152 | tf_op jit(solution)/shard_map/all_to_all | solution.py:66
  52.5 1.4 convert_element_type.112
  53.9 3.0 copy.130
  56.8 2.8 convert_element_type.114
  59.6 4.0 %copy.132 = f32[4,128,16,64]{3,2,1,0:T(8,128)} copy(f32[4,128,16,64]{1,3,2,0:T(8,128)} %bitcast.82) | data formatting | bytes 4194304 | tf_op jit(solution)/shard_map/convert_element_type | solution.py:88
  64.2 4.2 %all-to-all-start.3 = ((bf16[128,4,1024]{0,2,1:T(8,128)(2,1)}), bf16[128,4,1024]{0,2,1:T(8,128)(2,1)}, u32[]{:S(2)}, u32[]{:S(2)}) async-start(bf16[128,4,1024]{0,2,1:T(8,128)(2,1)} %bitcast.87), calls=%async_computation.3 | async-start | bytes 2097152 | tf_op jit(solution)/shard_map/all_to_all | solution.py:65
  68.4 2.7 convert_element_type.113
  71.2 4.1 %copy.128 = f32[4,128,16,64]{3,2,1,0:T(8,128)} copy(f32[4,128,16,64]{1,3,2,0:T(8,128)} %bitcast.84) | data formatting | bytes 4194304 | tf_op jit(solution)/shard_map/convert_element_type | solution.py:90
  75.3 2.5 fusion.57
  77.9 2.1 copy-done.3
  80.4 11.3 %exponential_multiply_fusion = (f32[4,128,16,64]{3,2,1,0:T(8,128)}, f32[4,128,16,64]{3,2,1,0:T(8,128)}, f32[4,128,16,64]{3,2,1,0:T(8,128)}, f32[4,128,16,64]{3,2,1,0:T(8,128)}) fusion(f32[4,128,16,64]{3,2,1,0:T(8,128)} %copy.132, f32[4,128,16,64]{3,2,1,0:T(8,128)} %copy-done.3, f32[4,128]{1,0:T(4,128)S(1)} %get-tuple-element.125, ...), kind=kLoop, calls=%fused_computation.21 | loop fusion | flops 4194304 | bytes 16797696 | tf_op jit(solution)/shard_map/mul | solution.py:95
  91.8 7.8 %fusion.7 = f32[4,16,64,64]{3,2,1,0:T(8,128)} fusion(bf16[4,128,16,64]{1,3,2,0:T(8,128)(2,1)} %bitcast.14, f32[4,128,16,64]{3,2,1,0:T(8,128)} %get-tuple-element.120), kind=kOutput, calls=%fused_computation.13 | convolution fusion | flops 402653184 | bytes 4194304 | tf_op jit(solution)/shard_map/cthd,cthe->chde/dot_general | solution.py:109
  99.6 8.8 %while.26 = (s32[]{:T(128)}, f32[16,64,64]{2,1,0:T(8,128)S(1)}, f32[4,16,64,64]{3,2,1,0:T(8,128)}, f32[4,16,64]{2,1,0:T(8,128)S(1)}, f32[4,16,64,64]{3,2,1,0:T(8,128)}, /*index=5*/s32[]{:T(128)}, s32[]{:T(128)}) while((s32[]{:T(128)}, f32[16,64,64]{2,1,0:T(8,128)S(1)}, f32[4,16,64,64]{3,2,1,0:T(8,128)}, ...), condition=%wide.region_3.4_spmd.clone, body=%wide.region_2.3_spmd.clone.sunk | while | flops 262147 | bytes 1585260 | solution.py:119
  100.5 1.3 bitcast_add_fusion.4
  102.7 1.3 bitcast_add_fusion.4
  104.9 1.3 bitcast_add_fusion.4
  109.5 2.1 pad_maximum_fusion
  111.5 2.9 collective-permute-start.2
  114.4 2.1 collective-permute-start.1
  116.5 11.9 %collective-permute-done.2 = f32[16,65,64]{1,2,0:T(8,128)S(1)} collective-permute-done((f32[16,65,64]{1,2,0:T(8,128)}, f32[16,65,64]{1,2,0:T(8,128)S(1)}, u32[]{:S(2)}, u32[]{:S(2)}) %collective-permute-start.2) | collective-permute-done | bytes 266272 | tf_op jit(solution)/shard_map/ppermute | solution.py:18
  130.6 1.9 collective-permute-done.1
  138.3 2.9 collective-permute-start.3
  141.2 11.5 %collective-permute-done.3 = f32[16,65,64]{1,2,0:T(8,128)S(1)} collective-permute-done((f32[16,65,64]{1,2,0:T(8,128)S(1)}, f32[16,65,64]{1,2,0:T(8,128)S(1)}, u32[]{:S(2)}, u32[]{:S(2)}) %collective-permute-start.3) | collective-permute-done | bytes 266272 | tf_op jit(solution)/shard_map/ppermute | solution.py:18
  157.4 2.7 collective-permute-start.4
  160.1 24.8 %collective-permute-done.4 = f32[16,65,64]{1,2,0:T(8,128)S(1)} collective-permute-done((f32[16,65,64]{1,2,0:T(8,128)S(1)}, f32[16,65,64]{1,2,0:T(8,128)S(1)}, u32[]{:S(2)}, u32[]{:S(2)}) %collective-permute-start.4) | collective-permute-done | bytes 266272 | tf_op jit(solution)/shard_map/ppermute | solution.py:18
  188.2 2.0 pad_maximum_fusion.3
  190.3 11.2 %collective-permute-start.5 = (f32[16,65,64]{1,2,0:T(8,128)}, f32[16,65,64]{1,2,0:T(8,128)S(1)}, u32[]{:S(2)}, u32[]{:S(2)}) collective-permute-start(f32[16,65,64]{1,2,0:T(8,128)} %pad_maximum_fusion.3), channel_id=1, source_target_pairs={{0,32},{4,36},{8,40},{12,44},{16,48},{20,52},{24,56},{28,60},{32,6... | collective-permute-start | bytes 798728 | tf_op jit(solution)/shard_map/ppermute | solution.py:18
  203.9 16.0 %collective-permute-done.5 = f32[16,65,64]{1,2,0:T(8,128)S(1)} collective-permute-done((f32[16,65,64]{1,2,0:T(8,128)}, f32[16,65,64]{1,2,0:T(8,128)S(1)}, u32[]{:S(2)}, u32[]{:S(2)}) %collective-permute-start.5) | collective-permute-done | bytes 266272 | tf_op jit(solution)/shard_map/ppermute | solution.py:18
  225.8 7.2 %collective-permute-start.6 = (f32[16,65,64]{1,2,0:T(8,128)S(1)}, f32[16,65,64]{1,2,0:T(8,128)S(1)}, u32[]{:S(2)}, u32[]{:S(2)}) collective-permute-start(f32[16,65,64]{1,2,0:T(8,128)S(1)} %pad_maximum_fusion.4), channel_id=1, source_target_pairs={{0,64},{4,68},{8,72},{12,76},{16,80},{20,84},{24,88},{28,92},{32,9... | collective-permute-start | bytes 798728 | tf_op jit(solution)/shard_map/ppermute | solution.py:18
  233.0 1.8 fusion
  234.8 8.0 %collective-permute-done.6 = f32[16,65,64]{1,2,0:T(8,128)S(1)} collective-permute-done((f32[16,65,64]{1,2,0:T(8,128)S(1)}, f32[16,65,64]{1,2,0:T(8,128)S(1)}, u32[]{:S(2)}, u32[]{:S(2)}) %collective-permute-start.6) | collective-permute-done | bytes 266272 | tf_op jit(solution)/shard_map/ppermute | solution.py:18
  243.8 13.7 %collective-permute-start.7 = (f32[16,65,64]{1,2,0:T(8,128)S(1)}, f32[16,65,64]{1,2,0:T(8,128)S(1)}, u32[]{:S(2)}, u32[]{:S(2)}) collective-permute-start(f32[16,65,64]{1,2,0:T(8,128)S(1)} %pad_maximum_fusion.5), channel_id=1, source_target_pairs={{0,128},{4,132},{8,136},{12,140},{16,144},{20,148},{24,152},{28,15... | collective-permute-start | bytes 798728 | tf_op jit(solution)/shard_map/ppermute | solution.py:18
  257.5 16.5 %fusion.9 = f32[4,16,128,128]{3,2,1,0:T(8,128)} fusion(f32[4,128,16,64]{3,2,1,0:T(8,128)} %get-tuple-element.119, f32[4,128,16,64]{3,2,1,0:T(8,128)} %get-tuple-element.122), kind=kOutput, calls=%fused_computation.15 | convolution fusion | flops 805306368 | bytes 8388608 | tf_op jit(solution)/shard_map/cthd,cshd->chts/dot_general | solution.py:96
  274.3 10.6 %fusion.5 = f32[4,16,64,128]{3,2,1,0:T(8,128)S(1)} fusion(f32[4,128,16,64]{3,2,1,0:T(8,128)} %get-tuple-element.121, f32[4,16,64,64]{3,2,1,0:T(8,128)} %get-tuple-element.56, f32[16,64,64]{2,1,0:T(8,128)S(1)} %copy.151, f32[4,16,64]{2,1,0:T(8,128)S(1)} %get-tuple-element.57), kind=kOutput, calls=%fused_computation.11 | convolution fusion | flops 403177472 | bytes 5521408 | tf_op jit(solution)/shard_map/cthd,chde->cthe/dot_general | solution.py:151
  284.9 6.1 %fusion.56 = (f32[4,128,16]{1,2,0:T(8,128)S(1)}, f32[4,128,16,64]{1,3,2,0:T(8,128)S(1)}) fusion(f32[4,16,64,128]{3,2,1,0:T(8,128)S(1)} %fusion.5, f32[4,128,16,64]{1,3,2,0:T(8,128)S(1)} %copy-done.5, bf16[4,128,16,64]{1,3,2,0:T(8,128)(2,1)} %bitcast.14, f32[4,16,128,128]{3,2,1,0:T(8,128)S(1)} %copy-done.4, pred[4,128,128]{2,1,0:T(8,128)(4,1)S(1)} %compare_and_fusion), kind=kOutput, calls=%fused_computation.98 | convolution fusion | flops 808968192 | bytes 11632640 | tf_op jit(solution)/shard_map/chts,cshd->cthd/dot_general | solution.py:102
  292.1 18.4 %all_to_all.68 = bf16[4,128,1024]{1,2,0:T(8,128)(2,1)S(1)} all-to-all(bf16[4,128,1024]{1,2,0:T(8,128)(2,1)S(1)} %bitcast.86), channel_id=1, replica_groups=mesh['seq'=64,'head'=4] {'head'}, dimensions={0} | all-to-all | bytes 2097152 | tf_op jit(solution)/shard_map/all_to_all | solution.py:162
  310.5 1.5 convert_element_type.115
  312.0 3.1 copy.158
  315.0 3.2 fusion.24
  (121 shorter events, 40.4 us)
Async XLA Ops:
  0.0 36.4 %copy-start = (bf16[128,4096]{1,0:T(8,128)(2,1)S(1)}, bf16[128,4096]{1,0:T(8,128)(2,1)}, u32[]{:S(2)}) copy-start(bf16[128,4096]{1,0:T(8,128)(2,1)} %param.26) | copy-start | bytes 3145732
  0.0 6.9 %copy-start.12 = (bf16[128,4096]{1,0:T(8,128)(2,1)S(1)}, bf16[128,4096]{1,0:T(8,128)(2,1)}, u32[]{:S(2)}) copy-start(bf16[128,4096]{1,0:T(8,128)(2,1)} %param.18) | copy-start | bytes 3145732
  2.4 19.6 %all-to-all-start = ((bf16[128,4,1024]{0,2,1:T(8,128)(2,1)}), bf16[128,4,1024]{0,2,1:T(8,128)(2,1)S(1)}, u32[]{:S(2)}, u32[]{:S(2)}) async-start(bf16[128,4,1024]{0,2,1:T(8,128)(2,1)} %bitcast.1), calls=%async_computation | async-start | bytes 2097152 | tf_op jit(solution)/shard_map/all_to_all | solution.py:63
  6.9 29.5 %copy-start.15 = (f32[4096]{0:T(1024)S(1)}, f32[4096]{0:T(1024)}, u32[]{:S(2)}) copy-start(f32[4096]{0:T(1024)} %param.24) | copy-start | bytes 49156
  6.9 29.5 %copy-start.16 = (f32[4096]{0:T(1024)S(1)}, f32[4096]{0:T(1024)}, u32[]{:S(2)}) copy-start(f32[4096]{0:T(1024)} %param.23) | copy-start | bytes 49156
  22.0 18.7 %copy-start.6 = (bf16[128,4,1024]{0,2,1:T(8,128)(2,1)}, bf16[128,4,1024]{0,2,1:T(8,128)(2,1)S(1)}, u32[]{:S(2)}) copy-start(bf16[128,4,1024]{0,2,1:T(8,128)(2,1)S(1)} %all-to-all-done) | copy-start | bytes 3145732
  22.0 21.1 %all-to-all-start.2 = ((bf16[128,4,1024]{0,2,1:T(8,128)(2,1)}), bf16[128,4,1024]{0,2,1:T(8,128)(2,1)S(1)}, u32[]{:S(2)}, u32[]{:S(2)}) async-start(bf16[128,4,1024]{0,2,1:T(8,128)(2,1)} %bitcast.88), calls=%async_computation.2 | async-start | bytes 2097152 | tf_op jit(solution)/shard_map/all_to_all | solution.py:64
  26.4 10.0 %collective-permute-start = (bf16[1,4096]{1,0:T(2,128)(2,1)S(1)}, bf16[1,4096]{1,0:T(2,128)(2,1)S(1)}, u32[]{:S(2)}, u32[]{:S(2)}) collective-permute-start(bf16[1,4096]{1,0:T(2,128)(2,1)S(1)} %slice.59), channel_id=1, source_target_pairs={{0,1},{1,2},{2,3},{3,4},{4,5},{5,6},{6,7},{7,8},{8,9},{9,10},{10,1... | collective-permute-start | bytes 24584 | tf_op jit(solution)/shard_map/ppermute | solution.py:18
  40.7 7.9 %copy-start.13 = (bf16[128,4096]{1,0:T(8,128)(2,1)S(1)}, bf16[128,4096]{1,0:T(8,128)(2,1)}, u32[]{:S(2)}) copy-start(bf16[128,4096]{1,0:T(8,128)(2,1)} %param.19) | copy-start | bytes 3145732
  43.1 5.5 %copy-start.7 = (bf16[128,4,1024]{0,2,1:T(8,128)(2,1)}, bf16[128,4,1024]{0,2,1:T(8,128)(2,1)S(1)}, u32[]{:S(2)}) copy-start(bf16[128,4,1024]{0,2,1:T(8,128)(2,1)S(1)} %all-to-all-done.2) | copy-start | bytes 3145732
  43.1 21.1 %all-to-all-start.1 = ((bf16[128,4,1024]{0,2,1:T(8,128)(2,1)}), bf16[128,4,1024]{0,2,1:T(8,128)(2,1)}, u32[]{:S(2)}, u32[]{:S(2)}) async-start(bf16[128,4,1024]{0,2,1:T(8,128)(2,1)} %bitcast.5), calls=%async_computation.1 | async-start | bytes 2097152 | tf_op jit(solution)/shard_map/all_to_all | solution.py:66
  64.2 27.6 %all-to-all-start.3 = ((bf16[128,4,1024]{0,2,1:T(8,128)(2,1)}), bf16[128,4,1024]{0,2,1:T(8,128)(2,1)}, u32[]{:S(2)}, u32[]{:S(2)}) async-start(bf16[128,4,1024]{0,2,1:T(8,128)(2,1)} %bitcast.87), calls=%async_computation.3 | async-start | bytes 2097152 | tf_op jit(solution)/shard_map/all_to_all | solution.py:65
  77.9 2.1 copy-start.3
  111.5 16.9 %collective-permute-start.2 = (f32[16,65,64]{1,2,0:T(8,128)}, f32[16,65,64]{1,2,0:T(8,128)S(1)}, u32[]{:S(2)}, u32[]{:S(2)}) collective-permute-start(f32[16,65,64]{1,2,0:T(8,128)} %pad_maximum_fusion), channel_id=1, source_target_pairs={{0,8},{4,12},{8,16},{12,20},{16,24},{20,28},{24,32},{28,36},{32,40... | collective-permute-start | bytes 798728 | tf_op jit(solution)/shard_map/ppermute | solution.py:18
  114.4 18.1 %collective-permute-start.1 = (f32[16,65,64]{1,2,0:T(8,128)}, f32[16,65,64]{1,2,0:T(8,128)S(1)}, u32[]{:S(2)}, u32[]{:S(2)}) collective-permute-start(f32[16,65,64]{1,2,0:T(8,128)} %pad_maximum_fusion), channel_id=1, source_target_pairs={{0,4},{4,8},{8,12},{12,16},{16,20},{20,24},{24,28},{28,32},{32,36}... | collective-permute-start | bytes 798728 | tf_op jit(solution)/shard_map/ppermute | solution.py:18
  132.6 3.3 %copy-start.10 = (f32[16,65,64]{1,2,0:T(8,128)}, f32[16,65,64]{1,2,0:T(8,128)S(1)}, u32[]{:S(2)}) copy-start(f32[16,65,64]{1,2,0:T(8,128)S(1)} %collective-permute-done.1) | copy-start | bytes 798724
  138.3 14.5 %collective-permute-start.3 = (f32[16,65,64]{1,2,0:T(8,128)S(1)}, f32[16,65,64]{1,2,0:T(8,128)S(1)}, u32[]{:S(2)}, u32[]{:S(2)}) collective-permute-start(f32[16,65,64]{1,2,0:T(8,128)S(1)} %pad_maximum_fusion.1), channel_id=1, source_target_pairs={{0,8},{4,12},{8,16},{12,20},{16,24},{20,28},{24,32},{28,36},{32,40... | collective-permute-start | bytes 798728 | tf_op jit(solution)/shard_map/ppermute | solution.py:18
  152.7 0.8 copy-start.11
  157.4 27.4 %collective-permute-start.4 = (f32[16,65,64]{1,2,0:T(8,128)S(1)}, f32[16,65,64]{1,2,0:T(8,128)S(1)}, u32[]{:S(2)}, u32[]{:S(2)}) collective-permute-start(f32[16,65,64]{1,2,0:T(8,128)S(1)} %pad_maximum_fusion.2), channel_id=1, source_target_pairs={{0,16},{4,20},{8,24},{12,28},{16,32},{20,36},{24,40},{28,44},{32,4... | collective-permute-start | bytes 798728 | tf_op jit(solution)/shard_map/ppermute | solution.py:18
  184.8 0.8 copy-start.9
  190.3 29.7 %collective-permute-start.5 = (f32[16,65,64]{1,2,0:T(8,128)}, f32[16,65,64]{1,2,0:T(8,128)S(1)}, u32[]{:S(2)}, u32[]{:S(2)}) collective-permute-start(f32[16,65,64]{1,2,0:T(8,128)} %pad_maximum_fusion.3), channel_id=1, source_target_pairs={{0,32},{4,36},{8,40},{12,44},{16,48},{20,52},{24,56},{28,60},{32,6... | collective-permute-start | bytes 798728 | tf_op jit(solution)/shard_map/ppermute | solution.py:18
  219.9 3.3 %copy-start.8 = (f32[16,65,64]{1,2,0:T(8,128)}, f32[16,65,64]{1,2,0:T(8,128)S(1)}, u32[]{:S(2)}) copy-start(f32[16,65,64]{1,2,0:T(8,128)S(1)} %collective-permute-done.5) | copy-start | bytes 798724
  223.3 9.7 %copy-start.2 = (f32[128,4,1024]{0,2,1:T(8,128)S(1)}, f32[128,4,1024]{0,2,1:T(8,128)}, u32[]{:S(2)}) copy-start(f32[128,4,1024]{0,2,1:T(8,128)} %convert_element_type.114) | copy-start | bytes 6291460
  225.8 17.1 %collective-permute-start.6 = (f32[16,65,64]{1,2,0:T(8,128)S(1)}, f32[16,65,64]{1,2,0:T(8,128)S(1)}, u32[]{:S(2)}, u32[]{:S(2)}) collective-permute-start(f32[16,65,64]{1,2,0:T(8,128)S(1)} %pad_maximum_fusion.4), channel_id=1, source_target_pairs={{0,64},{4,68},{8,72},{12,76},{16,80},{20,84},{24,88},{28,92},{32,9... | collective-permute-start | bytes 798728 | tf_op jit(solution)/shard_map/ppermute | solution.py:18
  243.8 30.2 %collective-permute-start.7 = (f32[16,65,64]{1,2,0:T(8,128)S(1)}, f32[16,65,64]{1,2,0:T(8,128)S(1)}, u32[]{:S(2)}, u32[]{:S(2)}) collective-permute-start(f32[16,65,64]{1,2,0:T(8,128)S(1)} %pad_maximum_fusion.5), channel_id=1, source_target_pairs={{0,128},{4,132},{8,136},{12,140},{16,144},{20,148},{24,152},{28,15... | collective-permute-start | bytes 798728 | tf_op jit(solution)/shard_map/ppermute | solution.py:18
  274.3 10.6 %copy-start.4 = (f32[4,16,128,128]{3,2,1,0:T(8,128)S(1)}, f32[4,16,128,128]{3,2,1,0:T(8,128)}, u32[]{:S(2)}) copy-start(f32[4,16,128,128]{3,2,1,0:T(8,128)} %fusion.9) | copy-start | bytes 12582916
  274.3 10.6 %copy-start.5 = (f32[4,128,16,64]{1,3,2,0:T(8,128)S(1)}, f32[4,128,16,64]{1,3,2,0:T(8,128)}, u32[]{:S(2)}) copy-start(f32[4,128,16,64]{1,3,2,0:T(8,128)} %fusion) | copy-start | bytes 6291460
  312.0 3.1 copy-start.14
  312.0 6.2 %copy-start.1 = (bf16[128,4096]{1,0:T(8,128)(2,1)S(1)}, bf16[128,4096]{1,0:T(8,128)(2,1)}, u32[]{:S(2)}) copy-start(bf16[128,4096]{1,0:T(8,128)(2,1)} %param.26) | copy-start | bytes 3145732

commit v2 on v0

--- a/solution.py
+++ b/solution.py
@@ -39,13 +39,13 @@
     cluster_mean_shift_add,
 ):
     head_count = lax.axis_size("head")
-    seq_index = lax.axis_index("seq")
+    seq_index = lax.axis_index(("x", "z", "core"))
     head_index = lax.axis_index("head")
     row_count = layer_entries.shape[0]
     block_start = (seq_index * head_count + head_index) * row_count
     own_seg = lax.dynamic_slice_in_dim(prompt_label, block_start, row_count, 0)
     prior_seg = jnp.concatenate([earlier_segment(prompt_label, block_start), own_seg[:-1]])
-    edge_row = shifted(layer_entries[-1:], ("seq", "head"), 1)
+    edge_row = shifted(layer_entries[-1:], ("x", "z", "core", "head"), 1)
     prev_rows = jnp.concatenate([edge_row, layer_entries[:-1]], axis=0)
     prev_rows = jnp.where((prior_seg == own_seg)[:, None], prev_rows, jnp.zeros_like(prev_rows))
     current = layer_entries.astype(jnp.float32)
@@ -125,10 +125,33 @@
         multiply, jnp.ones((local_heads, ATTENTION_SPAN), jnp.float32), stretch_decay
     )
 
-    def relay(iteration, incoming):
-        return shifted(span_decay[:, :, None] * incoming + span_state, "seq", 1)
-
-    incoming = lax.fori_loop(0, lax.axis_size("seq") - 1, relay, zero_state)
+    def fold(gathered, position):
+        count = gathered.shape[0]
+        prefix_state = jnp.zeros_like(gathered[0, :, :ATTENTION_SPAN])
+        prefix_decay = jnp.ones_like(gathered[0, :, ATTENTION_SPAN])
+        total_state, total_decay = prefix_state, prefix_decay
+        for k in range(count):
+            part_decay = gathered[k, :, ATTENTION_SPAN]
+            part_state = gathered[k, :, :ATTENTION_SPAN]
+            take = k < position
+            prefix_state = jnp.where(
+                take, part_decay[:, :, None] * prefix_state + part_state, prefix_state
+            )
+            prefix_decay = jnp.where(take, part_decay * prefix_decay, prefix_decay)
+            total_state = part_decay[:, :, None] * total_state + part_state
+            total_decay = part_decay * total_decay
+        return (
+            jnp.concatenate([prefix_state, prefix_decay[:, None, :]], axis=1),
+            jnp.concatenate([total_state, total_decay[:, None, :]], axis=1),
+        )
+
+    own = jnp.concatenate([span_state, span_decay[:, None, :]], axis=1)
+    core_prefix, core_total = fold(lax.all_gather(own, "core"), lax.axis_index("core"))
+    z_prefix, z_total = fold(lax.all_gather(core_total, "z"), lax.axis_index("z"))
+    x_prefix, _ = fold(lax.all_gather(z_total, "x"), lax.axis_index("x"))
+    incoming = x_prefix[:, :ATTENTION_SPAN]
+    for level in (z_prefix, core_prefix):
+        incoming = level[:, ATTENTION_SPAN][:, :, None] * incoming + level[:, :ATTENTION_SPAN]
     start_state = local_start + decay_before[:, :, :, None] * incoming[None]
     keep_first = (seg_block == stretch_prior[:, None]).astype(jnp.float32)
     carried = jnp.einsum(
@@ -149,15 +172,22 @@
 
 
 def solution(mesh):
+    seq_count, head_count = mesh.devices.shape
+    core_count = 2
+    z_count = min(8, seq_count // core_count)
+    fine_mesh = jax.sharding.Mesh(
+        mesh.devices.reshape(seq_count // (z_count * core_count), z_count, core_count, head_count),
+        ("x", "z", "core", "head"),
+    )
     return jax.shard_map(
         local,
-        mesh=mesh,
+        mesh=fine_mesh,
         in_specs=(
-            P(("seq", "head"), None),
-            P(("seq", "head"), None),
-            P(("seq", "head"), None),
-            P(("seq", "head"), None),
-            P(("seq", "head"), None),
+            P(("x", "z", "core", "head"), None),
+            P(("x", "z", "core", "head"), None),
+            P(("x", "z", "core", "head"), None),
+            P(("x", "z", "core", "head"), None),
+            P(("x", "z", "core", "head"), None),
             P(),
             P(),
             P(),
@@ -167,6 +197,6 @@
             P(),
             P(),
         ),
-        out_specs=P(("seq", "head"), None),
+        out_specs=P(("x", "z", "core", "head"), None),
         check_vma=False,
     )

time: 973 us -> 277 us (0.28)
  the two profiles are of different devices: /device:TPU:6 before, /device:TPU:1 now
where the time goes in v2:
time: 277 us; the launch traced here: 275 us
  waiting for transfers between devices  88.3 us (32%)
  other arithmetic  56 us (20%)
  matrix products  41.9 us (15%)
  local copies, waits for them, and re-layouts  31.3 us (11%)
  blocking collectives  21.9 us (8%)
  starting transfers between devices  20.6 us (7%)
  between operations  14.9 us (5%)
    all_gather x1, waiting for transfers between devices, local(): lax.all_gather(core_total, 'z')  56.1 us
    all_to_all x1, blocking collectives, local(): lax.all_to_all(normed, 'head', split_axis=0, concat_axis=1, tiled=True)  17.9 us
    all_gather x1, waiting for transfers between devices, local(): x_prefix, _ = fold(lax.all_gather(z_total, 'x'), lax.axis_index('x'))  14.9 us
    dot_general x1, matrix products, local(): jnp.einsum('cthd,cshd->chts', scaled_query, scaled_key, precision=highest)  13.5 us
    all_to_all x1, waiting for transfers between devices, local(): lax.all_to_all(acceptance_linear, 'head', split_axis=1, concat_axis=0, ti...  12.2 us
    mul x1, other arithmetic, local(): scaled_key = lookup_vectors * jnp.exp(-cumulative)  11.2 us
    dot_general x1, matrix products, local(): jnp.einsum('cthd,chde->cthe', scaled_query * keep_first[:, :, None, None]...  10.3 us
    dot_general x1, matrix products, local(): jnp.einsum('cthd,cthe->chde', tail_keys, payload_vectors, precision=highest)  7.8 us
  transfers between devices with their start and end apart: 7, of which 4 were waited for; matrix products, arithmetic and copies ran while one was open for 24% of the time, Pallas kernels for 0%

profile of v2, /device:TPU:1, one launch (start us, length us, event | category | flops | bytes accessed | tf_op | source)
XLA Modules:
  0.0 275.1 jit_solution(12129698403576386528)
XLA Ops:
  6.5 2.4 copy.438
  9.0 5.0 %all-to-all-start = ((bf16[128,4,1024]{0,2,1:T(8,128)(2,1)}), bf16[128,4,1024]{0,2,1:T(8,128)(2,1)S(1)}, u32[]{:S(2)}, u32[]{:S(2)}) async-start(bf16[128,4,1024]{0,2,1:T(8,128)(2,1)} %bitcast.1), calls=%async_computation | async-start | bytes 2097152 | tf_op jit(solution)/shard_map/all_to_all | solution.py:63
  14.0 1.3 copy.443
  15.3 12.2 %all-to-all-done = bf16[128,4,1024]{0,2,1:T(8,128)(2,1)S(1)} async-done(((bf16[128,4,1024]{0,2,1:T(8,128)(2,1)}), bf16[128,4,1024]{0,2,1:T(8,128)(2,1)S(1)}, u32[]{:S(2)}, u32[]{:S(2)}) %all-to-all-start) | async-done | bytes 1048608 | tf_op jit(solution)/shard_map/all_to_all | solution.py:63
  27.5 3.5 %all-to-all-start.2 = ((bf16[128,4,1024]{0,2,1:T(8,128)(2,1)}), bf16[128,4,1024]{0,2,1:T(8,128)(2,1)S(1)}, u32[]{:S(2)}, u32[]{:S(2)}) async-start(bf16[128,4,1024]{0,2,1:T(8,128)(2,1)} %bitcast.143), calls=%async_computation.2 | async-start | bytes 2097152 | tf_op jit(solution)/shard_map/all_to_all | solution.py:64
  31.9 3.3 %collective-permute-start = (bf16[1,4096]{1,0:T(2,128)(2,1)S(1)}, bf16[1,4096]{1,0:T(2,128)(2,1)S(1)}, u32[]{:S(2)}, u32[]{:S(2)}) collective-permute-start(bf16[1,4096]{1,0:T(2,128)(2,1)S(1)} %slice.104), channel_id=1, source_target_pairs={{0,1},{1,2},{2,3},{3,4},{4,5},{5,6},{6,7},{7,8},{8,9},{9,10},{10,1... | collective-permute-start | bytes 24584 | tf_op jit(solution)/shard_map/ppermute | solution.py:18
  36.0 1.3 fusion.68
  38.7 5.0 %collective-permute-done = bf16[1,4096]{1,0:T(2,128)(2,1)S(1)} collective-permute-done((bf16[1,4096]{1,0:T(2,128)(2,1)S(1)}, bf16[1,4096]{1,0:T(2,128)(2,1)S(1)}, u32[]{:S(2)}, u32[]{:S(2)}) %collective-permute-start) | collective-permute-done | bytes 8224 | tf_op jit(solution)/shard_map/ppermute | solution.py:18
  43.7 4.3 %fusion.4 = bf16[128,4096]{1,0:T(8,128)(2,1)} fusion(bf16[128,4096]{1,0:T(8,128)(2,1)S(1)} %copy-done, bf16[4096,128]{1,0:T(8,128)(2,1)} %param.25, bf16[128,4096]{1,0:T(8,128)(2,1)} %param.21, bf16[127,4096]{1,0:T(8,128)(2,1)} %bitcast.146, bf16[1,4096]{1,0:T(2,128)(2,1)S(1)} %collective-permute-done, f32[4096]{0:T(1024)S(1)} %copy-done.13, ...), kind=kOutput, calls=%fused_computation.10 | convolution fusion | flops 276316160 | bytes 5275776 | tf_op jit(solution)/shard_map/dot_general | solution.py:58
  48.0 2.3 copy.461
  50.3 4.4 %all-to-all-start.1 = ((bf16[128,4,1024]{0,2,1:T(8,128)(2,1)}), bf16[128,4,1024]{0,2,1:T(8,128)(2,1)}, u32[]{:S(2)}, u32[]{:S(2)}) async-start(bf16[128,4,1024]{0,2,1:T(8,128)(2,1)} %bitcast.5), calls=%async_computation.1 | async-start | bytes 2097152 | tf_op jit(solution)/shard_map/all_to_all | solution.py:66
  54.7 1.3 copy.462
  58.6 1.4 convert_element_type.112
  60.0 3.0 %copy.442 = f32[4,128,16,64]{3,2,1,0:T(8,128)} copy(f32[4,128,16,64]{1,3,2,0:T(8,128)S(1)} %bitcast.130) | data formatting | bytes 4194304 | tf_op jit(solution)/shard_map/convert_element_type | solution.py:87
  63.0 2.7 convert_element_type.114
  65.7 4.0 %copy.444 = f32[4,128,16,64]{3,2,1,0:T(8,128)} copy(f32[4,128,16,64]{1,3,2,0:T(8,128)} %bitcast.132) | data formatting | bytes 4194304 | tf_op jit(solution)/shard_map/convert_element_type | solution.py:88
  69.7 4.3 %all-to-all-start.3 = ((bf16[128,4,1024]{0,2,1:T(8,128)(2,1)}), bf16[128,4,1024]{0,2,1:T(8,128)(2,1)}, u32[]{:S(2)}, u32[]{:S(2)}) async-start(bf16[128,4,1024]{0,2,1:T(8,128)(2,1)} %bitcast.142), calls=%async_computation.3 | async-start | bytes 2097152 | tf_op jit(solution)/shard_map/all_to_all | solution.py:65
  74.1 2.7 convert_element_type.113
  76.7 4.1 %copy.440 = f32[4,128,16,64]{3,2,1,0:T(8,128)} copy(f32[4,128,16,64]{1,3,2,0:T(8,128)} %bitcast.139) | data formatting | bytes 4194304 | tf_op jit(solution)/shard_map/convert_element_type | solution.py:90
  80.9 2.5 fusion.70
  83.4 2.0 copy-done.3
  85.9 11.2 %exponential_multiply_fusion = (f32[4,128,16,64]{3,2,1,0:T(8,128)}, f32[4,128,16,64]{3,2,1,0:T(8,128)}, f32[4,128,16,64]{3,2,1,0:T(8,128)}, f32[4,128,16,64]{3,2,1,0:T(8,128)}) fusion(f32[4,128,16,64]{3,2,1,0:T(8,128)} %copy.444, f32[4,128,16,64]{3,2,1,0:T(8,128)} %copy-done.3, f32[4,128]{1,0:T(4,128)S(1)} %get-tuple-element.139, ...), kind=kLoop, calls=%fused_computation.21 | loop fusion | flops 4194304 | bytes 16797696 | tf_op jit(solution)/shard_map/mul | solution.py:95
  97.1 7.8 %fusion.7 = f32[4,16,64,64]{3,2,1,0:T(8,128)} fusion(bf16[4,128,16,64]{1,3,2,0:T(8,128)(2,1)} %bitcast.14, f32[4,128,16,64]{3,2,1,0:T(8,128)} %get-tuple-element.132), kind=kOutput, calls=%fused_computation.13 | convolution fusion | flops 402653184 | bytes 4194304 | tf_op jit(solution)/shard_map/cthd,cthe->chde/dot_general | solution.py:109
  104.9 8.9 %while.26 = (s32[]{:T(128)}, f32[16,64,64]{2,1,0:T(8,128)S(1)}, f32[4,16,64,64]{3,2,1,0:T(8,128)}, f32[4,16,64]{2,1,0:T(8,128)S(1)}, f32[4,16,64,64]{3,2,1,0:T(8,128)}, /*index=5*/s32[]{:T(128)}, s32[]{:T(128)}) while((s32[]{:T(128)}, f32[16,64,64]{2,1,0:T(8,128)S(1)}, f32[4,16,64,64]{3,2,1,0:T(8,128)}, ...), condition=%wide.region_3.4_spmd.clone, body=%wide.region_2.3_spmd.clone.sunk | while | flops 262147 | bytes 1585260 | solution.py:119
  105.8 1.3 bitcast_add_fusion.14
  108.0 1.3 bitcast_add_fusion.14
  109.4 0.9 bitcast_dynamic-update-slice_fusion.4
  110.3 1.3 bitcast_add_fusion.14
  111.6 0.9 bitcast_dynamic-update-slice_fusion.4
  112.5 1.3 bitcast_add_fusion.14
  113.8 1.0 copy.450
  114.8 1.2 pad_maximum_fusion
  116.1 4.0 %all-gather = f32[32,65,64]{1,2,0:T(8,128)S(1)} all-gather(f32[16,65,64]{1,2,0:T(8,128)S(1)} %pad_maximum_fusion), channel_id=2, replica_groups=mesh['x'=4,'z'=8,'core'=2,'head'=4] {'core'}, dimensions={0}, use_global_device_ids=true | all-gather | bytes 798720 | tf_op jit(solution)/shard_map/all_gather | solution.py:149
  121.0 1.0 pad_maximum_fusion.1
  124.4 56.1 %all-gather.6.cloned.1.call-done = f32[128,65,64]{1,2,0:T(8,128)} async-done(((f32[16,65,64]{1,2,0:T(8,128)}), f32[128,65,64]{1,2,0:T(8,128)}) %all-gather.6.cloned.1.call-update) | async-done | bytes 2129936 | tf_op jit(solution)/shard_map/all_gather | solution.py:150
  180.5 4.7 %select_reduce_fusion = (f32[16,64]{1,0:T(8,128)S(1)}, f32[16,64]{1,0:T(8,128)S(1)}, f32[16,64]{1,0:T(8,128)S(1)}, f32[16,64]{1,0:T(8,128)S(1)}, f32[16,64]{1,0:...) fusion(f32[8,16,65,64]{2,3,1,0:T(8,128)} %bitcast.127, ...), kind=kLoop, calls=%fused_computation.97 | loop fusion | flops 9216 | bytes 73729 | tf_op jit(solution)/shard_map/jit(_where)/select_n | solution.py:140
  185.9 1.0 pad_maximum_fusion.2
  187.1 3.5 %fusion = f32[4,128,16,64]{1,3,2,0:T(8,128)} fusion(f32[4,128,16,64]{1,3,2,0:T(8,128)} %bitcast.133, f32[4,128,16,64]{1,3,2,0:T(8,128)S(1)} %bitcast.131, f32[16,64]{1,0:T(8,128)S(1)} %mul.529), kind=kOutput, calls=%fused_computation.5 | output fusion | flops 1056831 | bytes 6295552 | tf_op jit(solution)/shard_map/mul | solution.py:104
  190.6 13.5 %fusion.9 = f32[4,16,128,128]{3,2,1,0:T(8,128)} fusion(f32[4,128,16,64]{3,2,1,0:T(8,128)S(1)} %copy-done.4, f32[4,128,16,64]{3,2,1,0:T(8,128)} %get-tuple-element.134), kind=kOutput, calls=%fused_computation.15 | convolution fusion | flops 805306368 | bytes 8388608 | tf_op jit(solution)/shard_map/cthd,cshd->chts/dot_general | solution.py:96
  204.1 14.9 %all-gather.8.cloned.1.call-done = f32[64,65,64]{1,2,0:T(8,128)} async-done(((f32[16,65,64]{1,2,0:T(8,128)}), f32[64,65,64]{1,2,0:T(8,128)}) %all-gather.8.cloned.1.call-update) | async-done | bytes 1064976 | tf_op jit(solution)/shard_map/all_gather | solution.py:151
  219.0 2.8 %slice_reduce_fusion.2 = (f32[16,64]{1,0:T(8,128)S(1)}, f32[16,64]{1,0:T(8,128)S(1)}, f32[16,64]{1,0:T(8,128)S(1)}, f32[16,64]{1,0:T(8,128)S(1)}) fusion(f32[4,16,65,64]{2,3,1,0:T(8,128)} %bitcast.137), kind=kLoop, calls=%fused_computation.73 | loop fusion | flops 1024 | bytes 32768 | tf_op jit(solution)/shard_map/slice | solution.py:134
  221.8 4.3 %fusion.48 = f32[16,64,64]{1,2,0:T(8,128)} fusion(f32[4,16,65,64]{2,3,1,0:T(8,128)S(1)} %bitcast.138, f32[8,16,65,64]{2,3,1,0:T(8,128)} %bitcast.128, f32[2,16,65,64]{2,3,1,0:T(8,128)S(1)} %bitcast.136, f32[16,64]{1,0:T(8,128)S(1)} %get-tuple-element.107, f32[16,64]{1,0:T(8,128)S(1)} %get-tuple-element.108, f32[16,64]{1,0:T(8,128)S(1)} %get-tuple-element.94, ...), kind=kLoop, calls=%fused_computation.62 | loop fusion | flops 2818048 | bytes 3997710 | tf_op jit(solution)/shard_map/mul | solution.py:155
  226.1 1.2 copy.456
  227.4 10.3 %fusion.5 = f32[4,16,64,128]{3,2,1,0:T(8,128)S(1)} fusion(f32[4,128,16,64]{3,2,1,0:T(8,128)} %get-tuple-element.133, f32[4,16,64,64]{3,2,1,0:T(8,128)S(1)} %copy-done.10, f32[16,64,64]{2,1,0:T(8,128)S(1)} %copy.456, f32[4,16,64]{2,1,0:T(8,128)S(1)} %get-tuple-element.57), kind=kOutput, calls=%fused_computation.11 | convolution fusion | flops 403177472 | bytes 5521408 | tf_op jit(solution)/shard_map/cthd,chde->cthe/dot_general | solution.py:157
  237.7 6.2 %fusion.69 = (f32[4,128,16]{1,2,0:T(8,128)S(1)}, f32[4,128,16,64]{1,3,2,0:T(8,128)S(1)}) fusion(f32[4,16,64,128]{3,2,1,0:T(8,128)S(1)} %fusion.5, f32[4,128,16,64]{1,3,2,0:T(8,128)S(1)} %copy-done.7, bf16[4,128,16,64]{1,3,2,0:T(8,128)(2,1)} %bitcast.14, f32[4,16,128,128]{3,2,1,0:T(8,128)S(1)} %copy-done.5, pred[4,128,128]{2,1,0:T(8,128)(4,1)S(1)} %compare_and_fusion), kind=kOutput, calls=%fused_computation.136 | convolution fusion | flops 808968192 | bytes 11632640 | tf_op jit(solution)/shard_map/chts,cshd->cthd/dot_general | solution.py:102
  245.0 17.9 %all_to_all.68 = bf16[4,128,1024]{1,2,0:T(8,128)(2,1)S(1)} all-to-all(bf16[4,128,1024]{1,2,0:T(8,128)(2,1)S(1)} %bitcast.141), channel_id=1, replica_groups=mesh['x'=4,'z'=8,'core'=2,'head'=4] {'head'}, dimensions={0} | all-to-all | bytes 2097152 | tf_op jit(solution)/shard_map/all_to_all | solution.py:168
  263.0 1.9 copy.464
  264.9 3.4 %fusion.24 = bf16[128,4096]{1,0:T(8,128)(2,1)} fusion(f32[128,4096]{1,0:T(8,128)} %copy.464, bf16[128,4096]{1,0:T(8,128)(2,1)} %param.20), kind=kLoop, calls=%fused_computation.43 | loop fusion | flops 3670016 | bytes 4194304 | tf_op jit(solution)/shard_map/convert_element_type | solution.py:169
  (84 shorter events, 12.1 us)
Async XLA Ops:
  6.5 37.2 %copy-start = (bf16[128,4096]{1,0:T(8,128)(2,1)S(1)}, bf16[128,4096]{1,0:T(8,128)(2,1)}, u32[]{:S(2)}) copy-start(bf16[128,4096]{1,0:T(8,128)(2,1)} %param.26) | copy-start | bytes 3145732
  6.5 7.4 %copy-start.11 = (bf16[128,4096]{1,0:T(8,128)(2,1)S(1)}, bf16[128,4096]{1,0:T(8,128)(2,1)}, u32[]{:S(2)}) copy-start(bf16[128,4096]{1,0:T(8,128)(2,1)} %param.18) | copy-start | bytes 3145732
  9.0 18.5 %all-to-all-start = ((bf16[128,4,1024]{0,2,1:T(8,128)(2,1)}), bf16[128,4,1024]{0,2,1:T(8,128)(2,1)S(1)}, u32[]{:S(2)}, u32[]{:S(2)}) async-start(bf16[128,4,1024]{0,2,1:T(8,128)(2,1)} %bitcast.1), calls=%async_computation | async-start | bytes 2097152 | tf_op jit(solution)/shard_map/all_to_all | solution.py:63
  14.0 29.8 %copy-start.13 = (f32[4096]{0:T(1024)S(1)}, f32[4096]{0:T(1024)}, u32[]{:S(2)}) copy-start(f32[4096]{0:T(1024)} %param.24) | copy-start | bytes 49156
  14.0 29.8 %copy-start.14 = (f32[4096]{0:T(1024)S(1)}, f32[4096]{0:T(1024)}, u32[]{:S(2)}) copy-start(f32[4096]{0:T(1024)} %param.23) | copy-start | bytes 49156
  27.5 20.5 %copy-start.8 = (bf16[128,4,1024]{0,2,1:T(8,128)(2,1)}, bf16[128,4,1024]{0,2,1:T(8,128)(2,1)S(1)}, u32[]{:S(2)}) copy-start(bf16[128,4,1024]{0,2,1:T(8,128)(2,1)S(1)} %all-to-all-done) | copy-start | bytes 3145732
  27.5 22.8 %all-to-all-start.2 = ((bf16[128,4,1024]{0,2,1:T(8,128)(2,1)}), bf16[128,4,1024]{0,2,1:T(8,128)(2,1)S(1)}, u32[]{:S(2)}, u32[]{:S(2)}) async-start(bf16[128,4,1024]{0,2,1:T(8,128)(2,1)} %bitcast.143), calls=%async_computation.2 | async-start | bytes 2097152 | tf_op jit(solution)/shard_map/all_to_all | solution.py:64
  31.9 11.9 %collective-permute-start = (bf16[1,4096]{1,0:T(2,128)(2,1)S(1)}, bf16[1,4096]{1,0:T(2,128)(2,1)S(1)}, u32[]{:S(2)}, u32[]{:S(2)}) collective-permute-start(bf16[1,4096]{1,0:T(2,128)(2,1)S(1)} %slice.104), channel_id=1, source_target_pairs={{0,1},{1,2},{2,3},{3,4},{4,5},{5,6},{6,7},{7,8},{8,9},{9,10},{10,1... | collective-permute-start | bytes 24584 | tf_op jit(solution)/shard_map/ppermute | solution.py:18
  50.3 4.5 %copy-start.12 = (bf16[128,4096]{1,0:T(8,128)(2,1)S(1)}, bf16[128,4096]{1,0:T(8,128)(2,1)}, u32[]{:S(2)}) copy-start(bf16[128,4096]{1,0:T(8,128)(2,1)} %param.19) | copy-start | bytes 3145732
  50.3 5.8 %copy-start.9 = (bf16[128,4,1024]{0,2,1:T(8,128)(2,1)}, bf16[128,4,1024]{0,2,1:T(8,128)(2,1)S(1)}, u32[]{:S(2)}) copy-start(bf16[128,4,1024]{0,2,1:T(8,128)(2,1)S(1)} %all-to-all-done.2) | copy-start | bytes 3145732
  50.3 19.5 %all-to-all-start.1 = ((bf16[128,4,1024]{0,2,1:T(8,128)(2,1)}), bf16[128,4,1024]{0,2,1:T(8,128)(2,1)}, u32[]{:S(2)}, u32[]{:S(2)}) async-start(bf16[128,4,1024]{0,2,1:T(8,128)(2,1)} %bitcast.5), calls=%async_computation.1 | async-start | bytes 2097152 | tf_op jit(solution)/shard_map/all_to_all | solution.py:66
  69.7 27.4 %all-to-all-start.3 = ((bf16[128,4,1024]{0,2,1:T(8,128)(2,1)}), bf16[128,4,1024]{0,2,1:T(8,128)(2,1)}, u32[]{:S(2)}, u32[]{:S(2)}) async-start(bf16[128,4,1024]{0,2,1:T(8,128)(2,1)} %bitcast.142), calls=%async_computation.3 | async-start | bytes 2097152 | tf_op jit(solution)/shard_map/all_to_all | solution.py:65
  74.0 106.5 %all-gather.6.cloned.1.call-start = ((), (), s32[]{:S(2)}) async-start(), calls=%async_computation.5 | async-start | bytes 4718592 | tf_op jit(solution)/shard_map/all_gather | solution.py:150
  83.4 2.0 copy-start.3
  122.0 96.9 %all-gather.8.cloned.1.call-start = ((), (), s32[]{:S(2)}) async-start(), calls=%async_computation.6 | async-start | bytes 2621440 | tf_op jit(solution)/shard_map/all_gather | solution.py:151
  180.5 4.7 %copy-start.2 = (f32[128,65,64]{1,2,0:T(8,128)S(1)}, f32[128,65,64]{1,2,0:T(8,128)}, u32[]{:S(2)}) copy-start(f32[128,65,64]{1,2,0:T(8,128)} %all-gather.6.cloned.1.call-done) | copy-start | bytes 6389764
  187.1 3.5 %copy-start.4 = (f32[4,128,16,64]{3,2,1,0:T(8,128)S(1)}, f32[4,128,16,64]{3,2,1,0:T(8,128)}, u32[]{:S(2)}) copy-start(f32[4,128,16,64]{3,2,1,0:T(8,128)} %get-tuple-element.131) | copy-start | bytes 6291460
  219.0 2.8 %copy-start.6 = (f32[64,65,64]{1,2,0:T(8,128)S(1)}, f32[64,65,64]{1,2,0:T(8,128)}, u32[]{:S(2)}) copy-start(f32[64,65,64]{1,2,0:T(8,128)} %all-gather.8.cloned.1.call-done) | copy-start | bytes 3194884
  221.8 5.5 %copy-start.10 = (f32[4,16,64,64]{3,2,1,0:T(8,128)S(1)}, f32[4,16,64,64]{3,2,1,0:T(8,128)}, u32[]{:S(2)}) copy-start(f32[4,16,64,64]{3,2,1,0:T(8,128)} %get-tuple-element.56) | copy-start | bytes 3145732
  227.4 10.3 %copy-start.5 = (f32[4,16,128,128]{3,2,1,0:T(8,128)S(1)}, f32[4,16,128,128]{3,2,1,0:T(8,128)}, u32[]{:S(2)}) copy-start(f32[4,16,128,128]{3,2,1,0:T(8,128)} %fusion.9) | copy-start | bytes 12582916
  227.4 10.3 %copy-start.7 = (f32[4,128,16,64]{1,3,2,0:T(8,128)S(1)}, f32[4,128,16,64]{1,3,2,0:T(8,128)}, u32[]{:S(2)}) copy-start(f32[4,128,16,64]{1,3,2,0:T(8,128)} %fusion) | copy-start | bytes 6291460
  263.0 5.3 %copy-start.1 = (bf16[128,4096]{1,0:T(8,128)(2,1)S(1)}, bf16[128,4096]{1,0:T(8,128)(2,1)}, u32[]{:S(2)}) copy-start(bf16[128,4096]{1,0:T(8,128)(2,1)} %param.26) | copy-start | bytes 3145732
Sparse Core Ops, SparseCore 0:
  122.1 58.3 all-gather.5
  187.0 31.8 all-gather.7

commit v3 on v2

--- a/solution.py
+++ b/solution.py
@@ -146,12 +146,22 @@
         )
 
     own = jnp.concatenate([span_state, span_decay[:, None, :]], axis=1)
-    core_prefix, core_total = fold(lax.all_gather(own, "core"), lax.axis_index("core"))
-    z_prefix, z_total = fold(lax.all_gather(core_total, "z"), lax.axis_index("z"))
+    core_index = lax.axis_index("core")
+    core_count = lax.axis_size("core")
+    core_prefix, core_total = fold(lax.all_gather(own, "core"), core_index)
+    share = local_heads // core_count
+    core_share = lax.dynamic_slice_in_dim(core_total, core_index * share, share, 0)
+    z_prefix, z_total = fold(lax.all_gather(core_share, "z"), lax.axis_index("z"))
     x_prefix, _ = fold(lax.all_gather(z_total, "x"), lax.axis_index("x"))
-    incoming = x_prefix[:, :ATTENTION_SPAN]
-    for level in (z_prefix, core_prefix):
-        incoming = level[:, ATTENTION_SPAN][:, :, None] * incoming + level[:, :ATTENTION_SPAN]
+    pair_incoming = (
+        z_prefix[:, ATTENTION_SPAN][:, :, None] * x_prefix[:, :ATTENTION_SPAN]
+        + z_prefix[:, :ATTENTION_SPAN]
+    )
+    pair_incoming = lax.all_gather(pair_incoming, "core", tiled=True)
+    incoming = (
+        core_prefix[:, ATTENTION_SPAN][:, :, None] * pair_incoming
+        + core_prefix[:, :ATTENTION_SPAN]
+    )
     start_state = local_start + decay_before[:, :, :, None] * incoming[None]
     keep_first = (seg_block == stretch_prior[:, None]).astype(jnp.float32)
     carried = jnp.einsum(

time: 277 us -> 244 us (0.88)
  waiting for transfers between devices: 88.3 us -> 38.4 us
  blocking collectives: 21.9 us -> 44.6 us
  other arithmetic: 56 us -> 48.9 us
    all_gather x2 -> x1, waiting for transfers between devices: 71 us -> 21.2 us  [local(): lax.all_gather(core_share, 'z')]
    all_gather x1 -> x3, blocking collectives: 4.02 us -> 26.5 us  [the longest x1 12.8 us: local(): x_prefix, _ = fold(lax.all_gather(z_total, 'x'), lax.axis_index('x'))]
    mul x1 -> x0, other arithmetic: 4.29 us -> none  [local(): start_state = local_start + decay_before[:, :, :, None] * incoming[None]]
    unnamed x32 -> x30, local copies, waits for them, and re-layouts: 5.8 us -> 5.8 us
  transfers between devices with their start and end apart: 7 -> 6, of which waited for: 4 -> 3; matrix products, arithmetic and copies ran while one was open for 24% -> 27% of each run, Pallas kernels for 0% -> 0%
where the time goes in v3:
time: 244 us; the launch traced here: 243 us
  other arithmetic  48.9 us (20%)
  blocking collectives  44.6 us (18%)
  matrix products  41.7 us (17%)
  waiting for transfers between devices  38.4 us (16%)
  local copies, waits for them, and re-layouts  33.6 us (14%)
  starting transfers between devices  20.5 us (8%)
  between operations  14.9 us (6%)
    all_gather x1, waiting for transfers between devices, local(): lax.all_gather(core_share, 'z')  21.2 us
    all_to_all x1, blocking collectives, local(): lax.all_to_all(normed, 'head', split_axis=0, concat_axis=1, tiled=True)  18.1 us
    dot_general x1, matrix products, local(): jnp.einsum('cthd,cshd->chts', scaled_query, scaled_key, precision=highest)  13.5 us
    all_gather x1, blocking collectives, local(): x_prefix, _ = fold(lax.all_gather(z_total, 'x'), lax.axis_index('x'))  12.8 us
    all_to_all x1, waiting for transfers between devices, local(): lax.all_to_all(acceptance_linear, 'head', split_axis=1, concat_axis=0, ti...  12.2 us
    mul x1, other arithmetic, local(): scaled_key = lookup_vectors * jnp.exp(-cumulative)  11.2 us
    dot_general x1, matrix products, local(): jnp.einsum('cthd,chde->cthe', scaled_query * keep_first[:, :, None, None]...  10 us
    all_gather x1, blocking collectives, local(): pair_incoming = lax.all_gather(pair_incoming, 'core', tiled=True)  9.67 us
  transfers between devices with their start and end apart: 6, of which 3 were waited for; matrix products, arithmetic and copies ran while one was open for 27% of the time, Pallas kernels for 0%

profile of v3, /device:TPU:1, one launch (start us, length us, event | category | flops | bytes accessed | tf_op | source)
XLA Modules:
  0.0 242.8 jit_solution(13639976917891125746)
XLA Ops:
  6.5 2.4 copy.405
  9.0 5.0 %all-to-all-start = ((bf16[128,4,1024]{0,2,1:T(8,128)(2,1)}), bf16[128,4,1024]{0,2,1:T(8,128)(2,1)S(1)}, u32[]{:S(2)}, u32[]{:S(2)}) async-start(bf16[128,4,1024]{0,2,1:T(8,128)(2,1)} %bitcast.1), calls=%async_computation | async-start | bytes 2097152 | tf_op jit(solution)/shard_map/all_to_all | solution.py:63
  14.0 1.3 copy.410
  15.3 12.2 %all-to-all-done = bf16[128,4,1024]{0,2,1:T(8,128)(2,1)S(1)} async-done(((bf16[128,4,1024]{0,2,1:T(8,128)(2,1)}), bf16[128,4,1024]{0,2,1:T(8,128)(2,1)S(1)}, u32[]{:S(2)}, u32[]{:S(2)}) %all-to-all-start) | async-done | bytes 1048608 | tf_op jit(solution)/shard_map/all_to_all | solution.py:63
  27.5 3.5 %all-to-all-start.2 = ((bf16[128,4,1024]{0,2,1:T(8,128)(2,1)}), bf16[128,4,1024]{0,2,1:T(8,128)(2,1)S(1)}, u32[]{:S(2)}, u32[]{:S(2)}) async-start(bf16[128,4,1024]{0,2,1:T(8,128)(2,1)} %bitcast.187), calls=%async_computation.2 | async-start | bytes 2097152 | tf_op jit(solution)/shard_map/all_to_all | solution.py:64
  31.9 3.3 %collective-permute-start = (bf16[1,4096]{1,0:T(2,128)(2,1)S(1)}, bf16[1,4096]{1,0:T(2,128)(2,1)S(1)}, u32[]{:S(2)}, u32[]{:S(2)}) collective-permute-start(bf16[1,4096]{1,0:T(2,128)(2,1)S(1)} %slice.104), channel_id=1, source_target_pairs={{0,1},{1,2},{2,3},{3,4},{4,5},{5,6},{6,7},{7,8},{8,9},{9,10},{10,1... | collective-permute-start | bytes 24584 | tf_op jit(solution)/shard_map/ppermute | solution.py:18
  36.0 1.3 fusion.64
  38.7 5.0 %collective-permute-done = bf16[1,4096]{1,0:T(2,128)(2,1)S(1)} collective-permute-done((bf16[1,4096]{1,0:T(2,128)(2,1)S(1)}, bf16[1,4096]{1,0:T(2,128)(2,1)S(1)}, u32[]{:S(2)}, u32[]{:S(2)}) %collective-permute-start) | collective-permute-done | bytes 8224 | tf_op jit(solution)/shard_map/ppermute | solution.py:18
  43.7 4.3 %fusion.4 = bf16[128,4096]{1,0:T(8,128)(2,1)} fusion(bf16[128,4096]{1,0:T(8,128)(2,1)S(1)} %copy-done, bf16[4096,128]{1,0:T(8,128)(2,1)} %param.25, bf16[128,4096]{1,0:T(8,128)(2,1)} %param.21, bf16[127,4096]{1,0:T(8,128)(2,1)} %bitcast.190, bf16[1,4096]{1,0:T(2,128)(2,1)S(1)} %collective-permute-done, f32[4096]{0:T(1024)S(1)} %copy-done.12, ...), kind=kOutput, calls=%fused_computation.10 | convolution fusion | flops 276316160 | bytes 5275776 | tf_op jit(solution)/shard_map/dot_general | solution.py:58
  48.0 2.3 copy.428
  50.3 4.4 %all-to-all-start.1 = ((bf16[128,4,1024]{0,2,1:T(8,128)(2,1)}), bf16[128,4,1024]{0,2,1:T(8,128)(2,1)}, u32[]{:S(2)}, u32[]{:S(2)}) async-start(bf16[128,4,1024]{0,2,1:T(8,128)(2,1)} %bitcast.5), calls=%async_computation.1 | async-start | bytes 2097152 | tf_op jit(solution)/shard_map/all_to_all | solution.py:66
  54.7 1.3 copy.429
  58.6 1.4 convert_element_type.112
  60.0 3.0 %copy.409 = f32[4,128,16,64]{3,2,1,0:T(8,128)} copy(f32[4,128,16,64]{1,3,2,0:T(8,128)S(1)} %bitcast.171) | data formatting | bytes 4194304 | tf_op jit(solution)/shard_map/convert_element_type | solution.py:87
  63.0 2.7 %convert_element_type.114 = f32[128,4,1024]{0,2,1:T(8,128)} convert(bf16[128,4,1024]{0,2,1:T(8,128)(2,1)} %copy-done.8) | non-fusion elementwise | flops 524288 | bytes 3145728 | tf_op jit(solution)/shard_map/convert_element_type | solution.py:88
  65.7 4.0 %copy.411 = f32[4,128,16,64]{3,2,1,0:T(8,128)} copy(f32[4,128,16,64]{1,3,2,0:T(8,128)} %bitcast.173) | data formatting | bytes 4194304 | tf_op jit(solution)/shard_map/convert_element_type | solution.py:88
  69.7 4.3 %all-to-all-start.3 = ((bf16[128,4,1024]{0,2,1:T(8,128)(2,1)}), bf16[128,4,1024]{0,2,1:T(8,128)(2,1)}, u32[]{:S(2)}, u32[]{:S(2)}) async-start(bf16[128,4,1024]{0,2,1:T(8,128)(2,1)} %bitcast.186), calls=%async_computation.3 | async-start | bytes 2097152 | tf_op jit(solution)/shard_map/all_to_all | solution.py:65
  74.1 2.7 %convert_element_type.113 = f32[128,4,1024]{0,2,1:T(8,128)} convert(bf16[128,4,1024]{0,2,1:T(8,128)(2,1)} %all-to-all-done.1) | non-fusion elementwise | flops 524288 | bytes 3145728 | tf_op jit(solution)/shard_map/convert_element_type | solution.py:90
  76.7 4.1 %copy.407 = f32[4,128,16,64]{3,2,1,0:T(8,128)} copy(f32[4,128,16,64]{1,3,2,0:T(8,128)} %bitcast.183) | data formatting | bytes 4194304 | tf_op jit(solution)/shard_map/convert_element_type | solution.py:90
  80.9 2.5 %fusion.66 = f32[4,128,16,64]{3,2,1,0:T(8,128)S(1)} fusion(f32[4,128,16,64]{3,2,1,0:T(8,128)} %copy.407), kind=kOutput, calls=%fused_computation.137 | output fusion | flops 66584576 | bytes 4194304 | tf_op jit(solution)/shard_map/jit(cumsum)/reduce_window_sum | solution.py:91
  83.4 2.0 copy-done.3
  85.9 11.2 %exponential_multiply_fusion = (f32[4,128,16,64]{3,2,1,0:T(8,128)}, f32[4,128,16,64]{3,2,1,0:T(8,128)}, f32[4,128,16,64]{3,2,1,0:T(8,128)}, f32[4,128,16,64]{3,2,1,0:T(8,128)}) fusion(f32[4,128,16,64]{3,2,1,0:T(8,128)} %copy.411, f32[4,128,16,64]{3,2,1,0:T(8,128)} %copy-done.3, f32[4,128]{1,0:T(4,128)S(1)} %get-tuple-element.139, ...), kind=kLoop, calls=%fused_computation.21 | loop fusion | flops 4194304 | bytes 16797696 | tf_op jit(solution)/shard_map/mul | solution.py:95
  97.1 7.8 %fusion.7 = f32[4,16,64,64]{3,2,1,0:T(8,128)} fusion(bf16[4,128,16,64]{1,3,2,0:T(8,128)(2,1)} %bitcast.14, f32[4,128,16,64]{3,2,1,0:T(8,128)} %get-tuple-element.132), kind=kOutput, calls=%fused_computation.13 | convolution fusion | flops 402653184 | bytes 4194304 | tf_op jit(solution)/shard_map/cthd,cthe->chde/dot_general | solution.py:109
  104.9 8.9 %while.26 = (s32[]{:T(128)}, f32[16,64,64]{2,1,0:T(8,128)S(1)}, f32[4,16,64,64]{3,2,1,0:T(8,128)}, f32[4,16,64]{2,1,0:T(8,128)S(1)}, f32[4,16,64,64]{3,2,1,0:T(8,128)}, /*index=5*/s32[]{:T(128)}, s32[]{:T(128)}) while((s32[]{:T(128)}, f32[16,64,64]{2,1,0:T(8,128)S(1)}, f32[4,16,64,64]{3,2,1,0:T(8,128)}, ...), condition=%wide.region_3.4_spmd.clone, body=%wide.region_2.3_spmd.clone.sunk | while | flops 262147 | bytes 1585260 | solution.py:119
  105.8 1.3 bitcast_add_fusion.4
  107.2 0.9 bitcast_dynamic-update-slice_fusion.4
  108.0 1.3 bitcast_add_fusion.4
  109.4 0.9 bitcast_dynamic-update-slice_fusion.4
  110.3 1.3 bitcast_add_fusion.4
  111.6 0.9 bitcast_dynamic-update-slice_fusion.4
  112.5 1.3 bitcast_add_fusion.4
  113.8 1.0 copy.417
  114.8 1.2 pad_maximum_fusion
  116.1 4.0 %all-gather = f32[32,65,64]{1,2,0:T(8,128)S(1)} all-gather(f32[16,65,64]{1,2,0:T(8,128)S(1)} %pad_maximum_fusion), channel_id=2, replica_groups=mesh['x'=4,'z'=8,'core'=2,'head'=4] {'core'}, dimensions={0}, use_global_device_ids=true | all-gather | bytes 798720 | tf_op jit(solution)/shard_map/all_gather | solution.py:151
  124.4 3.5 %fusion = f32[4,128,16,64]{1,3,2,0:T(8,128)} fusion(f32[4,128,16,64]{1,3,2,0:T(8,128)} %bitcast.174, f32[4,128,16,64]{1,3,2,0:T(8,128)S(1)} %bitcast.172, f32[16,64]{1,0:T(8,128)S(1)} %mul.497), kind=kOutput, calls=%fused_computation.5 | output fusion | flops 1056831 | bytes 6295552 | tf_op jit(solution)/shard_map/mul | solution.py:104
  127.9 13.5 %fusion.9 = f32[4,16,128,128]{3,2,1,0:T(8,128)} fusion(f32[4,128,16,64]{3,2,1,0:T(8,128)S(1)} %copy-done.4, f32[4,128,16,64]{3,2,1,0:T(8,128)} %get-tuple-element.134), kind=kOutput, calls=%fused_computation.15 | convolution fusion | flops 805306368 | bytes 8388608 | tf_op jit(solution)/shard_map/cthd,cshd->chts/dot_general | solution.py:96
  141.3 21.2 %all-gather.5.cloned.1.call-done = f32[64,65,64]{1,2,0:T(8,128)} async-done(((f32[8,65,64]{1,2,0:T(8,128)}), f32[64,65,64]{1,2,0:T(8,128)}) %all-gather.5.cloned.1.call-update) | async-done | bytes 1064976 | tf_op jit(solution)/shard_map/all_gather | solution.py:154
  162.5 2.9 %select_reduce_fusion.1 = (f32[8,64]{1,0:T(8,128)S(1)}, f32[8,64]{1,0:T(8,128)S(1)}, f32[8,64]{1,0:T(8,128)S(1)}, f32[8,64]{1,0:T(8,128)S(1)}, f32[8,64]{1,0:T(8...) fusion(f32[8,8,65,64]{2,3,1,0:T(8,128)} %bitcast.175, ...), kind=kLoop, calls=%fused_computation.102 | loop fusion | flops 4608 | bytes 36865 | tf_op jit(solution)/shard_map/jit(_where)/select_n | solution.py:140
  165.8 12.8 %all-gather.2 = f32[32,65,64]{1,2,0:T(8,128)S(1)} all-gather(f32[8,65,64]{1,2,0:T(8,128)S(1)} %pad_maximum_fusion.1), channel_id=4, replica_groups=mesh['x'=4,'z'=8,'core'=2,'head'=4] {'x'}, dimensions={0}, use_global_device_ids=true | all-gather | bytes 665600 | tf_op jit(solution)/shard_map/all_gather | solution.py:155
  179.9 9.7 %all_gather.27 = f32[16,64,64]{2,1,0:T(8,128)} all-gather(f32[8,64,64]{2,1,0:T(8,128)S(1)} %copy.421), channel_id=1, replica_groups=mesh['x'=4,'z'=8,'core'=2,'head'=4] {'core'}, dimensions={0}, use_global_device_ids=true | all-gather | bytes 393216 | tf_op jit(solution)/shard_map/all_gather | solution.py:160
  189.6 2.2 copy.422
  191.8 2.0 select_add_fusion
  193.8 1.2 copy.423
  195.1 10.0 %fusion.5 = f32[4,16,64,128]{3,2,1,0:T(8,128)S(1)} fusion(f32[4,128,16,64]{3,2,1,0:T(8,128)} %get-tuple-element.133, f32[4,16,64,64]{3,2,1,0:T(8,128)S(1)} %copy-done.9, f32[16,64,64]{2,1,0:T(8,128)S(1)} %copy.423, f32[4,16,64]{2,1,0:T(8,128)S(1)} %get-tuple-element.57), kind=kOutput, calls=%fused_computation.11 | convolution fusion | flops 403177472 | bytes 5521408 | tf_op jit(solution)/shard_map/cthd,chde->cthe/dot_general | solution.py:167
  205.2 6.2 %fusion.65 = (f32[4,128,16]{1,2,0:T(8,128)S(1)}, f32[4,128,16,64]{1,3,2,0:T(8,128)S(1)}) fusion(f32[4,16,64,128]{3,2,1,0:T(8,128)S(1)} %fusion.5, f32[4,128,16,64]{1,3,2,0:T(8,128)S(1)} %copy-done.6, bf16[4,128,16,64]{1,3,2,0:T(8,128)(2,1)} %bitcast.14, f32[4,16,128,128]{3,2,1,0:T(8,128)S(1)} %copy-done.5, pred[4,128,128]{2,1,0:T(8,128)(4,1)S(1)} %compare_and_fusion), kind=kOutput, calls=%fused_computation.136 | convolution fusion | flops 808968192 | bytes 11632640 | tf_op jit(solution)/shard_map/chts,cshd->cthd/dot_general | solution.py:102
  212.5 18.1 %all_to_all.68 = bf16[4,128,1024]{1,2,0:T(8,128)(2,1)S(1)} all-to-all(bf16[4,128,1024]{1,2,0:T(8,128)(2,1)S(1)} %bitcast.185), channel_id=1, replica_groups=mesh['x'=4,'z'=8,'core'=2,'head'=4] {'head'}, dimensions={0} | all-to-all | bytes 2097152 | tf_op jit(solution)/shard_map/all_to_all | solution.py:178
  230.7 1.9 copy.430
  232.5 3.4 %fusion.24 = bf16[128,4096]{1,0:T(8,128)(2,1)} fusion(f32[128,4096]{1,0:T(8,128)} %copy.430, bf16[128,4096]{1,0:T(8,128)(2,1)} %param.20), kind=kLoop, calls=%fused_computation.43 | loop fusion | flops 3670016 | bytes 4194304 | tf_op jit(solution)/shard_map/convert_element_type | solution.py:179
  (84 shorter events, 13.0 us)
Async XLA Ops:
  6.5 37.2 %copy-start = (bf16[128,4096]{1,0:T(8,128)(2,1)S(1)}, bf16[128,4096]{1,0:T(8,128)(2,1)}, u32[]{:S(2)}) copy-start(bf16[128,4096]{1,0:T(8,128)(2,1)} %param.26) | copy-start | bytes 3145732
  6.5 7.4 %copy-start.10 = (bf16[128,4096]{1,0:T(8,128)(2,1)S(1)}, bf16[128,4096]{1,0:T(8,128)(2,1)}, u32[]{:S(2)}) copy-start(bf16[128,4096]{1,0:T(8,128)(2,1)} %param.18) | copy-start | bytes 3145732
  9.0 18.5 %all-to-all-start = ((bf16[128,4,1024]{0,2,1:T(8,128)(2,1)}), bf16[128,4,1024]{0,2,1:T(8,128)(2,1)S(1)}, u32[]{:S(2)}, u32[]{:S(2)}) async-start(bf16[128,4,1024]{0,2,1:T(8,128)(2,1)} %bitcast.1), calls=%async_computation | async-start | bytes 2097152 | tf_op jit(solution)/shard_map/all_to_all | solution.py:63
  14.0 29.8 %copy-start.12 = (f32[4096]{0:T(1024)S(1)}, f32[4096]{0:T(1024)}, u32[]{:S(2)}) copy-start(f32[4096]{0:T(1024)} %param.24) | copy-start | bytes 49156
  14.0 29.8 %copy-start.13 = (f32[4096]{0:T(1024)S(1)}, f32[4096]{0:T(1024)}, u32[]{:S(2)}) copy-start(f32[4096]{0:T(1024)} %param.23) | copy-start | bytes 49156
  27.5 20.5 %copy-start.7 = (bf16[128,4,1024]{0,2,1:T(8,128)(2,1)}, bf16[128,4,1024]{0,2,1:T(8,128)(2,1)S(1)}, u32[]{:S(2)}) copy-start(bf16[128,4,1024]{0,2,1:T(8,128)(2,1)S(1)} %all-to-all-done) | copy-start | bytes 3145732
  27.5 22.8 %all-to-all-start.2 = ((bf16[128,4,1024]{0,2,1:T(8,128)(2,1)}), bf16[128,4,1024]{0,2,1:T(8,128)(2,1)S(1)}, u32[]{:S(2)}, u32[]{:S(2)}) async-start(bf16[128,4,1024]{0,2,1:T(8,128)(2,1)} %bitcast.187), calls=%async_computation.2 | async-start | bytes 2097152 | tf_op jit(solution)/shard_map/all_to_all | solution.py:64
  31.9 11.9 %collective-permute-start = (bf16[1,4096]{1,0:T(2,128)(2,1)S(1)}, bf16[1,4096]{1,0:T(2,128)(2,1)S(1)}, u32[]{:S(2)}, u32[]{:S(2)}) collective-permute-start(bf16[1,4096]{1,0:T(2,128)(2,1)S(1)} %slice.104), channel_id=1, source_target_pairs={{0,1},{1,2},{2,3},{3,4},{4,5},{5,6},{6,7},{7,8},{8,9},{9,10},{10,1... | collective-permute-start | bytes 24584 | tf_op jit(solution)/shard_map/ppermute | solution.py:18
  50.3 4.5 %copy-start.11 = (bf16[128,4096]{1,0:T(8,128)(2,1)S(1)}, bf16[128,4096]{1,0:T(8,128)(2,1)}, u32[]{:S(2)}) copy-start(bf16[128,4096]{1,0:T(8,128)(2,1)} %param.19) | copy-start | bytes 3145732
  50.3 5.8 %copy-start.8 = (bf16[128,4,1024]{0,2,1:T(8,128)(2,1)}, bf16[128,4,1024]{0,2,1:T(8,128)(2,1)S(1)}, u32[]{:S(2)}) copy-start(bf16[128,4,1024]{0,2,1:T(8,128)(2,1)S(1)} %all-to-all-done.2) | copy-start | bytes 3145732
  50.3 19.5 %all-to-all-start.1 = ((bf16[128,4,1024]{0,2,1:T(8,128)(2,1)}), bf16[128,4,1024]{0,2,1:T(8,128)(2,1)}, u32[]{:S(2)}, u32[]{:S(2)}) async-start(bf16[128,4,1024]{0,2,1:T(8,128)(2,1)} %bitcast.5), calls=%async_computation.1 | async-start | bytes 2097152 | tf_op jit(solution)/shard_map/all_to_all | solution.py:66
  69.7 27.4 %all-to-all-start.3 = ((bf16[128,4,1024]{0,2,1:T(8,128)(2,1)}), bf16[128,4,1024]{0,2,1:T(8,128)(2,1)}, u32[]{:S(2)}, u32[]{:S(2)}) async-start(bf16[128,4,1024]{0,2,1:T(8,128)(2,1)} %bitcast.186), calls=%async_computation.3 | async-start | bytes 2097152 | tf_op jit(solution)/shard_map/all_to_all | solution.py:65
  74.0 88.5 %all-gather.5.cloned.1.call-start = ((), (), s32[]{:S(2)}) async-start(), calls=%async_computation.5 | async-start | bytes 2359296 | tf_op jit(solution)/shard_map/all_gather | solution.py:154
  83.4 2.0 copy-start.3
  124.4 3.5 %copy-start.4 = (f32[4,128,16,64]{3,2,1,0:T(8,128)S(1)}, f32[4,128,16,64]{3,2,1,0:T(8,128)}, u32[]{:S(2)}) copy-start(f32[4,128,16,64]{3,2,1,0:T(8,128)} %get-tuple-element.131) | copy-start | bytes 6291460
  162.5 2.9 %copy-start.2 = (f32[64,65,64]{1,2,0:T(8,128)S(1)}, f32[64,65,64]{1,2,0:T(8,128)}, u32[]{:S(2)}) copy-start(f32[64,65,64]{1,2,0:T(8,128)} %all-gather.5.cloned.1.call-done) | copy-start | bytes 3194884
  189.6 5.5 %copy-start.9 = (f32[4,16,64,64]{3,2,1,0:T(8,128)S(1)}, f32[4,16,64,64]{3,2,1,0:T(8,128)}, u32[]{:S(2)}) copy-start(f32[4,16,64,64]{3,2,1,0:T(8,128)} %get-tuple-element.56) | copy-start | bytes 3145732
  195.1 10.1 %copy-start.5 = (f32[4,16,128,128]{3,2,1,0:T(8,128)S(1)}, f32[4,16,128,128]{3,2,1,0:T(8,128)}, u32[]{:S(2)}) copy-start(f32[4,16,128,128]{3,2,1,0:T(8,128)} %fusion.9) | copy-start | bytes 12582916
  195.1 10.1 %copy-start.6 = (f32[4,128,16,64]{1,3,2,0:T(8,128)S(1)}, f32[4,128,16,64]{1,3,2,0:T(8,128)}, u32[]{:S(2)}) copy-start(f32[4,128,16,64]{1,3,2,0:T(8,128)} %fusion) | copy-start | bytes 6291460
  230.7 5.3 %copy-start.1 = (bf16[128,4096]{1,0:T(8,128)(2,1)S(1)}, bf16[128,4096]{1,0:T(8,128)(2,1)}, u32[]{:S(2)}) copy-start(bf16[128,4096]{1,0:T(8,128)(2,1)} %param.26) | copy-start | bytes 3145732
Sparse Core Ops, SparseCore 0:
  122.0 40.4 all-gather.4

commit v4 on v3

--- a/solution.py
+++ b/solution.py
@@ -9,7 +9,7 @@
 
 norm_eps = 0.00064
 decay_floor = -0.5
-highest = lax.Precision.HIGHEST
+highest = lax.Precision.HIGH
 
 
 def shifted(value, axis, by):
@@ -111,19 +111,17 @@
         jnp.exp(ending) * (seg_block[:, -1] == stretch_prior).astype(jnp.float32)[:, None, None]
     )
 
-    def advance(carry_state, pieces):
-        factor, new_part = pieces
-        return (factor[:, :, None] * carry_state + new_part, carry_state)
-
     zero_state = jnp.zeros((local_heads, ATTENTION_SPAN, ATTENTION_SPAN), jnp.float32)
-    span_state, local_start = lax.scan(advance, zero_state, (stretch_decay, stretch_state))
-
-    def multiply(product, factor):
-        return (product * factor, product)
-
-    span_decay, decay_before = lax.scan(
-        multiply, jnp.ones((local_heads, ATTENTION_SPAN), jnp.float32), stretch_decay
-    )
+    span_state = zero_state
+    span_decay = jnp.ones((local_heads, ATTENTION_SPAN), jnp.float32)
+    starts, decays_before = [], []
+    for stretch in range(stretches):
+        starts.append(span_state)
+        decays_before.append(span_decay)
+        span_state = stretch_decay[stretch][:, :, None] * span_state + stretch_state[stretch]
+        span_decay = span_decay * stretch_decay[stretch]
+    local_start = jnp.stack(starts)
+    decay_before = jnp.stack(decays_before)
 
     def fold(gathered, position):
         count = gathered.shape[0]

time: 244 us -> 223 us (0.914)
  matrix products: 41.7 us -> 26.4 us
  other arithmetic: 48.9 us -> 37.9 us
  waiting for transfers between devices: 38.4 us -> 45.1 us
    all_gather x1, waiting for transfers between devices: 21.2 us -> 28.6 us  [local(): lax.all_gather(core_share, 'z')]
    dot_general x1, matrix products: 13.5 us -> 6.71 us  [local(): jnp.einsum('cthd,cshd->chts', scaled_query, scaled_key, precision=highest)]
    dynamic_update_slice x8 -> x0, other arithmetic: 3.47 us -> none  [the longest x4 3.45 us: local(): lax.scan(advance, zero_state, (stretch_decay, stretch_state))]
    add x4 -> x2, other arithmetic: 5.31 us -> 1.98 us  [local(): stretch_decay[stretch][:, :, None] * span_state + stretch_state[stretch]]
    dot_general x1, matrix products: 6.16 us -> 3.16 us  [local(): jnp.einsum('chts,cshd->cthd', scores, payload_vectors, precision=highest)]
    dot_general x1, matrix products: 7.8 us -> 4.89 us  [local(): jnp.einsum('cthd,cthe->chde', tail_keys, payload_vectors, precision=highest)]
    dot_general x1, matrix products: 10 us -> 7.38 us  [local(): jnp.einsum('cthd,chde->cthe', scaled_query * keep_first[:, :, None, None]...]
    unnamed x30 -> x42, local copies, waits for them, and re-layouts: 5.8 us -> 6.92 us
where the time goes in v4:
time: 223 us; the launch traced here: 221 us
  waiting for transfers between devices  45.1 us (20%)
  blocking collectives  44.6 us (20%)
  other arithmetic  37.9 us (17%)
  local copies, waits for them, and re-layouts  32 us (14%)
  matrix products  26.4 us (12%)
  starting transfers between devices  20.6 us (9%)
  between operations  14.9 us (7%)
    all_gather x1, waiting for transfers between devices, local(): lax.all_gather(core_share, 'z')  28.6 us
    all_to_all x1, blocking collectives, local(): lax.all_to_all(normed, 'head', split_axis=0, concat_axis=1, tiled=True)  18 us
    all_gather x1, blocking collectives, local(): x_prefix, _ = fold(lax.all_gather(z_total, 'x'), lax.axis_index('x'))  12.9 us
    all_to_all x1, waiting for transfers between devices, local(): lax.all_to_all(acceptance_linear, 'head', split_axis=1, concat_axis=0, ti...  12.2 us
    mul x1, other arithmetic, local(): scaled_key = lookup_vectors * jnp.exp(-cumulative)  11.3 us
    all_gather x1, blocking collectives, local(): pair_incoming = lax.all_gather(pair_incoming, 'core', tiled=True)  9.49 us
    dot_general x1, matrix products, local(): jnp.einsum('cthd,chde->cthe', scaled_query * keep_first[:, :, None, None]...  7.38 us
    unnamed x42, local copies, waits for them, and re-layouts  6.92 us
  transfers between devices with their start and end apart: 6, of which 3 were waited for; matrix products, arithmetic and copies ran while one was open for 27% of the time, Pallas kernels for 0%

profile of v4, /device:TPU:1, one launch (start us, length us, event | category | flops | bytes accessed | tf_op | source)
XLA Modules:
  0.0 221.4 jit_solution(15797405720559942649)
XLA Ops:
  6.5 2.4 %copy.327 = bf16[128,4096]{0,1:T(8,128)(2,1)} copy(bf16[128,4096]{1,0:T(8,128)(2,1)} %param.13) | data formatting | bytes 2097152 | tf_op args[0]
  9.0 5.0 %all-to-all-start = ((bf16[128,4,1024]{0,2,1:T(8,128)(2,1)}), bf16[128,4,1024]{0,2,1:T(8,128)(2,1)S(1)}, u32[]{:S(2)}, u32[]{:S(2)}) async-start(bf16[128,4,1024]{0,2,1:T(8,128)(2,1)} %bitcast.1), calls=%async_computation | async-start | bytes 2097152 | tf_op jit(solution)/shard_map/all_to_all | solution.py:63
  14.0 1.3 copy.332
  15.3 12.2 %all-to-all-done = bf16[128,4,1024]{0,2,1:T(8,128)(2,1)S(1)} async-done(((bf16[128,4,1024]{0,2,1:T(8,128)(2,1)}), bf16[128,4,1024]{0,2,1:T(8,128)(2,1)S(1)}, u32[]{:S(2)}, u32[]{:S(2)}) %all-to-all-start) | async-done | bytes 1048608 | tf_op jit(solution)/shard_map/all_to_all | solution.py:63
  27.5 3.5 %all-to-all-start.2 = ((bf16[128,4,1024]{0,2,1:T(8,128)(2,1)}), bf16[128,4,1024]{0,2,1:T(8,128)(2,1)S(1)}, u32[]{:S(2)}, u32[]{:S(2)}) async-start(bf16[128,4,1024]{0,2,1:T(8,128)(2,1)} %bitcast.201), calls=%async_computation.2 | async-start | bytes 2097152 | tf_op jit(solution)/shard_map/all_to_all | solution.py:64
  31.0 0.9 slice.132
  31.9 3.3 %collective-permute-start = (bf16[1,4096]{1,0:T(2,128)(2,1)S(1)}, bf16[1,4096]{1,0:T(2,128)(2,1)S(1)}, u32[]{:S(2)}, u32[]{:S(2)}) collective-permute-start(bf16[1,4096]{1,0:T(2,128)(2,1)S(1)} %slice.132), channel_id=1, source_target_pairs={{0,1},{1,2},{2,3},{3,4},{4,5},{5,6},{6,7},{7,8},{8,9},{9,10},{10,1... | collective-permute-start | bytes 24584 | tf_op jit(solution)/shard_map/ppermute | solution.py:18
  35.2 0.8 dynamic_slice.26
  36.0 1.3 fusion.74
  37.9 0.8 dynamic-slice_bitcast_fusion
  38.7 0.8 add_compare_fusion
  39.4 4.3 %collective-permute-done = bf16[1,4096]{1,0:T(2,128)(2,1)S(1)} collective-permute-done((bf16[1,4096]{1,0:T(2,128)(2,1)S(1)}, bf16[1,4096]{1,0:T(2,128)(2,1)S(1)}, u32[]{:S(2)}, u32[]{:S(2)}) %collective-permute-start) | collective-permute-done | bytes 8224 | tf_op jit(solution)/shard_map/ppermute | solution.py:18
  43.7 4.2 %fusion.4 = bf16[128,4096]{1,0:T(8,128)(2,1)} fusion(bf16[128,4096]{1,0:T(8,128)(2,1)S(1)} %copy-done, bf16[4096,128]{1,0:T(8,128)(2,1)} %param.21, bf16[128,4096]{1,0:T(8,128)(2,1)} %param.17, bf16[127,4096]{1,0:T(8,128)(2,1)} %bitcast.205, bf16[1,4096]{1,0:T(2,128)(2,1)S(1)} %collective-permute-done, f32[4096]{0:T(1024)S(1)} %copy-done.18, ...), kind=kOutput, calls=%fused_computation.5 | convolution fusion | flops 276316160 | bytes 5275776 | tf_op jit(solution)/shard_map/dot_general | solution.py:58
  48.0 2.3 %copy.346 = bf16[128,4096]{0,1:T(8,128)(2,1)} copy(bf16[128,4096]{1,0:T(8,128)(2,1)} %fusion.4) | data formatting | bytes 2097152 | tf_op jit(solution)/shard_map/all_to_all | solution.py:66
  50.3 4.5 %all-to-all-start.1 = ((bf16[128,4,1024]{0,2,1:T(8,128)(2,1)}), bf16[128,4,1024]{0,2,1:T(8,128)(2,1)}, u32[]{:S(2)}, u32[]{:S(2)}) async-start(bf16[128,4,1024]{0,2,1:T(8,128)(2,1)} %bitcast.203), calls=%async_computation.1 | async-start | bytes 2097152 | tf_op jit(solution)/shard_map/all_to_all | solution.py:66
  54.9 0.7 dynamic_slice.27
  56.3 0.7 dynamic_slice.31
  57.1 1.3 copy.347
  59.5 0.8 compare_convert_fusion.1
  60.4 3.0 %copy.331 = f32[4,128,16,64]{3,2,1,0:T(8,128)} copy(f32[4,128,16,64]{1,3,2,0:T(8,128)S(1)} %bitcast.184) | data formatting | bytes 4194304 | tf_op jit(solution)/shard_map/convert_element_type | solution.py:87
  63.4 1.5 convert_element_type.114
  64.9 4.0 %copy.333 = f32[4,128,16,64]{3,2,1,0:T(8,128)} copy(f32[4,128,16,64]{1,3,2,0:T(8,128)} %bitcast.186) | data formatting | bytes 4194304 | tf_op jit(solution)/shard_map/convert_element_type | solution.py:88
  68.9 4.2 %all-to-all-start.3 = ((bf16[128,4,1024]{0,2,1:T(8,128)(2,1)}), bf16[128,4,1024]{0,2,1:T(8,128)(2,1)S(1)}, u32[]{:S(2)}, u32[]{:S(2)}) async-start(bf16[128,4,1024]{0,2,1:T(8,128)(2,1)} %bitcast.202), calls=%async_computation.3 | async-start | bytes 2097152 | tf_op jit(solution)/shard_map/all_to_all | solution.py:65
  73.1 2.7 %convert_element_type.113 = f32[128,4,1024]{0,2,1:T(8,128)} convert(bf16[128,4,1024]{0,2,1:T(8,128)(2,1)} %all-to-all-done.1) | non-fusion elementwise | flops 524288 | bytes 3145728 | tf_op jit(solution)/shard_map/convert_element_type | solution.py:90
  75.8 4.0 %copy.329 = f32[4,128,16,64]{3,2,1,0:T(8,128)} copy(f32[4,128,16,64]{1,3,2,0:T(8,128)} %bitcast.198) | data formatting | bytes 4194304 | tf_op jit(solution)/shard_map/convert_element_type | solution.py:90
  79.8 2.5 %fusion.77 = f32[4,128,16,64]{3,2,1,0:T(8,128)S(1)} fusion(f32[4,128,16,64]{3,2,1,0:T(8,128)} %copy.329), kind=kOutput, calls=%fused_computation.159 | output fusion | flops 66584576 | bytes 4194304 | tf_op jit(solution)/shard_map/jit(cumsum)/reduce_window_sum | solution.py:91
  82.3 2.0 copy-done.3
  84.4 1.0 copy.339
  85.4 11.3 %exponential_multiply_fusion = (f32[4,128,16,64]{3,2,1,0:T(8,128)}, f32[4,128,16,64]{3,2,1,0:T(8,128)}, f32[4,128,16,64]{3,2,1,0:T(8,128)}, f32[4,128,16,64]{3,2,1,0:T(8,128)}) fusion(f32[4,128,16,64]{3,2,1,0:T(8,128)} %copy.333, f32[4,128,16,64]{3,2,1,0:T(8,128)} %copy-done.3, f32[4,128]{1,0:T(4,128)S(1)} %get-tuple-element.47, ...), kind=kLoop, calls=%fused_computation.16 | loop fusion | flops 4194304 | bytes 16797696 | tf_op jit(solution)/shard_map/mul | solution.py:95
  96.7 4.9 %fusion.7 = f32[4,16,64,64]{2,3,1,0:T(8,128)S(1)} fusion(bf16[4,128,16,64]{1,3,2,0:T(8,128)(2,1)S(1)} %bitcast.196, f32[4,128,16,64]{3,2,1,0:T(8,128)} %get-tuple-element.32), kind=kOutput, calls=%fused_computation.8 | convolution fusion | flops 201326592 | bytes 4194304 | tf_op jit(solution)/shard_map/cthd,cthe->chde/dot_general | solution.py:109
  101.9 1.1 copy-done.15
  103.3 4.2 %all-gather = f32[32,65,64]{1,2,0:T(8,128)S(1)} all-gather(f32[16,65,64]{1,2,0:T(8,128)S(1)} %pad_maximum_fusion), channel_id=2, replica_groups=mesh['x'=4,'z'=8,'core'=2,'head'=4] {'core'}, dimensions={0}, use_global_device_ids=true | all-gather | bytes 798720 | tf_op jit(solution)/shard_map/all_gather | solution.py:149
  107.4 0.8 select_reduce_fusion
  108.3 0.9 fusion.55
  109.4 3.6 %fusion = f32[4,128,16,64]{1,3,2,0:T(8,128)} fusion(f32[4,128,16,64]{1,3,2,0:T(8,128)} %bitcast.187, f32[4,128,16,64]{1,3,2,0:T(8,128)S(1)} %bitcast.185, f32[16,64]{1,0:T(8,128)S(1)} %mul.577), kind=kOutput, calls=%fused_computation | output fusion | flops 1056831 | bytes 6295552 | tf_op jit(solution)/shard_map/mul | solution.py:104
  113.0 1.7 multiply_add_fusion.1
  114.8 6.7 %fusion.9 = f32[4,16,128,128]{3,2,1,0:T(8,128)} fusion(f32[4,128,16,64]{3,2,1,0:T(8,128)S(1)} %copy-done.4, f32[4,128,16,64]{3,2,1,0:T(8,128)S(1)} %copy-done.5), kind=kOutput, calls=%fused_computation.10 | convolution fusion | flops 402653184 | bytes 8388608 | tf_op jit(solution)/shard_map/cthd,cshd->chts/dot_general | solution.py:96
  121.5 28.6 %all-gather.5.cloned.1.call-done = f32[64,65,64]{1,2,0:T(8,128)} async-done(((f32[8,65,64]{1,2,0:T(8,128)}), f32[64,65,64]{1,2,0:T(8,128)}) %all-gather.5.cloned.1.call-update) | async-done | bytes 1064976 | tf_op jit(solution)/shard_map/all_gather | solution.py:152
  150.1 2.9 %select_reduce_fusion.1 = (f32[8,64]{1,0:T(8,128)S(1)}, f32[8,64]{1,0:T(8,128)S(1)}, f32[8,64]{1,0:T(8,128)S(1)}, f32[8,64]{1,0:T(8,128)S(1)}, f32[8,64]{1,0:T(8...) fusion(f32[8,8,65,64]{2,3,1,0:T(8,128)} %bitcast.188, ...), kind=kLoop, calls=%fused_computation.114 | loop fusion | flops 4608 | bytes 36865 | tf_op jit(solution)/shard_map/jit(_where)/select_n | solution.py:138
  153.4 12.9 %all-gather.2 = f32[32,65,64]{1,2,0:T(8,128)S(1)} all-gather(f32[8,65,64]{1,2,0:T(8,128)S(1)} %pad_maximum_fusion.1), channel_id=4, replica_groups=mesh['x'=4,'z'=8,'core'=2,'head'=4] {'x'}, dimensions={0}, use_global_device_ids=true | all-gather | bytes 665600 | tf_op jit(solution)/shard_map/all_gather | solution.py:153
  167.6 9.5 %all_gather.27 = f32[16,64,64]{2,1,0:T(8,128)S(1)} all-gather(f32[8,64,64]{2,1,0:T(8,128)S(1)} %copy.342), channel_id=1, replica_groups=mesh['x'=4,'z'=8,'core'=2,'head'=4] {'core'}, dimensions={0}, use_global_device_ids=true | all-gather | bytes 393216 | tf_op jit(solution)/shard_map/all_gather | solution.py:158
  177.1 1.0 copy.343
  178.1 1.2 select_add_fusion
  179.4 7.4 %fusion.5 = f32[4,16,64,128]{3,2,1,0:T(8,128)S(1)} fusion(f32[4,128,16,64]{3,2,1,0:T(8,128)} %get-tuple-element.33, f32[1,16,64,64]{2,3,1,0:T(8,128)S(1)} %get-tuple-element.24, f32[1,16,64,64]{2,3,1,0:T(8,128)S(1)} %get-tuple-element.25, f32[1,16,64,64]{2,3,1,0:T(8,128)S(1)} %get-tuple-element.26, f32[4]{0:T(128)S(1)} %pad.10.clone, ...), kind=kOutput, calls=%fused_computation.6 | convolution fusion | flops 202637312 | bytes 5259280 | tf_op jit(solution)/shard_map/cthd,chde->cthe/dot_general | solution.py:165
  186.8 3.2 %fusion.76 = (f32[4,128,16]{1,2,0:T(8,128)S(1)}, f32[4,128,16,64]{1,3,2,0:T(8,128)S(1)}) fusion(f32[4,16,64,128]{3,2,1,0:T(8,128)S(1)} %fusion.5, f32[4,128,16,64]{1,3,2,0:T(8,128)S(1)} %copy-done.10, bf16[4,128,16,64]{1,3,2,0:T(8,128)(2,1)S(1)} %bitcast.197, f32[4,16,128,128]{3,2,1,0:T(8,128)S(1)} %copy-done.6, pred[4,128,128]{2,1,0:T(8,128)(4,1)S(1)} %compare_and_fusion), kind=kOutput, calls=%fused_computation.158 | convolution fusion | flops 406315008 | bytes 11632640 | tf_op jit(solution)/shard_map/chts,cshd->cthd/dot_general | solution.py:102
  191.1 18.0 %all_to_all.68 = bf16[4,128,1024]{1,2,0:T(8,128)(2,1)S(1)} all-to-all(bf16[4,128,1024]{1,2,0:T(8,128)(2,1)S(1)} %bitcast.200), channel_id=1, replica_groups=mesh['x'=4,'z'=8,'core'=2,'head'=4] {'head'}, dimensions={0} | all-to-all | bytes 2097152 | tf_op jit(solution)/shard_map/all_to_all | solution.py:176
  209.3 1.9 copy.348
  211.2 3.4 %fusion.28 = bf16[128,4096]{1,0:T(8,128)(2,1)} fusion(f32[128,4096]{1,0:T(8,128)} %copy.348, bf16[128,4096]{1,0:T(8,128)(2,1)} %param.16), kind=kLoop, calls=%fused_computation.43 | loop fusion | flops 3670016 | bytes 4194304 | tf_op jit(solution)/shard_map/convert_element_type | solution.py:177
  (74 shorter events, 5.4 us)
Async XLA Ops:
  6.5 37.2 %copy-start = (bf16[128,4096]{1,0:T(8,128)(2,1)S(1)}, bf16[128,4096]{1,0:T(8,128)(2,1)}, u32[]{:S(2)}) copy-start(bf16[128,4096]{1,0:T(8,128)(2,1)} %param.22) | copy-start | bytes 3145732
  6.5 7.4 %copy-start.16 = (bf16[128,4096]{1,0:T(8,128)(2,1)S(1)}, bf16[128,4096]{1,0:T(8,128)(2,1)}, u32[]{:S(2)}) copy-start(bf16[128,4096]{1,0:T(8,128)(2,1)} %param.14) | copy-start | bytes 3145732
  9.0 18.5 %all-to-all-start = ((bf16[128,4,1024]{0,2,1:T(8,128)(2,1)}), bf16[128,4,1024]{0,2,1:T(8,128)(2,1)S(1)}, u32[]{:S(2)}, u32[]{:S(2)}) async-start(bf16[128,4,1024]{0,2,1:T(8,128)(2,1)} %bitcast.1), calls=%async_computation | async-start | bytes 2097152 | tf_op jit(solution)/shard_map/all_to_all | solution.py:63
  14.0 29.8 %copy-start.18 = (f32[4096]{0:T(1024)S(1)}, f32[4096]{0:T(1024)}, u32[]{:S(2)}) copy-start(f32[4096]{0:T(1024)} %param.20) | copy-start | bytes 49156
  14.0 29.8 %copy-start.19 = (f32[4096]{0:T(1024)S(1)}, f32[4096]{0:T(1024)}, u32[]{:S(2)}) copy-start(f32[4096]{0:T(1024)} %param.19) | copy-start | bytes 49156
  27.5 20.5 %copy-start.11 = (bf16[128,4,1024]{0,2,1:T(8,128)(2,1)}, bf16[128,4,1024]{0,2,1:T(8,128)(2,1)S(1)}, u32[]{:S(2)}) copy-start(bf16[128,4,1024]{0,2,1:T(8,128)(2,1)S(1)} %all-to-all-done) | copy-start | bytes 3145732
  27.5 22.8 %all-to-all-start.2 = ((bf16[128,4,1024]{0,2,1:T(8,128)(2,1)}), bf16[128,4,1024]{0,2,1:T(8,128)(2,1)S(1)}, u32[]{:S(2)}, u32[]{:S(2)}) async-start(bf16[128,4,1024]{0,2,1:T(8,128)(2,1)} %bitcast.201), calls=%async_computation.2 | async-start | bytes 2097152 | tf_op jit(solution)/shard_map/all_to_all | solution.py:64
  31.9 11.9 %collective-permute-start = (bf16[1,4096]{1,0:T(2,128)(2,1)S(1)}, bf16[1,4096]{1,0:T(2,128)(2,1)S(1)}, u32[]{:S(2)}, u32[]{:S(2)}) collective-permute-start(bf16[1,4096]{1,0:T(2,128)(2,1)S(1)} %slice.132), channel_id=1, source_target_pairs={{0,1},{1,2},{2,3},{3,4},{4,5},{5,6},{6,7},{7,8},{8,9},{9,10},{10,1... | collective-permute-start | bytes 24584 | tf_op jit(solution)/shard_map/ppermute | solution.py:18
  50.3 6.9 %copy-start.17 = (bf16[128,4096]{1,0:T(8,128)(2,1)S(1)}, bf16[128,4096]{1,0:T(8,128)(2,1)}, u32[]{:S(2)}) copy-start(bf16[128,4096]{1,0:T(8,128)(2,1)} %param.15) | copy-start | bytes 3145732
  50.3 8.2 %copy-start.13 = (bf16[128,4,1024]{0,2,1:T(8,128)(2,1)}, bf16[128,4,1024]{0,2,1:T(8,128)(2,1)S(1)}, u32[]{:S(2)}) copy-start(bf16[128,4,1024]{0,2,1:T(8,128)(2,1)S(1)} %all-to-all-done.2) | copy-start | bytes 3145732
  50.3 10.0 %copy-start.12 = (bf16[128,4,1024]{0,2,1:T(8,128)(2,1)S(1)}, bf16[128,4,1024]{0,2,1:T(8,128)(2,1)}, u32[]{:S(2)}) copy-start(bf16[128,4,1024]{0,2,1:T(8,128)(2,1)} %copy-done.11) | copy-start | bytes 3145732
  50.3 18.6 %all-to-all-start.1 = ((bf16[128,4,1024]{0,2,1:T(8,128)(2,1)}), bf16[128,4,1024]{0,2,1:T(8,128)(2,1)}, u32[]{:S(2)}, u32[]{:S(2)}) async-start(bf16[128,4,1024]{0,2,1:T(8,128)(2,1)} %bitcast.203), calls=%async_computation.1 | async-start | bytes 2097152 | tf_op jit(solution)/shard_map/all_to_all | solution.py:66
  60.4 3.0 %copy-start.14 = (bf16[128,4,1024]{0,2,1:T(8,128)(2,1)S(1)}, bf16[128,4,1024]{0,2,1:T(8,128)(2,1)}, u32[]{:S(2)}) copy-start(bf16[128,4,1024]{0,2,1:T(8,128)(2,1)} %copy-done.13) | copy-start | bytes 3145732
  68.9 27.8 %all-to-all-start.3 = ((bf16[128,4,1024]{0,2,1:T(8,128)(2,1)}), bf16[128,4,1024]{0,2,1:T(8,128)(2,1)S(1)}, u32[]{:S(2)}, u32[]{:S(2)}) async-start(bf16[128,4,1024]{0,2,1:T(8,128)(2,1)} %bitcast.202), calls=%async_computation.3 | async-start | bytes 2097152 | tf_op jit(solution)/shard_map/all_to_all | solution.py:65
  73.1 77.0 %all-gather.5.cloned.1.call-start = ((), (), s32[]{:S(2)}) async-start(), calls=%async_computation.5 | async-start | bytes 2359296 | tf_op jit(solution)/shard_map/all_gather | solution.py:152
  82.3 2.0 copy-start.3
  96.7 4.9 %copy-start.8 = (bf16[128,4,1024]{0,2,1:T(8,128)(2,1)}, bf16[128,4,1024]{0,2,1:T(8,128)(2,1)S(1)}, u32[]{:S(2)}) copy-start(bf16[128,4,1024]{0,2,1:T(8,128)(2,1)S(1)} %all-to-all-done.3) | copy-start | bytes 3145732
  101.6 1.6 copy-start.7
  101.6 1.4 copy-start.15
  109.4 5.4 %copy-start.4 = (f32[4,128,16,64]{3,2,1,0:T(8,128)S(1)}, f32[4,128,16,64]{3,2,1,0:T(8,128)}, u32[]{:S(2)}) copy-start(f32[4,128,16,64]{3,2,1,0:T(8,128)} %get-tuple-element.31) | copy-start | bytes 6291460
  109.4 5.4 %copy-start.5 = (f32[4,128,16,64]{3,2,1,0:T(8,128)S(1)}, f32[4,128,16,64]{3,2,1,0:T(8,128)}, u32[]{:S(2)}) copy-start(f32[4,128,16,64]{3,2,1,0:T(8,128)} %get-tuple-element.34) | copy-start | bytes 6291460
  150.1 2.9 %copy-start.2 = (f32[64,65,64]{1,2,0:T(8,128)S(1)}, f32[64,65,64]{1,2,0:T(8,128)}, u32[]{:S(2)}) copy-start(f32[64,65,64]{1,2,0:T(8,128)} %all-gather.5.cloned.1.call-done) | copy-start | bytes 3194884
  179.4 7.4 %copy-start.6 = (f32[4,16,128,128]{3,2,1,0:T(8,128)S(1)}, f32[4,16,128,128]{3,2,1,0:T(8,128)}, u32[]{:S(2)}) copy-start(f32[4,16,128,128]{3,2,1,0:T(8,128)} %fusion.9) | copy-start | bytes 12582916
  179.4 7.4 %copy-start.9 = (bf16[128,4,1024]{0,2,1:T(8,128)(2,1)S(1)}, bf16[128,4,1024]{0,2,1:T(8,128)(2,1)}, u32[]{:S(2)}) copy-start(bf16[128,4,1024]{0,2,1:T(8,128)(2,1)} %copy-done.8) | copy-start | bytes 3145732
  179.4 7.4 %copy-start.10 = (f32[4,128,16,64]{1,3,2,0:T(8,128)S(1)}, f32[4,128,16,64]{1,3,2,0:T(8,128)}, u32[]{:S(2)}) copy-start(f32[4,128,16,64]{1,3,2,0:T(8,128)} %fusion) | copy-start | bytes 6291460
  209.3 5.3 %copy-start.1 = (bf16[128,4096]{1,0:T(8,128)(2,1)S(1)}, bf16[128,4096]{1,0:T(8,128)(2,1)}, u32[]{:S(2)}) copy-start(bf16[128,4096]{1,0:T(8,128)(2,1)} %param.22) | copy-start | bytes 3145732
Sparse Core Ops, SparseCore 0:
  109.3 40.6 all-gather.4

commit v5 on v4

--- a/solution.py
+++ b/solution.py
@@ -39,13 +39,13 @@
     cluster_mean_shift_add,
 ):
     head_count = lax.axis_size("head")
-    seq_index = lax.axis_index(("x", "z", "core"))
+    seq_index = lax.axis_index(("x", "zh", "zl", "core"))
     head_index = lax.axis_index("head")
     row_count = layer_entries.shape[0]
     block_start = (seq_index * head_count + head_index) * row_count
     own_seg = lax.dynamic_slice_in_dim(prompt_label, block_start, row_count, 0)
     prior_seg = jnp.concatenate([earlier_segment(prompt_label, block_start), own_seg[:-1]])
-    edge_row = shifted(layer_entries[-1:], ("x", "z", "core", "head"), 1)
+    edge_row = shifted(layer_entries[-1:], ("x", "zh", "zl", "core", "head"), 1)
     prev_rows = jnp.concatenate([edge_row, layer_entries[:-1]], axis=0)
     prev_rows = jnp.where((prior_seg == own_seg)[:, None], prev_rows, jnp.zeros_like(prev_rows))
     current = layer_entries.astype(jnp.float32)
@@ -148,13 +148,16 @@
     core_count = lax.axis_size("core")
     core_prefix, core_total = fold(lax.all_gather(own, "core"), core_index)
     share = local_heads // core_count
-    core_share = lax.dynamic_slice_in_dim(core_total, core_index * share, share, 0)
-    z_prefix, z_total = fold(lax.all_gather(core_share, "z"), lax.axis_index("z"))
-    x_prefix, _ = fold(lax.all_gather(z_total, "x"), lax.axis_index("x"))
-    pair_incoming = (
-        z_prefix[:, ATTENTION_SPAN][:, :, None] * x_prefix[:, :ATTENTION_SPAN]
-        + z_prefix[:, :ATTENTION_SPAN]
-    )
+    level_prefixes = []
+    running = lax.dynamic_slice_in_dim(core_total, core_index * share, share, 0)
+    for axis in ("zl", "zh", "x"):
+        prefix, running = fold(lax.all_gather(running, axis), lax.axis_index(axis))
+        level_prefixes.append(prefix)
+    pair_incoming = level_prefixes[-1][:, :ATTENTION_SPAN]
+    for prefix in level_prefixes[-2::-1]:
+        pair_incoming = (
+            prefix[:, ATTENTION_SPAN][:, :, None] * pair_incoming + prefix[:, :ATTENTION_SPAN]
+        )
     pair_incoming = lax.all_gather(pair_incoming, "core", tiled=True)
     incoming = (
         core_prefix[:, ATTENTION_SPAN][:, :, None] * pair_incoming
@@ -183,19 +186,22 @@
     seq_count, head_count = mesh.devices.shape
     core_count = 2
     z_count = min(8, seq_count // core_count)
+    z_low = min(4, z_count)
     fine_mesh = jax.sharding.Mesh(
-        mesh.devices.reshape(seq_count // (z_count * core_count), z_count, core_count, head_count),
-        ("x", "z", "core", "head"),
+        mesh.devices.reshape(
+            seq_count // (z_count * core_count), z_count // z_low, z_low, core_count, head_count
+        ),
+        ("x", "zh", "zl", "core", "head"),
     )
     return jax.shard_map(
         local,
         mesh=fine_mesh,
         in_specs=(
-            P(("x", "z", "core", "head"), None),
-            P(("x", "z", "core", "head"), None),
-            P(("x", "z", "core", "head"), None),
-            P(("x", "z", "core", "head"), None),
-            P(("x", "z", "core", "head"), None),
+            P(("x", "zh", "zl", "core", "head"), None),
+            P(("x", "zh", "zl", "core", "head"), None),
+            P(("x", "zh", "zl", "core", "head"), None),
+            P(("x", "zh", "zl", "core", "head"), None),
+            P(("x", "zh", "zl", "core", "head"), None),
             P(),
             P(),
             P(),
@@ -205,6 +211,6 @@
             P(),
             P(),
         ),
-        out_specs=P(("x", "z", "core", "head"), None),
+        out_specs=P(("x", "zh", "zl", "core", "head"), None),
         check_vma=False,
     )

time: 223 us -> 205 us (0.919)
  the two profiles are of different devices: /device:TPU:1 before, /device:TPU:96 now
where the time goes in v5:
time: 205 us; the launch traced here: 204 us
  blocking collectives  79.7 us (39%)
  other arithmetic  34 us (17%)
  local copies, waits for them, and re-layouts  32.7 us (16%)
  matrix products  26 us (13%)
  starting transfers between devices  20.3 us (10%)
  waiting for transfers between devices  9.48 us (5%)
    all_gather x3, blocking collectives, local(): prefix, running = fold(lax.all_gather(running, axis), lax.axis_index(axis))  54.9 us
    all_to_all x1, blocking collectives, local(): lax.all_to_all(normed, 'head', split_axis=0, concat_axis=1, tiled=True)  20 us
    mul x1, other arithmetic, local(): scaled_key = lookup_vectors * jnp.exp(-cumulative)  11.2 us
    dot_general x1, matrix products, local(): jnp.einsum('cthd,cshd->chts', scaled_query, scaled_key, precision=highest)  10 us
    all_to_all x1, waiting for transfers between devices, local(): lax.all_to_all(acceptance_linear, 'head', split_axis=1, concat_axis=0, ti...  8.17 us
    unnamed x30, local copies, waits for them, and re-layouts  6.46 us
    dot_general x1, matrix products, local(): jnp.einsum('cthd,chde->cthe', scaled_query * keep_first[:, :, None, None]...  4.87 us
    dot_general x1, matrix products, local(): jnp.einsum('cthd,cthe->chde', tail_keys, payload_vectors, precision=highest)  4.51 us
  transfers between devices with their start and end apart: 5, of which 3 were waited for; matrix products, arithmetic and copies ran while one was open for 24% of the time, Pallas kernels for 0%

profile of v5, /device:TPU:96, one launch (start us, length us, event | category | flops | bytes accessed | tf_op | source)
XLA Modules:
  0.0 203.7 jit_solution(17745057543117374505)
XLA Ops:
  0.0 2.4 %copy.287 = bf16[128,4096]{0,1:T(8,128)(2,1)} copy(bf16[128,4096]{1,0:T(8,128)(2,1)} %param.13) | data formatting | bytes 2097152 | tf_op args[0]
  2.4 4.5 %all-to-all-start = ((bf16[128,4,1024]{0,2,1:T(8,128)(2,1)}), bf16[128,4,1024]{0,2,1:T(8,128)(2,1)S(1)}, u32[]{:S(2)}, u32[]{:S(2)}) async-start(bf16[128,4,1024]{0,2,1:T(8,128)(2,1)} %bitcast.1), calls=%async_computation | async-start | bytes 2097152 | tf_op jit(solution)/shard_map/all_to_all | solution.py:63
  6.9 0.9 slice.120
  7.8 3.9 %collective-permute-start = (bf16[1,4096]{1,0:T(2,128)(2,1)S(1)}, bf16[1,4096]{1,0:T(2,128)(2,1)S(1)}, u32[]{:S(2)}, u32[]{:S(2)}) collective-permute-start(bf16[1,4096]{1,0:T(2,128)(2,1)S(1)} %slice.120), channel_id=1, source_target_pairs={{0,1},{1,2},{2,3},{3,4},{4,5},{5,6},{6,7},{7,8},{8,9},{9,10},{10,1... | collective-permute-start | bytes 24584 | tf_op jit(solution)/shard_map/ppermute | solution.py:18
  11.7 1.3 copy.292
  13.0 0.8 dynamic-slice_bitcast_fusion
  14.0 8.2 %all-to-all-done = bf16[128,4,1024]{0,2,1:T(8,128)(2,1)S(1)} async-done(((bf16[128,4,1024]{0,2,1:T(8,128)(2,1)}), bf16[128,4,1024]{0,2,1:T(8,128)(2,1)S(1)}, u32[]{:S(2)}, u32[]{:S(2)}) %all-to-all-start) | async-done | bytes 1048608 | tf_op jit(solution)/shard_map/all_to_all | solution.py:63
  22.2 3.6 %all-to-all-start.2 = ((bf16[128,4,1024]{0,2,1:T(8,128)(2,1)}), bf16[128,4,1024]{0,2,1:T(8,128)(2,1)S(1)}, u32[]{:S(2)}, u32[]{:S(2)}) async-start(bf16[128,4,1024]{0,2,1:T(8,128)(2,1)} %bitcast.201), calls=%async_computation.2 | async-start | bytes 2097152 | tf_op jit(solution)/shard_map/all_to_all | solution.py:64
  26.0 0.8 dynamic_slice.26
  26.8 1.4 fusion.77
  29.4 0.8 add_compare_fusion
  30.2 0.7 dynamic_slice.27
  31.7 0.7 dynamic_slice.31
  32.5 2.3 %copy.308 = bf16[128,4096]{0,1:T(8,128)(2,1)} copy(bf16[128,4096]{1,0:T(8,128)(2,1)} %param.15) | data formatting | bytes 2097152 | tf_op jit(solution)/shard_map/all_to_all | solution.py:65
  34.8 3.3 %fusion.4 = bf16[128,4096]{1,0:T(8,128)(2,1)S(1)} fusion(bf16[128,4096]{1,0:T(8,128)(2,1)S(1)} %copy-done, bf16[4096,128]{1,0:T(8,128)(2,1)} %param.21, bf16[128,4096]{1,0:T(8,128)(2,1)} %param.17, bf16[127,4096]{1,0:T(8,128)(2,1)} %bitcast.203, bf16[1,4096]{1,0:T(2,128)(2,1)S(1)} %collective-permute-done, f32[4096]{0:T(1024)S(1)} %copy-done.12, ...), kind=kOutput, calls=%fused_computation.5 | convolution fusion | flops 276316160 | bytes 5275776 | tf_op jit(solution)/shard_map/dot_general | solution.py:58
  38.1 1.3 copy.307
  39.9 4.3 %all-to-all-start.1 = ((bf16[128,4,1024]{0,2,1:T(8,128)(2,1)}), bf16[128,4,1024]{0,2,1:T(8,128)(2,1)}, u32[]{:S(2)}, u32[]{:S(2)}) async-start(bf16[128,4,1024]{0,2,1:T(8,128)(2,1)} %bitcast.5), calls=%async_computation.1 | async-start | bytes 2097152 | tf_op jit(solution)/shard_map/all_to_all | solution.py:66
  44.1 0.8 compare_convert_fusion.1
  45.2 2.9 %copy.291 = f32[4,128,16,64]{3,2,1,0:T(8,128)} copy(f32[4,128,16,64]{1,3,2,0:T(8,128)S(1)} %bitcast.181) | data formatting | bytes 4194304 | tf_op jit(solution)/shard_map/convert_element_type | solution.py:87
  48.1 1.5 convert_element_type.114
  49.6 4.0 %copy.293 = f32[4,128,16,64]{3,2,1,0:T(8,128)} copy(f32[4,128,16,64]{1,3,2,0:T(8,128)} %bitcast.183) | data formatting | bytes 4194304 | tf_op jit(solution)/shard_map/convert_element_type | solution.py:88
  53.6 3.3 %fusion = f32[4,128,16,64]{1,3,2,0:T(8,128)} fusion(f32[4,128,16,64]{1,3,2,0:T(8,128)} %bitcast.184, f32[4,128,16,64]{1,3,2,0:T(8,128)S(1)} %bitcast.182, f32[16,64]{1,0:T(8,128)S(1)} %mul.514), kind=kOutput, calls=%fused_computation | output fusion | flops 1056831 | bytes 6295552 | tf_op jit(solution)/shard_map/mul | solution.py:104
  56.9 0.9 all-to-all-done.1
  57.8 3.9 %all-to-all-start.3 = ((bf16[128,4,1024]{0,2,1:T(8,128)(2,1)}), bf16[128,4,1024]{0,2,1:T(8,128)(2,1)S(1)}, u32[]{:S(2)}, u32[]{:S(2)}) async-start(bf16[128,4,1024]{0,2,1:T(8,128)(2,1)} %bitcast.12), calls=%async_computation.3 | async-start | bytes 2097152 | tf_op jit(solution)/shard_map/all_to_all | solution.py:65
  61.7 2.7 %convert_element_type.113 = f32[128,4,1024]{0,2,1:T(8,128)} convert(bf16[128,4,1024]{0,2,1:T(8,128)(2,1)} %all-to-all-done.1) | non-fusion elementwise | flops 524288 | bytes 3145728 | tf_op jit(solution)/shard_map/convert_element_type | solution.py:90
  64.4 4.0 %copy.289 = f32[4,128,16,64]{3,2,1,0:T(8,128)} copy(f32[4,128,16,64]{1,3,2,0:T(8,128)} %bitcast.195) | data formatting | bytes 4194304 | tf_op jit(solution)/shard_map/convert_element_type | solution.py:90
  68.4 2.5 %fusion.80 = f32[4,128,16,64]{3,2,1,0:T(8,128)S(1)} fusion(f32[4,128,16,64]{3,2,1,0:T(8,128)} %copy.289), kind=kOutput, calls=%fused_computation.159 | output fusion | flops 66584576 | bytes 4194304 | tf_op jit(solution)/shard_map/jit(cumsum)/reduce_window_sum | solution.py:91
  71.0 1.9 copy-done.2
  73.3 11.2 %exponential_multiply_fusion = (f32[4,128,16,64]{3,2,1,0:T(8,128)}, f32[4,128,16,64]{3,2,1,0:T(8,128)}, f32[4,128,16,64]{3,2,1,0:T(8,128)}, f32[4,128,16,64]{3,2,1,0:T(8,128)}) fusion(f32[4,128,16,64]{3,2,1,0:T(8,128)} %copy.293, f32[4,128,16,64]{3,2,1,0:T(8,128)} %copy-done.2, f32[4,128]{1,0:T(4,128)S(1)} %get-tuple-element.47, ...), kind=kLoop, calls=%fused_computation.16 | loop fusion | flops 4194304 | bytes 16797696 | tf_op jit(solution)/shard_map/mul | solution.py:95
  84.4 4.5 %fusion.7 = f32[4,16,64,64]{2,3,1,0:T(8,128)S(1)} fusion(bf16[4,128,16,64]{1,3,2,0:T(8,128)(2,1)S(1)} %bitcast.193, f32[4,128,16,64]{3,2,1,0:T(8,128)} %get-tuple-element.31), kind=kOutput, calls=%fused_computation.8 | convolution fusion | flops 201326592 | bytes 4194304 | tf_op jit(solution)/shard_map/cthd,cthe->chde/dot_general | solution.py:109
  88.9 1.0 multiply_add_fusion.1
  90.4 2.6 %all-gather = f32[32,65,64]{1,2,0:T(8,128)S(1)} all-gather(f32[16,65,64]{1,2,0:T(8,128)S(1)} %pad_maximum_fusion), channel_id=2, replica_groups=mesh['x'=4,'zh'=2,'zl'=4,'core'=2,'head'=4] {'core'}, dimensions={0}, use_global_device_ids=true | all-gather | bytes 798720 | tf_op jit(solution)/shard_map/all_gather | solution.py:149
  93.0 0.8 select_reduce_fusion
  94.0 22.2 %all-gather.1 = f32[32,65,64]{1,2,0:T(8,128)S(1)} all-gather(f32[8,65,64]{1,2,0:T(8,128)S(1)} %fusion.55), channel_id=3, replica_groups=mesh['x'=4,'zh'=2,'zl'=4,'core'=2,'head'=4] {'zl'}, dimensions={0}, use_global_device_ids=true | all-gather | bytes 665600 | tf_op jit(solution)/shard_map/all_gather | solution.py:154
  116.2 0.7 select_reduce_fusion.2
  117.2 17.7 %all-gather.2 = f32[16,65,64]{1,2,0:T(8,128)S(1)} all-gather(f32[8,65,64]{1,2,0:T(8,128)S(1)} %pad_maximum_fusion.1), channel_id=4, replica_groups=mesh['x'=4,'zh'=2,'zl'=4,'core'=2,'head'=4] {'zh'}, dimensions={0}, use_global_device_ids=true | all-gather | bytes 399360 | tf_op jit(solution)/shard_map/all_gather | solution.py:154
  135.6 15.0 %all-gather.3 = f32[32,65,64]{1,2,0:T(8,128)S(1)} all-gather(f32[8,65,64]{1,2,0:T(8,128)S(1)} %pad_maximum_fusion.2), channel_id=5, replica_groups=mesh['x'=4,'zh'=2,'zl'=4,'core'=2,'head'=4] {'x'}, dimensions={0}, use_global_device_ids=true | all-gather | bytes 665600 | tf_op jit(solution)/shard_map/all_gather | solution.py:154
  151.2 1.1 fusion.61
  152.3 1.1 copy.303
  153.4 2.3 %all_gather.35 = f32[16,64,64]{2,1,0:T(8,128)} all-gather(f32[8,64,64]{2,1,0:T(8,128)S(1)} %copy.303), channel_id=1, replica_groups=mesh['x'=4,'zh'=2,'zl'=4,'core'=2,'head'=4] {'core'}, dimensions={0}, use_global_device_ids=true | all-gather | bytes 393216 | tf_op jit(solution)/shard_map/all_gather | solution.py:161
  155.7 2.1 %copy.304 = f32[16,64,64]{1,2,0:T(8,128)} copy(f32[16,64,64]{2,1,0:T(8,128)} %all_gather.35) | data formatting | bytes 524288 | tf_op jit(solution)/shard_map/all_gather | solution.py:161
  157.8 10.0 %fusion.9 = f32[4,16,128,128]{3,2,1,0:T(8,128)S(1)} fusion(f32[4,128,16,64]{3,2,1,0:T(8,128)} %get-tuple-element.30, f32[4,128,16,64]{3,2,1,0:T(8,128)} %get-tuple-element.33), kind=kOutput, calls=%fused_computation.10 | convolution fusion | flops 402653184 | bytes 8388608 | tf_op jit(solution)/shard_map/cthd,cshd->chts/dot_general | solution.py:96
  168.2 0.7 copy-done.9
  168.9 4.9 %fusion.5 = f32[4,16,64,128]{3,2,1,0:T(8,128)S(1)} fusion(f32[4,128,16,64]{3,2,1,0:T(8,128)S(1)} %copy-done.3, f32[1,16,64,64]{2,3,1,0:T(8,128)S(1)} %get-tuple-element.23, f32[1,16,64,64]{2,3,1,0:T(8,128)S(1)} %get-tuple-element.24, f32[1,16,64,64]{2,3,1,0:T(8,128)S(1)} %copy-done.9, f32[4]{0:T(128)S(1)} %pad.12.clone, ...), kind=kOutput, calls=%fused_computation.6 | convolution fusion | flops 202637312 | bytes 5259280 | tf_op jit(solution)/shard_map/cthd,chde->cthe/dot_general | solution.py:168
  173.8 3.3 %fusion.79 = (f32[4,128,16]{1,2,0:T(8,128)S(1)}, f32[4,128,16,64]{1,3,2,0:T(8,128)S(1)}) fusion(f32[4,16,64,128]{3,2,1,0:T(8,128)S(1)} %fusion.5, f32[4,128,16,64]{1,3,2,0:T(8,128)S(1)} %copy-done.4, bf16[4,128,16,64]{1,3,2,0:T(8,128)(2,1)S(1)} %bitcast.194, f32[4,16,128,128]{3,2,1,0:T(8,128)S(1)} %fusion.9, pred[4,128,128]{2,1,0:T(8,128)(4,1)S(1)} %compare_and_fusion), kind=kOutput, calls=%fused_computation.158 | convolution fusion | flops 406315008 | bytes 11632640 | tf_op jit(solution)/shard_map/chts,cshd->cthd/dot_general | solution.py:102
  178.3 20.0 %all_to_all.68 = bf16[4,128,1024]{1,2,0:T(8,128)(2,1)S(1)} all-to-all(bf16[4,128,1024]{1,2,0:T(8,128)(2,1)S(1)} %bitcast.200), channel_id=1, replica_groups=mesh['x'=4,'zh'=2,'zl'=4,'core'=2,'head'=4] {'head'}, dimensions={0} | all-to-all | bytes 2097152 | tf_op jit(solution)/shard_map/all_to_all | solution.py:179
  198.4 1.9 copy.309
  200.3 3.4 %fusion.28 = bf16[128,4096]{1,0:T(8,128)(2,1)} fusion(f32[128,4096]{1,0:T(8,128)} %copy.309, bf16[128,4096]{1,0:T(8,128)(2,1)} %param.16), kind=kLoop, calls=%fused_computation.43 | loop fusion | flops 3670016 | bytes 4194304 | tf_op jit(solution)/shard_map/convert_element_type | solution.py:180
  (65 shorter events, 6.2 us)
Async XLA Ops:
  0.0 34.8 %copy-start = (bf16[128,4096]{1,0:T(8,128)(2,1)S(1)}, bf16[128,4096]{1,0:T(8,128)(2,1)}, u32[]{:S(2)}) copy-start(bf16[128,4096]{1,0:T(8,128)(2,1)} %param.22) | copy-start | bytes 3145732
  0.0 11.7 %copy-start.11 = (bf16[128,4096]{1,0:T(8,128)(2,1)S(1)}, bf16[128,4096]{1,0:T(8,128)(2,1)}, u32[]{:S(2)}) copy-start(bf16[128,4096]{1,0:T(8,128)(2,1)} %param.14) | copy-start | bytes 3145732
  2.4 19.7 %all-to-all-start = ((bf16[128,4,1024]{0,2,1:T(8,128)(2,1)}), bf16[128,4,1024]{0,2,1:T(8,128)(2,1)S(1)}, u32[]{:S(2)}, u32[]{:S(2)}) async-start(bf16[128,4,1024]{0,2,1:T(8,128)(2,1)} %bitcast.1), calls=%async_computation | async-start | bytes 2097152 | tf_op jit(solution)/shard_map/all_to_all | solution.py:63
  7.8 27.0 %collective-permute-start = (bf16[1,4096]{1,0:T(2,128)(2,1)S(1)}, bf16[1,4096]{1,0:T(2,128)(2,1)S(1)}, u32[]{:S(2)}, u32[]{:S(2)}) collective-permute-start(bf16[1,4096]{1,0:T(2,128)(2,1)S(1)} %slice.120), channel_id=1, source_target_pairs={{0,1},{1,2},{2,3},{3,4},{4,5},{5,6},{6,7},{7,8},{8,9},{9,10},{10,1... | collective-permute-start | bytes 24584 | tf_op jit(solution)/shard_map/ppermute | solution.py:18
  22.2 12.6 %copy-start.5 = (bf16[128,4,1024]{0,2,1:T(8,128)(2,1)}, bf16[128,4,1024]{0,2,1:T(8,128)(2,1)S(1)}, u32[]{:S(2)}) copy-start(bf16[128,4,1024]{0,2,1:T(8,128)(2,1)S(1)} %all-to-all-done) | copy-start | bytes 3145732
  22.2 12.6 %copy-start.12 = (f32[4096]{0:T(1024)S(1)}, f32[4096]{0:T(1024)}, u32[]{:S(2)}) copy-start(f32[4096]{0:T(1024)} %param.20) | copy-start | bytes 49156
  22.2 12.6 %copy-start.13 = (f32[4096]{0:T(1024)S(1)}, f32[4096]{0:T(1024)}, u32[]{:S(2)}) copy-start(f32[4096]{0:T(1024)} %param.19) | copy-start | bytes 49156
  22.2 17.7 %all-to-all-start.2 = ((bf16[128,4,1024]{0,2,1:T(8,128)(2,1)}), bf16[128,4,1024]{0,2,1:T(8,128)(2,1)S(1)}, u32[]{:S(2)}, u32[]{:S(2)}) async-start(bf16[128,4,1024]{0,2,1:T(8,128)(2,1)} %bitcast.201), calls=%async_computation.2 | async-start | bytes 2097152 | tf_op jit(solution)/shard_map/all_to_all | solution.py:64
  38.1 7.0 %copy-start.6 = (bf16[128,4,1024]{0,2,1:T(8,128)(2,1)S(1)}, bf16[128,4,1024]{0,2,1:T(8,128)(2,1)}, u32[]{:S(2)}) copy-start(bf16[128,4,1024]{0,2,1:T(8,128)(2,1)} %copy-done.5) | copy-start | bytes 3145732
  39.9 5.0 %copy-start.7 = (bf16[128,4,1024]{0,2,1:T(8,128)(2,1)}, bf16[128,4,1024]{0,2,1:T(8,128)(2,1)S(1)}, u32[]{:S(2)}) copy-start(bf16[128,4,1024]{0,2,1:T(8,128)(2,1)S(1)} %all-to-all-done.2) | copy-start | bytes 3145732
  39.9 17.9 %all-to-all-start.1 = ((bf16[128,4,1024]{0,2,1:T(8,128)(2,1)}), bf16[128,4,1024]{0,2,1:T(8,128)(2,1)}, u32[]{:S(2)}, u32[]{:S(2)}) async-start(bf16[128,4,1024]{0,2,1:T(8,128)(2,1)} %bitcast.5), calls=%async_computation.1 | async-start | bytes 2097152 | tf_op jit(solution)/shard_map/all_to_all | solution.py:66
  45.2 2.9 %copy-start.8 = (bf16[128,4,1024]{0,2,1:T(8,128)(2,1)S(1)}, bf16[128,4,1024]{0,2,1:T(8,128)(2,1)}, u32[]{:S(2)}) copy-start(bf16[128,4,1024]{0,2,1:T(8,128)(2,1)} %copy-done.7) | copy-start | bytes 3145732
  57.8 26.6 %all-to-all-start.3 = ((bf16[128,4,1024]{0,2,1:T(8,128)(2,1)}), bf16[128,4,1024]{0,2,1:T(8,128)(2,1)S(1)}, u32[]{:S(2)}, u32[]{:S(2)}) async-start(bf16[128,4,1024]{0,2,1:T(8,128)(2,1)} %bitcast.12), calls=%async_computation.3 | async-start | bytes 2097152 | tf_op jit(solution)/shard_map/all_to_all | solution.py:65
  71.0 2.0 copy-start.2
  157.8 10.1 %copy-start.10 = (f32[16,64,64]{1,2,0:T(8,128)S(1)}, f32[16,64,64]{1,2,0:T(8,128)}, u32[]{:S(2)}) copy-start(f32[16,64,64]{1,2,0:T(8,128)} %copy.304) | copy-start | bytes 786436
  157.8 10.3 %copy-start.3 = (f32[4,128,16,64]{3,2,1,0:T(8,128)S(1)}, f32[4,128,16,64]{3,2,1,0:T(8,128)}, u32[]{:S(2)}) copy-start(f32[4,128,16,64]{3,2,1,0:T(8,128)} %get-tuple-element.32) | copy-start | bytes 6291460
  167.9 1.0 copy-start.9
  168.9 4.9 %copy-start.4 = (f32[4,128,16,64]{1,3,2,0:T(8,128)S(1)}, f32[4,128,16,64]{1,3,2,0:T(8,128)}, u32[]{:S(2)}) copy-start(f32[4,128,16,64]{1,3,2,0:T(8,128)} %fusion) | copy-start | bytes 6291460
  198.4 5.3 %copy-start.1 = (bf16[128,4096]{1,0:T(8,128)(2,1)S(1)}, bf16[128,4096]{1,0:T(8,128)(2,1)}, u32[]{:S(2)}) copy-start(bf16[128,4096]{1,0:T(8,128)(2,1)} %param.22) | copy-start | bytes 3145732

commit v6 on v5

--- a/solution.py
+++ b/solution.py
@@ -59,12 +59,14 @@
         decay_hidden_rows, fading_raise_map, preferred_element_type=jnp.float32
     )
     log_decay = jnp.maximum(-jnp.exp(decay_score), decay_floor).astype(jnp.bfloat16)
-    query_head, key_head, value_head, decay_head = (
-        lax.all_to_all(acceptance_linear, "head", split_axis=1, concat_axis=0, tiled=True),
-        lax.all_to_all(lookup_linear, "head", split_axis=1, concat_axis=0, tiled=True),
-        lax.all_to_all(payload_linear, "head", split_axis=1, concat_axis=0, tiled=True),
-        lax.all_to_all(log_decay, "head", split_axis=1, concat_axis=0, tiled=True),
-    )
+    moved = lax.all_to_all(
+        jnp.stack([acceptance_linear, lookup_linear, payload_linear, log_decay]),
+        "head",
+        split_axis=2,
+        concat_axis=1,
+        tiled=True,
+    )
+    query_head, key_head, value_head, decay_head = moved[0], moved[1], moved[2], moved[3]
     tokens = query_head.shape[0]
     partition_extent = query_head.shape[1]
     local_heads = partition_extent // ATTENTION_SPAN

time: 205 us -> 225 us (1.098)
  the two profiles are of different devices: /device:TPU:96 before, /device:TPU:1 now
where the time goes in v6:
time: 225 us; the launch traced here: 221 us
  blocking collectives  76.7 us (34%)
  waiting for transfers between devices  43 us (19%)
  local copies, waits for them, and re-layouts  34.9 us (16%)
  other arithmetic  30.9 us (14%)
  matrix products  24.8 us (11%)
  starting transfers between devices  8.87 us (4%)
    all_gather x3, blocking collectives, local(): prefix, running = fold(lax.all_gather(running, axis), lax.axis_index(axis))  46.8 us
    all_to_all x1, waiting for transfers between devices, local(): lax.all_to_all(jnp.stack([acceptance_linear, lookup_linear, payload_linea...  43 us
    all_to_all x1, blocking collectives, local(): lax.all_to_all(normed, 'head', split_axis=0, concat_axis=1, tiled=True)  17.2 us
    mul x1, other arithmetic, local(): scaled_key = lookup_vectors * jnp.exp(-cumulative)  10.5 us
    dot_general x1, matrix products, local(): jnp.einsum('cthd,cshd->chts', scaled_query, scaled_key, precision=highest)  10 us
    all_gather x1, blocking collectives, local(): pair_incoming = lax.all_gather(pair_incoming, 'core', tiled=True)  8.4 us
    another operation x1, local copies, waits for them, and re-layouts, local(): jnp.stack([acceptance_linear, lookup_linear, payload_linear, log_decay])  7.48 us
    dot_general x1, matrix products, local(): jnp.einsum('cthd,chde->cthe', scaled_query * keep_first[:, :, None, None]...  4.91 us
  transfers between devices with their start and end apart: 2, of which 1 were waited for; matrix products, arithmetic and copies ran while one was open for 3% of the time, Pallas kernels for 0%

profile of v6, /device:TPU:1, one launch (start us, length us, event | category | flops | bytes accessed | tf_op | source)
XLA Modules:
  0.0 220.9 jit_solution(1062731136262881348)
XLA Ops:
  0.0 0.9 slice.136
  1.0 4.0 %collective-permute-start = (bf16[1,4096]{1,0:T(2,128)(2,1)S(1)}, bf16[1,4096]{1,0:T(2,128)(2,1)S(1)}, u32[]{:S(2)}, u32[]{:S(2)}) collective-permute-start(bf16[1,4096]{1,0:T(2,128)(2,1)S(1)} %slice.136), channel_id=1, source_target_pairs={{0,1},{1,2},{2,3},{3,4},{4,5},{5,6},{6,7},{7,8},{8,9},{9,10},{10,1... | collective-permute-start | bytes 24584 | tf_op jit(solution)/shard_map/ppermute | solution.py:18
  5.0 0.8 dynamic_slice.25
  5.8 1.4 fusion.81
  7.9 0.8 add_compare_fusion
  8.7 4.4 %fusion.5 = bf16[1,128,4096]{2,1,0:T(8,128)(2,1)} fusion(bf16[128,4096]{1,0:T(8,128)(2,1)S(1)} %copy-done, bf16[4096,128]{1,0:T(8,128)(2,1)} %param.21, bf16[128,4096]{1,0:T(8,128)(2,1)} %param.17, bf16[127,4096]{1,0:T(8,128)(2,1)} %bitcast.203, bf16[1,4096]{1,0:T(2,128)(2,1)S(1)} %collective-permute-done, f32[4096]{0:T(1024)} %param.20, f32[4096]{0:T(1024)} %param.19, ...), kind=kOutput, calls=%fused_computation.6 | convolution fusion | flops 276316160 | bytes 5275776 | tf_op jit(solution)/shard_map/dot_general | solution.py:58
  13.1 3.4 %pad_maximum_fusion = bf16[4,128,4096]{2,1,0:T(8,128)(2,1)} fusion(bf16[1,128,4096]{2,1,0:T(8,128)(2,1)} %fusion.5, bf16[1,128,4096]{2,1,0:T(8,128)(2,1)S(1)} %bitcast.199, bf16[1,128,4096]{2,1,0:T(8,128)(2,1)S(1)} %bitcast.200, bf16[1,128,4096]{2,1,0:T(8,128)(2,1)} %bitcast.201), kind=kLoop, calls=%fused_computation.7 | loop fusion | flops 6291456 | bytes 8388608 | tf_op jit(solution)/shard_map/stack | solution.py:63
  16.5 7.5 %copy.260 = bf16[4,128,4096]{1,0,2:T(4,128)(2,1)} copy(bf16[4,128,4096]{2,1,0:T(8,128)(2,1)} %pad_maximum_fusion) | data formatting | bytes 8388608 | tf_op jit(solution)/shard_map/stack | solution.py:63
  24.0 4.8 %all-to-all-start = ((bf16[4,128,4096]{1,0,2:T(4,128)(2,1)}), bf16[4,128,4096]{1,0,2:T(4,128)(2,1)}, u32[]{:S(2)}, u32[]{:S(2)}) async-start(bf16[4,128,4096]{1,0,2:T(4,128)(2,1)} %copy.260), calls=%async_computation | async-start | bytes 8388608 | tf_op jit(solution)/shard_map/all_to_all | solution.py:62
  28.9 0.7 dynamic_slice.27
  29.7 0.7 dynamic_slice.30
  30.4 0.7 dynamic_slice.31
  31.8 0.8 dynamic-slice_bitcast_fusion
  33.0 0.8 compare_convert_fusion.1
  33.9 43.0 %all-to-all-done = bf16[4,128,4096]{1,0,2:T(4,128)(2,1)} async-done(((bf16[4,128,4096]{1,0,2:T(4,128)(2,1)}), bf16[4,128,4096]{1,0,2:T(4,128)(2,1)}, u32[]{:S(2)}, u32[]{:S(2)}) %all-to-all-start) | async-done | bytes 4194336 | tf_op jit(solution)/shard_map/all_to_all | solution.py:62
  76.9 2.7 %copy.261 = bf16[4,128,4096]{1,2,0:T(8,128)(2,1)S(1)} copy(bf16[4,128,4096]{1,0,2:T(4,128)(2,1)} %all-to-all-done) | data formatting | bytes 8388608 | tf_op jit(solution)/shard_map/all_to_all | solution.py:62
  79.6 1.3 fusion.80
  80.9 2.7 %copy.264 = f32[4,128,16,64]{3,2,1,0:T(8,128)} copy(bf16[4,128,16,64]{1,3,2,0:T(8,128)(2,1)S(1)} %bitcast.189) | data formatting | bytes 3145728 | tf_op jit(solution)/shard_map/convert_element_type | solution.py:89
  83.6 2.7 %copy.265 = f32[4,128,16,64]{3,2,1,0:T(8,128)} copy(bf16[4,128,16,64]{1,3,2,0:T(8,128)(2,1)S(1)} %bitcast.187) | data formatting | bytes 3145728 | tf_op jit(solution)/shard_map/convert_element_type | solution.py:90
  86.3 1.8 fusion
  88.1 3.6 %copy.262 = f32[4,128,16,64]{3,2,1,0:T(8,128)} copy(bf16[4,128,16,64]{1,3,2,0:T(8,128)(2,1)} %bitcast.198) | data formatting | bytes 3145728 | tf_op jit(solution)/shard_map/convert_element_type | solution.py:92
  91.7 2.5 %fusion.84 = f32[4,128,16,64]{3,2,1,0:T(8,128)S(1)} fusion(f32[4,128,16,64]{3,2,1,0:T(8,128)} %copy.262), kind=kOutput, calls=%fused_computation.164 | output fusion | flops 66584576 | bytes 4194304 | tf_op jit(solution)/shard_map/jit(cumsum)/reduce_window_sum | solution.py:93
  94.3 1.9 copy-done.2
  96.5 10.5 %exponential_multiply_fusion = (f32[4,128,16,64]{3,2,1,0:T(8,128)}, f32[4,128,16,64]{3,2,1,0:T(8,128)S(1)}, f32[4,128,16,64]{3,2,1,0:T(8,128)}, f32[4,128,16,64]{3,2,1,0:T(8,128)}) fusion(f32[4,128,16,64]{3,2,1,0:T(8,128)} %copy.265, f32[4,128,16,64]{3,2,1,0:T(8,128)} %copy-done.2, f32[4,128]{1,0:T(4,128)S(1)} %get-tuple-element.51, ...), kind=kLoop, calls=%fused_computation.18 | loop fusion | flops 4194304 | bytes 16797696 | tf_op jit(solution)/shard_map/mul | solution.py:97
  107.0 2.4 %fusion.8 = f32[4,16,64,64]{2,3,1,0:T(8,128)S(1)} fusion(bf16[4,128,16,64]{1,3,2,0:T(8,128)(2,1)S(1)} %bitcast.191, f32[4,128,16,64]{3,2,1,0:T(8,128)S(1)} %get-tuple-element.31), kind=kOutput, calls=%fused_computation.10 | convolution fusion | flops 201326592 | bytes 4194304 | tf_op jit(solution)/shard_map/cthd,cthe->chde/dot_general | solution.py:111
  109.4 1.0 multiply_add_fusion.1
  110.4 0.3 fusion.52
  110.9 4.3 %all-gather = f32[32,65,64]{1,2,0:T(8,128)S(1)} all-gather(f32[16,65,64]{1,2,0:T(8,128)S(1)} %pad_maximum_fusion.1), channel_id=2, replica_groups=mesh['x'=4,'zh'=2,'zl'=4,'core'=2,'head'=4] {'core'}, dimensions={0}, use_global_device_ids=true | all-gather | bytes 798720 | tf_op jit(solution)/shard_map/all_gather | solution.py:151
  115.2 0.8 select_reduce_fusion
  116.2 22.4 %all-gather.1 = f32[32,65,64]{1,2,0:T(8,128)S(1)} all-gather(f32[8,65,64]{1,2,0:T(8,128)S(1)} %fusion.58), channel_id=3, replica_groups=mesh['x'=4,'zh'=2,'zl'=4,'core'=2,'head'=4] {'zl'}, dimensions={0}, use_global_device_ids=true | all-gather | bytes 665600 | tf_op jit(solution)/shard_map/all_gather | solution.py:156
  138.7 0.7 select_reduce_fusion.2
  139.6 12.1 %all-gather.2 = f32[16,65,64]{1,2,0:T(8,128)S(1)} all-gather(f32[8,65,64]{1,2,0:T(8,128)S(1)} %pad_maximum_fusion.2), channel_id=4, replica_groups=mesh['x'=4,'zh'=2,'zl'=4,'core'=2,'head'=4] {'zh'}, dimensions={0}, use_global_device_ids=true | all-gather | bytes 399360 | tf_op jit(solution)/shard_map/all_gather | solution.py:156
  151.7 0.5 select_reduce_fusion.1
  152.4 12.3 %all-gather.3 = f32[32,65,64]{1,2,0:T(8,128)S(1)} all-gather(f32[8,65,64]{1,2,0:T(8,128)S(1)} %pad_maximum_fusion.3), channel_id=5, replica_groups=mesh['x'=4,'zh'=2,'zl'=4,'core'=2,'head'=4] {'x'}, dimensions={0}, use_global_device_ids=true | all-gather | bytes 665600 | tf_op jit(solution)/shard_map/all_gather | solution.py:156
  164.6 0.6 slice_reduce_fusion.3
  165.3 1.1 fusion.64
  166.4 1.1 copy.274
  167.5 8.4 %all_gather.35 = f32[16,64,64]{2,1,0:T(8,128)} all-gather(f32[8,64,64]{2,1,0:T(8,128)S(1)} %copy.274), channel_id=1, replica_groups=mesh['x'=4,'zh'=2,'zl'=4,'core'=2,'head'=4] {'core'}, dimensions={0}, use_global_device_ids=true | all-gather | bytes 393216 | tf_op jit(solution)/shard_map/all_gather | solution.py:163
  175.9 2.0 copy.275
  178.0 10.0 %fusion.10 = f32[4,16,128,128]{3,2,1,0:T(8,128)S(1)} fusion(f32[4,128,16,64]{3,2,1,0:T(8,128)} %get-tuple-element.30, f32[4,128,16,64]{3,2,1,0:T(8,128)} %get-tuple-element.33), kind=kOutput, calls=%fused_computation.12 | convolution fusion | flops 402653184 | bytes 8388608 | tf_op jit(solution)/shard_map/cthd,cshd->chts/dot_general | solution.py:98
  188.3 0.7 copy-done.5
  189.0 4.9 %fusion.6 = f32[4,16,64,128]{3,2,1,0:T(8,128)S(1)} fusion(f32[4,128,16,64]{3,2,1,0:T(8,128)S(1)} %copy-done.3, f32[1,16,64,64]{2,3,1,0:T(8,128)S(1)} %get-tuple-element.23, f32[1,16,64,64]{2,3,1,0:T(8,128)S(1)} %get-tuple-element.24, f32[1,16,64,64]{2,3,1,0:T(8,128)S(1)} %copy-done.5, f32[4]{0:T(128)S(1)} %pad.12.clone, ...), kind=kOutput, calls=%fused_computation.8 | convolution fusion | flops 202637312 | bytes 5259280 | tf_op jit(solution)/shard_map/cthd,chde->cthe/dot_general | solution.py:170
  194.0 3.1 %fusion.83 = (f32[4,128,16]{1,2,0:T(8,128)S(1)}, f32[4,128,16,64]{1,3,2,0:T(8,128)S(1)}) fusion(f32[4,16,64,128]{3,2,1,0:T(8,128)S(1)} %fusion.6, f32[4,128,16,64]{1,3,2,0:T(8,128)S(1)} %copy-done.4, bf16[4,128,16,64]{1,3,2,0:T(8,128)(2,1)S(1)} %bitcast.192, f32[4,16,128,128]{3,2,1,0:T(8,128)S(1)} %fusion.10, pred[4,128,128]{2,1,0:T(8,128)(4,1)S(1)} %compare_and_fusion), kind=kOutput, calls=%fused_computation.163 | convolution fusion | flops 406315008 | bytes 11632640 | tf_op jit(solution)/shard_map/chts,cshd->cthd/dot_general | solution.py:104
  197.1 0.5 multiply_reduce_fusion
  197.6 0.6 add_convert_fusion
  198.3 17.2 %all_to_all.28 = bf16[4,128,1024]{1,2,0:T(8,128)(2,1)S(1)} all-to-all(bf16[4,128,1024]{1,2,0:T(8,128)(2,1)S(1)} %bitcast.197), channel_id=1, replica_groups=mesh['x'=4,'zh'=2,'zl'=4,'core'=2,'head'=4] {'head'}, dimensions={0} | all-to-all | bytes 2097152 | tf_op jit(solution)/shard_map/all_to_all | solution.py:181
  215.7 1.9 copy.278
  217.5 3.4 %fusion.29 = bf16[128,4096]{1,0:T(8,128)(2,1)} fusion(f32[128,4096]{1,0:T(8,128)} %copy.278, bf16[128,4096]{1,0:T(8,128)(2,1)} %param.16), kind=kLoop, calls=%fused_computation.45 | loop fusion | flops 3670016 | bytes 4194304 | tf_op jit(solution)/shard_map/convert_element_type | solution.py:182
  (46 shorter events, 2.5 us)
Async XLA Ops:
  0.0 8.7 %copy-start = (bf16[128,4096]{1,0:T(8,128)(2,1)S(1)}, bf16[128,4096]{1,0:T(8,128)(2,1)}, u32[]{:S(2)}) copy-start(bf16[128,4096]{1,0:T(8,128)(2,1)} %param.22) | copy-start | bytes 3145732
  1.0 7.7 %collective-permute-start = (bf16[1,4096]{1,0:T(2,128)(2,1)S(1)}, bf16[1,4096]{1,0:T(2,128)(2,1)S(1)}, u32[]{:S(2)}, u32[]{:S(2)}) collective-permute-start(bf16[1,4096]{1,0:T(2,128)(2,1)S(1)} %slice.136), channel_id=1, source_target_pairs={{0,1},{1,2},{2,3},{3,4},{4,5},{5,6},{6,7},{7,8},{8,9},{9,10},{10,1... | collective-permute-start | bytes 24584 | tf_op jit(solution)/shard_map/ppermute | solution.py:18
  8.7 4.4 %copy-start.7 = (bf16[128,4096]{1,0:T(8,128)(2,1)S(1)}, bf16[128,4096]{1,0:T(8,128)(2,1)}, u32[]{:S(2)}) copy-start(bf16[128,4096]{1,0:T(8,128)(2,1)} %param.15) | copy-start | bytes 3145732
  8.7 4.4 %copy-start.8 = (bf16[128,4096]{1,0:T(8,128)(2,1)S(1)}, bf16[128,4096]{1,0:T(8,128)(2,1)}, u32[]{:S(2)}) copy-start(bf16[128,4096]{1,0:T(8,128)(2,1)} %param.14) | copy-start | bytes 3145732
  24.0 52.9 %all-to-all-start = ((bf16[4,128,4096]{1,0,2:T(4,128)(2,1)}), bf16[4,128,4096]{1,0,2:T(4,128)(2,1)}, u32[]{:S(2)}, u32[]{:S(2)}) async-start(bf16[4,128,4096]{1,0,2:T(4,128)(2,1)} %copy.260), calls=%async_computation | async-start | bytes 8388608 | tf_op jit(solution)/shard_map/all_to_all | solution.py:62
  94.3 1.9 copy-start.2
  178.0 10.1 %copy-start.6 = (f32[16,64,64]{1,2,0:T(8,128)S(1)}, f32[16,64,64]{1,2,0:T(8,128)}, u32[]{:S(2)}) copy-start(f32[16,64,64]{1,2,0:T(8,128)} %copy.275) | copy-start | bytes 786436
  178.0 10.4 %copy-start.3 = (f32[4,128,16,64]{3,2,1,0:T(8,128)S(1)}, f32[4,128,16,64]{3,2,1,0:T(8,128)}, u32[]{:S(2)}) copy-start(f32[4,128,16,64]{3,2,1,0:T(8,128)} %get-tuple-element.32) | copy-start | bytes 6291460
  188.0 1.0 copy-start.5
  189.0 4.9 %copy-start.4 = (f32[4,128,16,64]{1,3,2,0:T(8,128)S(1)}, f32[4,128,16,64]{1,3,2,0:T(8,128)}, u32[]{:S(2)}) copy-start(f32[4,128,16,64]{1,3,2,0:T(8,128)} %fusion) | copy-start | bytes 6291460
  215.6 5.3 %copy-start.1 = (bf16[128,4096]{1,0:T(8,128)(2,1)S(1)}, bf16[128,4096]{1,0:T(8,128)(2,1)}, u32[]{:S(2)}) copy-start(bf16[128,4096]{1,0:T(8,128)(2,1)} %param.22) | copy-start | bytes 3145732

commit v7 on v5

--- a/solution.py
+++ b/solution.py
@@ -186,7 +186,7 @@
     seq_count, head_count = mesh.devices.shape
     core_count = 2
     z_count = min(8, seq_count // core_count)
-    z_low = min(4, z_count)
+    z_low = min(2, z_count)
     fine_mesh = jax.sharding.Mesh(
         mesh.devices.reshape(
             seq_count // (z_count * core_count), z_count // z_low, z_low, core_count, head_count

time: 205 us -> 201 us (0.980)
  the two profiles are of different devices: /device:TPU:96 before, /device:TPU:1 now
where the time goes in v7:
time: 201 us; the launch traced here: 199 us
  blocking collectives  77.8 us (39%)
  other arithmetic  34 us (17%)
  local copies, waits for them, and re-layouts  32.7 us (16%)
  matrix products  26 us (13%)
  starting transfers between devices  20.5 us (10%)
  waiting for transfers between devices  6.97 us (3%)
    all_gather x3, blocking collectives, local(): prefix, running = fold(lax.all_gather(running, axis), lax.axis_index(axis))  44.9 us
    all_to_all x1, blocking collectives, local(): lax.all_to_all(normed, 'head', split_axis=0, concat_axis=1, tiled=True)  18.8 us
    mul x1, other arithmetic, local(): scaled_key = lookup_vectors * jnp.exp(-cumulative)  11.2 us
    dot_general x1, matrix products, local(): jnp.einsum('cthd,cshd->chts', scaled_query, scaled_key, precision=highest)  10 us
    all_gather x1, blocking collectives, local(): pair_incoming = lax.all_gather(pair_incoming, 'core', tiled=True)  8.09 us
    all_to_all x1, waiting for transfers between devices, local(): lax.all_to_all(acceptance_linear, 'head', split_axis=1, concat_axis=0, ti...  6.96 us
    unnamed x30, local copies, waits for them, and re-layouts  6.46 us
    all_gather x1, blocking collectives, local(): core_prefix, core_total = fold(lax.all_gather(own, 'core'), core_index)  5.99 us
  transfers between devices with their start and end apart: 5, of which 1 were waited for; matrix products, arithmetic and copies ran while one was open for 25% of the time, Pallas kernels for 0%

profile of v7, /device:TPU:1, one launch (start us, length us, event | category | flops | bytes accessed | tf_op | source)
XLA Modules:
  0.0 199.5 jit_solution(2241278802459825386)
XLA Ops:
  0.0 2.4 %copy.303 = bf16[128,4096]{0,1:T(8,128)(2,1)} copy(bf16[128,4096]{1,0:T(8,128)(2,1)} %param.13) | data formatting | bytes 2097152 | tf_op args[0]
  2.4 5.0 %all-to-all-start = ((bf16[128,4,1024]{0,2,1:T(8,128)(2,1)}), bf16[128,4,1024]{0,2,1:T(8,128)(2,1)S(1)}, u32[]{:S(2)}, u32[]{:S(2)}) async-start(bf16[128,4,1024]{0,2,1:T(8,128)(2,1)} %bitcast.1), calls=%async_computation | async-start | bytes 2097152 | tf_op jit(solution)/shard_map/all_to_all | solution.py:63
  7.4 0.9 slice.120
  8.3 3.4 %collective-permute-start = (bf16[1,4096]{1,0:T(2,128)(2,1)S(1)}, bf16[1,4096]{1,0:T(2,128)(2,1)S(1)}, u32[]{:S(2)}, u32[]{:S(2)}) collective-permute-start(bf16[1,4096]{1,0:T(2,128)(2,1)S(1)} %slice.120), channel_id=1, source_target_pairs={{0,1},{1,2},{2,3},{3,4},{4,5},{5,6},{6,7},{7,8},{8,9},{9,10},{10,1... | collective-permute-start | bytes 24584 | tf_op jit(solution)/shard_map/ppermute | solution.py:18
  11.7 1.3 copy.308
  13.0 0.8 dynamic-slice_bitcast_fusion
  14.0 7.0 %all-to-all-done = bf16[128,4,1024]{0,2,1:T(8,128)(2,1)S(1)} async-done(((bf16[128,4,1024]{0,2,1:T(8,128)(2,1)}), bf16[128,4,1024]{0,2,1:T(8,128)(2,1)S(1)}, u32[]{:S(2)}, u32[]{:S(2)}) %all-to-all-start) | async-done | bytes 1048608 | tf_op jit(solution)/shard_map/all_to_all | solution.py:63
  20.9 3.6 %all-to-all-start.2 = ((bf16[128,4,1024]{0,2,1:T(8,128)(2,1)}), bf16[128,4,1024]{0,2,1:T(8,128)(2,1)S(1)}, u32[]{:S(2)}, u32[]{:S(2)}) async-start(bf16[128,4,1024]{0,2,1:T(8,128)(2,1)} %bitcast.201), calls=%async_computation.2 | async-start | bytes 2097152 | tf_op jit(solution)/shard_map/all_to_all | solution.py:64
  24.8 0.8 dynamic_slice.26
  25.6 1.4 fusion.77
  28.2 0.8 add_compare_fusion
  29.0 0.7 dynamic_slice.27
  29.8 0.7 dynamic_slice.30
  30.4 0.7 dynamic_slice.31
  31.3 2.3 %copy.324 = bf16[128,4096]{0,1:T(8,128)(2,1)} copy(bf16[128,4096]{1,0:T(8,128)(2,1)} %param.15) | data formatting | bytes 2097152 | tf_op jit(solution)/shard_map/all_to_all | solution.py:65
  33.6 3.3 %fusion.4 = bf16[128,4096]{1,0:T(8,128)(2,1)S(1)} fusion(bf16[128,4096]{1,0:T(8,128)(2,1)S(1)} %copy-done, bf16[4096,128]{1,0:T(8,128)(2,1)} %param.21, bf16[128,4096]{1,0:T(8,128)(2,1)} %param.17, bf16[127,4096]{1,0:T(8,128)(2,1)} %bitcast.203, bf16[1,4096]{1,0:T(2,128)(2,1)S(1)} %collective-permute-done, f32[4096]{0:T(1024)S(1)} %copy-done.12, ...), kind=kOutput, calls=%fused_computation.5 | convolution fusion | flops 276316160 | bytes 5275776 | tf_op jit(solution)/shard_map/dot_general | solution.py:58
  36.9 1.3 copy.323
  38.2 4.3 %all-to-all-start.1 = ((bf16[128,4,1024]{0,2,1:T(8,128)(2,1)}), bf16[128,4,1024]{0,2,1:T(8,128)(2,1)}, u32[]{:S(2)}, u32[]{:S(2)}) async-start(bf16[128,4,1024]{0,2,1:T(8,128)(2,1)} %bitcast.5), calls=%async_computation.1 | async-start | bytes 2097152 | tf_op jit(solution)/shard_map/all_to_all | solution.py:66
  42.5 0.8 compare_convert_fusion.1
  43.5 2.9 %copy.307 = f32[4,128,16,64]{3,2,1,0:T(8,128)} copy(f32[4,128,16,64]{1,3,2,0:T(8,128)S(1)} %bitcast.181) | data formatting | bytes 4194304 | tf_op jit(solution)/shard_map/convert_element_type | solution.py:87
  46.5 1.5 convert_element_type.114
  47.9 4.0 %copy.309 = f32[4,128,16,64]{3,2,1,0:T(8,128)} copy(f32[4,128,16,64]{1,3,2,0:T(8,128)} %bitcast.183) | data formatting | bytes 4194304 | tf_op jit(solution)/shard_map/convert_element_type | solution.py:88
  51.9 3.3 %fusion = f32[4,128,16,64]{1,3,2,0:T(8,128)} fusion(f32[4,128,16,64]{1,3,2,0:T(8,128)} %bitcast.184, f32[4,128,16,64]{1,3,2,0:T(8,128)S(1)} %bitcast.182, f32[16,64]{1,0:T(8,128)S(1)} %mul.514), kind=kOutput, calls=%fused_computation | output fusion | flops 1056831 | bytes 6295552 | tf_op jit(solution)/shard_map/mul | solution.py:104
  55.3 4.2 %all-to-all-start.3 = ((bf16[128,4,1024]{0,2,1:T(8,128)(2,1)}), bf16[128,4,1024]{0,2,1:T(8,128)(2,1)S(1)}, u32[]{:S(2)}, u32[]{:S(2)}) async-start(bf16[128,4,1024]{0,2,1:T(8,128)(2,1)} %bitcast.12), calls=%async_computation.3 | async-start | bytes 2097152 | tf_op jit(solution)/shard_map/all_to_all | solution.py:65
  59.5 2.7 %convert_element_type.113 = f32[128,4,1024]{0,2,1:T(8,128)} convert(bf16[128,4,1024]{0,2,1:T(8,128)(2,1)} %all-to-all-done.1) | non-fusion elementwise | flops 524288 | bytes 3145728 | tf_op jit(solution)/shard_map/convert_element_type | solution.py:90
  62.2 4.0 %copy.305 = f32[4,128,16,64]{3,2,1,0:T(8,128)} copy(f32[4,128,16,64]{1,3,2,0:T(8,128)} %bitcast.195) | data formatting | bytes 4194304 | tf_op jit(solution)/shard_map/convert_element_type | solution.py:90
  66.2 2.5 %fusion.80 = f32[4,128,16,64]{3,2,1,0:T(8,128)S(1)} fusion(f32[4,128,16,64]{3,2,1,0:T(8,128)} %copy.305), kind=kOutput, calls=%fused_computation.159 | output fusion | flops 66584576 | bytes 4194304 | tf_op jit(solution)/shard_map/jit(cumsum)/reduce_window_sum | solution.py:91
  68.7 1.9 copy-done.2
  71.0 11.2 %exponential_multiply_fusion = (f32[4,128,16,64]{3,2,1,0:T(8,128)}, f32[4,128,16,64]{3,2,1,0:T(8,128)}, f32[4,128,16,64]{3,2,1,0:T(8,128)}, f32[4,128,16,64]{3,2,1,0:T(8,128)}) fusion(f32[4,128,16,64]{3,2,1,0:T(8,128)} %copy.309, f32[4,128,16,64]{3,2,1,0:T(8,128)} %copy-done.2, f32[4,128]{1,0:T(4,128)S(1)} %get-tuple-element.47, ...), kind=kLoop, calls=%fused_computation.16 | loop fusion | flops 4194304 | bytes 16797696 | tf_op jit(solution)/shard_map/mul | solution.py:95
  82.2 4.5 %fusion.7 = f32[4,16,64,64]{2,3,1,0:T(8,128)S(1)} fusion(bf16[4,128,16,64]{1,3,2,0:T(8,128)(2,1)S(1)} %bitcast.193, f32[4,128,16,64]{3,2,1,0:T(8,128)} %get-tuple-element.31), kind=kOutput, calls=%fused_computation.8 | convolution fusion | flops 201326592 | bytes 4194304 | tf_op jit(solution)/shard_map/cthd,cthe->chde/dot_general | solution.py:109
  86.7 1.0 multiply_add_fusion.1
  88.2 6.0 %all-gather = f32[32,65,64]{1,2,0:T(8,128)S(1)} all-gather(f32[16,65,64]{1,2,0:T(8,128)S(1)} %pad_maximum_fusion), channel_id=2, replica_groups=mesh['x'=4,'zh'=4,'zl'=2,'core'=2,'head'=4] {'core'}, dimensions={0}, use_global_device_ids=true | all-gather | bytes 798720 | tf_op jit(solution)/shard_map/all_gather | solution.py:149
  94.2 0.8 select_reduce_fusion
  95.2 8.6 %all-gather.1 = f32[16,65,64]{1,2,0:T(8,128)S(1)} all-gather(f32[8,65,64]{1,2,0:T(8,128)S(1)} %fusion.55), channel_id=3, replica_groups=mesh['x'=4,'zh'=4,'zl'=2,'core'=2,'head'=4] {'zl'}, dimensions={0}, use_global_device_ids=true | all-gather | bytes 399360 | tf_op jit(solution)/shard_map/all_gather | solution.py:154
  104.4 23.9 %all-gather.2 = f32[32,65,64]{1,2,0:T(8,128)S(1)} all-gather(f32[8,65,64]{1,2,0:T(8,128)S(1)} %pad_maximum_fusion.1), channel_id=4, replica_groups=mesh['x'=4,'zh'=4,'zl'=2,'core'=2,'head'=4] {'zh'}, dimensions={0}, use_global_device_ids=true | all-gather | bytes 665600 | tf_op jit(solution)/shard_map/all_gather | solution.py:154
  128.3 0.7 select_reduce_fusion.1
  129.3 12.4 %all-gather.3 = f32[32,65,64]{1,2,0:T(8,128)S(1)} all-gather(f32[8,65,64]{1,2,0:T(8,128)S(1)} %pad_maximum_fusion.2), channel_id=5, replica_groups=mesh['x'=4,'zh'=4,'zl'=2,'core'=2,'head'=4] {'x'}, dimensions={0}, use_global_device_ids=true | all-gather | bytes 665600 | tf_op jit(solution)/shard_map/all_gather | solution.py:154
  142.4 1.1 fusion.61
  143.5 1.1 copy.319
  144.6 8.1 %all_gather.35 = f32[16,64,64]{2,1,0:T(8,128)} all-gather(f32[8,64,64]{2,1,0:T(8,128)S(1)} %copy.319), channel_id=1, replica_groups=mesh['x'=4,'zh'=4,'zl'=2,'core'=2,'head'=4] {'core'}, dimensions={0}, use_global_device_ids=true | all-gather | bytes 393216 | tf_op jit(solution)/shard_map/all_gather | solution.py:161
  152.7 2.1 %copy.320 = f32[16,64,64]{1,2,0:T(8,128)} copy(f32[16,64,64]{2,1,0:T(8,128)} %all_gather.35) | data formatting | bytes 524288 | tf_op jit(solution)/shard_map/all_gather | solution.py:161
  154.8 10.0 %fusion.9 = f32[4,16,128,128]{3,2,1,0:T(8,128)S(1)} fusion(f32[4,128,16,64]{3,2,1,0:T(8,128)} %get-tuple-element.30, f32[4,128,16,64]{3,2,1,0:T(8,128)} %get-tuple-element.33), kind=kOutput, calls=%fused_computation.10 | convolution fusion | flops 402653184 | bytes 8388608 | tf_op jit(solution)/shard_map/cthd,cshd->chts/dot_general | solution.py:96
  165.1 0.7 copy-done.9
  165.8 4.9 %fusion.5 = f32[4,16,64,128]{3,2,1,0:T(8,128)S(1)} fusion(f32[4,128,16,64]{3,2,1,0:T(8,128)S(1)} %copy-done.3, f32[1,16,64,64]{2,3,1,0:T(8,128)S(1)} %get-tuple-element.23, f32[1,16,64,64]{2,3,1,0:T(8,128)S(1)} %get-tuple-element.24, f32[1,16,64,64]{2,3,1,0:T(8,128)S(1)} %copy-done.9, f32[4]{0:T(128)S(1)} %pad.12.clone, ...), kind=kOutput, calls=%fused_computation.6 | convolution fusion | flops 202637312 | bytes 5259280 | tf_op jit(solution)/shard_map/cthd,chde->cthe/dot_general | solution.py:168
  170.7 3.3 %fusion.79 = (f32[4,128,16]{1,2,0:T(8,128)S(1)}, f32[4,128,16,64]{1,3,2,0:T(8,128)S(1)}) fusion(f32[4,16,64,128]{3,2,1,0:T(8,128)S(1)} %fusion.5, f32[4,128,16,64]{1,3,2,0:T(8,128)S(1)} %copy-done.4, bf16[4,128,16,64]{1,3,2,0:T(8,128)(2,1)S(1)} %bitcast.194, f32[4,16,128,128]{3,2,1,0:T(8,128)S(1)} %fusion.9, pred[4,128,128]{2,1,0:T(8,128)(4,1)S(1)} %compare_and_fusion), kind=kOutput, calls=%fused_computation.158 | convolution fusion | flops 406315008 | bytes 11632640 | tf_op jit(solution)/shard_map/chts,cshd->cthd/dot_general | solution.py:102
  175.2 18.8 %all_to_all.68 = bf16[4,128,1024]{1,2,0:T(8,128)(2,1)S(1)} all-to-all(bf16[4,128,1024]{1,2,0:T(8,128)(2,1)S(1)} %bitcast.200), channel_id=1, replica_groups=mesh['x'=4,'zh'=4,'zl'=2,'core'=2,'head'=4] {'head'}, dimensions={0} | all-to-all | bytes 2097152 | tf_op jit(solution)/shard_map/all_to_all | solution.py:179
  194.2 1.9 copy.325
  196.1 3.4 %fusion.28 = bf16[128,4096]{1,0:T(8,128)(2,1)} fusion(f32[128,4096]{1,0:T(8,128)} %copy.325, bf16[128,4096]{1,0:T(8,128)(2,1)} %param.16), kind=kLoop, calls=%fused_computation.43 | loop fusion | flops 3670016 | bytes 4194304 | tf_op jit(solution)/shard_map/convert_element_type | solution.py:180
  (65 shorter events, 5.1 us)
Async XLA Ops:
  0.0 33.6 %copy-start = (bf16[128,4096]{1,0:T(8,128)(2,1)S(1)}, bf16[128,4096]{1,0:T(8,128)(2,1)}, u32[]{:S(2)}) copy-start(bf16[128,4096]{1,0:T(8,128)(2,1)} %param.22) | copy-start | bytes 3145732
  0.0 11.7 %copy-start.11 = (bf16[128,4096]{1,0:T(8,128)(2,1)S(1)}, bf16[128,4096]{1,0:T(8,128)(2,1)}, u32[]{:S(2)}) copy-start(bf16[128,4096]{1,0:T(8,128)(2,1)} %param.14) | copy-start | bytes 3145732
  2.4 18.5 %all-to-all-start = ((bf16[128,4,1024]{0,2,1:T(8,128)(2,1)}), bf16[128,4,1024]{0,2,1:T(8,128)(2,1)S(1)}, u32[]{:S(2)}, u32[]{:S(2)}) async-start(bf16[128,4,1024]{0,2,1:T(8,128)(2,1)} %bitcast.1), calls=%async_computation | async-start | bytes 2097152 | tf_op jit(solution)/shard_map/all_to_all | solution.py:63
  8.3 25.3 %collective-permute-start = (bf16[1,4096]{1,0:T(2,128)(2,1)S(1)}, bf16[1,4096]{1,0:T(2,128)(2,1)S(1)}, u32[]{:S(2)}, u32[]{:S(2)}) collective-permute-start(bf16[1,4096]{1,0:T(2,128)(2,1)S(1)} %slice.120), channel_id=1, source_target_pairs={{0,1},{1,2},{2,3},{3,4},{4,5},{5,6},{6,7},{7,8},{8,9},{9,10},{10,1... | collective-permute-start | bytes 24584 | tf_op jit(solution)/shard_map/ppermute | solution.py:18
  20.9 12.6 %copy-start.5 = (bf16[128,4,1024]{0,2,1:T(8,128)(2,1)}, bf16[128,4,1024]{0,2,1:T(8,128)(2,1)S(1)}, u32[]{:S(2)}) copy-start(bf16[128,4,1024]{0,2,1:T(8,128)(2,1)S(1)} %all-to-all-done) | copy-start | bytes 3145732
  20.9 12.6 %copy-start.12 = (f32[4096]{0:T(1024)S(1)}, f32[4096]{0:T(1024)}, u32[]{:S(2)}) copy-start(f32[4096]{0:T(1024)} %param.20) | copy-start | bytes 49156
  20.9 12.6 %copy-start.13 = (f32[4096]{0:T(1024)S(1)}, f32[4096]{0:T(1024)}, u32[]{:S(2)}) copy-start(f32[4096]{0:T(1024)} %param.19) | copy-start | bytes 49156
  20.9 17.3 %all-to-all-start.2 = ((bf16[128,4,1024]{0,2,1:T(8,128)(2,1)}), bf16[128,4,1024]{0,2,1:T(8,128)(2,1)S(1)}, u32[]{:S(2)}, u32[]{:S(2)}) async-start(bf16[128,4,1024]{0,2,1:T(8,128)(2,1)} %bitcast.201), calls=%async_computation.2 | async-start | bytes 2097152 | tf_op jit(solution)/shard_map/all_to_all | solution.py:64
  36.9 6.5 %copy-start.6 = (bf16[128,4,1024]{0,2,1:T(8,128)(2,1)S(1)}, bf16[128,4,1024]{0,2,1:T(8,128)(2,1)}, u32[]{:S(2)}) copy-start(bf16[128,4,1024]{0,2,1:T(8,128)(2,1)} %copy-done.5) | copy-start | bytes 3145732
  38.2 5.0 %copy-start.7 = (bf16[128,4,1024]{0,2,1:T(8,128)(2,1)}, bf16[128,4,1024]{0,2,1:T(8,128)(2,1)S(1)}, u32[]{:S(2)}) copy-start(bf16[128,4,1024]{0,2,1:T(8,128)(2,1)S(1)} %all-to-all-done.2) | copy-start | bytes 3145732
  38.2 17.1 %all-to-all-start.1 = ((bf16[128,4,1024]{0,2,1:T(8,128)(2,1)}), bf16[128,4,1024]{0,2,1:T(8,128)(2,1)}, u32[]{:S(2)}, u32[]{:S(2)}) async-start(bf16[128,4,1024]{0,2,1:T(8,128)(2,1)} %bitcast.5), calls=%async_computation.1 | async-start | bytes 2097152 | tf_op jit(solution)/shard_map/all_to_all | solution.py:66
  43.5 2.9 %copy-start.8 = (bf16[128,4,1024]{0,2,1:T(8,128)(2,1)S(1)}, bf16[128,4,1024]{0,2,1:T(8,128)(2,1)}, u32[]{:S(2)}) copy-start(bf16[128,4,1024]{0,2,1:T(8,128)(2,1)} %copy-done.7) | copy-start | bytes 3145732
  55.3 26.9 %all-to-all-start.3 = ((bf16[128,4,1024]{0,2,1:T(8,128)(2,1)}), bf16[128,4,1024]{0,2,1:T(8,128)(2,1)S(1)}, u32[]{:S(2)}, u32[]{:S(2)}) async-start(bf16[128,4,1024]{0,2,1:T(8,128)(2,1)} %bitcast.12), calls=%async_computation.3 | async-start | bytes 2097152 | tf_op jit(solution)/shard_map/all_to_all | solution.py:65
  68.7 2.0 copy-start.2
  154.8 10.1 %copy-start.10 = (f32[16,64,64]{1,2,0:T(8,128)S(1)}, f32[16,64,64]{1,2,0:T(8,128)}, u32[]{:S(2)}) copy-start(f32[16,64,64]{1,2,0:T(8,128)} %copy.320) | copy-start | bytes 786436
  154.8 10.3 %copy-start.3 = (f32[4,128,16,64]{3,2,1,0:T(8,128)S(1)}, f32[4,128,16,64]{3,2,1,0:T(8,128)}, u32[]{:S(2)}) copy-start(f32[4,128,16,64]{3,2,1,0:T(8,128)} %get-tuple-element.32) | copy-start | bytes 6291460
  164.8 1.0 copy-start.9
  165.8 4.9 %copy-start.4 = (f32[4,128,16,64]{1,3,2,0:T(8,128)S(1)}, f32[4,128,16,64]{1,3,2,0:T(8,128)}, u32[]{:S(2)}) copy-start(f32[4,128,16,64]{1,3,2,0:T(8,128)} %fusion) | copy-start | bytes 6291460
  194.2 5.3 %copy-start.1 = (bf16[128,4096]{1,0:T(8,128)(2,1)S(1)}, bf16[128,4096]{1,0:T(8,128)(2,1)}, u32[]{:S(2)}) copy-start(bf16[128,4096]{1,0:T(8,128)(2,1)} %param.22) | copy-start | bytes 3145732

commit v8 on v7

--- a/solution.py
+++ b/solution.py
@@ -151,7 +151,15 @@
     level_prefixes = []
     running = lax.dynamic_slice_in_dim(core_total, core_index * share, share, 0)
     for axis in ("zl", "zh", "x"):
-        prefix, running = fold(lax.all_gather(running, axis), lax.axis_index(axis))
+        position = lax.axis_index(axis)
+        if lax.axis_size(axis) == 2:
+            partner = lax.ppermute(running, axis, [(0, 1), (1, 0)])
+            gathered = jnp.where(
+                position == 0, jnp.stack([running, partner]), jnp.stack([partner, running])
+            )
+        else:
+            gathered = lax.all_gather(running, axis)
+        prefix, running = fold(gathered, position)
         level_prefixes.append(prefix)
     pair_incoming = level_prefixes[-1][:, :ATTENTION_SPAN]
     for prefix in level_prefixes[-2::-1]:

time: 201 us -> 196 us (0.975)
  blocking collectives: 77.8 us -> 69.6 us
    all_gather x3 -> x2, blocking collectives: 44.9 us -> 35.6 us  [local(): gathered = lax.all_gather(running, axis)]
    dot_general x1, matrix products: 10 us -> 6.72 us  [local(): jnp.einsum('cthd,cshd->chts', scaled_query, scaled_key, precision=highest)]
    dot_general x1, matrix products: 4.88 us -> 7.38 us  [local(): jnp.einsum('cthd,chde->cthe', scaled_query * keep_first[:, :, None, None]...]
    unnamed x30 -> x38, local copies, waits for them, and re-layouts: 6.46 us -> 5.75 us
  transfers between devices with their start and end apart: 5 -> 6, of which waited for: 1 -> 1; matrix products, arithmetic and copies ran while one was open for 25% -> 30% of each run, Pallas kernels for 0% -> 0%
where the time goes in v8:
time: 196 us; the launch traced here: 195 us
  blocking collectives  69.6 us (36%)
  other arithmetic  35.9 us (18%)
  local copies, waits for them, and re-layouts  33.2 us (17%)
  matrix products  25.1 us (13%)
  starting transfers between devices  22.3 us (11%)
  waiting for transfers between devices  6.97 us (4%)
    all_gather x2, blocking collectives, local(): gathered = lax.all_gather(running, axis)  35.6 us
    all_to_all x1, blocking collectives, local(): lax.all_to_all(normed, 'head', split_axis=0, concat_axis=1, tiled=True)  18.7 us
    mul x1, other arithmetic, local(): scaled_key = lookup_vectors * jnp.exp(-cumulative)  11.1 us
    all_gather x1, blocking collectives, local(): pair_incoming = lax.all_gather(pair_incoming, 'core', tiled=True)  9.13 us
    dot_general x1, matrix products, local(): jnp.einsum('cthd,chde->cthe', scaled_query * keep_first[:, :, None, None]...  7.38 us
    all_to_all x1, waiting for transfers between devices, local(): lax.all_to_all(acceptance_linear, 'head', split_axis=1, concat_axis=0, ti...  6.96 us
    dot_general x1, matrix products, local(): jnp.einsum('cthd,cshd->chts', scaled_query, scaled_key, precision=highest)  6.72 us
    all_gather x1, blocking collectives, local(): core_prefix, core_total = fold(lax.all_gather(own, 'core'), core_index)  6.13 us
  transfers between devices with their start and end apart: 6, of which 1 were waited for; matrix products, arithmetic and copies ran while one was open for 30% of the time, Pallas kernels for 0%

profile of v8, /device:TPU:1, one launch (start us, length us, event | category | flops | bytes accessed | tf_op | source)
XLA Modules:
  0.0 194.6 jit_solution(16628954002582598713)
XLA Ops:
  0.0 2.4 %copy.325 = bf16[128,4096]{0,1:T(8,128)(2,1)} copy(bf16[128,4096]{1,0:T(8,128)(2,1)} %param.13) | data formatting | bytes 2097152 | tf_op args[0]
  2.4 5.0 %all-to-all-start = ((bf16[128,4,1024]{0,2,1:T(8,128)(2,1)}), bf16[128,4,1024]{0,2,1:T(8,128)(2,1)S(1)}, u32[]{:S(2)}, u32[]{:S(2)}) async-start(bf16[128,4,1024]{0,2,1:T(8,128)(2,1)} %bitcast.1), calls=%async_computation | async-start | bytes 2097152 | tf_op jit(solution)/shard_map/all_to_all | solution.py:63
  7.4 0.9 slice.120
  8.3 3.4 %collective-permute-start = (bf16[1,4096]{1,0:T(2,128)(2,1)S(1)}, bf16[1,4096]{1,0:T(2,128)(2,1)S(1)}, u32[]{:S(2)}, u32[]{:S(2)}) collective-permute-start(bf16[1,4096]{1,0:T(2,128)(2,1)S(1)} %slice.120), channel_id=1, source_target_pairs={{0,1},{1,2},{2,3},{3,4},{4,5},{5,6},{6,7},{7,8},{8,9},{9,10},{10,1... | collective-permute-start | bytes 24584 | tf_op jit(solution)/shard_map/ppermute | solution.py:18
  11.7 1.3 copy.330
  13.0 0.8 dynamic-slice_bitcast_fusion
  14.0 7.0 %all-to-all-done = bf16[128,4,1024]{0,2,1:T(8,128)(2,1)S(1)} async-done(((bf16[128,4,1024]{0,2,1:T(8,128)(2,1)}), bf16[128,4,1024]{0,2,1:T(8,128)(2,1)S(1)}, u32[]{:S(2)}, u32[]{:S(2)}) %all-to-all-start) | async-done | bytes 1048608 | tf_op jit(solution)/shard_map/all_to_all | solution.py:63
  20.9 3.6 %all-to-all-start.2 = ((bf16[128,4,1024]{0,2,1:T(8,128)(2,1)}), bf16[128,4,1024]{0,2,1:T(8,128)(2,1)S(1)}, u32[]{:S(2)}, u32[]{:S(2)}) async-start(bf16[128,4,1024]{0,2,1:T(8,128)(2,1)} %bitcast.200), calls=%async_computation.2 | async-start | bytes 2097152 | tf_op jit(solution)/shard_map/all_to_all | solution.py:64
  24.8 0.8 dynamic_slice.26
  25.6 1.4 fusion.77
  28.2 0.8 add_compare_fusion
  30.2 0.7 dynamic_slice.27
  30.9 0.7 dynamic_slice.30
  31.6 0.7 dynamic_slice.31
  32.4 2.3 %copy.346 = bf16[128,4096]{0,1:T(8,128)(2,1)} copy(bf16[128,4096]{1,0:T(8,128)(2,1)} %param.15) | data formatting | bytes 2097152 | tf_op jit(solution)/shard_map/all_to_all | solution.py:65
  34.7 3.3 %fusion.4 = bf16[128,4096]{1,0:T(8,128)(2,1)S(1)} fusion(bf16[128,4096]{1,0:T(8,128)(2,1)S(1)} %copy-done, bf16[4096,128]{1,0:T(8,128)(2,1)} %param.21, bf16[128,4096]{1,0:T(8,128)(2,1)} %param.17, bf16[127,4096]{1,0:T(8,128)(2,1)} %bitcast.203, bf16[1,4096]{1,0:T(2,128)(2,1)S(1)} %collective-permute-done, f32[4096]{0:T(1024)S(1)} %copy-done.16, ...), kind=kOutput, calls=%fused_computation.5 | convolution fusion | flops 276316160 | bytes 5275776 | tf_op jit(solution)/shard_map/dot_general | solution.py:58
  38.1 1.3 copy.345
  39.4 4.3 %all-to-all-start.1 = ((bf16[128,4,1024]{0,2,1:T(8,128)(2,1)}), bf16[128,4,1024]{0,2,1:T(8,128)(2,1)}, u32[]{:S(2)}, u32[]{:S(2)}) async-start(bf16[128,4,1024]{0,2,1:T(8,128)(2,1)} %bitcast.5), calls=%async_computation.1 | async-start | bytes 2097152 | tf_op jit(solution)/shard_map/all_to_all | solution.py:66
  43.7 0.8 compare_convert_fusion.1
  44.8 3.0 %copy.329 = f32[4,128,16,64]{3,2,1,0:T(8,128)} copy(f32[4,128,16,64]{1,3,2,0:T(8,128)S(1)} %bitcast.183) | data formatting | bytes 4194304 | tf_op jit(solution)/shard_map/convert_element_type | solution.py:87
  47.7 1.5 convert_element_type.114
  49.2 4.0 %copy.331 = f32[4,128,16,64]{3,2,1,0:T(8,128)} copy(f32[4,128,16,64]{1,3,2,0:T(8,128)} %bitcast.185) | data formatting | bytes 4194304 | tf_op jit(solution)/shard_map/convert_element_type | solution.py:88
  53.2 3.3 %fusion = f32[4,128,16,64]{1,3,2,0:T(8,128)} fusion(f32[4,128,16,64]{1,3,2,0:T(8,128)} %bitcast.186, f32[4,128,16,64]{1,3,2,0:T(8,128)S(1)} %bitcast.184, f32[16,64]{1,0:T(8,128)S(1)} %mul.514), kind=kOutput, calls=%fused_computation | output fusion | flops 1056831 | bytes 6295552 | tf_op jit(solution)/shard_map/mul | solution.py:104
  56.6 4.2 %all-to-all-start.3 = ((bf16[128,4,1024]{0,2,1:T(8,128)(2,1)}), bf16[128,4,1024]{0,2,1:T(8,128)(2,1)S(1)}, u32[]{:S(2)}, u32[]{:S(2)}) async-start(bf16[128,4,1024]{0,2,1:T(8,128)(2,1)} %bitcast.12), calls=%async_computation.3 | async-start | bytes 2097152 | tf_op jit(solution)/shard_map/all_to_all | solution.py:65
  60.7 2.7 %convert_element_type.113 = f32[128,4,1024]{0,2,1:T(8,128)} convert(bf16[128,4,1024]{0,2,1:T(8,128)(2,1)} %all-to-all-done.1) | non-fusion elementwise | flops 524288 | bytes 3145728 | tf_op jit(solution)/shard_map/convert_element_type | solution.py:90
  63.5 4.0 %copy.327 = f32[4,128,16,64]{3,2,1,0:T(8,128)} copy(f32[4,128,16,64]{1,3,2,0:T(8,128)} %bitcast.197) | data formatting | bytes 4194304 | tf_op jit(solution)/shard_map/convert_element_type | solution.py:90
  67.4 2.5 %fusion.80 = f32[4,128,16,64]{3,2,1,0:T(8,128)S(1)} fusion(f32[4,128,16,64]{3,2,1,0:T(8,128)} %copy.327), kind=kOutput, calls=%fused_computation.160 | output fusion | flops 66584576 | bytes 4194304 | tf_op jit(solution)/shard_map/jit(cumsum)/reduce_window_sum | solution.py:91
  70.0 1.9 copy-done.2
  72.9 11.1 %exponential_multiply_fusion = (f32[4,128,16,64]{3,2,1,0:T(8,128)}, f32[4,128,16,64]{3,2,1,0:T(8,128)}, f32[4,128,16,64]{3,2,1,0:T(8,128)}, f32[4,128,16,64]{3,2,1,0:T(8,128)}) fusion(f32[4,128,16,64]{3,2,1,0:T(8,128)} %copy.331, f32[4,128,16,64]{3,2,1,0:T(8,128)} %copy-done.2, f32[4,128]{1,0:T(4,128)S(1)} %get-tuple-element.47, ...), kind=kLoop, calls=%fused_computation.16 | loop fusion | flops 4194304 | bytes 16797696 | tf_op jit(solution)/shard_map/mul | solution.py:95
  84.0 4.5 %fusion.7 = f32[4,16,64,64]{2,3,1,0:T(8,128)S(1)} fusion(bf16[4,128,16,64]{1,3,2,0:T(8,128)(2,1)S(1)} %bitcast.195, f32[4,128,16,64]{3,2,1,0:T(8,128)} %get-tuple-element.31), kind=kOutput, calls=%fused_computation.8 | convolution fusion | flops 201326592 | bytes 4194304 | tf_op jit(solution)/shard_map/cthd,cthe->chde/dot_general | solution.py:109
  88.5 1.0 multiply_add_fusion.1
  90.0 6.1 %all-gather = f32[32,65,64]{1,2,0:T(8,128)S(1)} all-gather(f32[16,65,64]{1,2,0:T(8,128)S(1)} %pad_maximum_fusion), channel_id=2, replica_groups=mesh['x'=4,'zh'=4,'zl'=2,'core'=2,'head'=4] {'core'}, dimensions={0}, use_global_device_ids=true | all-gather | bytes 798720 | tf_op jit(solution)/shard_map/all_gather | solution.py:149
  96.1 0.8 select_reduce_fusion
  97.2 1.9 collective-permute-start.1
  99.0 6.7 %fusion.9 = f32[4,16,128,128]{3,2,1,0:T(8,128)} fusion(f32[4,128,16,64]{3,2,1,0:T(8,128)S(1)} %copy-done.3, f32[4,128,16,64]{3,2,1,0:T(8,128)S(1)} %copy-done.4), kind=kOutput, calls=%fused_computation.10 | convolution fusion | flops 402653184 | bytes 8388608 | tf_op jit(solution)/shard_map/cthd,cshd->chts/dot_general | solution.py:96
  106.7 23.4 %all-gather.1 = f32[32,65,64]{1,2,0:T(8,128)S(1)} all-gather(f32[8,65,64]{1,2,0:T(8,128)S(1)} %pad_maximum_fusion.1), channel_id=3, replica_groups=mesh['x'=4,'zh'=4,'zl'=2,'core'=2,'head'=4] {'zh'}, dimensions={0}, use_global_device_ids=true | all-gather | bytes 665600 | tf_op jit(solution)/shard_map/all_gather | solution.py:161
  130.1 0.7 select_reduce_fusion.1
  131.1 12.2 %all-gather.2 = f32[32,65,64]{1,2,0:T(8,128)S(1)} all-gather(f32[8,65,64]{1,2,0:T(8,128)S(1)} %pad_maximum_fusion.2), channel_id=4, replica_groups=mesh['x'=4,'zh'=4,'zl'=2,'core'=2,'head'=4] {'x'}, dimensions={0}, use_global_device_ids=true | all-gather | bytes 665600 | tf_op jit(solution)/shard_map/all_gather | solution.py:161
  143.9 1.1 fusion.61
  145.1 1.1 copy.341
  146.2 9.1 %all_gather.27 = f32[16,64,64]{2,1,0:T(8,128)} all-gather(f32[8,64,64]{2,1,0:T(8,128)S(1)} %copy.341), channel_id=1, replica_groups=mesh['x'=4,'zh'=4,'zl'=2,'core'=2,'head'=4] {'core'}, dimensions={0}, use_global_device_ids=true | all-gather | bytes 393216 | tf_op jit(solution)/shard_map/all_gather | solution.py:169
  155.3 2.1 %copy.342 = f32[16,64,64]{1,2,0:T(8,128)} copy(f32[16,64,64]{2,1,0:T(8,128)} %all_gather.27) | data formatting | bytes 524288 | tf_op jit(solution)/shard_map/all_gather | solution.py:169
  157.4 1.3 select_add_fusion
  158.7 7.4 %fusion.5 = f32[4,16,64,128]{3,2,1,0:T(8,128)S(1)} fusion(f32[4,128,16,64]{3,2,1,0:T(8,128)} %get-tuple-element.32, f32[1,16,64,64]{2,3,1,0:T(8,128)S(1)} %get-tuple-element.23, f32[1,16,64,64]{2,3,1,0:T(8,128)S(1)} %get-tuple-element.24, f32[1,16,64,64]{2,3,1,0:T(8,128)S(1)} %copy-done.11, f32[4]{0:T(128)S(1)} %copy-done.14, ...), kind=kOutput, calls=%fused_computation.6 | convolution fusion | flops 202637312 | bytes 5259280 | tf_op jit(solution)/shard_map/cthd,chde->cthe/dot_general | solution.py:176
  166.2 3.2 %fusion.79 = (f32[4,128,16]{1,2,0:T(8,128)S(1)}, f32[4,128,16,64]{1,3,2,0:T(8,128)S(1)}) fusion(f32[4,16,64,128]{3,2,1,0:T(8,128)S(1)} %fusion.5, f32[4,128,16,64]{1,3,2,0:T(8,128)S(1)} %copy-done.6, bf16[4,128,16,64]{1,3,2,0:T(8,128)(2,1)S(1)} %bitcast.196, f32[4,16,128,128]{3,2,1,0:T(8,128)S(1)} %copy-done.5, pred[4,128,128]{2,1,0:T(8,128)(4,1)S(1)} %compare_and_fusion), kind=kOutput, calls=%fused_computation.159 | convolution fusion | flops 406315008 | bytes 11632640 | tf_op jit(solution)/shard_map/chts,cshd->cthd/dot_general | solution.py:102
  170.5 18.7 %all_to_all.68 = bf16[4,128,1024]{1,2,0:T(8,128)(2,1)S(1)} all-to-all(bf16[4,128,1024]{1,2,0:T(8,128)(2,1)S(1)} %bitcast.199), channel_id=1, replica_groups=mesh['x'=4,'zh'=4,'zl'=2,'core'=2,'head'=4] {'head'}, dimensions={0} | all-to-all | bytes 2097152 | tf_op jit(solution)/shard_map/all_to_all | solution.py:187
  189.4 1.9 copy.347
  191.2 3.4 %fusion.28 = bf16[128,4096]{1,0:T(8,128)(2,1)} fusion(f32[128,4096]{1,0:T(8,128)} %copy.347, bf16[128,4096]{1,0:T(8,128)(2,1)} %param.16), kind=kLoop, calls=%fused_computation.43 | loop fusion | flops 3670016 | bytes 4194304 | tf_op jit(solution)/shard_map/convert_element_type | solution.py:188
  (76 shorter events, 6.9 us)
Async XLA Ops:
  0.0 34.7 %copy-start = (bf16[128,4096]{1,0:T(8,128)(2,1)S(1)}, bf16[128,4096]{1,0:T(8,128)(2,1)}, u32[]{:S(2)}) copy-start(bf16[128,4096]{1,0:T(8,128)(2,1)} %param.22) | copy-start | bytes 3145732
  0.0 11.7 %copy-start.12 = (bf16[128,4096]{1,0:T(8,128)(2,1)S(1)}, bf16[128,4096]{1,0:T(8,128)(2,1)}, u32[]{:S(2)}) copy-start(bf16[128,4096]{1,0:T(8,128)(2,1)} %param.14) | copy-start | bytes 3145732
  2.4 18.5 %all-to-all-start = ((bf16[128,4,1024]{0,2,1:T(8,128)(2,1)}), bf16[128,4,1024]{0,2,1:T(8,128)(2,1)S(1)}, u32[]{:S(2)}, u32[]{:S(2)}) async-start(bf16[128,4,1024]{0,2,1:T(8,128)(2,1)} %bitcast.1), calls=%async_computation | async-start | bytes 2097152 | tf_op jit(solution)/shard_map/all_to_all | solution.py:63
  8.3 26.4 %collective-permute-start = (bf16[1,4096]{1,0:T(2,128)(2,1)S(1)}, bf16[1,4096]{1,0:T(2,128)(2,1)S(1)}, u32[]{:S(2)}, u32[]{:S(2)}) collective-permute-start(bf16[1,4096]{1,0:T(2,128)(2,1)S(1)} %slice.120), channel_id=1, source_target_pairs={{0,1},{1,2},{2,3},{3,4},{4,5},{5,6},{6,7},{7,8},{8,9},{9,10},{10,1... | collective-permute-start | bytes 24584 | tf_op jit(solution)/shard_map/ppermute | solution.py:18
  20.9 13.8 %copy-start.7 = (bf16[128,4,1024]{0,2,1:T(8,128)(2,1)}, bf16[128,4,1024]{0,2,1:T(8,128)(2,1)S(1)}, u32[]{:S(2)}) copy-start(bf16[128,4,1024]{0,2,1:T(8,128)(2,1)S(1)} %all-to-all-done) | copy-start | bytes 3145732
  20.9 13.8 %copy-start.16 = (f32[4096]{0:T(1024)S(1)}, f32[4096]{0:T(1024)}, u32[]{:S(2)}) copy-start(f32[4096]{0:T(1024)} %param.20) | copy-start | bytes 49156
  20.9 13.8 %copy-start.17 = (f32[4096]{0:T(1024)S(1)}, f32[4096]{0:T(1024)}, u32[]{:S(2)}) copy-start(f32[4096]{0:T(1024)} %param.19) | copy-start | bytes 49156
  20.9 18.5 %all-to-all-start.2 = ((bf16[128,4,1024]{0,2,1:T(8,128)(2,1)}), bf16[128,4,1024]{0,2,1:T(8,128)(2,1)S(1)}, u32[]{:S(2)}, u32[]{:S(2)}) async-start(bf16[128,4,1024]{0,2,1:T(8,128)(2,1)} %bitcast.200), calls=%async_computation.2 | async-start | bytes 2097152 | tf_op jit(solution)/shard_map/all_to_all | solution.py:64
  38.1 6.5 %copy-start.8 = (bf16[128,4,1024]{0,2,1:T(8,128)(2,1)S(1)}, bf16[128,4,1024]{0,2,1:T(8,128)(2,1)}, u32[]{:S(2)}) copy-start(bf16[128,4,1024]{0,2,1:T(8,128)(2,1)} %copy-done.7) | copy-start | bytes 3145732
  39.4 5.0 %copy-start.9 = (bf16[128,4,1024]{0,2,1:T(8,128)(2,1)}, bf16[128,4,1024]{0,2,1:T(8,128)(2,1)S(1)}, u32[]{:S(2)}) copy-start(bf16[128,4,1024]{0,2,1:T(8,128)(2,1)S(1)} %all-to-all-done.2) | copy-start | bytes 3145732
  39.4 17.2 %all-to-all-start.1 = ((bf16[128,4,1024]{0,2,1:T(8,128)(2,1)}), bf16[128,4,1024]{0,2,1:T(8,128)(2,1)}, u32[]{:S(2)}, u32[]{:S(2)}) async-start(bf16[128,4,1024]{0,2,1:T(8,128)(2,1)} %bitcast.5), calls=%async_computation.1 | async-start | bytes 2097152 | tf_op jit(solution)/shard_map/all_to_all | solution.py:66
  44.7 3.0 %copy-start.10 = (bf16[128,4,1024]{0,2,1:T(8,128)(2,1)S(1)}, bf16[128,4,1024]{0,2,1:T(8,128)(2,1)}, u32[]{:S(2)}) copy-start(bf16[128,4,1024]{0,2,1:T(8,128)(2,1)} %copy-done.9) | copy-start | bytes 3145732
  56.6 27.4 %all-to-all-start.3 = ((bf16[128,4,1024]{0,2,1:T(8,128)(2,1)}), bf16[128,4,1024]{0,2,1:T(8,128)(2,1)S(1)}, u32[]{:S(2)}, u32[]{:S(2)}) async-start(bf16[128,4,1024]{0,2,1:T(8,128)(2,1)} %bitcast.12), calls=%async_computation.3 | async-start | bytes 2097152 | tf_op jit(solution)/shard_map/all_to_all | solution.py:65
  70.0 2.0 %copy-start.2 = (f32[4,128,16,64]{3,2,1,0:T(8,128)}, f32[4,128,16,64]{3,2,1,0:T(8,128)S(1)}, u32[]{:S(2)}) copy-start(f32[4,128,16,64]{3,2,1,0:T(8,128)S(1)} %fusion.80) | copy-start | bytes 6291460
  89.5 9.5 %copy-start.4 = (f32[4,128,16,64]{3,2,1,0:T(8,128)S(1)}, f32[4,128,16,64]{3,2,1,0:T(8,128)}, u32[]{:S(2)}) copy-start(f32[4,128,16,64]{3,2,1,0:T(8,128)} %get-tuple-element.33) | copy-start | bytes 6291460
  96.1 2.9 %copy-start.3 = (f32[4,128,16,64]{3,2,1,0:T(8,128)S(1)}, f32[4,128,16,64]{3,2,1,0:T(8,128)}, u32[]{:S(2)}) copy-start(f32[4,128,16,64]{3,2,1,0:T(8,128)} %get-tuple-element.30) | copy-start | bytes 6291460
  97.2 8.8 %collective-permute-start.1 = (f32[8,65,64]{1,2,0:T(8,128)S(1)}, f32[8,65,64]{1,2,0:T(8,128)S(1)}, u32[]{:S(2)}, u32[]{:S(2)}) collective-permute-start(f32[8,65,64]{1,2,0:T(8,128)S(1)} %fusion.55), channel_id=1, source_target_pairs={{0,8},{8,0},{1,9},{9,1},{2,10},{10,2},{3,11},{11,3},{4,12},{12,4},... | collective-permute-start | bytes 399368 | tf_op jit(solution)/shard_map/ppermute | solution.py:156
  99.0 6.7 %copy-start.13 = (f32[1,16,64]{2,1,0:T(8,128)S(1)}, f32[1,16,64]{2,1,0:T(8,128)}, u32[]{:S(2)}) copy-start(f32[1,16,64]{2,1,0:T(8,128)} %get-tuple-element.43) | copy-start | bytes 12292
  99.0 6.7 %copy-start.15 = (f32[4]{0:T(128)S(1)}, f32[4]{0:T(128)}, u32[]{:S(2)}) copy-start(f32[4]{0:T(128)} %pad.12.clone) | copy-start | bytes 52
  146.1 12.6 %copy-start.14 = (f32[4]{0:T(128)S(1)}, f32[4]{0:T(128)}, u32[]{:S(2)}) copy-start(f32[4]{0:T(128)} %pad.16.clone) | copy-start | bytes 52
  157.4 1.3 copy-start.11
  158.7 7.4 %copy-start.5 = (f32[4,16,128,128]{3,2,1,0:T(8,128)S(1)}, f32[4,16,128,128]{3,2,1,0:T(8,128)}, u32[]{:S(2)}) copy-start(f32[4,16,128,128]{3,2,1,0:T(8,128)} %fusion.9) | copy-start | bytes 12582916
  158.7 7.4 %copy-start.6 = (f32[4,128,16,64]{1,3,2,0:T(8,128)S(1)}, f32[4,128,16,64]{1,3,2,0:T(8,128)}, u32[]{:S(2)}) copy-start(f32[4,128,16,64]{1,3,2,0:T(8,128)} %fusion) | copy-start | bytes 6291460
  189.3 5.3 %copy-start.1 = (bf16[128,4096]{1,0:T(8,128)(2,1)S(1)}, bf16[128,4096]{1,0:T(8,128)(2,1)}, u32[]{:S(2)}) copy-start(bf16[128,4096]{1,0:T(8,128)(2,1)} %param.22) | copy-start | bytes 3145732

commit v9 on v8

--- a/solution.py
+++ b/solution.py
@@ -152,13 +152,19 @@
     running = lax.dynamic_slice_in_dim(core_total, core_index * share, share, 0)
     for axis in ("zl", "zh", "x"):
         position = lax.axis_index(axis)
-        if lax.axis_size(axis) == 2:
-            partner = lax.ppermute(running, axis, [(0, 1), (1, 0)])
+        count = lax.axis_size(axis)
+        gathered = running[None]
+        distance = 1
+        while distance < count:
+            partner = lax.ppermute(
+                gathered, axis, [(i, i ^ distance) for i in range(count)]
+            )
             gathered = jnp.where(
-                position == 0, jnp.stack([running, partner]), jnp.stack([partner, running])
+                (position // distance) % 2 == 0,
+                jnp.concatenate([gathered, partner]),
+                jnp.concatenate([partner, gathered]),
             )
-        else:
-            gathered = lax.all_gather(running, axis)
+            distance *= 2
         prefix, running = fold(gathered, position)
         level_prefixes.append(prefix)
     pair_incoming = level_prefixes[-1][:, :ATTENTION_SPAN]

time: 196 us -> 216 us (1.10)
  waiting for transfers between devices: 6.97 us -> 54.9 us
  blocking collectives: 69.6 us -> 30.3 us
  starting transfers between devices: 22.3 us -> 35.3 us
    ppermute x1 -> x5, waiting for transfers between devices: 0.01 us -> 48 us  [local(): lax.ppermute(gathered, axis, [(i, i ^ distance) for i in range(count)])]
    all_gather x2 -> x0, blocking collectives: 35.6 us -> none  [local(): gathered = lax.all_gather(running, axis)]
    ppermute x1 -> x5, starting transfers between devices: 1.85 us -> 14.8 us  [local(): lax.ppermute(gathered, axis, [(i, i ^ distance) for i in range(count)])]
    all_gather x1, blocking collectives: 9.13 us -> 5.57 us  [local(): pair_incoming = lax.all_gather(pair_incoming, 'core', tiled=True)]
    unnamed x38 -> x32, local copies, waits for them, and re-layouts: 5.75 us -> 5.74 us
  transfers between devices with their start and end apart: 6 -> 10, of which waited for: 1 -> 5; matrix products, arithmetic and copies ran while one was open for 30% -> 26% of each run, Pallas kernels for 0% -> 0%
where the time goes in v9:
time: 216 us; the launch traced here: 215 us
  waiting for transfers between devices  54.9 us (25%)
  other arithmetic  35.4 us (16%)
  starting transfers between devices  35.3 us (16%)
  local copies, waits for them, and re-layouts  32 us (15%)
  blocking collectives  30.3 us (14%)
  matrix products  25 us (12%)
    ppermute x5, waiting for transfers between devices, local(): lax.ppermute(gathered, axis, [(i, i ^ distance) for i in range(count)])  48 us
    all_to_all x1, blocking collectives, local(): lax.all_to_all(normed, 'head', split_axis=0, concat_axis=1, tiled=True)  18.6 us
    ppermute x5, starting transfers between devices, local(): lax.ppermute(gathered, axis, [(i, i ^ distance) for i in range(count)])  14.8 us
    mul x1, other arithmetic, local(): scaled_key = lookup_vectors * jnp.exp(-cumulative)  11.2 us
    dot_general x1, matrix products, local(): jnp.einsum('cthd,chde->cthe', scaled_query * keep_first[:, :, None, None]...  7.38 us
    all_to_all x1, waiting for transfers between devices, local(): lax.all_to_all(acceptance_linear, 'head', split_axis=1, concat_axis=0, ti...  6.96 us
    dot_general x1, matrix products, local(): jnp.einsum('cthd,cshd->chts', scaled_query, scaled_key, precision=highest)  6.64 us
    all_gather x1, blocking collectives, local(): core_prefix, core_total = fold(lax.all_gather(own, 'core'), core_index)  6.13 us
  transfers between devices with their start and end apart: 10, of which 5 were waited for; matrix products, arithmetic and copies ran while one was open for 26% of the time, Pallas kernels for 0%

profile of v9, /device:TPU:1, one launch (start us, length us, event | category | flops | bytes accessed | tf_op | source)
XLA Modules:
  0.0 214.5 jit_solution(13817043356772029324)
XLA Ops:
  0.0 2.4 %copy.334 = bf16[128,4096]{0,1:T(8,128)(2,1)} copy(bf16[128,4096]{1,0:T(8,128)(2,1)} %param.13) | data formatting | bytes 2097152 | tf_op args[0]
  2.4 5.0 %all-to-all-start = ((bf16[128,4,1024]{0,2,1:T(8,128)(2,1)}), bf16[128,4,1024]{0,2,1:T(8,128)(2,1)S(1)}, u32[]{:S(2)}, u32[]{:S(2)}) async-start(bf16[128,4,1024]{0,2,1:T(8,128)(2,1)} %bitcast.1), calls=%async_computation | async-start | bytes 2097152 | tf_op jit(solution)/shard_map/all_to_all | solution.py:63
  7.4 0.9 slice.120
  8.3 3.4 %collective-permute-start = (bf16[1,4096]{1,0:T(2,128)(2,1)S(1)}, bf16[1,4096]{1,0:T(2,128)(2,1)S(1)}, u32[]{:S(2)}, u32[]{:S(2)}) collective-permute-start(bf16[1,4096]{1,0:T(2,128)(2,1)S(1)} %slice.120), channel_id=1, source_target_pairs={{0,1},{1,2},{2,3},{3,4},{4,5},{5,6},{6,7},{7,8},{8,9},{9,10},{10,1... | collective-permute-start | bytes 24584 | tf_op jit(solution)/shard_map/ppermute | solution.py:18
  11.7 1.3 copy.339
  14.0 7.0 %all-to-all-done = bf16[128,4,1024]{0,2,1:T(8,128)(2,1)S(1)} async-done(((bf16[128,4,1024]{0,2,1:T(8,128)(2,1)}), bf16[128,4,1024]{0,2,1:T(8,128)(2,1)S(1)}, u32[]{:S(2)}, u32[]{:S(2)}) %all-to-all-start) | async-done | bytes 1048608 | tf_op jit(solution)/shard_map/all_to_all | solution.py:63
  20.9 3.6 %all-to-all-start.2 = ((bf16[128,4,1024]{0,2,1:T(8,128)(2,1)}), bf16[128,4,1024]{0,2,1:T(8,128)(2,1)S(1)}, u32[]{:S(2)}, u32[]{:S(2)}) async-start(bf16[128,4,1024]{0,2,1:T(8,128)(2,1)} %bitcast.196), calls=%async_computation.2 | async-start | bytes 2097152 | tf_op jit(solution)/shard_map/all_to_all | solution.py:64
  24.8 0.8 dynamic_slice.26
  25.6 1.4 fusion.78
  31.3 2.3 %copy.355 = bf16[128,4096]{0,1:T(8,128)(2,1)} copy(bf16[128,4096]{1,0:T(8,128)(2,1)} %param.15) | data formatting | bytes 2097152 | tf_op jit(solution)/shard_map/all_to_all | solution.py:65
  33.7 3.3 %fusion.4 = bf16[128,4096]{1,0:T(8,128)(2,1)S(1)} fusion(bf16[128,4096]{1,0:T(8,128)(2,1)S(1)} %copy-done, bf16[4096,128]{1,0:T(8,128)(2,1)} %param.21, bf16[128,4096]{1,0:T(8,128)(2,1)} %param.17, bf16[127,4096]{1,0:T(8,128)(2,1)} %bitcast.198, bf16[1,4096]{1,0:T(2,128)(2,1)S(1)} %collective-permute-done, f32[4096]{0:T(1024)S(1)} %copy-done.13, ...), kind=kOutput, calls=%fused_computation.5 | convolution fusion | flops 276316160 | bytes 5275776 | tf_op jit(solution)/shard_map/dot_general | solution.py:58
  37.0 1.3 copy.354
  38.3 4.3 %all-to-all-start.1 = ((bf16[128,4,1024]{0,2,1:T(8,128)(2,1)}), bf16[128,4,1024]{0,2,1:T(8,128)(2,1)}, u32[]{:S(2)}, u32[]{:S(2)}) async-start(bf16[128,4,1024]{0,2,1:T(8,128)(2,1)} %bitcast.5), calls=%async_computation.1 | async-start | bytes 2097152 | tf_op jit(solution)/shard_map/all_to_all | solution.py:66
  42.6 0.8 compare_convert_fusion.1
  43.6 2.9 %copy.338 = f32[4,128,16,64]{3,2,1,0:T(8,128)} copy(f32[4,128,16,64]{1,3,2,0:T(8,128)S(1)} %bitcast.184) | data formatting | bytes 4194304 | tf_op jit(solution)/shard_map/convert_element_type | solution.py:87
  46.6 1.5 convert_element_type.114
  48.0 4.0 %copy.340 = f32[4,128,16,64]{3,2,1,0:T(8,128)} copy(f32[4,128,16,64]{1,3,2,0:T(8,128)} %bitcast.186) | data formatting | bytes 4194304 | tf_op jit(solution)/shard_map/convert_element_type | solution.py:88
  52.0 3.3 %fusion = f32[4,128,16,64]{1,3,2,0:T(8,128)} fusion(f32[4,128,16,64]{1,3,2,0:T(8,128)} %bitcast.187, f32[4,128,16,64]{1,3,2,0:T(8,128)S(1)} %bitcast.185, f32[16,64]{1,0:T(8,128)S(1)} %mul.514), kind=kOutput, calls=%fused_computation | output fusion | flops 1056831 | bytes 6295552 | tf_op jit(solution)/shard_map/mul | solution.py:104
  55.4 4.2 %all-to-all-start.3 = ((bf16[128,4,1024]{0,2,1:T(8,128)(2,1)}), bf16[128,4,1024]{0,2,1:T(8,128)(2,1)S(1)}, u32[]{:S(2)}, u32[]{:S(2)}) async-start(bf16[128,4,1024]{0,2,1:T(8,128)(2,1)} %bitcast.12), calls=%async_computation.3 | async-start | bytes 2097152 | tf_op jit(solution)/shard_map/all_to_all | solution.py:65
  59.6 2.7 %convert_element_type.113 = f32[128,4,1024]{0,2,1:T(8,128)} convert(bf16[128,4,1024]{0,2,1:T(8,128)(2,1)} %all-to-all-done.1) | non-fusion elementwise | flops 524288 | bytes 3145728 | tf_op jit(solution)/shard_map/convert_element_type | solution.py:90
  62.3 4.0 %copy.336 = f32[4,128,16,64]{3,2,1,0:T(8,128)} copy(f32[4,128,16,64]{1,3,2,0:T(8,128)} %bitcast.193) | data formatting | bytes 4194304 | tf_op jit(solution)/shard_map/convert_element_type | solution.py:90
  66.3 2.5 %fusion.81 = f32[4,128,16,64]{3,2,1,0:T(8,128)S(1)} fusion(f32[4,128,16,64]{3,2,1,0:T(8,128)} %copy.336), kind=kOutput, calls=%fused_computation.165 | output fusion | flops 66584576 | bytes 4194304 | tf_op jit(solution)/shard_map/jit(cumsum)/reduce_window_sum | solution.py:91
  68.8 1.9 copy-done.2
  71.1 11.2 %exponential_multiply_fusion = (f32[4,128,16,64]{3,2,1,0:T(8,128)}, f32[4,128,16,64]{3,2,1,0:T(8,128)}, f32[4,128,16,64]{3,2,1,0:T(8,128)}, f32[4,128,16,64]{3,2,1,0:T(8,128)}) fusion(f32[4,128,16,64]{3,2,1,0:T(8,128)} %copy.340, f32[4,128,16,64]{3,2,1,0:T(8,128)} %copy-done.2, f32[4,128]{1,0:T(4,128)S(1)} %get-tuple-element.47, ...), kind=kLoop, calls=%fused_computation.16 | loop fusion | flops 4194304 | bytes 16797696 | tf_op jit(solution)/shard_map/mul | solution.py:95
  82.3 4.5 %fusion.7 = f32[4,16,64,64]{2,3,1,0:T(8,128)S(1)} fusion(bf16[4,128,16,64]{1,3,2,0:T(8,128)(2,1)S(1)} %bitcast.191, f32[4,128,16,64]{3,2,1,0:T(8,128)} %get-tuple-element.31), kind=kOutput, calls=%fused_computation.8 | convolution fusion | flops 201326592 | bytes 4194304 | tf_op jit(solution)/shard_map/cthd,cthe->chde/dot_general | solution.py:109
  87.3 6.1 %all-gather = f32[32,65,64]{1,2,0:T(8,128)S(1)} all-gather(f32[16,65,64]{1,2,0:T(8,128)S(1)} %pad_maximum_fusion), channel_id=2, replica_groups=mesh['x'=4,'zh'=4,'zl'=2,'core'=2,'head'=4] {'core'}, dimensions={0}, use_global_device_ids=true | all-gather | bytes 798720 | tf_op jit(solution)/shard_map/all_gather | solution.py:149
  93.4 0.8 select_reduce_fusion
  94.5 1.8 collective-permute-start.1
  96.3 6.6 %fusion.9 = f32[4,16,128,128]{3,2,1,0:T(8,128)} fusion(f32[4,128,16,64]{3,2,1,0:T(8,128)S(1)} %copy-done.3, f32[4,128,16,64]{3,2,1,0:T(8,128)S(1)} %copy-done.4), kind=kOutput, calls=%fused_computation.10 | convolution fusion | flops 402653184 | bytes 8388608 | tf_op jit(solution)/shard_map/cthd,cshd->chts/dot_general | solution.py:96
  103.7 3.1 %collective-permute-start.2 = (f32[1,8,65,64]{2,3,1,0:T(8,128)S(1)}, f32[1,8,65,64]{2,3,1,0:T(8,128)S(1)}, u32[]{:S(2)}, u32[]{:S(2)}) collective-permute-start(f32[1,8,65,64]{2,3,1,0:T(8,128)S(1)} %maximum_bitcast_fusion), channel_id=1, source_target_pairs={{0,16},{16,0},{32,48},{48,32},{1,17},{17,1},{33,49},{49,33},{2,18}... | collective-permute-start | bytes 399368 | tf_op jit(solution)/shard_map/ppermute | solution.py:159
  106.8 11.7 %collective-permute-done.2 = f32[1,8,65,64]{2,3,1,0:T(8,128)S(1)} collective-permute-done((f32[1,8,65,64]{2,3,1,0:T(8,128)S(1)}, f32[1,8,65,64]{2,3,1,0:T(8,128)S(1)}, u32[]{:S(2)}, u32[]{:S(2)}) %collective-permute-start.2) | collective-permute-done | bytes 133152 | tf_op jit(solution)/shard_map/ppermute | solution.py:159
  118.6 5.8 %collective-permute-start.3 = (f32[2,8,65,64]{2,3,1,0:T(8,128)S(1)}, f32[2,8,65,64]{2,3,1,0:T(8,128)S(1)}, u32[]{:S(2)}, u32[]{:S(2)}) collective-permute-start(f32[2,8,65,64]{2,3,1,0:T(8,128)S(1)} %maximum_select_fusion.6), channel_id=1, source_target_pairs={{0,32},{16,48},{32,0},{48,16},{1,33},{17,49},{33,1},{49,17},{2,34}... | collective-permute-start | bytes 798728 | tf_op jit(solution)/shard_map/ppermute | solution.py:159
  124.3 1.0 multiply_add_fusion.1
  125.3 21.6 %collective-permute-done.3 = f32[2,8,65,64]{2,3,1,0:T(8,128)S(1)} collective-permute-done((f32[2,8,65,64]{2,3,1,0:T(8,128)S(1)}, f32[2,8,65,64]{2,3,1,0:T(8,128)S(1)}, u32[]{:S(2)}, u32[]{:S(2)}) %collective-permute-start.3) | collective-permute-done | bytes 266272 | tf_op jit(solution)/shard_map/ppermute | solution.py:159
  148.0 1.3 collective-permute-start.4
  149.3 5.0 %collective-permute-done.4 = f32[1,8,65,64]{2,3,1,0:T(8,128)S(1)} collective-permute-done((f32[1,8,65,64]{2,3,1,0:T(8,128)S(1)}, f32[1,8,65,64]{2,3,1,0:T(8,128)S(1)}, u32[]{:S(2)}, u32[]{:S(2)}) %collective-permute-start.4) | collective-permute-done | bytes 133152 | tf_op jit(solution)/shard_map/ppermute | solution.py:159
  154.3 2.8 %collective-permute-start.5 = (f32[2,8,65,64]{2,3,1,0:T(8,128)S(1)}, f32[2,8,65,64]{2,3,1,0:T(8,128)S(1)}, u32[]{:S(2)}, u32[]{:S(2)}) collective-permute-start(f32[2,8,65,64]{2,3,1,0:T(8,128)S(1)} %maximum_select_fusion.7), channel_id=1, source_target_pairs={{0,128},{64,192},{128,0},{192,64},{1,129},{65,193},{129,1},{193,65... | collective-permute-start | bytes 798728 | tf_op jit(solution)/shard_map/ppermute | solution.py:159
  157.1 9.7 %collective-permute-done.5 = f32[2,8,65,64]{2,3,1,0:T(8,128)S(1)} collective-permute-done((f32[2,8,65,64]{2,3,1,0:T(8,128)S(1)}, f32[2,8,65,64]{2,3,1,0:T(8,128)S(1)}, u32[]{:S(2)}, u32[]{:S(2)}) %collective-permute-start.5) | collective-permute-done | bytes 266272 | tf_op jit(solution)/shard_map/ppermute | solution.py:159
  167.5 1.2 fusion.62
  168.7 1.1 copy.350
  169.8 5.6 %all_gather.11 = f32[16,64,64]{2,1,0:T(8,128)} all-gather(f32[8,64,64]{2,1,0:T(8,128)S(1)} %copy.350), channel_id=1, replica_groups=mesh['x'=4,'zh'=4,'zl'=2,'core'=2,'head'=4] {'core'}, dimensions={0}, use_global_device_ids=true | all-gather | bytes 393216 | tf_op jit(solution)/shard_map/all_gather | solution.py:175
  175.4 2.1 copy.351
  177.5 1.3 select_add_fusion
  178.8 7.4 %fusion.5 = f32[4,16,64,128]{3,2,1,0:T(8,128)S(1)} fusion(f32[4,128,16,64]{3,2,1,0:T(8,128)} %get-tuple-element.32, f32[1,16,64,64]{2,3,1,0:T(8,128)S(1)} %get-tuple-element.23, f32[1,16,64,64]{2,3,1,0:T(8,128)S(1)} %get-tuple-element.24, f32[1,16,64,64]{2,3,1,0:T(8,128)S(1)} %copy-done.11, f32[4]{0:T(128)S(1)} %pad.32.clone, ...), kind=kOutput, calls=%fused_computation.6 | convolution fusion | flops 202637312 | bytes 5259280 | tf_op jit(solution)/shard_map/cthd,chde->cthe/dot_general | solution.py:182
  186.2 3.2 %fusion.80 = (f32[4,128,16]{1,2,0:T(8,128)S(1)}, f32[4,128,16,64]{1,3,2,0:T(8,128)S(1)}) fusion(f32[4,16,64,128]{3,2,1,0:T(8,128)S(1)} %fusion.5, f32[4,128,16,64]{1,3,2,0:T(8,128)S(1)} %copy-done.6, bf16[4,128,16,64]{1,3,2,0:T(8,128)(2,1)S(1)} %bitcast.192, f32[4,16,128,128]{3,2,1,0:T(8,128)S(1)} %copy-done.5, pred[4,128,128]{2,1,0:T(8,128)(4,1)S(1)} %compare_and_fusion), kind=kOutput, calls=%fused_computation.164 | convolution fusion | flops 406315008 | bytes 11632640 | tf_op jit(solution)/shard_map/chts,cshd->cthd/dot_general | solution.py:102
  190.5 18.6 %all_to_all.68 = bf16[4,128,1024]{1,2,0:T(8,128)(2,1)S(1)} all-to-all(bf16[4,128,1024]{1,2,0:T(8,128)(2,1)S(1)} %bitcast.195), channel_id=1, replica_groups=mesh['x'=4,'zh'=4,'zl'=2,'core'=2,'head'=4] {'head'}, dimensions={0} | all-to-all | bytes 2097152 | tf_op jit(solution)/shard_map/all_to_all | solution.py:193
  209.3 1.9 copy.356
  211.1 3.4 %fusion.28 = bf16[128,4096]{1,0:T(8,128)(2,1)} fusion(f32[128,4096]{1,0:T(8,128)} %copy.356, bf16[128,4096]{1,0:T(8,128)(2,1)} %param.16), kind=kLoop, calls=%fused_computation.43 | loop fusion | flops 3670016 | bytes 4194304 | tf_op jit(solution)/shard_map/convert_element_type | solution.py:194
  (79 shorter events, 9.5 us)
Async XLA Ops:
  0.0 33.6 %copy-start = (bf16[128,4096]{1,0:T(8,128)(2,1)S(1)}, bf16[128,4096]{1,0:T(8,128)(2,1)}, u32[]{:S(2)}) copy-start(bf16[128,4096]{1,0:T(8,128)(2,1)} %param.22) | copy-start | bytes 3145732
  0.0 11.7 %copy-start.12 = (bf16[128,4096]{1,0:T(8,128)(2,1)S(1)}, bf16[128,4096]{1,0:T(8,128)(2,1)}, u32[]{:S(2)}) copy-start(bf16[128,4096]{1,0:T(8,128)(2,1)} %param.14) | copy-start | bytes 3145732
  2.4 18.5 %all-to-all-start = ((bf16[128,4,1024]{0,2,1:T(8,128)(2,1)}), bf16[128,4,1024]{0,2,1:T(8,128)(2,1)S(1)}, u32[]{:S(2)}, u32[]{:S(2)}) async-start(bf16[128,4,1024]{0,2,1:T(8,128)(2,1)} %bitcast.1), calls=%async_computation | async-start | bytes 2097152 | tf_op jit(solution)/shard_map/all_to_all | solution.py:63
  8.3 25.3 %collective-permute-start = (bf16[1,4096]{1,0:T(2,128)(2,1)S(1)}, bf16[1,4096]{1,0:T(2,128)(2,1)S(1)}, u32[]{:S(2)}, u32[]{:S(2)}) collective-permute-start(bf16[1,4096]{1,0:T(2,128)(2,1)S(1)} %slice.120), channel_id=1, source_target_pairs={{0,1},{1,2},{2,3},{3,4},{4,5},{5,6},{6,7},{7,8},{8,9},{9,10},{10,1... | collective-permute-start | bytes 24584 | tf_op jit(solution)/shard_map/ppermute | solution.py:18
  20.9 12.7 %copy-start.7 = (bf16[128,4,1024]{0,2,1:T(8,128)(2,1)}, bf16[128,4,1024]{0,2,1:T(8,128)(2,1)S(1)}, u32[]{:S(2)}) copy-start(bf16[128,4,1024]{0,2,1:T(8,128)(2,1)S(1)} %all-to-all-done) | copy-start | bytes 3145732
  20.9 12.7 %copy-start.13 = (f32[4096]{0:T(1024)S(1)}, f32[4096]{0:T(1024)}, u32[]{:S(2)}) copy-start(f32[4096]{0:T(1024)} %param.20) | copy-start | bytes 49156
  20.9 12.7 %copy-start.14 = (f32[4096]{0:T(1024)S(1)}, f32[4096]{0:T(1024)}, u32[]{:S(2)}) copy-start(f32[4096]{0:T(1024)} %param.19) | copy-start | bytes 49156
  20.9 17.4 %all-to-all-start.2 = ((bf16[128,4,1024]{0,2,1:T(8,128)(2,1)}), bf16[128,4,1024]{0,2,1:T(8,128)(2,1)S(1)}, u32[]{:S(2)}, u32[]{:S(2)}) async-start(bf16[128,4,1024]{0,2,1:T(8,128)(2,1)} %bitcast.196), calls=%async_computation.2 | async-start | bytes 2097152 | tf_op jit(solution)/shard_map/all_to_all | solution.py:64
  37.0 6.5 %copy-start.8 = (bf16[128,4,1024]{0,2,1:T(8,128)(2,1)S(1)}, bf16[128,4,1024]{0,2,1:T(8,128)(2,1)}, u32[]{:S(2)}) copy-start(bf16[128,4,1024]{0,2,1:T(8,128)(2,1)} %copy-done.7) | copy-start | bytes 3145732
  38.3 5.0 %copy-start.9 = (bf16[128,4,1024]{0,2,1:T(8,128)(2,1)}, bf16[128,4,1024]{0,2,1:T(8,128)(2,1)S(1)}, u32[]{:S(2)}) copy-start(bf16[128,4,1024]{0,2,1:T(8,128)(2,1)S(1)} %all-to-all-done.2) | copy-start | bytes 3145732
  38.3 17.1 %all-to-all-start.1 = ((bf16[128,4,1024]{0,2,1:T(8,128)(2,1)}), bf16[128,4,1024]{0,2,1:T(8,128)(2,1)}, u32[]{:S(2)}, u32[]{:S(2)}) async-start(bf16[128,4,1024]{0,2,1:T(8,128)(2,1)} %bitcast.5), calls=%async_computation.1 | async-start | bytes 2097152 | tf_op jit(solution)/shard_map/all_to_all | solution.py:66
  43.6 2.9 %copy-start.10 = (bf16[128,4,1024]{0,2,1:T(8,128)(2,1)S(1)}, bf16[128,4,1024]{0,2,1:T(8,128)(2,1)}, u32[]{:S(2)}) copy-start(bf16[128,4,1024]{0,2,1:T(8,128)(2,1)} %copy-done.9) | copy-start | bytes 3145732
  55.4 26.9 %all-to-all-start.3 = ((bf16[128,4,1024]{0,2,1:T(8,128)(2,1)}), bf16[128,4,1024]{0,2,1:T(8,128)(2,1)S(1)}, u32[]{:S(2)}, u32[]{:S(2)}) async-start(bf16[128,4,1024]{0,2,1:T(8,128)(2,1)} %bitcast.12), calls=%async_computation.3 | async-start | bytes 2097152 | tf_op jit(solution)/shard_map/all_to_all | solution.py:65
  68.8 2.0 copy-start.2
  86.8 9.5 %copy-start.4 = (f32[4,128,16,64]{3,2,1,0:T(8,128)S(1)}, f32[4,128,16,64]{3,2,1,0:T(8,128)}, u32[]{:S(2)}) copy-start(f32[4,128,16,64]{3,2,1,0:T(8,128)} %get-tuple-element.33) | copy-start | bytes 6291460
  93.4 2.9 %copy-start.3 = (f32[4,128,16,64]{3,2,1,0:T(8,128)S(1)}, f32[4,128,16,64]{3,2,1,0:T(8,128)}, u32[]{:S(2)}) copy-start(f32[4,128,16,64]{3,2,1,0:T(8,128)} %get-tuple-element.30) | copy-start | bytes 6291460
  94.5 8.5 %collective-permute-start.1 = (f32[1,8,65,64]{2,3,1,0:T(8,128)S(1)}, f32[1,8,65,64]{2,3,1,0:T(8,128)S(1)}, u32[]{:S(2)}, u32[]{:S(2)}) collective-permute-start(f32[1,8,65,64]{2,3,1,0:T(8,128)S(1)} %fusion.56), channel_id=1, source_target_pairs={{0,8},{8,0},{1,9},{9,1},{2,10},{10,2},{3,11},{11,3},{4,12},{12,4},... | collective-permute-start | bytes 399368 | tf_op jit(solution)/shard_map/ppermute | solution.py:159
  103.7 14.9 %collective-permute-start.2 = (f32[1,8,65,64]{2,3,1,0:T(8,128)S(1)}, f32[1,8,65,64]{2,3,1,0:T(8,128)S(1)}, u32[]{:S(2)}, u32[]{:S(2)}) collective-permute-start(f32[1,8,65,64]{2,3,1,0:T(8,128)S(1)} %maximum_bitcast_fusion), channel_id=1, source_target_pairs={{0,16},{16,0},{32,48},{48,32},{1,17},{17,1},{33,49},{49,33},{2,18}... | collective-permute-start | bytes 399368 | tf_op jit(solution)/shard_map/ppermute | solution.py:159
  118.6 28.3 %collective-permute-start.3 = (f32[2,8,65,64]{2,3,1,0:T(8,128)S(1)}, f32[2,8,65,64]{2,3,1,0:T(8,128)S(1)}, u32[]{:S(2)}, u32[]{:S(2)}) collective-permute-start(f32[2,8,65,64]{2,3,1,0:T(8,128)S(1)} %maximum_select_fusion.6), channel_id=1, source_target_pairs={{0,32},{16,48},{32,0},{48,16},{1,33},{17,49},{33,1},{49,17},{2,34}... | collective-permute-start | bytes 798728 | tf_op jit(solution)/shard_map/ppermute | solution.py:159
  148.0 6.2 %collective-permute-start.4 = (f32[1,8,65,64]{2,3,1,0:T(8,128)S(1)}, f32[1,8,65,64]{2,3,1,0:T(8,128)S(1)}, u32[]{:S(2)}, u32[]{:S(2)}) collective-permute-start(f32[1,8,65,64]{2,3,1,0:T(8,128)S(1)} %maximum_bitcast_fusion.1), channel_id=1, source_target_pairs={{0,64},{64,0},{128,192},{192,128},{1,65},{65,1},{129,193},{193,129... | collective-permute-start | bytes 399368 | tf_op jit(solution)/shard_map/ppermute | solution.py:159
  154.3 12.5 %collective-permute-start.5 = (f32[2,8,65,64]{2,3,1,0:T(8,128)S(1)}, f32[2,8,65,64]{2,3,1,0:T(8,128)S(1)}, u32[]{:S(2)}, u32[]{:S(2)}) collective-permute-start(f32[2,8,65,64]{2,3,1,0:T(8,128)S(1)} %maximum_select_fusion.7), channel_id=1, source_target_pairs={{0,128},{64,192},{128,0},{192,64},{1,129},{65,193},{129,1},{193,65... | collective-permute-start | bytes 798728 | tf_op jit(solution)/shard_map/ppermute | solution.py:159
  177.5 1.3 copy-start.11
  178.8 7.4 %copy-start.5 = (f32[4,16,128,128]{3,2,1,0:T(8,128)S(1)}, f32[4,16,128,128]{3,2,1,0:T(8,128)}, u32[]{:S(2)}) copy-start(f32[4,16,128,128]{3,2,1,0:T(8,128)} %fusion.9) | copy-start | bytes 12582916
  178.8 7.4 %copy-start.6 = (f32[4,128,16,64]{1,3,2,0:T(8,128)S(1)}, f32[4,128,16,64]{1,3,2,0:T(8,128)}, u32[]{:S(2)}) copy-start(f32[4,128,16,64]{1,3,2,0:T(8,128)} %fusion) | copy-start | bytes 6291460
  209.3 5.3 %copy-start.1 = (bf16[128,4096]{1,0:T(8,128)(2,1)S(1)}, bf16[128,4096]{1,0:T(8,128)(2,1)}, u32[]{:S(2)}) copy-start(bf16[128,4096]{1,0:T(8,128)(2,1)} %param.22) | copy-start | bytes 3145732

commit v10 on v8

--- a/solution.py
+++ b/solution.py
@@ -179,7 +179,8 @@
         start_state,
         precision=highest,
     )
-    mixing = within + diagonal_contribution + carried
+    local_part = lax.optimization_barrier(within + diagonal_contribution)
+    mixing = local_part + carried
     center = mixing - jnp.mean(mixing, axis=3, keepdims=True)
     spread = jnp.mean(center * center, axis=3, keepdims=True)
     normed = center * lax.rsqrt(spread + norm_eps) * gain_local + bias_local

time: 196 us -> 194 us (0.990)
  local copies, waits for them, and re-layouts: 33.2 us -> 31.2 us
    unnamed x38 -> x36, local copies, waits for them, and re-layouts: 5.75 us -> 5.86 us
  transfers between devices with their start and end apart: 6 -> 6, of which waited for: 1 -> 1; matrix products, arithmetic and copies ran while one was open for 30% -> 31% of each run, Pallas kernels for 0% -> 0%
where the time goes in v10:
time: 194 us; the launch traced here: 193 us
  blocking collectives  69.5 us (36%)
  other arithmetic  35 us (18%)
  local copies, waits for them, and re-layouts  31.2 us (16%)
  matrix products  26.4 us (14%)
  starting transfers between devices  22.3 us (11%)
  waiting for transfers between devices  6.97 us (4%)
    all_gather x2, blocking collectives, local(): gathered = lax.all_gather(running, axis)  36 us
    all_to_all x1, blocking collectives, local(): lax.all_to_all(normed, 'head', split_axis=0, concat_axis=1, tiled=True)  19.8 us
    mul x1, other arithmetic, local(): lookup_vectors * jnp.exp(ending[:, None] - cumulative)  11.2 us
    all_gather x1, blocking collectives, local(): pair_incoming = lax.all_gather(pair_incoming, 'core', tiled=True)  7.58 us
    dot_general x1, matrix products, local(): jnp.einsum('cthd,chde->cthe', scaled_query * keep_first[:, :, None, None]...  7.56 us
    all_to_all x1, waiting for transfers between devices, local(): lax.all_to_all(acceptance_linear, 'head', split_axis=1, concat_axis=0, ti...  6.96 us
    dot_general x1, matrix products, local(): jnp.einsum('cthd,cshd->chts', scaled_query, scaled_key, precision=highest)  6.67 us
    all_gather x1, blocking collectives, local(): core_prefix, core_total = fold(lax.all_gather(own, 'core'), core_index)  6.13 us
  transfers between devices with their start and end apart: 6, of which 1 were waited for; matrix products, arithmetic and copies ran while one was open for 31% of the time, Pallas kernels for 0%

profile of v10, /device:TPU:1, one launch (start us, length us, event | category | flops | bytes accessed | tf_op | source)
XLA Modules:
  0.0 193.1 jit_solution(8255153285274162272)
XLA Ops:
  0.0 2.4 %copy.325 = bf16[128,4096]{0,1:T(8,128)(2,1)} copy(bf16[128,4096]{1,0:T(8,128)(2,1)} %param.13) | data formatting | bytes 2097152 | tf_op args[0]
  2.4 5.0 %all-to-all-start = ((bf16[128,4,1024]{0,2,1:T(8,128)(2,1)}), bf16[128,4,1024]{0,2,1:T(8,128)(2,1)S(1)}, u32[]{:S(2)}, u32[]{:S(2)}) async-start(bf16[128,4,1024]{0,2,1:T(8,128)(2,1)} %bitcast.1), calls=%async_computation | async-start | bytes 2097152 | tf_op jit(solution)/shard_map/all_to_all | solution.py:63
  7.4 0.9 slice.120
  8.3 3.4 %collective-permute-start = (bf16[1,4096]{1,0:T(2,128)(2,1)S(1)}, bf16[1,4096]{1,0:T(2,128)(2,1)S(1)}, u32[]{:S(2)}, u32[]{:S(2)}) collective-permute-start(bf16[1,4096]{1,0:T(2,128)(2,1)S(1)} %slice.120), channel_id=1, source_target_pairs={{0,1},{1,2},{2,3},{3,4},{4,5},{5,6},{6,7},{7,8},{8,9},{9,10},{10,1... | collective-permute-start | bytes 24584 | tf_op jit(solution)/shard_map/ppermute | solution.py:18
  11.7 1.3 copy.330
  13.0 0.8 dynamic-slice_bitcast_fusion
  14.0 7.0 %all-to-all-done = bf16[128,4,1024]{0,2,1:T(8,128)(2,1)S(1)} async-done(((bf16[128,4,1024]{0,2,1:T(8,128)(2,1)}), bf16[128,4,1024]{0,2,1:T(8,128)(2,1)S(1)}, u32[]{:S(2)}, u32[]{:S(2)}) %all-to-all-start) | async-done | bytes 1048608 | tf_op jit(solution)/shard_map/all_to_all | solution.py:63
  20.9 3.6 %all-to-all-start.2 = ((bf16[128,4,1024]{0,2,1:T(8,128)(2,1)}), bf16[128,4,1024]{0,2,1:T(8,128)(2,1)S(1)}, u32[]{:S(2)}, u32[]{:S(2)}) async-start(bf16[128,4,1024]{0,2,1:T(8,128)(2,1)} %bitcast.198), calls=%async_computation.2 | async-start | bytes 2097152 | tf_op jit(solution)/shard_map/all_to_all | solution.py:64
  24.8 0.8 dynamic_slice.26
  25.6 1.4 fusion.79
  28.3 0.8 add_compare_fusion
  29.1 0.7 dynamic_slice.27
  29.9 0.7 dynamic_slice.30
  30.6 0.7 dynamic_slice.31
  31.4 2.3 %copy.346 = bf16[128,4096]{0,1:T(8,128)(2,1)} copy(bf16[128,4096]{1,0:T(8,128)(2,1)} %param.15) | data formatting | bytes 2097152 | tf_op jit(solution)/shard_map/all_to_all | solution.py:65
  33.7 3.3 %fusion.4 = bf16[128,4096]{1,0:T(8,128)(2,1)S(1)} fusion(bf16[128,4096]{1,0:T(8,128)(2,1)S(1)} %copy-done, bf16[4096,128]{1,0:T(8,128)(2,1)} %param.21, bf16[128,4096]{1,0:T(8,128)(2,1)} %param.17, bf16[127,4096]{1,0:T(8,128)(2,1)} %bitcast.201, bf16[1,4096]{1,0:T(2,128)(2,1)S(1)} %collective-permute-done, f32[4096]{0:T(1024)S(1)} %copy-done.15, ...), kind=kOutput, calls=%fused_computation.5 | convolution fusion | flops 276316160 | bytes 5275776 | tf_op jit(solution)/shard_map/dot_general | solution.py:58
  37.0 1.3 copy.345
  38.3 4.3 %all-to-all-start.1 = ((bf16[128,4,1024]{0,2,1:T(8,128)(2,1)}), bf16[128,4,1024]{0,2,1:T(8,128)(2,1)}, u32[]{:S(2)}, u32[]{:S(2)}) async-start(bf16[128,4,1024]{0,2,1:T(8,128)(2,1)} %bitcast.5), calls=%async_computation.1 | async-start | bytes 2097152 | tf_op jit(solution)/shard_map/all_to_all | solution.py:66
  42.6 0.8 compare_convert_fusion.1
  43.7 3.0 %copy.329 = f32[4,128,16,64]{3,2,1,0:T(8,128)} copy(f32[4,128,16,64]{1,3,2,0:T(8,128)S(1)} %bitcast.181) | data formatting | bytes 4194304 | tf_op jit(solution)/shard_map/convert_element_type | solution.py:87
  46.6 1.5 convert_element_type.114
  48.1 4.0 %copy.331 = f32[4,128,16,64]{3,2,1,0:T(8,128)} copy(f32[4,128,16,64]{1,3,2,0:T(8,128)} %bitcast.183) | data formatting | bytes 4194304 | tf_op jit(solution)/shard_map/convert_element_type | solution.py:88
  52.1 3.4 %fusion = f32[4,128,16,64]{1,3,2,0:T(8,128)} fusion(f32[4,128,16,64]{1,3,2,0:T(8,128)} %bitcast.184, f32[4,128,16,64]{1,3,2,0:T(8,128)S(1)} %bitcast.182, f32[16,64]{1,0:T(8,128)S(1)} %mul.514), kind=kOutput, calls=%fused_computation | output fusion | flops 1056831 | bytes 6295552 | tf_op jit(solution)/shard_map/mul | solution.py:104
  55.5 4.2 %all-to-all-start.3 = ((bf16[128,4,1024]{0,2,1:T(8,128)(2,1)}), bf16[128,4,1024]{0,2,1:T(8,128)(2,1)S(1)}, u32[]{:S(2)}, u32[]{:S(2)}) async-start(bf16[128,4,1024]{0,2,1:T(8,128)(2,1)} %bitcast.12), calls=%async_computation.3 | async-start | bytes 2097152 | tf_op jit(solution)/shard_map/all_to_all | solution.py:65
  59.7 2.7 %convert_element_type.113 = f32[128,4,1024]{0,2,1:T(8,128)} convert(bf16[128,4,1024]{0,2,1:T(8,128)(2,1)} %all-to-all-done.1) | non-fusion elementwise | flops 524288 | bytes 3145728 | tf_op jit(solution)/shard_map/convert_element_type | solution.py:90
  62.4 4.0 %copy.327 = f32[4,128,16,64]{3,2,1,0:T(8,128)} copy(f32[4,128,16,64]{1,3,2,0:T(8,128)} %bitcast.195) | data formatting | bytes 4194304 | tf_op jit(solution)/shard_map/convert_element_type | solution.py:90
  66.4 2.5 %fusion.82 = f32[4,128,16,64]{3,2,1,0:T(8,128)S(1)} fusion(f32[4,128,16,64]{3,2,1,0:T(8,128)} %copy.327), kind=kOutput, calls=%fused_computation.160 | output fusion | flops 66584576 | bytes 4194304 | tf_op jit(solution)/shard_map/jit(cumsum)/reduce_window_sum | solution.py:91
  68.9 1.9 %copy-done.2 = f32[4,128,16,64]{3,2,1,0:T(8,128)} copy-done((f32[4,128,16,64]{3,2,1,0:T(8,128)}, f32[4,128,16,64]{3,2,1,0:T(8,128)S(1)}, u32[]{:S(2)}) %copy-start.2) | copy-done | bytes 2097176
  71.2 11.2 %multiply_multiply_fusion = (f32[4,128,16,64]{3,2,1,0:T(8,128)}, f32[4,128,16,64]{3,2,1,0:T(8,128)}, f32[4,128,16,64]{3,2,1,0:T(8,128)}, f32[4,128,16,64]{3,2,1,0:T(8,128)}) fusion(f32[4,128,16,64]{3,2,1,0:T(8,128)} %copy.331, f32[4,128,16,64]{3,2,1,0:T(8,128)} %copy-done.2, f32[4,128]{1,0:T(4,128)S(1)} %get-tuple-element.47, ...), kind=kLoop, calls=%fused_computation.13 | loop fusion | flops 4194304 | bytes 16797696 | tf_op jit(solution)/shard_map/mul | solution.py:108
  82.4 4.5 %fusion.7 = f32[4,16,64,64]{2,3,1,0:T(8,128)S(1)} fusion(bf16[4,128,16,64]{1,3,2,0:T(8,128)(2,1)S(1)} %bitcast.191, f32[4,128,16,64]{3,2,1,0:T(8,128)} %get-tuple-element.30), kind=kOutput, calls=%fused_computation.8 | convolution fusion | flops 201326592 | bytes 4194304 | tf_op jit(solution)/shard_map/cthd,cthe->chde/dot_general | solution.py:109
  86.9 1.3 multiply_add_fusion.1
  88.7 6.1 %all-gather = f32[32,65,64]{1,2,0:T(8,128)S(1)} all-gather(f32[16,65,64]{1,2,0:T(8,128)S(1)} %pad_maximum_fusion), channel_id=2, replica_groups=mesh['x'=4,'zh'=4,'zl'=2,'core'=2,'head'=4] {'core'}, dimensions={0}, use_global_device_ids=true | all-gather | bytes 798720 | tf_op jit(solution)/shard_map/all_gather | solution.py:149
  94.8 0.8 select_reduce_fusion
  95.9 1.8 collective-permute-start.1
  97.7 6.7 %fusion.9 = f32[4,16,128,128]{3,2,1,0:T(8,128)S(1)} fusion(f32[4,128,16,64]{3,2,1,0:T(8,128)S(1)} %copy-done.3, f32[4,128,16,64]{3,2,1,0:T(8,128)S(1)} %copy-done.4), kind=kOutput, calls=%fused_computation.10 | convolution fusion | flops 402653184 | bytes 8388608 | tf_op jit(solution)/shard_map/cthd,cshd->chts/dot_general | solution.py:96
  104.4 4.4 %bitcast_add_fusion.1 = f32[4,128,16,64]{1,3,2,0:T(8,128)} fusion(f32[4,128,16,64]{1,3,2,0:T(8,128)S(1)} %copy-done.5, bf16[4,128,16,64]{1,3,2,0:T(8,128)(2,1)S(1)} %bitcast.192, f32[4,16,128,128]{3,2,1,0:T(8,128)S(1)} %fusion.9, pred[4,128,128]{2,1,0:T(8,128)(4,1)S(1)} %compare_and_fusion), kind=kOutput, calls=%fused_computation.35 | convolution fusion | flops 405274624 | bytes 9502720 | tf_op jit(solution)/shard_map/chts,cshd->cthd/dot_general | solution.py:102
  109.8 24.1 %all-gather.1 = f32[32,65,64]{1,2,0:T(8,128)S(1)} all-gather(f32[8,65,64]{1,2,0:T(8,128)S(1)} %pad_maximum_fusion.1), channel_id=3, replica_groups=mesh['x'=4,'zh'=4,'zl'=2,'core'=2,'head'=4] {'zh'}, dimensions={0}, use_global_device_ids=true | all-gather | bytes 665600 | tf_op jit(solution)/shard_map/all_gather | solution.py:161
  133.9 0.7 select_reduce_fusion.1
  134.9 11.9 %all-gather.2 = f32[32,65,64]{1,2,0:T(8,128)S(1)} all-gather(f32[8,65,64]{1,2,0:T(8,128)S(1)} %pad_maximum_fusion.2), channel_id=4, replica_groups=mesh['x'=4,'zh'=4,'zl'=2,'core'=2,'head'=4] {'x'}, dimensions={0}, use_global_device_ids=true | all-gather | bytes 665600 | tf_op jit(solution)/shard_map/all_gather | solution.py:161
  146.7 0.6 slice_reduce_fusion.3
  148.0 7.6 %all_gather.27 = f32[16,64,64]{2,1,0:T(8,128)} all-gather(f32[8,64,64]{2,1,0:T(8,128)S(1)} %copy.341), channel_id=1, replica_groups=mesh['x'=4,'zh'=4,'zl'=2,'core'=2,'head'=4] {'core'}, dimensions={0}, use_global_device_ids=true | all-gather | bytes 393216 | tf_op jit(solution)/shard_map/all_gather | solution.py:169
  155.6 2.1 %copy.342 = f32[16,64,64]{1,2,0:T(8,128)} copy(f32[16,64,64]{2,1,0:T(8,128)} %all_gather.27) | data formatting | bytes 524288 | tf_op jit(solution)/shard_map/all_gather | solution.py:169
  157.6 1.4 select_add_fusion
  159.1 7.6 %fusion.81 = (f32[4,128,16]{1,2,0:T(8,128)S(1)}, f32[4,128,16,64]{1,3,2,0:T(8,128)S(1)}) fusion(f32[4,128,16,64]{1,3,2,0:T(8,128)S(1)} %copy-done.6, f32[4,128,16,64]{3,2,1,0:T(8,128)} %get-tuple-element.32, f32[1,16,64,64]{2,3,1,0:T(8,128)S(1)} %copy-done.11, f32[1,16,64,64]{2,3,1,0:T(8,128)S(1)} %copy-done.12, f32[1,16,64,64]{2,3,1,0:T(8,128)S(1)} %copy-done.13, ...), kind=kOutput, calls=%fused_computation.159 | convolution fusion | flops 203677696 | bytes 7389200 | tf_op jit(solution)/shard_map/cthd,chde->cthe/dot_general | solution.py:176
  167.2 0.6 add_convert_fusion
  167.8 19.8 %all_to_all.68 = bf16[4,128,1024]{1,2,0:T(8,128)(2,1)S(1)} all-to-all(bf16[4,128,1024]{1,2,0:T(8,128)(2,1)S(1)} %bitcast.197), channel_id=1, replica_groups=mesh['x'=4,'zh'=4,'zl'=2,'core'=2,'head'=4] {'head'}, dimensions={0} | all-to-all | bytes 2097152 | tf_op jit(solution)/shard_map/all_to_all | solution.py:188
  187.8 1.9 copy.347
  189.7 3.4 %fusion.28 = bf16[128,4096]{1,0:T(8,128)(2,1)} fusion(f32[128,4096]{1,0:T(8,128)} %copy.347, bf16[128,4096]{1,0:T(8,128)(2,1)} %param.16), kind=kLoop, calls=%fused_computation.43 | loop fusion | flops 3670016 | bytes 4194304 | tf_op jit(solution)/shard_map/convert_element_type | solution.py:189
  (74 shorter events, 4.5 us)
Async XLA Ops:
  0.0 33.7 %copy-start = (bf16[128,4096]{1,0:T(8,128)(2,1)S(1)}, bf16[128,4096]{1,0:T(8,128)(2,1)}, u32[]{:S(2)}) copy-start(bf16[128,4096]{1,0:T(8,128)(2,1)} %param.22) | copy-start | bytes 3145732
  0.0 11.7 %copy-start.14 = (bf16[128,4096]{1,0:T(8,128)(2,1)S(1)}, bf16[128,4096]{1,0:T(8,128)(2,1)}, u32[]{:S(2)}) copy-start(bf16[128,4096]{1,0:T(8,128)(2,1)} %param.14) | copy-start | bytes 3145732
  2.4 18.5 %all-to-all-start = ((bf16[128,4,1024]{0,2,1:T(8,128)(2,1)}), bf16[128,4,1024]{0,2,1:T(8,128)(2,1)S(1)}, u32[]{:S(2)}, u32[]{:S(2)}) async-start(bf16[128,4,1024]{0,2,1:T(8,128)(2,1)} %bitcast.1), calls=%async_computation | async-start | bytes 2097152 | tf_op jit(solution)/shard_map/all_to_all | solution.py:63
  8.3 25.4 %collective-permute-start = (bf16[1,4096]{1,0:T(2,128)(2,1)S(1)}, bf16[1,4096]{1,0:T(2,128)(2,1)S(1)}, u32[]{:S(2)}, u32[]{:S(2)}) collective-permute-start(bf16[1,4096]{1,0:T(2,128)(2,1)S(1)} %slice.120), channel_id=1, source_target_pairs={{0,1},{1,2},{2,3},{3,4},{4,5},{5,6},{6,7},{7,8},{8,9},{9,10},{10,1... | collective-permute-start | bytes 24584 | tf_op jit(solution)/shard_map/ppermute | solution.py:18
  20.9 12.7 %copy-start.7 = (bf16[128,4,1024]{0,2,1:T(8,128)(2,1)}, bf16[128,4,1024]{0,2,1:T(8,128)(2,1)S(1)}, u32[]{:S(2)}) copy-start(bf16[128,4,1024]{0,2,1:T(8,128)(2,1)S(1)} %all-to-all-done) | copy-start | bytes 3145732
  20.9 12.7 %copy-start.15 = (f32[4096]{0:T(1024)S(1)}, f32[4096]{0:T(1024)}, u32[]{:S(2)}) copy-start(f32[4096]{0:T(1024)} %param.20) | copy-start | bytes 49156
  20.9 12.8 %copy-start.16 = (f32[4096]{0:T(1024)S(1)}, f32[4096]{0:T(1024)}, u32[]{:S(2)}) copy-start(f32[4096]{0:T(1024)} %param.19) | copy-start | bytes 49156
  20.9 17.4 %all-to-all-start.2 = ((bf16[128,4,1024]{0,2,1:T(8,128)(2,1)}), bf16[128,4,1024]{0,2,1:T(8,128)(2,1)S(1)}, u32[]{:S(2)}, u32[]{:S(2)}) async-start(bf16[128,4,1024]{0,2,1:T(8,128)(2,1)} %bitcast.198), calls=%async_computation.2 | async-start | bytes 2097152 | tf_op jit(solution)/shard_map/all_to_all | solution.py:64
  37.0 6.5 %copy-start.8 = (bf16[128,4,1024]{0,2,1:T(8,128)(2,1)S(1)}, bf16[128,4,1024]{0,2,1:T(8,128)(2,1)}, u32[]{:S(2)}) copy-start(bf16[128,4,1024]{0,2,1:T(8,128)(2,1)} %copy-done.7) | copy-start | bytes 3145732
  38.3 5.0 %copy-start.9 = (bf16[128,4,1024]{0,2,1:T(8,128)(2,1)}, bf16[128,4,1024]{0,2,1:T(8,128)(2,1)S(1)}, u32[]{:S(2)}) copy-start(bf16[128,4,1024]{0,2,1:T(8,128)(2,1)S(1)} %all-to-all-done.2) | copy-start | bytes 3145732
  38.3 17.2 %all-to-all-start.1 = ((bf16[128,4,1024]{0,2,1:T(8,128)(2,1)}), bf16[128,4,1024]{0,2,1:T(8,128)(2,1)}, u32[]{:S(2)}, u32[]{:S(2)}) async-start(bf16[128,4,1024]{0,2,1:T(8,128)(2,1)} %bitcast.5), calls=%async_computation.1 | async-start | bytes 2097152 | tf_op jit(solution)/shard_map/all_to_all | solution.py:66
  43.7 3.0 %copy-start.10 = (bf16[128,4,1024]{0,2,1:T(8,128)(2,1)S(1)}, bf16[128,4,1024]{0,2,1:T(8,128)(2,1)}, u32[]{:S(2)}) copy-start(bf16[128,4,1024]{0,2,1:T(8,128)(2,1)} %copy-done.9) | copy-start | bytes 3145732
  55.5 26.9 %all-to-all-start.3 = ((bf16[128,4,1024]{0,2,1:T(8,128)(2,1)}), bf16[128,4,1024]{0,2,1:T(8,128)(2,1)S(1)}, u32[]{:S(2)}, u32[]{:S(2)}) async-start(bf16[128,4,1024]{0,2,1:T(8,128)(2,1)} %bitcast.12), calls=%async_computation.3 | async-start | bytes 2097152 | tf_op jit(solution)/shard_map/all_to_all | solution.py:65
  68.9 2.0 %copy-start.2 = (f32[4,128,16,64]{3,2,1,0:T(8,128)}, f32[4,128,16,64]{3,2,1,0:T(8,128)S(1)}, u32[]{:S(2)}) copy-start(f32[4,128,16,64]{3,2,1,0:T(8,128)S(1)} %fusion.82) | copy-start | bytes 6291460
  88.2 9.5 %copy-start.4 = (f32[4,128,16,64]{3,2,1,0:T(8,128)S(1)}, f32[4,128,16,64]{3,2,1,0:T(8,128)}, u32[]{:S(2)}) copy-start(f32[4,128,16,64]{3,2,1,0:T(8,128)} %get-tuple-element.33) | copy-start | bytes 6291460
  94.8 2.9 %copy-start.3 = (f32[4,128,16,64]{3,2,1,0:T(8,128)S(1)}, f32[4,128,16,64]{3,2,1,0:T(8,128)}, u32[]{:S(2)}) copy-start(f32[4,128,16,64]{3,2,1,0:T(8,128)} %get-tuple-element.31) | copy-start | bytes 6291460
  95.9 13.2 %collective-permute-start.1 = (f32[8,65,64]{1,2,0:T(8,128)S(1)}, f32[8,65,64]{1,2,0:T(8,128)S(1)}, u32[]{:S(2)}, u32[]{:S(2)}) collective-permute-start(f32[8,65,64]{1,2,0:T(8,128)S(1)} %fusion.57), channel_id=1, source_target_pairs={{0,8},{8,0},{1,9},{9,1},{2,10},{10,2},{3,11},{11,3},{4,12},{12,4},... | collective-permute-start | bytes 399368 | tf_op jit(solution)/shard_map/ppermute | solution.py:156
  97.7 6.7 %copy-start.5 = (f32[4,128,16,64]{1,3,2,0:T(8,128)S(1)}, f32[4,128,16,64]{1,3,2,0:T(8,128)}, u32[]{:S(2)}) copy-start(f32[4,128,16,64]{1,3,2,0:T(8,128)} %fusion) | copy-start | bytes 6291460
  148.0 11.0 %copy-start.6 = (f32[4,128,16,64]{1,3,2,0:T(8,128)S(1)}, f32[4,128,16,64]{1,3,2,0:T(8,128)}, u32[]{:S(2)}) copy-start(f32[4,128,16,64]{1,3,2,0:T(8,128)} %bitcast_add_fusion.1) | copy-start | bytes 6291460
  157.6 1.4 copy-start.11
  157.6 1.4 copy-start.12
  157.6 1.5 copy-start.13
  187.8 5.3 %copy-start.1 = (bf16[128,4096]{1,0:T(8,128)(2,1)S(1)}, bf16[128,4096]{1,0:T(8,128)(2,1)}, u32[]{:S(2)}) copy-start(bf16[128,4096]{1,0:T(8,128)(2,1)} %param.22) | copy-start | bytes 3145732

commit v11 on v10

--- a/solution.py
+++ b/solution.py
@@ -173,19 +173,25 @@
     )
     start_state = local_start + decay_before[:, :, :, None] * incoming[None]
     keep_first = (seg_block == stretch_prior[:, None]).astype(jnp.float32)
-    carried = jnp.einsum(
-        "cthd,chde->cthe",
-        scaled_query * keep_first[:, :, None, None],
-        start_state,
-        precision=highest,
-    )
     local_part = lax.optimization_barrier(within + diagonal_contribution)
-    mixing = local_part + carried
-    center = mixing - jnp.mean(mixing, axis=3, keepdims=True)
-    spread = jnp.mean(center * center, axis=3, keepdims=True)
-    normed = center * lax.rsqrt(spread + norm_eps) * gain_local + bias_local
-    normed = normed.astype(jnp.bfloat16).reshape(tokens, partition_extent)
-    returned = lax.all_to_all(normed, "head", split_axis=0, concat_axis=1, tiled=True)
+    half = local_heads // 2
+    pieces = []
+    for low in (0, half):
+        heads = slice(low, low + half)
+        carried = jnp.einsum(
+            "cthd,chde->cthe",
+            scaled_query[:, :, heads] * keep_first[:, :, None, None],
+            start_state[:, heads],
+            precision=highest,
+        )
+        mixing = local_part[:, :, heads] + carried
+        center = mixing - jnp.mean(mixing, axis=3, keepdims=True)
+        spread = jnp.mean(center * center, axis=3, keepdims=True)
+        normed = center * lax.rsqrt(spread + norm_eps) * gain_local[heads] + bias_local[heads]
+        normed = normed.astype(jnp.bfloat16).reshape(tokens, half * ATTENTION_SPAN)
+        piece = lax.all_to_all(normed, "head", split_axis=0, concat_axis=1, tiled=True)
+        pieces.append(piece.reshape(row_count, head_count, half * ATTENTION_SPAN))
+    returned = jnp.concatenate(pieces, axis=2).reshape(layer_entries.shape)
     return (returned.astype(jnp.float32) * jax.nn.silu(valve_linear.astype(jnp.float32))).astype(
         jnp.bfloat16
     )

time: 194 us -> 206 us (1.062)
  waiting for transfers between devices: 6.97 us -> 23.6 us
  blocking collectives: 69.5 us -> 60.4 us
  starting transfers between devices: 22.3 us -> 27.7 us
    all_to_all x1, blocking collectives: 19.8 us -> 10.2 us  [local(): lax.all_to_all(normed, 'head', split_axis=0, concat_axis=1, tiled=True)]
    all_to_all x0 -> x1, waiting for transfers between devices: none -> 8.42 us  [local(): lax.all_to_all(normed, 'head', split_axis=0, concat_axis=1, tiled=True)]
    all_to_all x0 -> x1, starting transfers between devices: none -> 4.96 us  [local(): lax.all_to_all(normed, 'head', split_axis=0, concat_axis=1, tiled=True)]
    all_to_all x1, waiting for transfers between devices: 0.01 us -> 4.21 us  [local(): lax.all_to_all(lookup_linear, 'head', split_axis=1, concat_axis=0, tiled=...]
    all_to_all x1, waiting for transfers between devices: 6.96 us -> 9.34 us  [local(): lax.all_to_all(acceptance_linear, 'head', split_axis=1, concat_axis=0, ti...]
    dot_general x1 -> x2, matrix products: 7.56 us -> 5.91 us  [local(): jnp.einsum('cthd,chde->cthe', scaled_query[:, :, heads] * keep_first[:, :...]
    unnamed x36 -> x38, local copies, waits for them, and re-layouts: 5.86 us -> 5.72 us
    mul x1 -> x2, other arithmetic: 11.2 us -> 11.1 us  [the longest x1 8.8 us: local(): scaled_key = lookup_vectors * jnp.exp(-cumulative)]
  transfers between devices with their start and end apart: 6 -> 7, of which waited for: 1 -> 4; matrix products, arithmetic and copies ran while one was open for 31% -> 30% of each run, Pallas kernels for 0% -> 0%
where the time goes in v11:
time: 206 us; the launch traced here: 204 us
  blocking collectives  60.4 us (29%)
  other arithmetic  35.8 us (17%)
  local copies, waits for them, and re-layouts  29.9 us (15%)
  starting transfers between devices  27.7 us (13%)
  matrix products  24.8 us (12%)
  waiting for transfers between devices  23.6 us (11%)
    all_gather x2, blocking collectives, local(): gathered = lax.all_gather(running, axis)  35.8 us
    all_to_all x1, blocking collectives, local(): lax.all_to_all(normed, 'head', split_axis=0, concat_axis=1, tiled=True)  10.2 us
    all_to_all x1, waiting for transfers between devices, local(): lax.all_to_all(acceptance_linear, 'head', split_axis=1, concat_axis=0, ti...  9.34 us
    all_gather x1, blocking collectives, local(): pair_incoming = lax.all_gather(pair_incoming, 'core', tiled=True)  9.33 us
    mul x1, other arithmetic, local(): scaled_key = lookup_vectors * jnp.exp(-cumulative)  8.8 us
    all_to_all x1, waiting for transfers between devices, local(): lax.all_to_all(normed, 'head', split_axis=0, concat_axis=1, tiled=True)  8.42 us
    dot_general x1, matrix products, local(): jnp.einsum('cthd,cshd->chts', scaled_query, scaled_key, precision=highest)  6.64 us
    dot_general x2, matrix products, local(): jnp.einsum('cthd,chde->cthe', scaled_query[:, :, heads] * keep_first[:, :...  5.91 us
  transfers between devices with their start and end apart: 7, of which 4 were waited for; matrix products, arithmetic and copies ran while one was open for 30% of the time, Pallas kernels for 0%

profile of v11, /device:TPU:1, one launch (start us, length us, event | category | flops | bytes accessed | tf_op | source)
XLA Modules:
  0.0 203.9 jit_solution(17606757118228039359)
XLA Ops:
  0.0 0.9 slice.186
  1.0 4.2 %collective-permute-start = (bf16[1,4096]{1,0:T(2,128)(2,1)S(1)}, bf16[1,4096]{1,0:T(2,128)(2,1)S(1)}, u32[]{:S(2)}, u32[]{:S(2)}) collective-permute-start(bf16[1,4096]{1,0:T(2,128)(2,1)S(1)} %slice.186), channel_id=1, source_target_pairs={{0,1},{1,2},{2,3},{3,4},{4,5},{5,6},{6,7},{7,8},{8,9},{9,10},{10,1... | collective-permute-start | bytes 24584 | tf_op jit(solution)/shard_map/ppermute | solution.py:18
  5.1 2.3 %copy.335 = bf16[128,4096]{0,1:T(8,128)(2,1)} copy(bf16[128,4096]{1,0:T(8,128)(2,1)} %param.13) | data formatting | bytes 2097152 | tf_op args[0]
  7.4 4.6 %all-to-all-start = ((bf16[128,4,1024]{0,2,1:T(8,128)(2,1)}), bf16[128,4,1024]{0,2,1:T(8,128)(2,1)S(1)}, u32[]{:S(2)}, u32[]{:S(2)}) async-start(bf16[128,4,1024]{0,2,1:T(8,128)(2,1)} %bitcast.1), calls=%async_computation | async-start | bytes 2097152 | tf_op jit(solution)/shard_map/all_to_all | solution.py:63
  12.0 1.3 copy.340
  14.0 1.4 fusion.89
  16.0 0.8 dynamic-slice_bitcast_fusion
  17.3 9.3 %all-to-all-done = bf16[128,4,1024]{0,2,1:T(8,128)(2,1)S(1)} async-done(((bf16[128,4,1024]{0,2,1:T(8,128)(2,1)}), bf16[128,4,1024]{0,2,1:T(8,128)(2,1)S(1)}, u32[]{:S(2)}, u32[]{:S(2)}) %all-to-all-start) | async-done | bytes 1048608 | tf_op jit(solution)/shard_map/all_to_all | solution.py:63
  26.6 3.6 %all-to-all-start.2 = ((bf16[128,4,1024]{0,2,1:T(8,128)(2,1)}), bf16[128,4,1024]{0,2,1:T(8,128)(2,1)S(1)}, u32[]{:S(2)}, u32[]{:S(2)}) async-start(bf16[128,4,1024]{0,2,1:T(8,128)(2,1)} %bitcast.205), calls=%async_computation.2 | async-start | bytes 2097152 | tf_op jit(solution)/shard_map/all_to_all | solution.py:64
  31.6 0.8 add_compare_fusion
  32.8 2.3 %copy.357 = bf16[128,4096]{0,1:T(8,128)(2,1)} copy(bf16[128,4096]{1,0:T(8,128)(2,1)} %param.15) | data formatting | bytes 2097152 | tf_op jit(solution)/shard_map/all_to_all | solution.py:65
  35.1 3.3 %fusion.4 = bf16[128,4096]{1,0:T(8,128)(2,1)S(1)} fusion(bf16[128,4096]{1,0:T(8,128)(2,1)S(1)} %copy-done, bf16[4096,128]{1,0:T(8,128)(2,1)} %param.21, bf16[128,4096]{1,0:T(8,128)(2,1)} %param.17, bf16[127,4096]{1,0:T(8,128)(2,1)} %bitcast.211, bf16[1,4096]{1,0:T(2,128)(2,1)S(1)} %collective-permute-done, f32[4096]{0:T(1024)S(1)} %copy-done.16, ...), kind=kOutput, calls=%fused_computation.5 | convolution fusion | flops 276316160 | bytes 5275776 | tf_op jit(solution)/shard_map/dot_general | solution.py:58
  38.5 1.3 copy.356
  39.8 4.2 %all-to-all-done.2 = bf16[128,4,1024]{0,2,1:T(8,128)(2,1)S(1)} async-done(((bf16[128,4,1024]{0,2,1:T(8,128)(2,1)}), bf16[128,4,1024]{0,2,1:T(8,128)(2,1)S(1)}, u32[]{:S(2)}, u32[]{:S(2)}) %all-to-all-start.2) | async-done | bytes 1048608 | tf_op jit(solution)/shard_map/all_to_all | solution.py:64
  44.0 4.3 %all-to-all-start.1 = ((bf16[128,4,1024]{0,2,1:T(8,128)(2,1)}), bf16[128,4,1024]{0,2,1:T(8,128)(2,1)}, u32[]{:S(2)}, u32[]{:S(2)}) async-start(bf16[128,4,1024]{0,2,1:T(8,128)(2,1)} %bitcast.5), calls=%async_computation.1 | async-start | bytes 2097152 | tf_op jit(solution)/shard_map/all_to_all | solution.py:66
  48.3 0.8 compare_convert_fusion.1
  49.4 2.9 %copy.339 = f32[4,128,16,64]{3,2,1,0:T(8,128)} copy(f32[4,128,16,64]{1,3,2,0:T(8,128)S(1)} %bitcast.190) | data formatting | bytes 4194304 | tf_op jit(solution)/shard_map/convert_element_type | solution.py:87
  52.3 1.5 convert_element_type.114
  53.8 4.0 %copy.341 = f32[4,128,16,64]{3,2,1,0:T(8,128)} copy(f32[4,128,16,64]{1,3,2,0:T(8,128)} %bitcast.192) | data formatting | bytes 4194304 | tf_op jit(solution)/shard_map/convert_element_type | solution.py:88
  57.9 3.4 %fusion = f32[4,128,16,64]{1,3,2,0:T(8,128)} fusion(f32[4,128,16,64]{1,3,2,0:T(8,128)} %bitcast.193, f32[4,128,16,64]{1,3,2,0:T(8,128)S(1)} %bitcast.191, f32[16,64]{1,0:T(8,128)S(1)} %mul.541), kind=kOutput, calls=%fused_computation | output fusion | flops 1056831 | bytes 6295552 | tf_op jit(solution)/shard_map/mul | solution.py:104
  61.3 4.2 %all-to-all-start.3 = ((bf16[128,4,1024]{0,2,1:T(8,128)(2,1)}), bf16[128,4,1024]{0,2,1:T(8,128)(2,1)S(1)}, u32[]{:S(2)}, u32[]{:S(2)}) async-start(bf16[128,4,1024]{0,2,1:T(8,128)(2,1)} %bitcast.12), calls=%async_computation.3 | async-start | bytes 2097152 | tf_op jit(solution)/shard_map/all_to_all | solution.py:65
  65.4 2.7 %convert_element_type.113 = f32[128,4,1024]{0,2,1:T(8,128)} convert(bf16[128,4,1024]{0,2,1:T(8,128)(2,1)} %all-to-all-done.1) | non-fusion elementwise | flops 524288 | bytes 3145728 | tf_op jit(solution)/shard_map/convert_element_type | solution.py:90
  68.1 4.0 %copy.337 = f32[4,128,16,64]{3,2,1,0:T(8,128)} copy(f32[4,128,16,64]{1,3,2,0:T(8,128)} %bitcast.204) | data formatting | bytes 4194304 | tf_op jit(solution)/shard_map/convert_element_type | solution.py:90
  72.1 2.5 %fusion.95 = f32[4,128,16,64]{3,2,1,0:T(8,128)S(1)} fusion(f32[4,128,16,64]{3,2,1,0:T(8,128)} %copy.337), kind=kOutput, calls=%fused_computation.173 | output fusion | flops 66584576 | bytes 4194304 | tf_op jit(solution)/shard_map/jit(cumsum)/reduce_window_sum | solution.py:91
  74.7 1.9 copy-done.2
  77.0 8.8 %exponential_multiply_fusion = (f32[4,128,16,64]{3,2,1,0:T(8,128)S(1)}, f32[4,128,16,64]{3,2,1,0:T(8,128)}, f32[4,128,16,64]{3,2,1,0:T(8,128)S(1)}) fusion(f32[4,128,16,64]{3,2,1,0:T(8,128)} %copy.341, f32[4,128,16,64]{3,2,1,0:T(8,128)} %copy-done.2, f32[4,128]{1,0:T(4,128)S(1)} %get-tuple-element.50, f32[4,16,64]{2,1,0:T(8,128)S(1)} %slice_bitcast_fusion.13, ...), kind=kLoop, calls=%fused_computation.14 | loop fusion | flops 3670016 | bytes 14698496 | tf_op jit(solution)/shard_map/mul | solution.py:95
  85.8 2.3 %slice_multiply_fusion.1 = (f32[4,128,8,64]{3,2,1,0:T(8,128)}, f32[4,128,8,64]{3,2,1,0:T(8,128)}) fusion(f32[4,128,16,64]{3,2,1,0:T(8,128)S(1)} %get-tuple-element.32, f32[4,128]{1,0:T(4,128)S(1)} %get-tuple-element.51), kind=kLoop, calls=%fused_computation.27 | loop fusion | flops 524288 | bytes 4196352 | tf_op jit(solution)/shard_map/mul | solution.py:183
  88.1 6.6 %fusion.7 = f32[4,16,128,128]{3,2,1,0:T(8,128)} fusion(f32[4,128,16,64]{3,2,1,0:T(8,128)S(1)} %get-tuple-element.28, f32[4,128,16,64]{3,2,1,0:T(8,128)S(1)} %get-tuple-element.32), kind=kOutput, calls=%fused_computation.8 | convolution fusion | flops 402653184 | bytes 8388608 | tf_op jit(solution)/shard_map/cthd,cshd->chts/dot_general | solution.py:96
  94.7 4.5 %fusion.5 = f32[4,16,64,64]{2,3,1,0:T(8,128)S(1)} fusion(bf16[4,128,16,64]{1,3,2,0:T(8,128)(2,1)S(1)} %bitcast.200, f32[4,128,16,64]{3,2,1,0:T(8,128)} %get-tuple-element.29), kind=kOutput, calls=%fused_computation.6 | convolution fusion | flops 201326592 | bytes 4194304 | tf_op jit(solution)/shard_map/cthd,cthe->chde/dot_general | solution.py:109
  99.2 1.3 multiply_add_fusion.1
  101.0 5.2 %all-gather = f32[32,65,64]{1,2,0:T(8,128)S(1)} all-gather(f32[16,65,64]{1,2,0:T(8,128)S(1)} %pad_maximum_fusion.1), channel_id=2, replica_groups=mesh['x'=4,'zh'=4,'zl'=2,'core'=2,'head'=4] {'core'}, dimensions={0}, use_global_device_ids=true | all-gather | bytes 798720 | tf_op jit(solution)/shard_map/all_gather | solution.py:149
  106.2 0.8 select_reduce_fusion
  107.2 1.9 collective-permute-start.1
  109.2 4.4 %bitcast_add_fusion = f32[4,128,16,64]{1,3,2,0:T(8,128)} fusion(f32[4,128,16,64]{1,3,2,0:T(8,128)S(1)} %copy-done.4, bf16[4,128,16,64]{1,3,2,0:T(8,128)(2,1)S(1)} %bitcast.201, f32[4,16,128,128]{3,2,1,0:T(8,128)S(1)} %copy-done.3, pred[4,128,128]{2,1,0:T(8,128)(4,1)S(1)} %compare_and_fusion), kind=kOutput, calls=%fused_computation.29 | convolution fusion | flops 405274624 | bytes 9502720 | tf_op jit(solution)/shard_map/chts,cshd->cthd/dot_general | solution.py:102
  113.8 1.6 collective-permute-done.1
  116.1 23.5 %all-gather.1 = f32[32,65,64]{1,2,0:T(8,128)S(1)} all-gather(f32[8,65,64]{1,2,0:T(8,128)S(1)} %pad_maximum_fusion.2), channel_id=3, replica_groups=mesh['x'=4,'zh'=4,'zl'=2,'core'=2,'head'=4] {'zh'}, dimensions={0}, use_global_device_ids=true | all-gather | bytes 665600 | tf_op jit(solution)/shard_map/all_gather | solution.py:161
  140.5 12.3 %all-gather.2 = f32[32,65,64]{1,2,0:T(8,128)S(1)} all-gather(f32[8,65,64]{1,2,0:T(8,128)S(1)} %pad_maximum_fusion.3), channel_id=4, replica_groups=mesh['x'=4,'zh'=4,'zl'=2,'core'=2,'head'=4] {'x'}, dimensions={0}, use_global_device_ids=true | all-gather | bytes 665600 | tf_op jit(solution)/shard_map/all_gather | solution.py:161
  154.1 9.3 %all_gather.27 = f32[16,64,64]{2,1,0:T(8,128)} all-gather(f32[8,64,64]{2,1,0:T(8,128)S(1)} %copy.351), channel_id=1, replica_groups=mesh['x'=4,'zh'=4,'zl'=2,'core'=2,'head'=4] {'core'}, dimensions={0}, use_global_device_ids=true | all-gather | bytes 393216 | tf_op jit(solution)/shard_map/all_gather | solution.py:169
  163.4 2.1 %copy.352 = f32[16,64,64]{1,2,0:T(8,128)} copy(f32[16,64,64]{2,1,0:T(8,128)} %all_gather.27) | data formatting | bytes 524288 | tf_op jit(solution)/shard_map/all_gather | solution.py:169
  165.4 1.4 select_add_fusion
  167.0 3.6 %fusion.93 = (f32[4,128,8]{1,2,0:T(8,128)S(1)}, f32[4,128,8,64]{1,3,2,0:T(8,128)S(1)}) fusion(f32[4,128,8,64]{3,2,1,0:T(8,128)S(1)} %copy-done.10, f32[1,16,64,64]{2,3,1,0:T(8,128)S(1)} %copy-done.13, f32[1,16,64,64]{2,3,1,0:T(8,128)S(1)} %copy-done.14, f32[1,16,64,64]{2,3,1,0:T(8,128)S(1)} %copy-done.15, f32[4]{0:T(128)S(1)} %pad.18.clone, ...), kind=kOutput, calls=%fused_computation.171 | convolution fusion | flops 102494208 | bytes 4227088 | tf_op jit(solution)/shard_map/cthd,chde->cthe/dot_general | solution.py:181
  170.6 2.3 %fusion.94 = (f32[4,128,8]{1,2,0:T(8,128)S(1)}, f32[4,128,8,64]{1,3,2,0:T(8,128)S(1)}) fusion(f32[4,128,8,64]{3,2,1,0:T(8,128)S(1)} %copy-done.9, f32[1,16,64,64]{2,3,1,0:T(8,128)S(1)} %copy-done.13, f32[1,16,64,64]{2,3,1,0:T(8,128)S(1)} %copy-done.14, f32[1,16,64,64]{2,3,1,0:T(8,128)S(1)} %copy-done.15, f32[4]{0:T(128)S(1)} %pad.18.clone, ...), kind=kOutput, calls=%fused_computation.172 | convolution fusion | flops 102494208 | bytes 4227088 | tf_op jit(solution)/shard_map/cthd,chde->cthe/dot_general | solution.py:181
  173.1 1.1 add_convert_fusion
  174.3 5.0 %all-to-all-start.5 = ((bf16[4,128,512]{1,2,0:T(8,128)(2,1)}), bf16[4,128,512]{1,2,0:T(8,128)(2,1)S(1)}, u32[]{:S(2)}, u32[]{:S(2)}) async-start(bf16[4,128,512]{1,2,0:T(8,128)(2,1)} %bitcast.54), calls=%async_computation.5 | async-start | bytes 1048576 | tf_op jit(solution)/shard_map/all_to_all | solution.py:192
  179.7 8.4 %all-to-all-done.5 = bf16[4,128,512]{1,2,0:T(8,128)(2,1)S(1)} async-done(((bf16[4,128,512]{1,2,0:T(8,128)(2,1)}), bf16[4,128,512]{1,2,0:T(8,128)(2,1)S(1)}, u32[]{:S(2)}, u32[]{:S(2)}) %all-to-all-start.5) | async-done | bytes 524320 | tf_op jit(solution)/shard_map/all_to_all | solution.py:192
  188.1 10.2 %all_to_all.87 = bf16[4,128,512]{1,2,0:T(8,128)(2,1)S(1)} all-to-all(bf16[4,128,512]{1,2,0:T(8,128)(2,1)S(1)} %bitcast.206), channel_id=1, replica_groups=mesh['x'=4,'zh'=4,'zl'=2,'core'=2,'head'=4] {'head'}, dimensions={0} | all-to-all | bytes 1048576 | tf_op jit(solution)/shard_map/all_to_all | solution.py:192
  198.6 1.9 copy.358
  200.5 3.4 %fusion.24 = bf16[128,4096]{1,0:T(8,128)(2,1)} fusion(f32[128,4096]{1,0:T(8,128)} %copy.358, bf16[128,4096]{1,0:T(8,128)(2,1)} %param.16), kind=kLoop, calls=%fused_computation.37 | loop fusion | flops 3670016 | bytes 4194304 | tf_op jit(solution)/shard_map/convert_element_type | solution.py:195
  (91 shorter events, 7.9 us)
Async XLA Ops:
  0.0 35.1 %copy-start = (bf16[128,4096]{1,0:T(8,128)(2,1)S(1)}, bf16[128,4096]{1,0:T(8,128)(2,1)}, u32[]{:S(2)}) copy-start(bf16[128,4096]{1,0:T(8,128)(2,1)} %param.22) | copy-start | bytes 3145732
  1.0 11.0 %copy-start.12 = (bf16[128,4096]{1,0:T(8,128)(2,1)S(1)}, bf16[128,4096]{1,0:T(8,128)(2,1)}, u32[]{:S(2)}) copy-start(bf16[128,4096]{1,0:T(8,128)(2,1)} %param.14) | copy-start | bytes 3145732
  1.0 34.1 %collective-permute-start = (bf16[1,4096]{1,0:T(2,128)(2,1)S(1)}, bf16[1,4096]{1,0:T(2,128)(2,1)S(1)}, u32[]{:S(2)}, u32[]{:S(2)}) collective-permute-start(bf16[1,4096]{1,0:T(2,128)(2,1)S(1)} %slice.186), channel_id=1, source_target_pairs={{0,1},{1,2},{2,3},{3,4},{4,5},{5,6},{6,7},{7,8},{8,9},{9,10},{10,1... | collective-permute-start | bytes 24584 | tf_op jit(solution)/shard_map/ppermute | solution.py:18
  7.4 19.2 %all-to-all-start = ((bf16[128,4,1024]{0,2,1:T(8,128)(2,1)}), bf16[128,4,1024]{0,2,1:T(8,128)(2,1)S(1)}, u32[]{:S(2)}, u32[]{:S(2)}) async-start(bf16[128,4,1024]{0,2,1:T(8,128)(2,1)} %bitcast.1), calls=%async_computation | async-start | bytes 2097152 | tf_op jit(solution)/shard_map/all_to_all | solution.py:63
  13.3 18.4 %dynamic-slice-start.1 = ((f32[4096]{0:T(1024)}, s32[]{:T(128)}), f32[1024]{0:T(1024)S(1)}, s32[]{:S(2)}) async-start(f32[4096]{0:T(1024)} %param.25, s32[]{:T(128)} %select_n.221), calls=%async_computation.7 | async-start | bytes 8704 | tf_op jit(solution)/shard_map/dynamic_slice | solution.py:83
  13.3 19.2 %dynamic-slice-start = ((f32[4096]{0:T(1024)}, s32[]{:T(128)}), f32[1024]{0:T(1024)S(1)}, s32[]{:S(2)}) async-start(f32[4096]{0:T(1024)} %param.23, s32[]{:T(128)} %select_n.221), calls=%async_computation.6 | async-start | bytes 8704 | tf_op jit(solution)/shard_map/dynamic_slice | solution.py:77
  26.6 8.5 %copy-start.5 = (bf16[128,4,1024]{0,2,1:T(8,128)(2,1)}, bf16[128,4,1024]{0,2,1:T(8,128)(2,1)S(1)}, u32[]{:S(2)}) copy-start(bf16[128,4,1024]{0,2,1:T(8,128)(2,1)S(1)} %all-to-all-done) | copy-start | bytes 3145732
  26.6 8.5 %copy-start.16 = (f32[4096]{0:T(1024)S(1)}, f32[4096]{0:T(1024)}, u32[]{:S(2)}) copy-start(f32[4096]{0:T(1024)} %param.20) | copy-start | bytes 49156
  26.6 8.5 %copy-start.17 = (f32[4096]{0:T(1024)S(1)}, f32[4096]{0:T(1024)}, u32[]{:S(2)}) copy-start(f32[4096]{0:T(1024)} %param.19) | copy-start | bytes 49156
  26.6 17.4 %all-to-all-start.2 = ((bf16[128,4,1024]{0,2,1:T(8,128)(2,1)}), bf16[128,4,1024]{0,2,1:T(8,128)(2,1)S(1)}, u32[]{:S(2)}, u32[]{:S(2)}) async-start(bf16[128,4,1024]{0,2,1:T(8,128)(2,1)} %bitcast.205), calls=%async_computation.2 | async-start | bytes 2097152 | tf_op jit(solution)/shard_map/all_to_all | solution.py:64
  38.5 10.7 %copy-start.6 = (bf16[128,4,1024]{0,2,1:T(8,128)(2,1)S(1)}, bf16[128,4,1024]{0,2,1:T(8,128)(2,1)}, u32[]{:S(2)}) copy-start(bf16[128,4,1024]{0,2,1:T(8,128)(2,1)} %copy-done.5) | copy-start | bytes 3145732
  44.0 5.0 %copy-start.7 = (bf16[128,4,1024]{0,2,1:T(8,128)(2,1)}, bf16[128,4,1024]{0,2,1:T(8,128)(2,1)S(1)}, u32[]{:S(2)}) copy-start(bf16[128,4,1024]{0,2,1:T(8,128)(2,1)S(1)} %all-to-all-done.2) | copy-start | bytes 3145732
  44.0 17.2 %all-to-all-start.1 = ((bf16[128,4,1024]{0,2,1:T(8,128)(2,1)}), bf16[128,4,1024]{0,2,1:T(8,128)(2,1)}, u32[]{:S(2)}, u32[]{:S(2)}) async-start(bf16[128,4,1024]{0,2,1:T(8,128)(2,1)} %bitcast.5), calls=%async_computation.1 | async-start | bytes 2097152 | tf_op jit(solution)/shard_map/all_to_all | solution.py:66
  49.3 2.9 %copy-start.8 = (bf16[128,4,1024]{0,2,1:T(8,128)(2,1)S(1)}, bf16[128,4,1024]{0,2,1:T(8,128)(2,1)}, u32[]{:S(2)}) copy-start(bf16[128,4,1024]{0,2,1:T(8,128)(2,1)} %copy-done.7) | copy-start | bytes 3145732
  61.3 33.5 %all-to-all-start.3 = ((bf16[128,4,1024]{0,2,1:T(8,128)(2,1)}), bf16[128,4,1024]{0,2,1:T(8,128)(2,1)S(1)}, u32[]{:S(2)}, u32[]{:S(2)}) async-start(bf16[128,4,1024]{0,2,1:T(8,128)(2,1)} %bitcast.12), calls=%async_computation.3 | async-start | bytes 2097152 | tf_op jit(solution)/shard_map/all_to_all | solution.py:65
  74.7 2.0 copy-start.2
  100.8 8.4 %copy-start.4 = (f32[4,128,16,64]{1,3,2,0:T(8,128)S(1)}, f32[4,128,16,64]{1,3,2,0:T(8,128)}, u32[]{:S(2)}) copy-start(f32[4,128,16,64]{1,3,2,0:T(8,128)} %fusion) | copy-start | bytes 6291460
  106.2 3.0 %copy-start.3 = (f32[4,16,128,128]{3,2,1,0:T(8,128)S(1)}, f32[4,16,128,128]{3,2,1,0:T(8,128)}, u32[]{:S(2)}) copy-start(f32[4,16,128,128]{3,2,1,0:T(8,128)} %fusion.7) | copy-start | bytes 12582916
  107.2 8.2 %collective-permute-start.1 = (f32[8,65,64]{1,2,0:T(8,128)S(1)}, f32[8,65,64]{1,2,0:T(8,128)S(1)}, u32[]{:S(2)}, u32[]{:S(2)}) collective-permute-start(f32[8,65,64]{1,2,0:T(8,128)S(1)} %fusion.66), channel_id=1, source_target_pairs={{0,8},{8,0},{1,9},{9,1},{2,10},{10,2},{3,11},{11,3},{4,12},{12,4},... | collective-permute-start | bytes 399368 | tf_op jit(solution)/shard_map/ppermute | solution.py:156
  154.0 12.8 %copy-start.10 = (f32[4,128,8,64]{3,2,1,0:T(8,128)S(1)}, f32[4,128,8,64]{3,2,1,0:T(8,128)}, u32[]{:S(2)}) copy-start(f32[4,128,8,64]{3,2,1,0:T(8,128)} %get-tuple-element.31) | copy-start | bytes 3145732
  165.4 1.4 copy-start.13
  165.4 1.4 copy-start.14
  165.4 1.5 copy-start.15
  167.0 3.7 %copy-start.9 = (f32[4,128,8,64]{3,2,1,0:T(8,128)S(1)}, f32[4,128,8,64]{3,2,1,0:T(8,128)}, u32[]{:S(2)}) copy-start(f32[4,128,8,64]{3,2,1,0:T(8,128)} %get-tuple-element.30) | copy-start | bytes 3145732
  167.0 3.7 %copy-start.11 = (f32[4,128,16,64]{1,3,2,0:T(8,128)S(1)}, f32[4,128,16,64]{1,3,2,0:T(8,128)}, u32[]{:S(2)}) copy-start(f32[4,128,16,64]{1,3,2,0:T(8,128)} %bitcast_add_fusion) | copy-start | bytes 6291460
  174.3 13.9 %all-to-all-start.5 = ((bf16[4,128,512]{1,2,0:T(8,128)(2,1)}), bf16[4,128,512]{1,2,0:T(8,128)(2,1)S(1)}, u32[]{:S(2)}, u32[]{:S(2)}) async-start(bf16[4,128,512]{1,2,0:T(8,128)(2,1)} %bitcast.54), calls=%async_computation.5 | async-start | bytes 1048576 | tf_op jit(solution)/shard_map/all_to_all | solution.py:192
  198.6 5.3 %copy-start.1 = (bf16[128,4096]{1,0:T(8,128)(2,1)S(1)}, bf16[128,4096]{1,0:T(8,128)(2,1)}, u32[]{:S(2)}) copy-start(bf16[128,4096]{1,0:T(8,128)(2,1)} %param.22) | copy-start | bytes 3145732

commit v12 on v10

--- a/solution.py
+++ b/solution.py
@@ -91,8 +91,11 @@
     cumulative = jnp.cumsum(decays, axis=1)
     before = cumulative - decays
     ending = cumulative[:, -1]
-    scaled_query = request_vectors * jnp.exp(before)
-    scaled_key = lookup_vectors * jnp.exp(-cumulative)
+    query_in, before_in, key_in, cumulative_in = lax.optimization_barrier(
+        (request_vectors, before, lookup_vectors, cumulative)
+    )
+    scaled_query = query_in * jnp.exp(before_in)
+    scaled_key = key_in * jnp.exp(-cumulative_in)
     scores = jnp.einsum("cthd,cshd->chts", scaled_query, scaled_key, precision=highest)
     causal = lax.broadcasted_iota(jnp.int32, (CH, CH), 0) > lax.broadcasted_iota(
         jnp.int32, (CH, CH), 1

time: 194 us -> 206 us (1.062)
  local copies, waits for them, and re-layouts: 31.2 us -> 40.9 us
  waiting for transfers between devices: 6.97 us -> 11.3 us
    mul x1, other arithmetic: 11.2 us -> 3.73 us  [local(): lookup_vectors * jnp.exp(ending[:, None] - cumulative)]
    all_to_all x1, waiting for transfers between devices: 6.96 us -> 0.01 us  [local(): lax.all_to_all(acceptance_linear, 'head', split_axis=1, concat_axis=0, ti...]
    optimization_barrier x0 -> x2, local copies, waits for them, and re-layouts: none -> 6.94 us  [local(): lax.optimization_barrier((request_vectors, before, lookup_vectors, cumula...]
    all_to_all x1, waiting for transfers between devices: 0.01 us -> 6.94 us  [local(): lax.all_to_all(lookup_linear, 'head', split_axis=1, concat_axis=0, tiled=...]
    mul x0 -> x2, other arithmetic: none -> 6.5 us  [the longest x1 4.18 us: local(): scaled_key = key_in * jnp.exp(-cumulative_in)]
    unnamed x36 -> x60, local copies, waits for them, and re-layouts: 5.86 us -> 10.7 us
    all_to_all x1, waiting for transfers between devices: 0.01 us -> 4.31 us  [local(): lax.all_to_all(log_decay, 'head', split_axis=1, concat_axis=0, tiled=True)]
    convert_element_type x1 -> x0, local copies, waits for them, and re-layouts: 2.97 us -> none  [local(): request_vectors = query_head.reshape(blocked).astype(jnp.float32)]
  transfers between devices with their start and end apart: 6 -> 6, of which waited for: 1 -> 2; matrix products, arithmetic and copies ran while one was open for 31% -> 29% of each run, Pallas kernels for 0% -> 0%
where the time goes in v12:
time: 206 us; the launch traced here: 205 us
  blocking collectives  69.3 us (34%)
  local copies, waits for them, and re-layouts  40.9 us (20%)
  other arithmetic  33.7 us (16%)
  matrix products  25.6 us (12%)
  starting transfers between devices  22.4 us (11%)
  waiting for transfers between devices  11.3 us (5%)
    all_gather x2, blocking collectives, local(): gathered = lax.all_gather(running, axis)  36.4 us
    all_to_all x1, blocking collectives, local(): lax.all_to_all(normed, 'head', split_axis=0, concat_axis=1, tiled=True)  18.1 us
    unnamed x60, local copies, waits for them, and re-layouts  10.7 us
    all_gather x1, blocking collectives, local(): pair_incoming = lax.all_gather(pair_incoming, 'core', tiled=True)  8.18 us
    dot_general x1, matrix products, local(): jnp.einsum('cthd,chde->cthe', scaled_query * keep_first[:, :, None, None]...  7.56 us
    optimization_barrier x2, local copies, waits for them, and re-layouts, local(): lax.optimization_barrier((request_vectors, before, lookup_vectors, cumula...  6.94 us
    all_to_all x1, waiting for transfers between devices, local(): lax.all_to_all(lookup_linear, 'head', split_axis=1, concat_axis=0, tiled=...  6.94 us
    dot_general x1, matrix products, local(): jnp.einsum('cthd,cshd->chts', scaled_query, scaled_key, precision=highest)  6.68 us
  transfers between devices with their start and end apart: 6, of which 2 were waited for; matrix products, arithmetic and copies ran while one was open for 29% of the time, Pallas kernels for 0%

profile of v12, /device:TPU:1, one launch (start us, length us, event | category | flops | bytes accessed | tf_op | source)
XLA Modules:
  0.0 204.9 jit_solution(9769330568557497654)
XLA Ops:
  0.0 2.4 %copy.329 = bf16[128,4096]{0,1:T(8,128)(2,1)} copy(bf16[128,4096]{1,0:T(8,128)(2,1)} %param.14) | data formatting | bytes 2097152 | tf_op args[1]
  2.4 5.0 %all-to-all-start.2 = ((bf16[128,4,1024]{0,2,1:T(8,128)(2,1)}), bf16[128,4,1024]{0,2,1:T(8,128)(2,1)S(1)}, u32[]{:S(2)}, u32[]{:S(2)}) async-start(bf16[128,4,1024]{0,2,1:T(8,128)(2,1)} %bitcast.9), calls=%async_computation.2 | async-start | bytes 2097152 | tf_op jit(solution)/shard_map/all_to_all | solution.py:64
  7.4 0.9 slice.120
  8.3 3.4 %collective-permute-start = (bf16[1,4096]{1,0:T(2,128)(2,1)S(1)}, bf16[1,4096]{1,0:T(2,128)(2,1)S(1)}, u32[]{:S(2)}, u32[]{:S(2)}) collective-permute-start(bf16[1,4096]{1,0:T(2,128)(2,1)S(1)} %slice.120), channel_id=1, source_target_pairs={{0,1},{1,2},{2,3},{3,4},{4,5},{5,6},{6,7},{7,8},{8,9},{9,10},{10,1... | collective-permute-start | bytes 24584 | tf_op jit(solution)/shard_map/ppermute | solution.py:18
  11.7 1.3 copy.325
  14.0 6.9 %all-to-all-done.2 = bf16[128,4,1024]{0,2,1:T(8,128)(2,1)S(1)} async-done(((bf16[128,4,1024]{0,2,1:T(8,128)(2,1)}), bf16[128,4,1024]{0,2,1:T(8,128)(2,1)S(1)}, u32[]{:S(2)}, u32[]{:S(2)}) %all-to-all-start.2) | async-done | bytes 1048608 | tf_op jit(solution)/shard_map/all_to_all | solution.py:64
  20.9 3.6 %all-to-all-start = ((bf16[128,4,1024]{0,2,1:T(8,128)(2,1)}), bf16[128,4,1024]{0,2,1:T(8,128)(2,1)S(1)}, u32[]{:S(2)}, u32[]{:S(2)}) async-start(bf16[128,4,1024]{0,2,1:T(8,128)(2,1)} %bitcast.199), calls=%async_computation | async-start | bytes 2097152 | tf_op jit(solution)/shard_map/all_to_all | solution.py:63
  25.5 1.4 fusion.79
  29.1 2.3 %copy.346 = bf16[128,4096]{0,1:T(8,128)(2,1)} copy(bf16[128,4096]{1,0:T(8,128)(2,1)} %param.15) | data formatting | bytes 2097152 | tf_op jit(solution)/shard_map/all_to_all | solution.py:65
  34.7 3.3 %fusion.4 = bf16[128,4096]{1,0:T(8,128)(2,1)S(1)} fusion(bf16[128,4096]{1,0:T(8,128)(2,1)S(1)} %copy-done, bf16[4096,128]{1,0:T(8,128)(2,1)} %param.21, bf16[128,4096]{1,0:T(8,128)(2,1)} %param.17, bf16[127,4096]{1,0:T(8,128)(2,1)} %bitcast.202, bf16[1,4096]{1,0:T(2,128)(2,1)S(1)} %collective-permute-done, f32[4096]{0:T(1024)S(1)} %copy-done.27, ...), kind=kOutput, calls=%fused_computation.5 | convolution fusion | flops 276316160 | bytes 5275776 | tf_op jit(solution)/shard_map/dot_general | solution.py:58
  38.0 1.3 copy.345
  39.3 4.2 %all-to-all-start.1 = ((bf16[128,4,1024]{0,2,1:T(8,128)(2,1)}), bf16[128,4,1024]{0,2,1:T(8,128)(2,1)}, u32[]{:S(2)}, u32[]{:S(2)}) async-start(bf16[128,4,1024]{0,2,1:T(8,128)(2,1)} %bitcast.5), calls=%async_computation.1 | async-start | bytes 2097152 | tf_op jit(solution)/shard_map/all_to_all | solution.py:66
  44.7 3.0 %copy.335 = f32[4,128,16,64]{3,2,1,0:T(8,128)} copy(f32[4,128,16,64]{1,3,2,0:T(8,128)S(1)} %bitcast.181) | data formatting | bytes 4194304 | tf_op jit(solution)/shard_map/convert_element_type | solution.py:88
  47.8 1.4 copy-done.4
  49.1 1.8 fusion
  51.0 4.3 %all-to-all-done.1 = bf16[128,4,1024]{0,2,1:T(8,128)(2,1)} async-done(((bf16[128,4,1024]{0,2,1:T(8,128)(2,1)}), bf16[128,4,1024]{0,2,1:T(8,128)(2,1)}, u32[]{:S(2)}, u32[]{:S(2)}) %all-to-all-start.1) | async-done | bytes 1048608 | tf_op jit(solution)/shard_map/all_to_all | solution.py:66
  55.3 3.5 %all-to-all-start.3 = ((bf16[128,4,1024]{0,2,1:T(8,128)(2,1)}), bf16[128,4,1024]{0,2,1:T(8,128)(2,1)S(1)}, u32[]{:S(2)}, u32[]{:S(2)}) async-start(bf16[128,4,1024]{0,2,1:T(8,128)(2,1)} %bitcast.200), calls=%async_computation.3 | async-start | bytes 2097152 | tf_op jit(solution)/shard_map/all_to_all | solution.py:65
  58.8 2.7 %convert_element_type.113 = f32[128,4,1024]{0,2,1:T(8,128)} convert(bf16[128,4,1024]{0,2,1:T(8,128)(2,1)} %all-to-all-done.1) | non-fusion elementwise | flops 524288 | bytes 3145728 | tf_op jit(solution)/shard_map/convert_element_type | solution.py:90
  61.5 4.0 %copy.327 = f32[4,128,16,64]{3,2,1,0:T(8,128)} copy(f32[4,128,16,64]{1,3,2,0:T(8,128)} %bitcast.196) | data formatting | bytes 4194304 | tf_op jit(solution)/shard_map/convert_element_type | solution.py:90
  65.5 2.7 %fusion.82 = f32[4,128,16,64]{3,2,1,0:T(8,128)S(1)} fusion(f32[4,128,16,64]{3,2,1,0:T(8,128)} %copy.327), kind=kOutput, calls=%fused_computation.160 | output fusion | flops 66584576 | bytes 4194304 | tf_op jit(solution)/shard_map/jit(cumsum)/reduce_window_sum | solution.py:91
  68.9 1.5 copy-done.2
  70.3 1.4 copy-done.7
  71.7 3.7 %multiply_multiply_fusion = (f32[4,128,16,64]{3,2,1,0:T(8,128)}, f32[4,128,16,64]{3,2,1,0:T(8,128)}) fusion(f32[4,128,16,64]{3,2,1,0:T(8,128)S(1)} %copy-done.7, f32[4,128,16,64]{3,2,1,0:T(8,128)S(1)} %fusion.82, f32[4,128]{1,0:T(4,128)S(1)} %get-tuple-element.53, f32[4,16,64]{2,1,0:T(8,128)S(1)} %slice_bitcast_fusion.13, f32[4,128,16,64]{3,2,1,0:T(8,128)S(1)} %copy-done.3), kind=kLoop, calls=%fused_computation.13 | loop fusion | flops 2097152 | bytes 10504192 | tf_op jit(solution)/shard_map/mul | solution.py:111
  75.5 4.9 %fusion.7 = f32[4,16,64,64]{2,3,1,0:T(8,128)S(1)} fusion(bf16[4,128,16,64]{1,3,2,0:T(8,128)(2,1)S(1)} %bitcast.192, f32[4,128,16,64]{3,2,1,0:T(8,128)} %get-tuple-element.38), kind=kOutput, calls=%fused_computation.8 | convolution fusion | flops 201326592 | bytes 4194304 | tf_op jit(solution)/shard_map/cthd,cthe->chde/dot_general | solution.py:112
  80.4 1.3 multiply_add_fusion.1
  82.4 6.6 %all-gather = f32[32,65,64]{1,2,0:T(8,128)S(1)} all-gather(f32[16,65,64]{1,2,0:T(8,128)S(1)} %pad_maximum_fusion), channel_id=2, replica_groups=mesh['x'=4,'zh'=4,'zl'=2,'core'=2,'head'=4] {'core'}, dimensions={0}, use_global_device_ids=true | all-gather | bytes 798720 | tf_op jit(solution)/shard_map/all_gather | solution.py:152
  89.0 0.8 select_reduce_fusion
  90.0 0.8 copy-done.11
  90.9 2.6 %collective-permute-start.1 = (f32[8,65,64]{1,2,0:T(8,128)S(1)}, f32[8,65,64]{1,2,0:T(8,128)}, u32[]{:S(2)}, u32[]{:S(2)}) collective-permute-start(f32[8,65,64]{1,2,0:T(8,128)S(1)} %fusion.57), channel_id=1, source_target_pairs={{0,8},{8,0},{1,9},{9,1},{2,10},{10,2},{3,11},{11,3},{4,12},{12,4},... | collective-permute-start | bytes 399368 | tf_op jit(solution)/shard_map/ppermute | solution.py:159
  93.6 4.0 %copy.330 = f32[4,128,16,64]{3,2,1,0:T(8,128)} copy(f32[4,128,16,64]{1,3,2,0:T(8,128)} %bitcast.185) | data formatting | bytes 4194304 | tf_op jit(solution)/shard_map/optimization_barrier | solution.py:94
  97.6 3.0 %copy.331 = f32[4,128,16,64]{3,2,1,0:T(8,128)} copy(f32[4,128,16,64]{1,3,2,0:T(8,128)S(1)} %bitcast.183) | data formatting | bytes 4194304 | tf_op jit(solution)/shard_map/optimization_barrier | solution.py:94
  100.5 4.2 %exponential_multiply_fusion = f32[4,128,16,64]{3,2,1,0:T(8,128)S(1)} fusion(f32[4,128,16,64]{3,2,1,0:T(8,128)} %copy.331, f32[4,128,16,64]{3,2,1,0:T(8,128)} %copy-done.2), kind=kLoop, calls=%fused_computation.16 | loop fusion | flops 1048576 | bytes 6291456 | tf_op jit(solution)/shard_map/mul | solution.py:98
  105.2 1.3 copy-done.6
  106.4 2.3 %broadcast_multiply_fusion = (f32[4,128,16,64]{3,2,1,0:T(8,128)}, f32[4,128,16,64]{3,2,1,0:T(8,128)S(1)}) fusion(f32[4,128]{1,0:T(4,128)S(1)} %get-tuple-element.54, f32[4,128,16,64]{3,2,1,0:T(8,128)S(1)} %copy-done.5, f32[4,128,16,64]{3,2,1,0:T(8,128)S(1)} %copy-done.6), kind=kLoop, calls=%fused_computation.38 | loop fusion | flops 1048576 | bytes 8390656 | tf_op jit(solution)/shard_map/mul | solution.py:181
  108.8 6.7 %fusion.9 = f32[4,16,128,128]{3,2,1,0:T(8,128)S(1)} fusion(f32[4,128,16,64]{3,2,1,0:T(8,128)S(1)} %exponential_multiply_fusion, f32[4,128,16,64]{3,2,1,0:T(8,128)S(1)} %get-tuple-element.37), kind=kOutput, calls=%fused_computation.10 | convolution fusion | flops 402653184 | bytes 8388608 | tf_op jit(solution)/shard_map/cthd,cshd->chts/dot_general | solution.py:99
  115.5 3.1 %bitcast_add_fusion.1 = f32[4,128,16,64]{1,3,2,0:T(8,128)S(1)} fusion(f32[4,128,16,64]{1,3,2,0:T(8,128)S(1)} %copy-done.10, bf16[4,128,16,64]{1,3,2,0:T(8,128)(2,1)S(1)} %bitcast.193, f32[4,16,128,128]{3,2,1,0:T(8,128)S(1)} %fusion.9, pred[4,128,128]{2,1,0:T(8,128)(4,1)S(1)} %compare_and_fusion), kind=kOutput, calls=%fused_computation.35 | convolution fusion | flops 405274624 | bytes 9502720 | tf_op jit(solution)/shard_map/chts,cshd->cthd/dot_general | solution.py:105
  118.9 1.1 maximum_select_fusion.3
  120.7 24.0 %all-gather.1 = f32[32,65,64]{1,2,0:T(8,128)S(1)} all-gather(f32[8,65,64]{1,2,0:T(8,128)S(1)} %pad_maximum_fusion.1), channel_id=3, replica_groups=mesh['x'=4,'zh'=4,'zl'=2,'core'=2,'head'=4] {'zh'}, dimensions={0}, use_global_device_ids=true | all-gather | bytes 665600 | tf_op jit(solution)/shard_map/all_gather | solution.py:164
  145.6 12.4 %all-gather.2 = f32[32,65,64]{1,2,0:T(8,128)S(1)} all-gather(f32[8,65,64]{1,2,0:T(8,128)S(1)} %pad_maximum_fusion.2), channel_id=4, replica_groups=mesh['x'=4,'zh'=4,'zl'=2,'core'=2,'head'=4] {'x'}, dimensions={0}, use_global_device_ids=true | all-gather | bytes 665600 | tf_op jit(solution)/shard_map/all_gather | solution.py:164
  158.7 1.1 fusion.63
  159.8 1.1 copy.341
  160.9 8.2 %all_gather.27 = f32[16,64,64]{2,1,0:T(8,128)} all-gather(f32[8,64,64]{2,1,0:T(8,128)S(1)} %copy.341), channel_id=1, replica_groups=mesh['x'=4,'zh'=4,'zl'=2,'core'=2,'head'=4] {'core'}, dimensions={0}, use_global_device_ids=true | all-gather | bytes 393216 | tf_op jit(solution)/shard_map/all_gather | solution.py:172
  169.1 2.0 copy.342
  171.2 1.4 select_add_fusion
  172.7 7.6 %fusion.81 = (f32[4,128,16]{1,2,0:T(8,128)S(1)}, f32[4,128,16,64]{1,3,2,0:T(8,128)S(1)}) fusion(f32[4,128,16,64]{1,3,2,0:T(8,128)S(1)} %bitcast_add_fusion.1, f32[4,128,16,64]{3,2,1,0:T(8,128)} %get-tuple-element.36, f32[1,16,64,64]{2,3,1,0:T(8,128)S(1)} %copy-done.19, f32[1,16,64,64]{2,3,1,0:T(8,128)S(1)} %copy-done.20, ...), kind=kOutput, calls=%fused_computation.159 | convolution fusion | flops 203677696 | bytes 7389200 | tf_op jit(solution)/shard_map/cthd,chde->cthe/dot_general | solution.py:179
  181.4 18.1 %all_to_all.68 = bf16[4,128,1024]{1,2,0:T(8,128)(2,1)S(1)} all-to-all(bf16[4,128,1024]{1,2,0:T(8,128)(2,1)S(1)} %bitcast.198), channel_id=1, replica_groups=mesh['x'=4,'zh'=4,'zl'=2,'core'=2,'head'=4] {'head'}, dimensions={0} | all-to-all | bytes 2097152 | tf_op jit(solution)/shard_map/all_to_all | solution.py:191
  199.6 1.9 copy.347
  201.5 3.4 %fusion.28 = bf16[128,4096]{1,0:T(8,128)(2,1)} fusion(f32[128,4096]{1,0:T(8,128)} %copy.347, bf16[128,4096]{1,0:T(8,128)(2,1)} %param.16), kind=kLoop, calls=%fused_computation.43 | loop fusion | flops 3670016 | bytes 4194304 | tf_op jit(solution)/shard_map/convert_element_type | solution.py:192
  (101 shorter events, 13.2 us)
Async XLA Ops:
  0.0 34.6 %copy-start = (bf16[128,4096]{1,0:T(8,128)(2,1)S(1)}, bf16[128,4096]{1,0:T(8,128)(2,1)}, u32[]{:S(2)}) copy-start(bf16[128,4096]{1,0:T(8,128)(2,1)} %param.22) | copy-start | bytes 3145732
  0.0 11.7 %copy-start.22 = (bf16[128,4096]{1,0:T(8,128)(2,1)S(1)}, bf16[128,4096]{1,0:T(8,128)(2,1)}, u32[]{:S(2)}) copy-start(bf16[128,4096]{1,0:T(8,128)(2,1)} %param.13) | copy-start | bytes 3145732
  2.4 18.5 %all-to-all-start.2 = ((bf16[128,4,1024]{0,2,1:T(8,128)(2,1)}), bf16[128,4,1024]{0,2,1:T(8,128)(2,1)S(1)}, u32[]{:S(2)}, u32[]{:S(2)}) async-start(bf16[128,4,1024]{0,2,1:T(8,128)(2,1)} %bitcast.9), calls=%async_computation.2 | async-start | bytes 2097152 | tf_op jit(solution)/shard_map/all_to_all | solution.py:64
  8.3 26.4 %collective-permute-start = (bf16[1,4096]{1,0:T(2,128)(2,1)S(1)}, bf16[1,4096]{1,0:T(2,128)(2,1)S(1)}, u32[]{:S(2)}, u32[]{:S(2)}) collective-permute-start(bf16[1,4096]{1,0:T(2,128)(2,1)S(1)} %slice.120), channel_id=1, source_target_pairs={{0,1},{1,2},{2,3},{3,4},{4,5},{5,6},{6,7},{7,8},{8,9},{9,10},{10,1... | collective-permute-start | bytes 24584 | tf_op jit(solution)/shard_map/ppermute | solution.py:18
  20.9 10.4 %copy-start.15 = (bf16[128,4,1024]{0,2,1:T(8,128)(2,1)}, bf16[128,4,1024]{0,2,1:T(8,128)(2,1)S(1)}, u32[]{:S(2)}) copy-start(bf16[128,4,1024]{0,2,1:T(8,128)(2,1)S(1)} %all-to-all-done.2) | copy-start | bytes 3145732
  20.9 13.7 %copy-start.27 = (f32[4096]{0:T(1024)S(1)}, f32[4096]{0:T(1024)}, u32[]{:S(2)}) copy-start(f32[4096]{0:T(1024)} %param.20) | copy-start | bytes 49156
  20.9 13.7 %copy-start.28 = (f32[4096]{0:T(1024)S(1)}, f32[4096]{0:T(1024)}, u32[]{:S(2)}) copy-start(f32[4096]{0:T(1024)} %param.19) | copy-start | bytes 49156
  20.9 18.4 %all-to-all-start = ((bf16[128,4,1024]{0,2,1:T(8,128)(2,1)}), bf16[128,4,1024]{0,2,1:T(8,128)(2,1)S(1)}, u32[]{:S(2)}, u32[]{:S(2)}) async-start(bf16[128,4,1024]{0,2,1:T(8,128)(2,1)} %bitcast.199), calls=%async_computation | async-start | bytes 2097152 | tf_op jit(solution)/shard_map/all_to_all | solution.py:63
  38.0 6.5 %copy-start.16 = (bf16[128,4,1024]{0,2,1:T(8,128)(2,1)S(1)}, bf16[128,4,1024]{0,2,1:T(8,128)(2,1)}, u32[]{:S(2)}) copy-start(bf16[128,4,1024]{0,2,1:T(8,128)(2,1)} %copy-done.15) | copy-start | bytes 3145732
  39.3 5.0 %copy-start.17 = (bf16[128,4,1024]{0,2,1:T(8,128)(2,1)}, bf16[128,4,1024]{0,2,1:T(8,128)(2,1)S(1)}, u32[]{:S(2)}) copy-start(bf16[128,4,1024]{0,2,1:T(8,128)(2,1)S(1)} %all-to-all-done) | copy-start | bytes 3145732
  39.3 15.9 %all-to-all-start.1 = ((bf16[128,4,1024]{0,2,1:T(8,128)(2,1)}), bf16[128,4,1024]{0,2,1:T(8,128)(2,1)}, u32[]{:S(2)}, u32[]{:S(2)}) async-start(bf16[128,4,1024]{0,2,1:T(8,128)(2,1)} %bitcast.5), calls=%async_computation.1 | async-start | bytes 2097152 | tf_op jit(solution)/shard_map/all_to_all | solution.py:66
  44.7 3.0 %copy-start.18 = (bf16[128,4,1024]{0,2,1:T(8,128)(2,1)S(1)}, bf16[128,4,1024]{0,2,1:T(8,128)(2,1)}, u32[]{:S(2)}) copy-start(bf16[128,4,1024]{0,2,1:T(8,128)(2,1)} %copy-done.17) | copy-start | bytes 3145732
  47.8 1.4 copy-start.4
  55.3 20.2 %all-to-all-start.3 = ((bf16[128,4,1024]{0,2,1:T(8,128)(2,1)}), bf16[128,4,1024]{0,2,1:T(8,128)(2,1)S(1)}, u32[]{:S(2)}, u32[]{:S(2)}) async-start(bf16[128,4,1024]{0,2,1:T(8,128)(2,1)} %bitcast.200), calls=%async_computation.3 | async-start | bytes 2097152 | tf_op jit(solution)/shard_map/all_to_all | solution.py:65
  65.5 4.9 %copy-start.3 = (f32[4,128,16,64]{3,2,1,0:T(8,128)S(1)}, f32[4,128,16,64]{3,2,1,0:T(8,128)}, u32[]{:S(2)}) copy-start(f32[4,128,16,64]{3,2,1,0:T(8,128)} %copy.327) | copy-start | bytes 6291460
  65.5 6.2 %copy-start.7 = (f32[4,128,16,64]{3,2,1,0:T(8,128)S(1)}, f32[4,128,16,64]{3,2,1,0:T(8,128)}, u32[]{:S(2)}) copy-start(f32[4,128,16,64]{3,2,1,0:T(8,128)} %copy.335) | copy-start | bytes 6291460
  68.2 2.2 %copy-start.2 = (f32[4,128,16,64]{3,2,1,0:T(8,128)}, f32[4,128,16,64]{3,2,1,0:T(8,128)S(1)}, u32[]{:S(2)}) copy-start(f32[4,128,16,64]{3,2,1,0:T(8,128)S(1)} %fusion.82) | copy-start | bytes 6291460
  75.5 4.9 %copy-start.8 = (bf16[128,4,1024]{0,2,1:T(8,128)(2,1)}, bf16[128,4,1024]{0,2,1:T(8,128)(2,1)S(1)}, u32[]{:S(2)}) copy-start(bf16[128,4,1024]{0,2,1:T(8,128)(2,1)S(1)} %all-to-all-done.3) | copy-start | bytes 3145732
  89.8 1.1 copy-start.13
  89.9 0.8 copy-start.11
  90.9 28.0 %collective-permute-start.1 = (f32[8,65,64]{1,2,0:T(8,128)S(1)}, f32[8,65,64]{1,2,0:T(8,128)}, u32[]{:S(2)}, u32[]{:S(2)}) collective-permute-start(f32[8,65,64]{1,2,0:T(8,128)S(1)} %fusion.57), channel_id=1, source_target_pairs={{0,8},{8,0},{1,9},{9,1},{2,10},{10,2},{3,11},{11,3},{4,12},{12,4},... | collective-permute-start | bytes 399368 | tf_op jit(solution)/shard_map/ppermute | solution.py:159
  100.5 4.6 %copy-start.5 = (f32[4,128,16,64]{3,2,1,0:T(8,128)S(1)}, f32[4,128,16,64]{3,2,1,0:T(8,128)}, u32[]{:S(2)}) copy-start(f32[4,128,16,64]{3,2,1,0:T(8,128)} %copy.330) | copy-start | bytes 6291460
  100.5 5.9 %copy-start.6 = (f32[4,128,16,64]{3,2,1,0:T(8,128)S(1)}, f32[4,128,16,64]{3,2,1,0:T(8,128)}, u32[]{:S(2)}) copy-start(f32[4,128,16,64]{3,2,1,0:T(8,128)} %get-tuple-element.10) | copy-start | bytes 6291460
  108.8 6.7 %copy-start.9 = (bf16[128,4,1024]{0,2,1:T(8,128)(2,1)S(1)}, bf16[128,4,1024]{0,2,1:T(8,128)(2,1)}, u32[]{:S(2)}) copy-start(bf16[128,4,1024]{0,2,1:T(8,128)(2,1)} %copy-done.8) | copy-start | bytes 3145732
  108.8 6.7 %copy-start.10 = (f32[4,128,16,64]{1,3,2,0:T(8,128)S(1)}, f32[4,128,16,64]{1,3,2,0:T(8,128)}, u32[]{:S(2)}) copy-start(f32[4,128,16,64]{1,3,2,0:T(8,128)} %fusion) | copy-start | bytes 6291460
  115.5 3.1 %copy-start.23 = (f32[1,16,64]{2,1,0:T(8,128)S(1)}, f32[1,16,64]{2,1,0:T(8,128)}, u32[]{:S(2)}) copy-start(f32[1,16,64]{2,1,0:T(8,128)} %get-tuple-element.48) | copy-start | bytes 12292
  115.5 3.1 %copy-start.24 = (f32[1,16,64]{2,1,0:T(8,128)S(1)}, f32[1,16,64]{2,1,0:T(8,128)}, u32[]{:S(2)}) copy-start(f32[1,16,64]{2,1,0:T(8,128)} %get-tuple-element.49) | copy-start | bytes 12292
  115.5 3.1 %copy-start.25 = (f32[4]{0:T(128)S(1)}, f32[4]{0:T(128)}, u32[]{:S(2)}) copy-start(f32[4]{0:T(128)} %pad.12.clone) | copy-start | bytes 52
  115.5 3.2 %copy-start.12 = (f32[16,64,64]{1,2,0:T(8,128)S(1)}, f32[16,64,64]{1,2,0:T(8,128)}, u32[]{:S(2)}) copy-start(f32[16,64,64]{1,2,0:T(8,128)} %copy-done.11) | copy-start | bytes 786436
  115.5 3.2 %copy-start.14 = (f32[16,1,64]{1,2,0:T(8,128)S(1)}, f32[16,1,64]{1,2,0:T(8,128)}, u32[]{:S(2)}) copy-start(f32[16,1,64]{1,2,0:T(8,128)} %copy-done.13) | copy-start | bytes 12292
  160.9 11.6 %copy-start.26 = (f32[4]{0:T(128)S(1)}, f32[4]{0:T(128)}, u32[]{:S(2)}) copy-start(f32[4]{0:T(128)} %pad.16.clone) | copy-start | bytes 52
  171.1 1.4 copy-start.19
  171.2 1.4 copy-start.20
  171.2 1.5 copy-start.21
  199.6 5.3 %copy-start.1 = (bf16[128,4096]{1,0:T(8,128)(2,1)S(1)}, bf16[128,4096]{1,0:T(8,128)(2,1)}, u32[]{:S(2)}) copy-start(bf16[128,4096]{1,0:T(8,128)(2,1)} %param.22) | copy-start | bytes 3145732

commit v13 on v10

--- a/solution.py
+++ b/solution.py
@@ -146,7 +146,11 @@
     own = jnp.concatenate([span_state, span_decay[:, None, :]], axis=1)
     core_index = lax.axis_index("core")
     core_count = lax.axis_size("core")
-    core_prefix, core_total = fold(lax.all_gather(own, "core"), core_index)
+    core_partner = lax.ppermute(own, "core", [(0, 1), (1, 0)])
+    core_pair = jnp.where(
+        core_index == 0, jnp.stack([own, core_partner]), jnp.stack([core_partner, own])
+    )
+    core_prefix, core_total = fold(core_pair, core_index)
     share = local_heads // core_count
     level_prefixes = []
     running = lax.dynamic_slice_in_dim(core_total, core_index * share, share, 0)
@@ -166,7 +170,12 @@
         pair_incoming = (
             prefix[:, ATTENTION_SPAN][:, :, None] * pair_incoming + prefix[:, :ATTENTION_SPAN]
         )
-    pair_incoming = lax.all_gather(pair_incoming, "core", tiled=True)
+    incoming_partner = lax.ppermute(pair_incoming, "core", [(0, 1), (1, 0)])
+    pair_incoming = jnp.where(
+        core_index == 0,
+        jnp.concatenate([pair_incoming, incoming_partner]),
+        jnp.concatenate([incoming_partner, pair_incoming]),
+    )
     incoming = (
         core_prefix[:, ATTENTION_SPAN][:, :, None] * pair_incoming
         + core_prefix[:, :ATTENTION_SPAN]

time: 194 us -> 187 us (0.964)
  blocking collectives: 69.5 us -> 54.2 us
  starting transfers between devices: 22.3 us -> 34.6 us
  waiting for transfers between devices: 6.97 us -> 12.9 us
  matrix products: 26.4 us -> 22.8 us
  local copies, waits for them, and re-layouts: 31.2 us -> 27.8 us
  other arithmetic: 35 us -> 32.2 us
    all_gather x2 -> x0, blocking collectives: 13.7 us -> none  [the longest x1 7.58 us: local(): pair_incoming = lax.all_gather(pair_incoming, 'core', tiled=True)]
    ppermute x0 -> x2, starting transfers between devices: none -> 12.4 us  [the longest x1 8.36 us: local(): incoming_partner = lax.ppermute(pair_incoming, 'core', [(0, 1), (1, 0)])]
    ppermute x1, waiting for transfers between devices: 0.01 us -> 5.17 us  [local(): partner = lax.ppermute(running, axis, [(0, 1), (1, 0)])]
    dot_general x1, matrix products: 7.56 us -> 5.14 us  [local(): jnp.einsum('cthd,chde->cthe', scaled_query * keep_first[:, :, None, None]...]
    all_gather x1 -> x0, local copies, waits for them, and re-layouts: 2.06 us -> none  [local(): pair_incoming = lax.all_gather(pair_incoming, 'core', tiled=True)]
    unnamed x36 -> x30, local copies, waits for them, and re-layouts: 5.86 us -> 5.74 us
  transfers between devices with their start and end apart: 6 -> 8, of which waited for: 1 -> 3; matrix products, arithmetic and copies ran while one was open for 31% -> 31% of each run, Pallas kernels for 0% -> 0%
where the time goes in v13:
time: 187 us; the launch traced here: 186 us
  blocking collectives  54.2 us (29%)
  starting transfers between devices  34.6 us (19%)
  other arithmetic  32.2 us (17%)
  local copies, waits for them, and re-layouts  27.8 us (15%)
  matrix products  22.8 us (12%)
  waiting for transfers between devices  12.9 us (7%)
    all_gather x2, blocking collectives, local(): gathered = lax.all_gather(running, axis)  35.3 us
    all_to_all x1, blocking collectives, local(): lax.all_to_all(normed, 'head', split_axis=0, concat_axis=1, tiled=True)  18.9 us
    mul x1, other arithmetic, local(): lookup_vectors * jnp.exp(ending[:, None] - cumulative)  11.1 us
    ppermute x1, starting transfers between devices, local(): incoming_partner = lax.ppermute(pair_incoming, 'core', [(0, 1), (1, 0)])  8.36 us
    all_to_all x1, waiting for transfers between devices, local(): lax.all_to_all(acceptance_linear, 'head', split_axis=1, concat_axis=0, ti...  6.96 us
    dot_general x1, matrix products, local(): jnp.einsum('cthd,cshd->chts', scaled_query, scaled_key, precision=highest)  6.66 us
    unnamed x30, local copies, waits for them, and re-layouts  5.74 us
    ppermute x1, waiting for transfers between devices, local(): partner = lax.ppermute(running, axis, [(0, 1), (1, 0)])  5.17 us
  transfers between devices with their start and end apart: 8, of which 3 were waited for; matrix products, arithmetic and copies ran while one was open for 31% of the time, Pallas kernels for 0%

profile of v13, /device:TPU:1, one launch (start us, length us, event | category | flops | bytes accessed | tf_op | source)
XLA Modules:
  0.0 186.2 jit_solution(2560766321688460986)
XLA Ops:
  0.0 2.4 %copy.230 = bf16[128,4096]{0,1:T(8,128)(2,1)} copy(bf16[128,4096]{1,0:T(8,128)(2,1)} %param.13) | data formatting | bytes 2097152 | tf_op args[0]
  2.4 5.0 %all-to-all-start = ((bf16[128,4,1024]{0,2,1:T(8,128)(2,1)}), bf16[128,4,1024]{0,2,1:T(8,128)(2,1)S(1)}, u32[]{:S(2)}, u32[]{:S(2)}) async-start(bf16[128,4,1024]{0,2,1:T(8,128)(2,1)} %bitcast.1), calls=%async_computation | async-start | bytes 2097152 | tf_op jit(solution)/shard_map/all_to_all | solution.py:63
  7.4 0.9 slice.120
  8.3 3.4 %collective-permute-start = (bf16[1,4096]{1,0:T(2,128)(2,1)S(1)}, bf16[1,4096]{1,0:T(2,128)(2,1)S(1)}, u32[]{:S(2)}, u32[]{:S(2)}) collective-permute-start(bf16[1,4096]{1,0:T(2,128)(2,1)S(1)} %slice.120), channel_id=1, source_target_pairs={{0,1},{1,2},{2,3},{3,4},{4,5},{5,6},{6,7},{7,8},{8,9},{9,10},{10,1... | collective-permute-start | bytes 24584 | tf_op jit(solution)/shard_map/ppermute | solution.py:18
  11.7 1.3 copy.235
  13.0 0.8 dynamic-slice_bitcast_fusion
  14.0 7.0 %all-to-all-done = bf16[128,4,1024]{0,2,1:T(8,128)(2,1)S(1)} async-done(((bf16[128,4,1024]{0,2,1:T(8,128)(2,1)}), bf16[128,4,1024]{0,2,1:T(8,128)(2,1)S(1)}, u32[]{:S(2)}, u32[]{:S(2)}) %all-to-all-start) | async-done | bytes 1048608 | tf_op jit(solution)/shard_map/all_to_all | solution.py:63
  20.9 3.6 %all-to-all-start.2 = ((bf16[128,4,1024]{0,2,1:T(8,128)(2,1)}), bf16[128,4,1024]{0,2,1:T(8,128)(2,1)S(1)}, u32[]{:S(2)}, u32[]{:S(2)}) async-start(bf16[128,4,1024]{0,2,1:T(8,128)(2,1)} %bitcast.195), calls=%async_computation.2 | async-start | bytes 2097152 | tf_op jit(solution)/shard_map/all_to_all | solution.py:64
  24.8 0.8 dynamic_slice.26
  25.6 1.4 fusion.82
  28.3 0.8 add_compare_fusion
  29.1 0.7 dynamic_slice.27
  29.8 0.7 dynamic_slice.30
  30.5 0.7 dynamic_slice.31
  31.4 2.3 %copy.251 = bf16[128,4096]{0,1:T(8,128)(2,1)} copy(bf16[128,4096]{1,0:T(8,128)(2,1)} %param.15) | data formatting | bytes 2097152 | tf_op jit(solution)/shard_map/all_to_all | solution.py:65
  33.7 3.3 %fusion.4 = bf16[128,4096]{1,0:T(8,128)(2,1)S(1)} fusion(bf16[128,4096]{1,0:T(8,128)(2,1)S(1)} %copy-done, bf16[4096,128]{1,0:T(8,128)(2,1)} %param.21, bf16[128,4096]{1,0:T(8,128)(2,1)} %param.17, bf16[127,4096]{1,0:T(8,128)(2,1)} %bitcast.201, bf16[1,4096]{1,0:T(2,128)(2,1)S(1)} %collective-permute-done, f32[4096]{0:T(1024)S(1)} %copy-done.12, ...), kind=kOutput, calls=%fused_computation.5 | convolution fusion | flops 276316160 | bytes 5275776 | tf_op jit(solution)/shard_map/dot_general | solution.py:58
  37.0 1.3 copy.250
  38.3 4.3 %all-to-all-start.1 = ((bf16[128,4,1024]{0,2,1:T(8,128)(2,1)}), bf16[128,4,1024]{0,2,1:T(8,128)(2,1)}, u32[]{:S(2)}, u32[]{:S(2)}) async-start(bf16[128,4,1024]{0,2,1:T(8,128)(2,1)} %bitcast.5), calls=%async_computation.1 | async-start | bytes 2097152 | tf_op jit(solution)/shard_map/all_to_all | solution.py:66
  42.6 0.8 compare_convert_fusion.1
  43.6 2.9 %copy.234 = f32[4,128,16,64]{3,2,1,0:T(8,128)} copy(f32[4,128,16,64]{1,3,2,0:T(8,128)S(1)} %bitcast.183) | data formatting | bytes 4194304 | tf_op jit(solution)/shard_map/convert_element_type | solution.py:87
  46.6 1.5 convert_element_type.114
  48.0 4.0 %copy.236 = f32[4,128,16,64]{3,2,1,0:T(8,128)} copy(f32[4,128,16,64]{1,3,2,0:T(8,128)} %bitcast.185) | data formatting | bytes 4194304 | tf_op jit(solution)/shard_map/convert_element_type | solution.py:88
  52.0 3.4 %fusion = f32[4,128,16,64]{1,3,2,0:T(8,128)} fusion(f32[4,128,16,64]{1,3,2,0:T(8,128)} %bitcast.186, f32[4,128,16,64]{1,3,2,0:T(8,128)S(1)} %bitcast.184, f32[16,64]{1,0:T(8,128)S(1)} %mul.579), kind=kOutput, calls=%fused_computation | output fusion | flops 1056831 | bytes 6295552 | tf_op jit(solution)/shard_map/mul | solution.py:104
  55.4 4.2 %all-to-all-start.3 = ((bf16[128,4,1024]{0,2,1:T(8,128)(2,1)}), bf16[128,4,1024]{0,2,1:T(8,128)(2,1)S(1)}, u32[]{:S(2)}, u32[]{:S(2)}) async-start(bf16[128,4,1024]{0,2,1:T(8,128)(2,1)} %bitcast.196), calls=%async_computation.3 | async-start | bytes 2097152 | tf_op jit(solution)/shard_map/all_to_all | solution.py:65
  59.6 1.4 convert_element_type.113
  60.9 2.9 %copy.232 = f32[4,128,16,64]{3,2,1,0:T(8,128)} copy(f32[4,128,16,64]{1,3,2,0:T(8,128)S(1)} %bitcast.192) | data formatting | bytes 4194304 | tf_op jit(solution)/shard_map/convert_element_type | solution.py:90
  63.9 2.5 %fusion.85 = f32[4,128,16,64]{3,2,1,0:T(8,128)S(1)} fusion(f32[4,128,16,64]{3,2,1,0:T(8,128)} %copy.232), kind=kOutput, calls=%fused_computation.166 | output fusion | flops 66584576 | bytes 4194304 | tf_op jit(solution)/shard_map/jit(cumsum)/reduce_window_sum | solution.py:91
  66.4 2.0 %copy-done.2 = f32[4,128,16,64]{3,2,1,0:T(8,128)} copy-done((f32[4,128,16,64]{3,2,1,0:T(8,128)}, f32[4,128,16,64]{3,2,1,0:T(8,128)S(1)}, u32[]{:S(2)}) %copy-start.2) | copy-done | bytes 2097176
  68.7 11.1 %multiply_multiply_fusion = (f32[4,128,16,64]{3,2,1,0:T(8,128)}, f32[4,128,16,64]{3,2,1,0:T(8,128)}, f32[4,128,16,64]{3,2,1,0:T(8,128)}, f32[4,128,16,64]{3,2,1,0:T(8,128)}) fusion(f32[4,128,16,64]{3,2,1,0:T(8,128)} %copy.236, f32[4,128,16,64]{3,2,1,0:T(8,128)} %copy-done.2, f32[4,128]{1,0:T(4,128)S(1)} %get-tuple-element.47, ...), kind=kLoop, calls=%fused_computation.13 | loop fusion | flops 4194304 | bytes 16797696 | tf_op jit(solution)/shard_map/mul | solution.py:108
  79.9 4.7 %fusion.7 = f32[4,16,64,64]{2,3,1,0:T(8,128)S(1)} fusion(bf16[4,128,16,64]{1,3,2,0:T(8,128)(2,1)S(1)} %bitcast.190, f32[4,128,16,64]{3,2,1,0:T(8,128)} %get-tuple-element.30), kind=kOutput, calls=%fused_computation.8 | convolution fusion | flops 201326592 | bytes 4194304 | tf_op jit(solution)/shard_map/cthd,cthe->chde/dot_general | solution.py:109
  85.3 4.1 %collective-permute-start.1 = (f32[16,65,64]{1,2,0:T(8,128)S(1)}, f32[16,65,64]{1,2,0:T(8,128)S(1)}, u32[]{:S(2)}, u32[]{:S(2)}) collective-permute-start(f32[16,65,64]{1,2,0:T(8,128)S(1)} %pad_maximum_fusion), channel_id=1, source_target_pairs={{0,4},{4,0},{1,5},{5,1},{2,6},{6,2},{3,7},{7,3},{8,12},{12,8},{9,1... | collective-permute-start | bytes 798728 | tf_op jit(solution)/shard_map/ppermute | solution.py:149
  89.4 6.7 %fusion.9 = f32[4,16,128,128]{3,2,1,0:T(8,128)S(1)} fusion(f32[4,128,16,64]{3,2,1,0:T(8,128)S(1)} %copy-done.3, f32[4,128,16,64]{3,2,1,0:T(8,128)S(1)} %copy-done.4), kind=kOutput, calls=%fused_computation.10 | convolution fusion | flops 402653184 | bytes 8388608 | tf_op jit(solution)/shard_map/cthd,cshd->chts/dot_general | solution.py:96
  96.1 3.1 %bitcast_add_fusion.1 = f32[4,128,16,64]{1,3,2,0:T(8,128)S(1)} fusion(f32[4,128,16,64]{1,3,2,0:T(8,128)S(1)} %copy-done.6, bf16[4,128,16,64]{1,3,2,0:T(8,128)(2,1)S(1)} %bitcast.191, f32[4,16,128,128]{3,2,1,0:T(8,128)S(1)} %fusion.9, pred[4,128,128]{2,1,0:T(8,128)(4,1)S(1)} %compare_and_fusion), kind=kOutput, calls=%fused_computation.36 | convolution fusion | flops 405274624 | bytes 9502720 | tf_op jit(solution)/shard_map/chts,cshd->cthd/dot_general | solution.py:102
  99.7 0.8 select_reduce_fusion
  100.7 1.7 collective-permute-start.2
  102.5 5.2 %collective-permute-done.2 = f32[8,65,64]{1,2,0:T(8,128)S(1)} collective-permute-done((f32[8,65,64]{1,2,0:T(8,128)S(1)}, f32[8,65,64]{1,2,0:T(8,128)S(1)}, u32[]{:S(2)}, u32[]{:S(2)}) %collective-permute-start.2) | collective-permute-done | bytes 133152 | tf_op jit(solution)/shard_map/ppermute | solution.py:160
  108.4 22.9 %all-gather = f32[32,65,64]{1,2,0:T(8,128)S(1)} all-gather(f32[8,65,64]{1,2,0:T(8,128)S(1)} %pad_maximum_fusion.1), channel_id=2, replica_groups=mesh['x'=4,'zh'=4,'zl'=2,'core'=2,'head'=4] {'zh'}, dimensions={0}, use_global_device_ids=true | all-gather | bytes 665600 | tf_op jit(solution)/shard_map/all_gather | solution.py:165
  131.3 0.7 select_reduce_fusion.1
  132.3 12.4 %all-gather.1 = f32[32,65,64]{1,2,0:T(8,128)S(1)} all-gather(f32[8,65,64]{1,2,0:T(8,128)S(1)} %pad_maximum_fusion.2), channel_id=3, replica_groups=mesh['x'=4,'zh'=4,'zl'=2,'core'=2,'head'=4] {'x'}, dimensions={0}, use_global_device_ids=true | all-gather | bytes 665600 | tf_op jit(solution)/shard_map/all_gather | solution.py:165
  144.7 0.6 slice_reduce_fusion.3
  145.8 8.4 %collective-permute-start.3 = (f32[8,64,64]{1,2,0:T(8,128)S(1)}, f32[8,64,64]{1,2,0:T(8,128)S(1)}, u32[]{:S(2)}, u32[]{:S(2)}) collective-permute-start(f32[8,64,64]{1,2,0:T(8,128)S(1)} %fusion.66), channel_id=1, source_target_pairs={{0,4},{4,0},{1,5},{5,1},{2,6},{6,2},{3,7},{7,3},{8,12},{12,8},{9,1... | collective-permute-start | bytes 393224 | tf_op jit(solution)/shard_map/ppermute | solution.py:173
  154.6 0.7 collective-permute-done.3
  155.6 5.1 %fusion.84 = (f32[4,128,16]{1,2,0:T(8,128)S(1)}, f32[4,128,16,64]{1,3,2,0:T(8,128)S(1)}) fusion(f32[4,128,16,64]{1,3,2,0:T(8,128)S(1)} %bitcast_add_fusion.1, f32[4,128,16,64]{3,2,1,0:T(8,128)S(1)} %copy-done.5, f32[1,16,64,64]{2,3,1,0:T(8,128)S(1)} %get-tuple-element.23, f32[1,16,64,64]{2,3,1,0:T(8,128)S(1)} %get-tuple-element.24, ...), kind=kOutput, calls=%fused_computation.165 | convolution fusion | flops 203677696 | bytes 7651328 | tf_op jit(solution)/shard_map/cthd,chde->cthe/dot_general | solution.py:185
  160.7 0.5 multiply_reduce_fusion
  161.3 0.6 add_convert_fusion
  161.9 18.9 %all_to_all.68 = bf16[4,128,1024]{1,2,0:T(8,128)(2,1)S(1)} all-to-all(bf16[4,128,1024]{1,2,0:T(8,128)(2,1)S(1)} %bitcast.194), channel_id=1, replica_groups=mesh['x'=4,'zh'=4,'zl'=2,'core'=2,'head'=4] {'head'}, dimensions={0} | all-to-all | bytes 2097152 | tf_op jit(solution)/shard_map/all_to_all | solution.py:197
  180.9 1.9 copy.253
  182.8 3.4 %fusion.29 = bf16[128,4096]{1,0:T(8,128)(2,1)} fusion(f32[128,4096]{1,0:T(8,128)} %copy.253, bf16[128,4096]{1,0:T(8,128)(2,1)} %param.16), kind=kLoop, calls=%fused_computation.44 | loop fusion | flops 3670016 | bytes 4194304 | tf_op jit(solution)/shard_map/convert_element_type | solution.py:198
  (71 shorter events, 5.1 us)
Async XLA Ops:
  0.0 33.7 %copy-start = (bf16[128,4096]{1,0:T(8,128)(2,1)S(1)}, bf16[128,4096]{1,0:T(8,128)(2,1)}, u32[]{:S(2)}) copy-start(bf16[128,4096]{1,0:T(8,128)(2,1)} %param.22) | copy-start | bytes 3145732
  0.0 11.7 %copy-start.11 = (bf16[128,4096]{1,0:T(8,128)(2,1)S(1)}, bf16[128,4096]{1,0:T(8,128)(2,1)}, u32[]{:S(2)}) copy-start(bf16[128,4096]{1,0:T(8,128)(2,1)} %param.14) | copy-start | bytes 3145732
  2.4 18.5 %all-to-all-start = ((bf16[128,4,1024]{0,2,1:T(8,128)(2,1)}), bf16[128,4,1024]{0,2,1:T(8,128)(2,1)S(1)}, u32[]{:S(2)}, u32[]{:S(2)}) async-start(bf16[128,4,1024]{0,2,1:T(8,128)(2,1)} %bitcast.1), calls=%async_computation | async-start | bytes 2097152 | tf_op jit(solution)/shard_map/all_to_all | solution.py:63
  8.3 25.4 %collective-permute-start = (bf16[1,4096]{1,0:T(2,128)(2,1)S(1)}, bf16[1,4096]{1,0:T(2,128)(2,1)S(1)}, u32[]{:S(2)}, u32[]{:S(2)}) collective-permute-start(bf16[1,4096]{1,0:T(2,128)(2,1)S(1)} %slice.120), channel_id=1, source_target_pairs={{0,1},{1,2},{2,3},{3,4},{4,5},{5,6},{6,7},{7,8},{8,9},{9,10},{10,1... | collective-permute-start | bytes 24584 | tf_op jit(solution)/shard_map/ppermute | solution.py:18
  20.9 12.7 %copy-start.7 = (bf16[128,4,1024]{0,2,1:T(8,128)(2,1)}, bf16[128,4,1024]{0,2,1:T(8,128)(2,1)S(1)}, u32[]{:S(2)}) copy-start(bf16[128,4,1024]{0,2,1:T(8,128)(2,1)S(1)} %all-to-all-done) | copy-start | bytes 3145732
  20.9 12.7 %copy-start.12 = (f32[4096]{0:T(1024)S(1)}, f32[4096]{0:T(1024)}, u32[]{:S(2)}) copy-start(f32[4096]{0:T(1024)} %param.20) | copy-start | bytes 49156
  20.9 12.7 %copy-start.13 = (f32[4096]{0:T(1024)S(1)}, f32[4096]{0:T(1024)}, u32[]{:S(2)}) copy-start(f32[4096]{0:T(1024)} %param.19) | copy-start | bytes 49156
  20.9 17.4 %all-to-all-start.2 = ((bf16[128,4,1024]{0,2,1:T(8,128)(2,1)}), bf16[128,4,1024]{0,2,1:T(8,128)(2,1)S(1)}, u32[]{:S(2)}, u32[]{:S(2)}) async-start(bf16[128,4,1024]{0,2,1:T(8,128)(2,1)} %bitcast.195), calls=%async_computation.2 | async-start | bytes 2097152 | tf_op jit(solution)/shard_map/all_to_all | solution.py:64
  37.0 6.5 %copy-start.8 = (bf16[128,4,1024]{0,2,1:T(8,128)(2,1)S(1)}, bf16[128,4,1024]{0,2,1:T(8,128)(2,1)}, u32[]{:S(2)}) copy-start(bf16[128,4,1024]{0,2,1:T(8,128)(2,1)} %copy-done.7) | copy-start | bytes 3145732
  38.3 5.0 %copy-start.9 = (bf16[128,4,1024]{0,2,1:T(8,128)(2,1)}, bf16[128,4,1024]{0,2,1:T(8,128)(2,1)S(1)}, u32[]{:S(2)}) copy-start(bf16[128,4,1024]{0,2,1:T(8,128)(2,1)S(1)} %all-to-all-done.2) | copy-start | bytes 3145732
  38.3 17.1 %all-to-all-start.1 = ((bf16[128,4,1024]{0,2,1:T(8,128)(2,1)}), bf16[128,4,1024]{0,2,1:T(8,128)(2,1)}, u32[]{:S(2)}, u32[]{:S(2)}) async-start(bf16[128,4,1024]{0,2,1:T(8,128)(2,1)} %bitcast.5), calls=%async_computation.1 | async-start | bytes 2097152 | tf_op jit(solution)/shard_map/all_to_all | solution.py:66
  43.6 2.9 %copy-start.10 = (bf16[128,4,1024]{0,2,1:T(8,128)(2,1)S(1)}, bf16[128,4,1024]{0,2,1:T(8,128)(2,1)}, u32[]{:S(2)}) copy-start(bf16[128,4,1024]{0,2,1:T(8,128)(2,1)} %copy-done.9) | copy-start | bytes 3145732
  55.4 24.5 %all-to-all-start.3 = ((bf16[128,4,1024]{0,2,1:T(8,128)(2,1)}), bf16[128,4,1024]{0,2,1:T(8,128)(2,1)S(1)}, u32[]{:S(2)}, u32[]{:S(2)}) async-start(bf16[128,4,1024]{0,2,1:T(8,128)(2,1)} %bitcast.196), calls=%async_computation.3 | async-start | bytes 2097152 | tf_op jit(solution)/shard_map/all_to_all | solution.py:65
  66.4 2.0 %copy-start.2 = (f32[4,128,16,64]{3,2,1,0:T(8,128)}, f32[4,128,16,64]{3,2,1,0:T(8,128)S(1)}, u32[]{:S(2)}) copy-start(f32[4,128,16,64]{3,2,1,0:T(8,128)S(1)} %fusion.85) | copy-start | bytes 6291460
  79.9 9.5 %copy-start.4 = (f32[4,128,16,64]{3,2,1,0:T(8,128)S(1)}, f32[4,128,16,64]{3,2,1,0:T(8,128)}, u32[]{:S(2)}) copy-start(f32[4,128,16,64]{3,2,1,0:T(8,128)} %get-tuple-element.33) | copy-start | bytes 6291460
  84.6 4.8 %copy-start.3 = (f32[4,128,16,64]{3,2,1,0:T(8,128)S(1)}, f32[4,128,16,64]{3,2,1,0:T(8,128)}, u32[]{:S(2)}) copy-start(f32[4,128,16,64]{3,2,1,0:T(8,128)} %get-tuple-element.31) | copy-start | bytes 6291460
  85.3 14.2 %collective-permute-start.1 = (f32[16,65,64]{1,2,0:T(8,128)S(1)}, f32[16,65,64]{1,2,0:T(8,128)S(1)}, u32[]{:S(2)}, u32[]{:S(2)}) collective-permute-start(f32[16,65,64]{1,2,0:T(8,128)S(1)} %pad_maximum_fusion), channel_id=1, source_target_pairs={{0,4},{4,0},{1,5},{5,1},{2,6},{6,2},{3,7},{7,3},{8,12},{12,8},{9,1... | collective-permute-start | bytes 798728 | tf_op jit(solution)/shard_map/ppermute | solution.py:149
  89.4 6.7 %copy-start.6 = (f32[4,128,16,64]{1,3,2,0:T(8,128)S(1)}, f32[4,128,16,64]{1,3,2,0:T(8,128)}, u32[]{:S(2)}) copy-start(f32[4,128,16,64]{1,3,2,0:T(8,128)} %fusion) | copy-start | bytes 6291460
  100.7 7.0 %collective-permute-start.2 = (f32[8,65,64]{1,2,0:T(8,128)S(1)}, f32[8,65,64]{1,2,0:T(8,128)S(1)}, u32[]{:S(2)}, u32[]{:S(2)}) collective-permute-start(f32[8,65,64]{1,2,0:T(8,128)S(1)} %fusion.60), channel_id=1, source_target_pairs={{0,8},{8,0},{1,9},{9,1},{2,10},{10,2},{3,11},{11,3},{4,12},{12,4},... | collective-permute-start | bytes 399368 | tf_op jit(solution)/shard_map/ppermute | solution.py:160
  145.8 9.8 %copy-start.5 = (f32[4,128,16,64]{3,2,1,0:T(8,128)S(1)}, f32[4,128,16,64]{3,2,1,0:T(8,128)}, u32[]{:S(2)}) copy-start(f32[4,128,16,64]{3,2,1,0:T(8,128)} %get-tuple-element.32) | copy-start | bytes 6291460
  145.8 9.5 %collective-permute-start.3 = (f32[8,64,64]{1,2,0:T(8,128)S(1)}, f32[8,64,64]{1,2,0:T(8,128)S(1)}, u32[]{:S(2)}, u32[]{:S(2)}) collective-permute-start(f32[8,64,64]{1,2,0:T(8,128)S(1)} %fusion.66), channel_id=1, source_target_pairs={{0,4},{4,0},{1,5},{5,1},{2,6},{6,2},{3,7},{7,3},{8,12},{12,8},{9,1... | collective-permute-start | bytes 393224 | tf_op jit(solution)/shard_map/ppermute | solution.py:173
  180.9 5.3 %copy-start.1 = (bf16[128,4096]{1,0:T(8,128)(2,1)S(1)}, bf16[128,4096]{1,0:T(8,128)(2,1)}, u32[]{:S(2)}) copy-start(bf16[128,4096]{1,0:T(8,128)(2,1)} %param.22) | copy-start | bytes 3145732
